TPU v7x, 32 devices: a whole 2x2x4 slice. The times are simulated.
32 devices in a mesh: seq: 4 (over y, x), tp: 8 (over z, core).
Axes of the slice: x: 2, y: 2, z: 4, core: 2. Of those that a mesh axis runs over, the one named last changes fastest.
Arguments:
- streams: bfloat16 [3, 4096, 1024], P(None, 'tp', 'seq'), may hold values from -6 to 6
- feat_weight: float32 [3, 4096, 7], P(None, 'tp'), may hold values from -2 to 2
- long_filter: float32 [4096, 128], P('tp'), may hold values from -0.5 to 0.5
- skip_gain: float32 [4096], P('tp'), may hold values from -1 to 1
- out_weight: bfloat16 [4096, 4096], P('tp', 'seq'), may hold values from -0.125 to 0.125
- out_grad: bfloat16 [4096, 1024], P('tp', 'seq'), may hold values from -6 to 6
Outputs:
- mixed: bfloat16 [4096, 1024], P('tp', 'seq')
- stream_grad: bfloat16 [3, 4096, 1024], P(None, 'tp', 'seq')
- weight_grad: bfloat16 [4096, 4096], P('tp', 'seq')
All inputs are finite; a program needn't handle non-finite values.
Results may differ from a plain program's by a relative error of at most 0.009.
Values may be sent and summed in bfloat16 or wider, within the bound.
No kernel may reach another device: no remote copies, remote signals or barrier semaphores. Data moves between devices by JAX's collectives and lax.ppermute only.
A program may use at most 64 MiB of HBM per device.

v0:
```python
import math

import jax
import jax.numpy as jnp
from jax import lax
from jax.sharding import PartitionSpec as P


def extended(block, sides, width):
    for axis, dim in sides:
        count = lax.axis_size(axis)
        forward = [(i, i + 1) for i in range(count - 1)]
        backward = [(target, source) for source, target in forward]
        low = lax.ppermute(
            lax.slice_in_dim(block, block.shape[dim] - width, None, axis=dim), axis, forward
        )
        high = lax.ppermute(lax.slice_in_dim(block, 0, width, axis=dim), axis, backward)
        block = jnp.concatenate([low, block, high], axis=dim)
    return block


def from_behind(block, axis, distance):
    devices = range(lax.axis_size(axis))
    route = [(i - distance, i) for i in devices if i - distance in devices]
    return lax.ppermute(block, axis, route)


def correlate(signal, taps):
    return lax.conv_general_dilated(
        signal[None],
        taps[:, None, :],
        (1,),
        "VALID",
        dimension_numbers=("NCH", "OIH", "NCH"),
        feature_group_count=signal.shape[0],
        precision=lax.Precision.HIGHEST,
    )[0]


def shards(streams, feat_weight, long_filter, skip_gain, out_weight, out_grad):
    channels = streams.shape[1]
    length = streams.shape[2]
    taps_long = long_filter.shape[1]
    taps_short = feat_weight.shape[2]
    reach = taps_long + taps_short - 2
    widened = extended(streams, (("seq", 2),), reach).astype(jnp.float32)
    short_taps = feat_weight.reshape(3 * channels, taps_short)
    feats = correlate(
        widened.reshape(3 * channels, length + 2 * reach), short_taps[:, ::-1]
    ).reshape(3, channels, -1)
    query_feat, key_feat, value_feat = (feats[0], feats[1], feats[2])
    product = key_feat * value_feat
    convolved = correlate(product, long_filter[:, ::-1])
    summed = convolved + skip_gain[:, None] * product[:, taps_long - 1 :]
    query_tail = query_feat[:, taps_long - 1 :]
    gated = (query_tail[:, :length] * summed[:, :length]).astype(jnp.bfloat16)
    weight_rows = lax.all_gather(out_weight, "seq", axis=1, tiled=True)
    part = weight_rows
    output_sum = lax.psum_scatter(
        lax.dot_general(part, gated, (((0,), (0,)), ((), ())), preferred_element_type=jnp.float32),
        "tp",
        scatter_dimension=0,
        tiled=True,
    )
    mixed = output_sum.astype(jnp.bfloat16)
    scale = 1.0 / math.sqrt(length * lax.axis_size("seq"))
    full_width = weight_rows.shape[1]
    piece = lax.all_gather(out_grad, "tp", axis=0, tiled=True)
    weight_part = jnp.zeros((channels, full_width), jnp.bfloat16)
    part = weight_rows
    gathered_grad = jnp.dot(part, piece, preferred_element_type=jnp.float32)
    block = (
        lax.dot_general(gated, piece, (((1,), (1,)), ((), ())), preferred_element_type=jnp.float32)
        * scale
    ).astype(jnp.bfloat16)
    weight_part = lax.dynamic_update_slice_in_dim(weight_part, block, jnp.int32(0), 1)
    gated_grad, weight_part = (gathered_grad, weight_part)
    weight_part = lax.optimization_barrier(weight_part)
    weight_grad = lax.psum_scatter(
        weight_part.astype(jnp.float32).astype(jnp.bfloat16), "seq", scatter_dimension=1, tiled=True
    )
    next_grad = from_behind(gated_grad[:, :reach].astype(jnp.bfloat16), "seq", -1).astype(
        jnp.float32
    )
    grad_ext = jnp.concatenate([gated_grad, next_grad], axis=1)
    conv_grad = grad_ext * query_tail
    keep = length + taps_short - 1
    prod_grad = correlate(conv_grad, long_filter) + skip_gain[:, None] * conv_grad[:, :keep]
    query_grad = grad_ext[:, :keep] * summed[:, :keep]
    key_grad = prod_grad * value_feat[:, taps_long - 1 : taps_long - 1 + keep]
    value_grad = prod_grad * key_feat[:, taps_long - 1 : taps_long - 1 + keep]
    feat_grad = jnp.stack([query_grad, key_grad, value_grad]).reshape(3 * channels, keep)
    stream_grad = correlate(feat_grad, short_taps).reshape(3, channels, length).astype(jnp.bfloat16)
    return (mixed, stream_grad, weight_grad)


def solution(mesh):
    return jax.shard_map(
        shards,
        mesh=mesh,
        in_specs=(
            P(None, "tp", "seq"),
            P(None, "tp", None),
            P("tp", None),
            P("tp"),
            P("tp", "seq"),
            P("tp", "seq"),
        ),
        out_specs=(P("tp", "seq"), P(None, "tp", "seq"), P("tp", "seq")),
        check_vma=False,
    )
```

profile of v0, /device:TPU:27, one launch (start us, length us, event | category | flops | bytes accessed | tf_op | source)
XLA Modules:
  0.0 216.7 jit_solution(10533259813248823851)
XLA Ops:
  8.9 2.2 collective-permute-start.1
  12.1 4.0 %collective-permute-start = (bf16[3,512,133]{1,2,0:T(8,128)(2,1)}, bf16[3,512,133]{1,2,0:T(8,128)(2,1)S(1)}, u32[]{:S(2)}, u32[]{:S(2)}) collective-permute-start(bf16[3,512,133]{1,2,0:T(8,128)(2,1)} %copy.73), channel_id=1, source_target_pairs={{0,8},{8,16},{16,24},{1,9},{9,17},{17,25},{2,10},{10,18},{18,26},{... | collective-permute-start | bytes 1225736 | tf_op jit(solution)/shard_map/ppermute | solution.py:14
  18.4 4.5 %collective-permute-done.1 = bf16[3,512,133]{1,2,0:T(8,128)(2,1)S(1)} collective-permute-done((bf16[3,512,133]{1,2,0:T(8,128)(2,1)S(1)}, bf16[3,512,133]{1,2,0:T(8,128)(2,1)S(1)}, u32[]{:S(2)}, u32[]{:S(2)}) %collective-permute-start.1) | collective-permute-done | bytes 408608 | tf_op jit(solution)/shard_map/ppermute | solution.py:17
  23.2 14.0 %collective-permute-done = bf16[3,512,133]{1,2,0:T(8,128)(2,1)S(1)} collective-permute-done((bf16[3,512,133]{1,2,0:T(8,128)(2,1)}, bf16[3,512,133]{1,2,0:T(8,128)(2,1)S(1)}, u32[]{:S(2)}, u32[]{:S(2)}) %collective-permute-start) | collective-permute-done | bytes 408608 | tf_op jit(solution)/shard_map/ppermute | solution.py:14
  38.3 2.1 pad_maximum_fusion
  40.4 2.3 %copy.53 = bf16[1536,1,522]{0,2,1:T(8,128)(2,1)} copy(bf16[1536,1,522]{2,0,1:T(8,128)(2,1)S(1)} %bitcast.61) | data formatting | bytes 3207168 | tf_op jit(solution)/shard_map/broadcast_in_dim;reshape | solution.py:30
  42.7 1.5 pad
  45.5 1.7 convolution_select_fusion
  50.5 1.9 copy.60
  54.1 2.3 %reshape.51 = f32[1,528,512]{2,0,1:T(1,128)} reshape(f32[8,66,512]{2,1,0:T(8,128)S(1)} %copy.57) | data formatting | bytes 2162688 | tf_op jit(solution)/shard_map/mul | solution.py:52
  59.8 1.6 slice_bitcast_fusion
  61.4 21.2 %fusion.36 = f32[1,512,389]{1,0,2:T(1,128)S(1)} fusion(f32[1,528,512]{2,0,1:T(1,128)S(1)} %copy-done.5, f32[512,1,128]{0,1,2:T(1,128)S(1)} %copy-done.8), kind=kOutput, calls=%fused_computation.57 | convolution fusion | flops 305922048 | bytes 2140160 | tf_op jit(solution)/shard_map/conv_general_dilated | solution.py:29
  84.0 5.5 %convolution_bitcast_fusion = f32[4096,256]{0,1:T(8,128)} fusion(bf16[512,256]{0,1:T(8,128)(2,1)S(1)} %fusion.26, bf16[512,4096]{1,0:T(8,128)(2,1)} %all-gather.3.cloned.1.call-done), kind=kOutput, calls=%fused_computation.1 | convolution fusion | flops 1073741824 | bytes 8650752 | tf_op jit(solution)/shard_map/dot_general | solution.py:60
  89.7 13.3 %all-gather.5.cloned.1.call-done = bf16[4096,256]{1,0:T(8,128)(2,1)} async-done(((bf16[512,256]{1,0:T(8,128)(2,1)}), bf16[4096,256]{1,0:T(8,128)(2,1)}) %all-gather.5.cloned.1.call-update) | async-done | bytes 2097168 | tf_op jit(solution)/shard_map/all_gather | solution.py:68
  103.0 4.9 %multiply_convert_fusion = bf16[512,4096]{1,0:T(8,128)(2,1)} fusion(bf16[512,256]{0,1:T(8,128)(2,1)S(1)} %fusion.26, bf16[4096,256]{1,0:T(8,128)(2,1)} %all-gather.5.cloned.1.call-done), kind=kOutput, calls=%fused_computation | convolution fusion | flops 1077936128 | bytes 6553600 | tf_op jit(solution)/shard_map/dot_general | solution.py:73
  108.0 4.2 %fusion.37 = f32[512,256]{0,1:T(8,128)S(1)} fusion(bf16[512,4096]{1,0:T(8,128)(2,1)} %all-gather.3.cloned.1.call-done, bf16[4096,256]{1,0:T(8,128)(2,1)} %all-gather.5.cloned.1.call-done), kind=kOutput, calls=%fused_computation.58 | convolution fusion | flops 1073741824 | bytes 6815744 | tf_op jit(solution)/shard_map/dot_general | solution.py:71
  113.6 2.2 %collective-permute-start.2 = (bf16[512,133]{0,1:T(8,128)(2,1)}, bf16[512,133]{0,1:T(8,128)(2,1)}, u32[]{:S(2)}, u32[]{:S(2)}) collective-permute-start(bf16[512,133]{0,1:T(8,128)(2,1)} %slice.138), channel_id=1, source_target_pairs={{8,0},{16,8},{24,16},{9,1},{17,9},{25,17},{10,2},{18,10},{26,18},{... | collective-permute-start | bytes 408584 | tf_op jit(solution)/shard_map/ppermute | solution.py:25
  116.7 5.0 %collective-permute-done.2 = bf16[512,133]{0,1:T(8,128)(2,1)} collective-permute-done((bf16[512,133]{0,1:T(8,128)(2,1)}, bf16[512,133]{0,1:T(8,128)(2,1)}, u32[]{:S(2)}, u32[]{:S(2)}) %collective-permute-start.2) | collective-permute-done | bytes 136224 | tf_op jit(solution)/shard_map/ppermute | solution.py:25
  124.2 5.4 %fusion.18 = f32[1,512,262]{1,0,2:T(1,128)S(1)} fusion(f32[512,1,128]{0,1,2:T(1,128)S(1)} %copy-done.9, f32[1,512,389]{1,2,0:T(8,128)S(1)} %bitcast.62), kind=kOutput, calls=%fused_computation.32 | convolution fusion | flops 206045184 | bytes 1595392 | tf_op jit(solution)/shard_map/conv_general_dilated | solution.py:29
  131.1 2.4 %reshape.45 = f32[1536,1,262]{0,2,1:T(8,128)} reshape(f32[3,512,262]{1,0,2:T(4,128)S(1)} %copy.64) | data formatting | bytes 3219456 | tf_op jit(solution)/shard_map/broadcast_in_dim;reshape | solution.py:30
  133.5 1.6 pad.2
  135.1 1.9 reshape.31
  141.1 12.1 %reduce-scatter.3.cloned.1.call-done = f32[512,256]{0,1:T(8,128)} async-done(((f32[4096,256]{0,1:T(8,128)}), f32[512,256]{0,1:T(8,128)}) %reduce-scatter.3.cloned.1.call-update) | async-done | bytes 524304 | tf_op jit(solution)/shard_map/reduce_scatter | solution.py:59
  155.2 55.0 %reduce-scatter.5.cloned.1.call-done = bf16[512,1024]{1,0:T(8,128)(2,1)} async-done(((bf16[512,4096]{1,0:T(8,128)(2,1)}), bf16[512,1024]{1,0:T(8,128)(2,1)}) %reduce-scatter.5.cloned.1.call-update) | async-done | bytes 1048592 | tf_op jit(solution)/shard_map/reduce_scatter | solution.py:79
  (80 shorter events, 29.8 us)
Async XLA Ops:
  7.2 1.1 copy-start
  7.2 76.8 %all-gather.3.cloned.1.call-start = ((), (), s32[]{:S(2)}) async-start(), calls=%async_computation.2 | async-start | bytes 5242880 | tf_op jit(solution)/shard_map/all_gather | solution.py:57
  7.9 95.1 %all-gather.5.cloned.1.call-start = ((), (), s32[]{:S(2)}) async-start(), calls=%async_computation.4 | async-start | bytes 2359296 | tf_op jit(solution)/shard_map/all_gather | solution.py:68
  8.7 7.5 %copy-start.10 = (f32[3,512,7]{1,2,0:T(8,128)S(1)}, f32[3,512,7]{1,2,0:T(8,128)}, u32[]{:S(2)}) copy-start(f32[3,512,7]{1,2,0:T(8,128)} %param.7) | copy-start | bytes 129028
  8.7 8.5 %copy-start.6 = (f32[512,128]{1,0:T(8,128)S(1)}, f32[512,128]{1,0:T(8,128)}, u32[]{:S(2)}) copy-start(f32[512,128]{1,0:T(8,128)} %param.8) | copy-start | bytes 786436
  8.9 14.0 %collective-permute-start.1 = (bf16[3,512,133]{1,2,0:T(8,128)(2,1)S(1)}, bf16[3,512,133]{1,2,0:T(8,128)(2,1)S(1)}, u32[]{:S(2)}, u32[]{:S(2)}) collective-permute-start(bf16[3,512,133]{1,2,0:T(8,128)(2,1)S(1)} %copy.74), channel_id=1, source_target_pairs={{8,0},{16,8},{24,16},{9,1},{17,9},{25,17},{10,2},{18,10},{26,18},{... | collective-permute-start | bytes 1225736 | tf_op jit(solution)/shard_map/ppermute | solution.py:17
  12.1 25.0 %collective-permute-start = (bf16[3,512,133]{1,2,0:T(8,128)(2,1)}, bf16[3,512,133]{1,2,0:T(8,128)(2,1)S(1)}, u32[]{:S(2)}, u32[]{:S(2)}) collective-permute-start(bf16[3,512,133]{1,2,0:T(8,128)(2,1)} %copy.73), channel_id=1, source_target_pairs={{0,8},{8,16},{16,24},{1,9},{9,17},{17,25},{2,10},{10,18},{18,26},{... | collective-permute-start | bytes 1225736 | tf_op jit(solution)/shard_map/ppermute | solution.py:14
  16.1 137.1 %reduce-scatter.3.cloned.1.call-start = ((), (), s32[]{:S(2)}) async-start(), calls=%async_computation.3 | async-start | bytes 4718592 | tf_op jit(solution)/shard_map/reduce_scatter | solution.py:59
  44.8 0.8 copy-start.12
  44.8 0.8 copy-start.14
  58.2 1.6 copy-start.2
  59.8 1.6 copy-start.5
  59.8 1.6 copy-start.8
  61.4 21.3 %copy-start.13 = (f32[512]{0:T(512)S(1)}, f32[512]{0:T(512)}, u32[]{:S(2)}) copy-start(f32[512]{0:T(512)} %param.9) | copy-start | bytes 6148
  82.9 0.9 copy-start.1
  89.5 120.7 %reduce-scatter.5.cloned.1.call-start = ((), (), s32[]{:S(2)}) async-start(), calls=%async_computation.5 | async-start | bytes 5242880 | tf_op jit(solution)/shard_map/reduce_scatter | solution.py:79
  107.9 7.9 %copy-start.7 = (f32[512,128]{1,0:T(8,128)S(1)}, f32[512,128]{1,0:T(8,128)}, u32[]{:S(2)}) copy-start(f32[512,128]{1,0:T(8,128)} %param.8) | copy-start | bytes 786436
  112.2 0.8 copy-start.3
  113.6 8.0 %collective-permute-start.2 = (bf16[512,133]{0,1:T(8,128)(2,1)}, bf16[512,133]{0,1:T(8,128)(2,1)}, u32[]{:S(2)}, u32[]{:S(2)}) collective-permute-start(bf16[512,133]{0,1:T(8,128)(2,1)} %slice.138), channel_id=1, source_target_pairs={{8,0},{16,8},{24,16},{9,1},{17,9},{25,17},{10,2},{18,10},{26,18},{... | collective-permute-start | bytes 408584 | tf_op jit(solution)/shard_map/ppermute | solution.py:25
  116.7 7.3 %copy-start.4 = (f32[512,256]{0,1:T(8,128)S(1)}, f32[512,256]{0,1:T(8,128)}, u32[]{:S(2)}) copy-start(f32[512,256]{0,1:T(8,128)} %copy-done.3) | copy-start | bytes 1572868
  122.6 1.6 copy-start.9
  137.1 0.8 copy-start.11
  137.1 0.8 copy-start.15
Sparse Core Ops, SparseCore 0:
  9.8 63.3 all-gather.2
  74.8 28.1 all-gather.4
  105.3 47.9 reduce-scatter.2
  156.7 53.4 reduce-scatter.4
where the time goes:
time: 219 us; the launch traced here: 217 us
  waiting for transfers between devices  105 us (48%)
  matrix products  44.5 us (20%)
  local copies, waits for them, and re-layouts  36.9 us (17%)
  between operations  14.2 us (6%)
  starting transfers between devices  8.69 us (4%)
  other arithmetic  7.82 us (4%)
    reduce_scatter x1, waiting for transfers between devices, shards(): lax.psum_scatter(weight_part.astype(jnp.float32).astype(jnp.bfloat16), 's...  55 us
    conv_general_dilated x4, matrix products, correlate(): lax.conv_general_dilated(signal[None], taps[:, None, :], (1,), 'VALID', d...  29.9 us
    ppermute x1, waiting for transfers between devices, extended(): lax.ppermute(lax.slice_in_dim(block, block.shape[dim] - width, None, axis...  14 us
    all_gather x1, waiting for transfers between devices, shards(): piece = lax.all_gather(out_grad, 'tp', axis=0, tiled=True)  13.3 us
    reduce_scatter x1, waiting for transfers between devices, shards(): lax.psum_scatter(lax.dot_general(part, gated, (((0,), (0,)), ((), ())), p...  12.1 us
    conv_general_dilated x12, local copies, waits for them, and re-layouts, correlate(): lax.conv_general_dilated(signal[None], taps[:, None, :], (1,), 'VALID', d...  9.75 us
    another operation x4, local copies, waits for them, and re-layouts, correlate(): signal[None]  7.84 us
    dot_general x1, matrix products, shards(): lax.dot_general(part, gated, (((0,), (0,)), ((), ())), preferred_element_...  5.5 us
  transfers between devices with their start and end apart: 7, of which 6 were waited for; matrix products, arithmetic and copies ran while one was open for 40% of the time, Pallas kernels for 0%

commit v1 on v0

--- a/solution.py
+++ b/solution.py
@@ -37,12 +37,35 @@
     )[0]
 
 
+def rows_of_slab(out_grad, n_seq, n_tp):
+    rows, length = out_grad.shape
+    piece = rows // n_seq
+    split = out_grad.reshape(n_seq, piece, length)
+    mine = lax.all_to_all(split, "seq", 0, 0)
+    mine = jnp.transpose(mine, (1, 0, 2)).reshape(piece, n_seq * length)
+    route = []
+    for a in range(n_seq):
+        for b in range(n_tp):
+            flat = n_seq * b + a
+            route.append((a * n_tp + b, (flat // n_tp) * n_tp + flat % n_tp))
+    moved = lax.ppermute(mine, ("seq", "tp"), route)
+    return lax.all_gather(moved, "tp", axis=0, tiled=True)
+
+
 def shards(streams, feat_weight, long_filter, skip_gain, out_weight, out_grad):
     channels = streams.shape[1]
     length = streams.shape[2]
     taps_long = long_filter.shape[1]
     taps_short = feat_weight.shape[2]
+    n_seq = lax.axis_size("seq")
+    n_tp = lax.axis_size("tp")
     reach = taps_long + taps_short - 2
+
+    slab_grad = rows_of_slab(out_grad, n_seq, n_tp)
+    slab_width = slab_grad.shape[0]
+    partial_grad = jnp.dot(out_weight, slab_grad, preferred_element_type=jnp.float32)
+    gated_grad = lax.psum_scatter(partial_grad, "seq", scatter_dimension=1, tiled=True)
+
     widened = extended(streams, (("seq", 2),), reach).astype(jnp.float32)
     short_taps = feat_weight.reshape(3 * channels, taps_short)
     feats = correlate(
@@ -54,31 +77,35 @@
     summed = convolved + skip_gain[:, None] * product[:, taps_long - 1 :]
     query_tail = query_feat[:, taps_long - 1 :]
     gated = (query_tail[:, :length] * summed[:, :length]).astype(jnp.bfloat16)
-    weight_rows = lax.all_gather(out_weight, "seq", axis=1, tiled=True)
-    part = weight_rows
-    output_sum = lax.psum_scatter(
-        lax.dot_general(part, gated, (((0,), (0,)), ((), ())), preferred_element_type=jnp.float32),
-        "tp",
-        scatter_dimension=0,
-        tiled=True,
+
+    gated_all = lax.all_gather(gated, "seq", axis=1, tiled=True)
+    partial_out = lax.dot_general(
+        out_weight, gated_all, (((0,), (0,)), ((), ())), preferred_element_type=jnp.float32
     )
-    mixed = output_sum.astype(jnp.bfloat16)
-    scale = 1.0 / math.sqrt(length * lax.axis_size("seq"))
-    full_width = weight_rows.shape[1]
-    piece = lax.all_gather(out_grad, "tp", axis=0, tiled=True)
-    weight_part = jnp.zeros((channels, full_width), jnp.bfloat16)
-    part = weight_rows
-    gathered_grad = jnp.dot(part, piece, preferred_element_type=jnp.float32)
-    block = (
-        lax.dot_general(gated, piece, (((1,), (1,)), ((), ())), preferred_element_type=jnp.float32)
-        * scale
-    ).astype(jnp.bfloat16)
-    weight_part = lax.dynamic_update_slice_in_dim(weight_part, block, jnp.int32(0), 1)
-    gated_grad, weight_part = (gathered_grad, weight_part)
-    weight_part = lax.optimization_barrier(weight_part)
-    weight_grad = lax.psum_scatter(
-        weight_part.astype(jnp.float32).astype(jnp.bfloat16), "seq", scatter_dimension=1, tiled=True
+    group = n_tp // n_seq
+    out_rows = slab_width // group
+    partial_out = (
+        partial_out.reshape(group, out_rows, n_seq, length)
+        .transpose(0, 2, 1, 3)
+        .reshape(n_tp * out_rows, length)
     )
+    output_sum = lax.psum_scatter(partial_out, "tp", scatter_dimension=0, tiled=True)
+    route = []
+    for s in range(n_seq):
+        for p in range(n_tp):
+            route.append((s * n_tp + p, (p % n_seq) * n_tp + group * s + p // n_seq))
+    mixed = lax.ppermute(output_sum.astype(jnp.bfloat16), ("seq", "tp"), route)
+
+    scale = 1.0 / math.sqrt(length * n_seq)
+    terms = lax.dot_general(
+        gated_all.reshape(channels, n_seq, length),
+        slab_grad.reshape(slab_width, n_seq, length),
+        (((2,), (2,)), ((1,), (1,))),
+        preferred_element_type=jnp.float32,
+    )
+    terms = lax.reduce_precision(terms * scale, exponent_bits=8, mantissa_bits=7)
+    weight_grad = jnp.sum(terms, axis=0).astype(jnp.bfloat16)
+
     next_grad = from_behind(gated_grad[:, :reach].astype(jnp.bfloat16), "seq", -1).astype(
         jnp.float32
     )

time: 219 us -> 243 us (1.11)
  local copies, waits for them, and re-layouts: 36.9 us -> 60.1 us
  starting transfers between devices: 8.69 us -> 19.1 us
  waiting for transfers between devices: 105 us -> 96.2 us
    reduce_scatter x2, waiting for transfers between devices: 67.1 us -> 41 us  [the longest x1 22.3 us: shards(): lax.psum_scatter(partial_out, 'tp', scatter_dimension=0, tiled=True)]
    ppermute x0 -> x2, waiting for transfers between devices: none -> 16 us  [the longest x1 16 us: shards(): mixed = lax.ppermute(output_sum.astype(jnp.bfloat16), ('seq', 'tp'), route)]
    ppermute x1, waiting for transfers between devices: 14 us -> 1 us  [extended(): lax.ppermute(lax.slice_in_dim(block, block.shape[dim] - width, None, axis...]
    all_gather x2, waiting for transfers between devices: 13.3 us -> 25.2 us  [the longest x1 25.2 us: shards(): gated_all = lax.all_gather(gated, 'seq', axis=1, tiled=True)]
    ppermute x1, waiting for transfers between devices: 4.54 us -> 12.6 us  [extended(): lax.ppermute(lax.slice_in_dim(block, 0, width, axis=dim), axis, backward)]
    transpose x0 -> x2, local copies, waits for them, and re-layouts: none -> 7.47 us  [the longest x1 7.3 us: shards(): partial_out = partial_out.reshape(group, out_rows, n_seq, length).transpo...]
    ppermute x0 -> x2, starting transfers between devices: none -> 7.3 us  [the longest x1 4.32 us: shards(): mixed = lax.ppermute(output_sum.astype(jnp.bfloat16), ('seq', 'tp'), route)]
    reshape x0 -> x1, local copies, waits for them, and re-layouts: none -> 6.66 us  [shards(): partial_out.reshape(group, out_rows, n_seq, length).transpose(0, 2, 1, 3)]
  transfers between devices with their start and end apart: 7 -> 10, of which waited for: 6 -> 7; matrix products, arithmetic and copies ran while one was open for 40% -> 43% of each run, Pallas kernels for 0% -> 0%
where the time goes in v1:
time: 243 us; the launch traced here: 240 us
  waiting for transfers between devices  96.2 us (40%)
  local copies, waits for them, and re-layouts  60.1 us (25%)
  matrix products  43.2 us (18%)
  starting transfers between devices  19.1 us (8%)
  between operations  14.2 us (6%)
  other arithmetic  7.26 us (3%)
    conv_general_dilated x4, matrix products, correlate(): lax.conv_general_dilated(signal[None], taps[:, None, :], (1,), 'VALID', d...  29.8 us
    all_gather x1, waiting for transfers between devices, shards(): gated_all = lax.all_gather(gated, 'seq', axis=1, tiled=True)  25.2 us
    reduce_scatter x1, waiting for transfers between devices, shards(): lax.psum_scatter(partial_out, 'tp', scatter_dimension=0, tiled=True)  22.3 us
    reduce_scatter x1, waiting for transfers between devices, shards(): lax.psum_scatter(partial_grad, 'seq', scatter_dimension=1, tiled=True)  18.7 us
    ppermute x1, waiting for transfers between devices, shards(): mixed = lax.ppermute(output_sum.astype(jnp.bfloat16), ('seq', 'tp'), route)  16 us
    conv_general_dilated x12, local copies, waits for them, and re-layouts, correlate(): lax.conv_general_dilated(signal[None], taps[:, None, :], (1,), 'VALID', d...  13.3 us
    ppermute x1, waiting for transfers between devices, extended(): lax.ppermute(lax.slice_in_dim(block, 0, width, axis=dim), axis, backward)  12.6 us
    another operation x4, local copies, waits for them, and re-layouts, correlate(): signal[None]  10 us
  transfers between devices with their start and end apart: 10, of which 7 were waited for; matrix products, arithmetic and copies ran while one was open for 43% of the time, Pallas kernels for 0%

profile of v1, /device:TPU:27, one launch (start us, length us, event | category | flops | bytes accessed | tf_op | source)
XLA Modules:
  0.0 240.0 jit_solution(13884115816914673931)
XLA Ops:
  7.2 3.8 %all-to-all-start = ((bf16[4,128,256]{2,1,0:T(8,128)(2,1)}), bf16[4,128,256]{2,1,0:T(8,128)(2,1)S(1)}, u32[]{:S(2)}, u32[]{:S(2)}) async-start(bf16[4,128,256]{2,1,0:T(8,128)(2,1)} %bitcast.78), calls=%async_computation.1 | async-start | bytes 524288 | tf_op jit(solution)/shard_map/all_to_all | solution.py:44
  13.9 3.1 %collective-permute-start = (bf16[3,512,133]{1,2,0:T(8,128)(2,1)}, bf16[3,512,133]{1,2,0:T(8,128)(2,1)S(1)}, u32[]{:S(2)}, u32[]{:S(2)}) collective-permute-start(bf16[3,512,133]{1,2,0:T(8,128)(2,1)} %copy.89), channel_id=1, source_target_pairs={{0,8},{8,16},{16,24},{1,9},{9,17},{17,25},{2,10},{10,18},{18,26},{... | collective-permute-start | bytes 1225736 | tf_op jit(solution)/shard_map/ppermute | solution.py:14
  18.0 2.2 collective-permute-start.1
  20.4 3.0 %collective-permute-start.3 = (bf16[128,1024]{0,1:T(8,128)(2,1)S(1)}, bf16[128,1024]{0,1:T(8,128)(2,1)S(1)}, u32[]{:S(2)}, u32[]{:S(2)}) collective-permute-start(bf16[128,1024]{0,1:T(8,128)(2,1)S(1)} %bitcast.79), channel_id=1, source_target_pairs={{0,0},{1,4},{2,8},{3,12},{4,16},{5,20},{6,24},{7,28},{8,1},{9,5},{... | collective-permute-start | bytes 786440 | tf_op jit(solution)/shard_map/ppermute | solution.py:51
  27.1 12.6 %collective-permute-done.1 = bf16[3,512,133]{1,2,0:T(8,128)(2,1)S(1)} collective-permute-done((bf16[3,512,133]{1,2,0:T(8,128)(2,1)}, bf16[3,512,133]{1,2,0:T(8,128)(2,1)S(1)}, u32[]{:S(2)}, u32[]{:S(2)}) %collective-permute-start.1) | collective-permute-done | bytes 408608 | tf_op jit(solution)/shard_map/ppermute | solution.py:17
  41.8 2.6 %pad_maximum_fusion = bf16[3,512,522]{2,1,0:T(8,128)(2,1)S(1)} fusion(bf16[3,512,133]{2,1,0:T(8,128)(2,1)} %copy.61, bf16[3,512,256]{2,1,0:T(8,128)(2,1)} %param.6, bf16[3,512,133]{2,1,0:T(8,128)(2,1)} %copy.60), kind=kLoop, calls=%fused_computation.7 | loop fusion | flops 4810752 | bytes 3207168 | tf_op jit(solution)/shard_map/concatenate | solution.py:18
  44.4 2.2 copy.62
  46.6 2.7 %pad = bf16[1536,1,528]{0,2,1:T(8,128)(2,1)} pad(bf16[1536,1,522]{0,2,1:T(8,128)(2,1)} %copy.62, bf16[]{:T(256)} %constant.12), padding=0_0x0_0x0_6 | pad | bytes 3225602 | tf_op jit(solution)/shard_map/broadcast_in_dim;reshape | solution.py:30
  63.5 2.3 reshape.75
  69.0 21.2 %fusion.36 = f32[1,512,389]{1,0,2:T(1,128)S(1)} fusion(f32[1,528,512]{2,0,1:T(1,128)S(1)} %copy-done.9, f32[512,1,128]{0,1,2:T(1,128)S(1)} %copy-done.13), kind=kOutput, calls=%fused_computation.57 | convolution fusion | flops 305922048 | bytes 2140160 | tf_op jit(solution)/shard_map/conv_general_dilated | solution.py:29
  92.3 4.2 %fusion.37 = f32[512,1024]{0,1:T(8,128)} fusion(bf16[512,1024]{1,0:T(8,128)(2,1)S(1)} %copy-done, bf16[1024,1024]{0,1:T(8,128)(2,1)} %all-gather.5.cloned.1.call-done), kind=kOutput, calls=%fused_computation.58 | convolution fusion | flops 1073741824 | bytes 5242880 | tf_op jit(solution)/shard_map/dot_general | solution.py:66
  96.9 25.2 %all-gather.3.cloned.1.call-done = bf16[512,1024]{0,1:T(8,128)(2,1)} async-done(((bf16[512,256]{0,1:T(8,128)(2,1)}), bf16[512,1024]{0,1:T(8,128)(2,1)}) %all-gather.3.cloned.1.call-update) | async-done | bytes 1048592 | tf_op jit(solution)/shard_map/all_gather | solution.py:81
  122.1 4.4 %convolution_bitcast_fusion = f32[1024,1024]{0,1:T(8,128)} fusion(bf16[512,1024]{0,1:T(8,128)(2,1)} %all-gather.3.cloned.1.call-done, bf16[512,1024]{1,0:T(8,128)(2,1)S(1)} %copy-done), kind=kOutput, calls=%fused_computation.6 | convolution fusion | flops 1073741824 | bytes 6291456 | tf_op jit(solution)/shard_map/dot_general | solution.py:82
  126.5 6.7 %reshape.36 = f32[2,512,4,256]{1,0,3,2:T(2,128)} reshape(f32[1024,1024]{0,1:T(8,128)} %convolution_bitcast_fusion) | data formatting | bytes 8388608 | tf_op jit(solution)/shard_map/reshape | solution.py:88
  133.2 7.3 %copy.71 = f32[2,4,512,256]{3,2,1,0:T(8,128)} copy(f32[2,4,512,256]{2,0,3,1:T(2,128)} %bitcast.71) | data formatting | bytes 8388608 | tf_op jit(solution)/shard_map/transpose | solution.py:89
  141.6 18.7 %reduce-scatter.5.cloned.1.call-done = f32[512,256]{0,1:T(8,128)} async-done(((f32[512,1024]{0,1:T(8,128)}), f32[512,256]{0,1:T(8,128)}) %reduce-scatter.5.cloned.1.call-update) | async-done | bytes 524304 | tf_op jit(solution)/shard_map/reduce_scatter | solution.py:67
  163.4 4.7 %reduce-precision_reduce_fusion = bf16[512,1024]{1,0:T(8,128)(2,1)} fusion(bf16[512,4,256]{0,2,1:T(8,128)(2,1)} %bitcast.83, bf16[1024,4,256]{0,2,1:T(8,128)(2,1)} %bitcast.82), kind=kOutput, calls=%fused_computation | convolution fusion | flops 1079508992 | bytes 4194304 | tf_op jit(solution)/shard_map/dot_general | solution.py:100
  169.7 5.4 %fusion.18 = f32[1,512,262]{1,0,2:T(1,128)S(1)} fusion(f32[512,1,128]{0,1,2:T(1,128)S(1)} %copy.75, f32[1,512,389]{1,2,0:T(8,128)S(1)} %bitcast.73), kind=kOutput, calls=%fused_computation.32 | convolution fusion | flops 206045184 | bytes 1595392 | tf_op jit(solution)/shard_map/conv_general_dilated | solution.py:29
  176.6 2.4 reshape.69
  179.0 2.7 %pad.2 = f32[1536,1,264]{0,2,1:T(8,128)} pad(f32[1536,1,262]{0,2,1:T(8,128)} %reshape.69, f32[]{:T(128)} %constant.11.clone.1), padding=0_0x0_0x0_2 | pad | bytes 3231748 | tf_op jit(solution)/shard_map/broadcast_in_dim;reshape | solution.py:30
  181.7 3.3 %reshape.55 = f32[1536,1,8,33]{0,1,3,2:T(1,128)S(1)} reshape(f32[1536,1,264]{0,2,1:T(8,128)} %pad.2) | data formatting | bytes 3244032 | tf_op jit(solution)/shard_map/conv_general_dilated | solution.py:29
  187.7 22.3 %reduce-scatter.3.cloned.1.call-done = f32[512,256]{1,0:T(8,128)} async-done(((f32[4096,256]{1,0:T(8,128)}), f32[512,256]{1,0:T(8,128)}) %reduce-scatter.3.cloned.1.call-update) | async-done | bytes 524304 | tf_op jit(solution)/shard_map/reduce_scatter | solution.py:92
  211.2 4.3 %collective-permute-start.2 = (bf16[512,256]{1,0:T(8,128)(2,1)S(1)}, bf16[512,256]{1,0:T(8,128)(2,1)S(1)}, u32[]{:S(2)}, u32[]{:S(2)}) collective-permute-start(bf16[512,256]{1,0:T(8,128)(2,1)S(1)} %convert_element_type.21), channel_id=1, source_target_pairs={{0,0},{1,8},{2,16},{3,24},{4,1},{5,9},{6,17},{7,25},{8,2},{9,10},{... | collective-permute-start | bytes 786440 | tf_op jit(solution)/shard_map/ppermute | solution.py:97
  216.7 16.0 %collective-permute-done.2 = bf16[512,256]{1,0:T(8,128)(2,1)S(1)} collective-permute-done((bf16[512,256]{1,0:T(8,128)(2,1)S(1)}, bf16[512,256]{1,0:T(8,128)(2,1)S(1)}, u32[]{:S(2)}, u32[]{:S(2)}) %collective-permute-start.2) | collective-permute-done | bytes 262176 | tf_op jit(solution)/shard_map/ppermute | solution.py:97
  (93 shorter events, 42.6 us)
Async XLA Ops:
  7.2 85.2 %copy-start = (bf16[512,1024]{1,0:T(8,128)(2,1)S(1)}, bf16[512,1024]{1,0:T(8,128)(2,1)}, u32[]{:S(2)}) copy-start(bf16[512,1024]{1,0:T(8,128)(2,1)} %param.10) | copy-start | bytes 3145732
  7.2 13.0 %all-to-all-start = ((bf16[4,128,256]{2,1,0:T(8,128)(2,1)}), bf16[4,128,256]{2,1,0:T(8,128)(2,1)S(1)}, u32[]{:S(2)}, u32[]{:S(2)}) async-start(bf16[4,128,256]{2,1,0:T(8,128)(2,1)} %bitcast.78), calls=%async_computation.1 | async-start | bytes 524288 | tf_op jit(solution)/shard_map/all_to_all | solution.py:44
  11.0 81.3 %all-gather.5.cloned.1.call-start = ((), (), s32[]{:S(2)}) async-start(), calls=%async_computation.5 | async-start | bytes 2359296 | tf_op jit(solution)/shard_map/all_gather | solution.py:52
  12.8 10.5 %copy-start.14 = (f32[3,512,7]{1,2,0:T(8,128)S(1)}, f32[3,512,7]{1,2,0:T(8,128)}, u32[]{:S(2)}) copy-start(f32[3,512,7]{1,2,0:T(8,128)} %param.7) | copy-start | bytes 129028
  12.9 10.9 %copy-start.10 = (f32[512,128]{1,0:T(8,128)S(1)}, f32[512,128]{1,0:T(8,128)}, u32[]{:S(2)}) copy-start(f32[512,128]{1,0:T(8,128)} %param.8) | copy-start | bytes 786436
  13.9 12.1 %collective-permute-start = (bf16[3,512,133]{1,2,0:T(8,128)(2,1)}, bf16[3,512,133]{1,2,0:T(8,128)(2,1)S(1)}, u32[]{:S(2)}, u32[]{:S(2)}) collective-permute-start(bf16[3,512,133]{1,2,0:T(8,128)(2,1)} %copy.89), channel_id=1, source_target_pairs={{0,8},{8,16},{16,24},{1,9},{9,17},{17,25},{2,10},{10,18},{18,26},{... | collective-permute-start | bytes 1225736 | tf_op jit(solution)/shard_map/ppermute | solution.py:14
  18.0 21.7 %collective-permute-start.1 = (bf16[3,512,133]{1,2,0:T(8,128)(2,1)}, bf16[3,512,133]{1,2,0:T(8,128)(2,1)S(1)}, u32[]{:S(2)}, u32[]{:S(2)}) collective-permute-start(bf16[3,512,133]{1,2,0:T(8,128)(2,1)} %copy.90), channel_id=1, source_target_pairs={{8,0},{16,8},{24,16},{9,1},{17,9},{25,17},{10,2},{18,10},{26,18},{... | collective-permute-start | bytes 1225736 | tf_op jit(solution)/shard_map/ppermute | solution.py:17
  20.4 20.5 %collective-permute-start.3 = (bf16[128,1024]{0,1:T(8,128)(2,1)S(1)}, bf16[128,1024]{0,1:T(8,128)(2,1)S(1)}, u32[]{:S(2)}, u32[]{:S(2)}) collective-permute-start(bf16[128,1024]{0,1:T(8,128)(2,1)S(1)} %bitcast.79), channel_id=1, source_target_pairs={{0,0},{1,4},{2,8},{3,12},{4,16},{5,20},{6,24},{7,28},{8,1},{9,5},{... | collective-permute-start | bytes 786440 | tf_op jit(solution)/shard_map/ppermute | solution.py:51
  41.6 80.5 %all-gather.3.cloned.1.call-start = ((), (), s32[]{:S(2)}) async-start(), calls=%async_computation.3 | async-start | bytes 1310720 | tf_op jit(solution)/shard_map/all_gather | solution.py:81
  63.5 2.3 copy-start.6
  65.8 1.2 copy-start.7
  67.0 23.5 %copy-start.2 = (f32[512,516]{0,1:T(8,128)}, f32[512,516]{0,1:T(8,128)S(1)}, u32[]{:S(2)}) copy-start(f32[512,516]{0,1:T(8,128)S(1)} %slice_bitcast_fusion.2) | copy-start | bytes 3170308
  67.0 2.0 copy-start.9
  67.0 2.0 copy-start.13
  69.0 21.2 %copy-start.15 = (f32[512]{0:T(512)S(1)}, f32[512]{0:T(512)}, u32[]{:S(2)}) copy-start(f32[512]{0:T(512)} %param.9) | copy-start | bytes 6148
  92.2 68.0 %reduce-scatter.5.cloned.1.call-start = ((), (), s32[]{:S(2)}) async-start(), calls=%async_computation.6 | async-start | bytes 2621440 | tf_op jit(solution)/shard_map/reduce_scatter | solution.py:67
  96.6 113.4 %reduce-scatter.3.cloned.1.call-start = ((), (), s32[]{:S(2)}) async-start(), calls=%async_computation.4 | async-start | bytes 4718592 | tf_op jit(solution)/shard_map/reduce_scatter | solution.py:92
  140.5 1.0 copy-start.11
  161.2 7.2 %collective-permute-start.4 = (bf16[512,133]{0,1:T(8,128)(2,1)S(1)}, bf16[512,133]{0,1:T(8,128)(2,1)S(1)}, u32[]{:S(2)}, u32[]{:S(2)}) collective-permute-start(bf16[512,133]{0,1:T(8,128)(2,1)S(1)} %slice.138), channel_id=1, source_target_pairs={{8,0},{16,8},{24,16},{9,1},{17,9},{25,17},{10,2},{18,10},{26,18},{... | collective-permute-start | bytes 408584 | tf_op jit(solution)/shard_map/ppermute | solution.py:25
  163.4 5.0 %copy-start.5 = (f32[512,389]{0,1:T(8,128)S(1)}, f32[512,389]{0,1:T(8,128)}, u32[]{:S(2)}) copy-start(f32[512,389]{0,1:T(8,128)} %copy-done.4) | copy-start | bytes 2390020
  163.4 5.0 %copy-start.8 = (f32[512,256]{0,1:T(8,128)S(1)}, f32[512,256]{0,1:T(8,128)}, u32[]{:S(2)}) copy-start(f32[512,256]{0,1:T(8,128)} %reduce-scatter.5.cloned.1.call-done) | copy-start | bytes 1572868
  168.1 1.4 copy-start.3
  210.0 23.4 %copy-start.1 = (bf16[512,1024]{1,0:T(8,128)(2,1)S(1)}, bf16[512,1024]{1,0:T(8,128)(2,1)}, u32[]{:S(2)}) copy-start(bf16[512,1024]{1,0:T(8,128)(2,1)} %param.10) | copy-start | bytes 3145732
  211.2 21.6 %collective-permute-start.2 = (bf16[512,256]{1,0:T(8,128)(2,1)S(1)}, bf16[512,256]{1,0:T(8,128)(2,1)S(1)}, u32[]{:S(2)}, u32[]{:S(2)}) collective-permute-start(bf16[512,256]{1,0:T(8,128)(2,1)S(1)} %convert_element_type.21), channel_id=1, source_target_pairs={{0,0},{1,8},{2,16},{3,24},{4,1},{5,9},{6,17},{7,25},{8,2},{9,10},{... | collective-permute-start | bytes 786440 | tf_op jit(solution)/shard_map/ppermute | solution.py:97
  (4 other events, 3.0 us)
Sparse Core Ops, SparseCore 0:
  41.7 31.8 all-gather.4
  92.4 29.6 all-gather.2
  125.0 35.1 reduce-scatter.4
  162.4 47.5 reduce-scatter.2

commit v2 on v1

v2 whole, which is shorter than its diff:
```python
import math

import jax
import jax.numpy as jnp
from jax import lax
from jax.sharding import PartitionSpec as P


def extended(block, axis, width):
    count = lax.axis_size(axis)
    forward = [(i, i + 1) for i in range(count - 1)]
    backward = [(target, source) for source, target in forward]
    low = lax.ppermute(block[..., block.shape[-1] - width :], axis, forward)
    high = lax.ppermute(block[..., :width], axis, backward)
    return jnp.concatenate([low, block, high], axis=-1)


def from_behind(block, axis, distance):
    devices = range(lax.axis_size(axis))
    route = [(i - distance, i) for i in devices if i - distance in devices]
    return lax.ppermute(block, axis, route)


def correlate(signal, taps):
    return lax.conv_general_dilated(
        signal[None],
        taps[:, None, :],
        (1,),
        "VALID",
        dimension_numbers=("NCH", "OIH", "NCH"),
        feature_group_count=signal.shape[0],
        precision=lax.Precision.HIGHEST,
    )[0]


def short_correlate(signal, taps):
    span = signal.shape[-1] - taps.shape[-1] + 1
    total = taps[..., 0:1] * signal[..., 0:span]
    for k in range(1, taps.shape[-1]):
        total = total + taps[..., k : k + 1] * signal[..., k : k + span]
    return total


def partner(index, step, count):
    if count & (count - 1) == 0:
        return index ^ step
    return (index + step) % count


def exchange(block_of, axis):
    count = lax.axis_size(axis)
    got = []
    for step in range(1, count):
        route = [(i, partner(i, step, count)) for i in range(count)]
        got.append(lax.ppermute(block_of(step), axis, route))
    return got


def rows_of_slab(out_grad, n_seq, n_tp):
    rows, length = out_grad.shape
    piece = rows // n_seq
    mine = lax.all_to_all(out_grad.reshape(n_seq, piece, length), "seq", 0, 0)
    mine = jnp.transpose(mine, (1, 0, 2)).reshape(piece, n_seq * length)
    route = []
    for a in range(n_seq):
        for b in range(n_tp):
            flat = n_seq * b + a
            route.append((a * n_tp + b, (flat // n_tp) * n_tp + flat % n_tp))
    moved = lax.ppermute(mine, ("seq", "tp"), route)
    return lax.all_gather(moved, "tp", axis=0, tiled=True)


def shards(streams, feat_weight, long_filter, skip_gain, out_weight, out_grad):
    channels = streams.shape[1]
    length = streams.shape[2]
    taps_long = long_filter.shape[1]
    taps_short = feat_weight.shape[2]
    n_seq = lax.axis_size("seq")
    n_tp = lax.axis_size("tp")
    me = lax.axis_index("seq")
    reach = taps_long + taps_short - 2
    keep = length + taps_short - 1

    slab_grad = rows_of_slab(out_grad, n_seq, n_tp)
    slab_width = slab_grad.shape[0]
    partial_grad = jnp.dot(out_weight, slab_grad, preferred_element_type=jnp.float32)

    def grad_block(step):
        start = partner(me, step, n_seq) * length
        return lax.dynamic_slice_in_dim(partial_grad, start, length, axis=1)

    arrived = exchange(grad_block, "seq")
    gated_grad = lax.dynamic_slice_in_dim(partial_grad, me * length, length, axis=1)
    for block in arrived:
        gated_grad = gated_grad + block

    widened = extended(streams, "seq", reach).astype(jnp.float32)
    key_value = short_correlate(
        widened[1:, :, : taps_long - 1 + keep + taps_short - 1], feat_weight[1:, :, ::-1]
    )
    key_feat, value_feat = key_value[0], key_value[1]
    query_tail = short_correlate(widened[0, :, taps_long - 1 :], feat_weight[0, :, ::-1])
    product = key_feat * value_feat
    convolved = correlate(product, long_filter[:, ::-1])
    summed = convolved + skip_gain[:, None] * product[:, taps_long - 1 :]
    gated = (query_tail[:, :length] * summed[:, :length]).astype(jnp.bfloat16)

    gated_blocks = [gated] + exchange(lambda step: gated, "seq")
    group = n_tp // n_seq
    out_rows = slab_width // group
    pieces = []
    for j in range(group):
        rows = out_weight[:, j * out_rows : (j + 1) * out_rows]
        for block in gated_blocks:
            pieces.append(
                lax.dot_general(
                    rows, block, (((0,), (0,)), ((), ())), preferred_element_type=jnp.float32
                )
            )
    partial_out = jnp.concatenate(pieces, axis=0)
    output_sum = lax.psum_scatter(partial_out, "tp", scatter_dimension=0, tiled=True)
    route = []
    for s in range(n_seq):
        for p in range(n_tp):
            target = partner(s, p % n_seq, n_seq) if p % n_seq else s
            route.append((s * n_tp + p, target * n_tp + group * s + p // n_seq))
    mixed = lax.ppermute(output_sum.astype(jnp.bfloat16), ("seq", "tp"), route)

    scale = 1.0 / math.sqrt(length * n_seq)
    weight_sum = None
    for step, block in enumerate(gated_blocks):
        source = partner(me, step, n_seq) if step else me
        grad_part = lax.dynamic_slice_in_dim(slab_grad, source * length, length, axis=1)
        term = lax.dot_general(
            block, grad_part, (((1,), (1,)), ((), ())), preferred_element_type=jnp.float32
        )
        term = lax.reduce_precision(term * scale, exponent_bits=8, mantissa_bits=7)
        weight_sum = term if weight_sum is None else weight_sum + term
    weight_grad = weight_sum.astype(jnp.bfloat16)

    next_grad = from_behind(gated_grad[:, :reach].astype(jnp.bfloat16), "seq", -1).astype(
        jnp.float32
    )
    grad_ext = jnp.concatenate([gated_grad, next_grad], axis=1)
    conv_grad = grad_ext * query_tail
    prod_grad = correlate(conv_grad, long_filter) + skip_gain[:, None] * conv_grad[:, :keep]
    query_grad = grad_ext[:, :keep] * summed[:, :keep]
    key_grad = prod_grad * value_feat[:, taps_long - 1 : taps_long - 1 + keep]
    value_grad = prod_grad * key_feat[:, taps_long - 1 : taps_long - 1 + keep]
    feat_grad = jnp.stack([query_grad, key_grad, value_grad])
    stream_grad = short_correlate(feat_grad, feat_weight).astype(jnp.bfloat16)
    return (mixed, stream_grad, weight_grad)


def solution(mesh):
    return jax.shard_map(
        shards,
        mesh=mesh,
        in_specs=(
            P(None, "tp", "seq"),
            P(None, "tp", None),
            P("tp", None),
            P("tp"),
            P("tp", "seq"),
            P("tp", "seq"),
        ),
        out_specs=(P("tp", "seq"), P(None, "tp", "seq"), P("tp", "seq")),
        check_vma=False,
    )
```

time: 243 us -> 207 us (0.85)
  the two profiles are of different devices: /device:TPU:27 before, /device:TPU:6 now
where the time goes in v2:
time: 207 us; the launch traced here: 206 us
  waiting for transfers between devices  111 us (54%)
  matrix products  32.8 us (16%)
  starting transfers between devices  24.2 us (12%)
  between operations  14.4 us (7%)
  other arithmetic  8.61 us (4%)
  blocking collectives  7.92 us (4%)
  local copies, waits for them, and re-layouts  7.85 us (4%)
    reduce_scatter x1, waiting for transfers between devices, shards(): lax.psum_scatter(partial_out, 'tp', scatter_dimension=0, tiled=True)  41 us
    ppermute x6, waiting for transfers between devices, exchange(): got.append(lax.ppermute(block_of(step), axis, route))  25.9 us
    ppermute x1, waiting for transfers between devices, shards(): mixed = lax.ppermute(output_sum.astype(jnp.bfloat16), ('seq', 'tp'), route)  13.7 us
    ppermute x1, waiting for transfers between devices, rows_of_slab(): moved = lax.ppermute(mine, ('seq', 'tp'), route)  11.3 us
    conv_general_dilated x2, matrix products, correlate(): lax.conv_general_dilated(signal[None], taps[:, None, :], (1,), 'VALID', d...  10.8 us
    all_gather x1, waiting for transfers between devices, rows_of_slab(): return lax.all_gather(moved, 'tp', axis=0, tiled=True)  10.1 us
    dot_general x4, matrix products, shards(): lax.dot_general(block, grad_part, (((1,), (1,)), ((), ())), preferred_ele...  9.6 us
    dot_general x8, matrix products, shards(): lax.dot_general(rows, block, (((0,), (0,)), ((), ())), preferred_element_...  9.16 us
  transfers between devices with their start and end apart: 13, of which 10 were waited for; matrix products, arithmetic and copies ran while one was open for 14% of the time, Pallas kernels for 0%

profile of v2, /device:TPU:6, one launch (start us, length us, event | category | flops | bytes accessed | tf_op | source)
XLA Modules:
  0.0 206.3 jit_solution(11767713657915984876)
XLA Ops:
  7.2 7.9 %all_to_all.5 = bf16[4,128,256]{2,1,0:T(8,128)(2,1)S(1)} all-to-all(bf16[4,128,256]{2,1,0:T(8,128)(2,1)} %bitcast.117), channel_id=1, replica_groups=mesh['seq'=4,'tp'=8] {'seq'}, dimensions={0} | all-to-all | bytes 524288 | tf_op jit(solution)/shard_map/all_to_all | solution.py:62
  15.3 3.0 %collective-permute-start.6 = (bf16[128,1024]{0,1:T(8,128)(2,1)S(1)}, bf16[128,1024]{0,1:T(8,128)(2,1)S(1)}, u32[]{:S(2)}, u32[]{:S(2)}) collective-permute-start(bf16[128,1024]{0,1:T(8,128)(2,1)S(1)} %bitcast.118), channel_id=1, source_target_pairs={{0,0},{1,4},{2,8},{3,12},{4,16},{5,20},{6,24},{7,28},{8,1},{9,5},{... | collective-permute-start | bytes 786440 | tf_op jit(solution)/shard_map/ppermute | solution.py:69
  18.4 11.3 %collective-permute-done.6 = bf16[128,1024]{0,1:T(8,128)(2,1)S(1)} collective-permute-done((bf16[128,1024]{0,1:T(8,128)(2,1)S(1)}, bf16[128,1024]{0,1:T(8,128)(2,1)S(1)}, u32[]{:S(2)}, u32[]{:S(2)}) %collective-permute-start.6) | collective-permute-done | bytes 262176 | tf_op jit(solution)/shard_map/ppermute | solution.py:69
  33.3 5.3 %collective-permute-start.1 = (bf16[3,512,133]{1,2,0:T(8,128)(2,1)S(1)}, bf16[3,512,133]{1,2,0:T(8,128)(2,1)}, u32[]{:S(2)}, u32[]{:S(2)}) collective-permute-start(bf16[3,512,133]{1,2,0:T(8,128)(2,1)S(1)} %get-tuple-element.27), channel_id=1, source_target_pairs={{8,0},{16,8},{24,16},{9,1},{17,9},{25,17},{10,2},{18,10},{26,18},{... | collective-permute-start | bytes 1225736 | tf_op jit(solution)/shard_map/ppermute | solution.py:14
  40.1 6.2 %collective-permute-done = bf16[3,512,133]{1,2,0:T(8,128)(2,1)S(1)} collective-permute-done((bf16[3,512,133]{1,2,0:T(8,128)(2,1)S(1)}, bf16[3,512,133]{1,2,0:T(8,128)(2,1)S(1)}, u32[]{:S(2)}, u32[]{:S(2)}) %collective-permute-start) | collective-permute-done | bytes 408608 | tf_op jit(solution)/shard_map/ppermute | solution.py:13
  47.1 1.8 maximum_convert_fusion
  51.8 10.1 %all-gather.2.cloned.1.call-done = bf16[1024,1024]{0,1:T(8,128)(2,1)} async-done(((bf16[128,1024]{0,1:T(8,128)(2,1)}), bf16[1024,1024]{0,1:T(8,128)(2,1)}) %all-gather.2.cloned.1.call-update) | async-done | bytes 2097168 | tf_op jit(solution)/shard_map/all_gather | solution.py:70
  61.9 3.2 %fusion.61 = f32[512,1024]{0,1:T(8,128)S(1)} fusion(bf16[512,1024]{1,0:T(8,128)(2,1)} %param.10, bf16[1024,1024]{0,1:T(8,128)(2,1)} %all-gather.2.cloned.1.call-done), kind=kOutput, calls=%fused_computation.123 | convolution fusion | flops 1073741824 | bytes 5242880 | tf_op jit(solution)/shard_map/dot_general | solution.py:86
  66.5 2.3 %collective-permute-start.9 = (f32[512,256]{0,1:T(8,128)S(1)}, f32[512,256]{0,1:T(8,128)S(1)}, u32[]{:S(2)}, u32[]{:S(2)}) collective-permute-start(f32[512,256]{0,1:T(8,128)S(1)} %get-tuple-element.18), channel_id=1, source_target_pairs={{0,24},{8,16},{16,8},{24,0},{1,25},{9,17},{17,9},{25,1},{2,26},{10... | collective-permute-start | bytes 1572872 | tf_op jit(solution)/shard_map/ppermute | solution.py:55
  68.9 5.4 %fusion.30 = f32[1,512,262]{1,0,2:T(1,128)S(1)} fusion(f32[512,1,128]{0,1,2:T(1,128)S(1)} %copy-done.9, f32[1,512,389]{1,2,0:T(8,128)S(1)} %copy-done.6), kind=kOutput, calls=%fused_computation.66 | convolution fusion | flops 206045184 | bytes 1595392 | tf_op jit(solution)/shard_map/conv_general_dilated | solution.py:25
  74.3 5.9 %collective-permute-done.7 = f32[512,256]{0,1:T(8,128)S(1)} collective-permute-done((f32[512,256]{0,1:T(8,128)S(1)}, f32[512,256]{0,1:T(8,128)S(1)}, u32[]{:S(2)}, u32[]{:S(2)}) %collective-permute-start.7) | collective-permute-done | bytes 524320 | tf_op jit(solution)/shard_map/ppermute | solution.py:55
  80.2 10.8 %collective-permute-done.8 = f32[512,256]{0,1:T(8,128)S(1)} collective-permute-done((f32[512,256]{0,1:T(8,128)S(1)}, f32[512,256]{0,1:T(8,128)S(1)}, u32[]{:S(2)}, u32[]{:S(2)}) %collective-permute-start.8) | collective-permute-done | bytes 524320 | tf_op jit(solution)/shard_map/ppermute | solution.py:55
  91.2 3.6 %collective-permute-start.10 = (bf16[512,133]{0,1:T(8,128)(2,1)S(1)}, bf16[512,133]{0,1:T(8,128)(2,1)S(1)}, u32[]{:S(2)}, u32[]{:S(2)}) collective-permute-start(bf16[512,133]{0,1:T(8,128)(2,1)S(1)} %slice.441), channel_id=1, source_target_pairs={{8,0},{16,8},{24,16},{9,1},{17,9},{25,17},{10,2},{18,10},{26,18},{... | collective-permute-start | bytes 408584 | tf_op jit(solution)/shard_map/ppermute | solution.py:21
  94.9 2.3 %collective-permute-done.10 = bf16[512,133]{0,1:T(8,128)(2,1)S(1)} collective-permute-done((bf16[512,133]{0,1:T(8,128)(2,1)S(1)}, bf16[512,133]{0,1:T(8,128)(2,1)S(1)}, u32[]{:S(2)}, u32[]{:S(2)}) %collective-permute-start.10) | collective-permute-done | bytes 136224 | tf_op jit(solution)/shard_map/ppermute | solution.py:21
  97.9 5.4 %fusion.28 = f32[1,512,262]{1,0,2:T(1,128)S(1)} fusion(f32[512,1,128]{0,1,2:T(1,128)S(1)} %copy.46, f32[1,512,389]{1,2,0:T(8,128)S(1)} %bitcast.113), kind=kOutput, calls=%fused_computation.64 | convolution fusion | flops 206045184 | bytes 1595392 | tf_op jit(solution)/shard_map/conv_general_dilated | solution.py:25
  103.9 2.5 %collective-permute-start.2 = (bf16[512,256]{0,1:T(8,128)(2,1)S(1)}, bf16[512,256]{0,1:T(8,128)(2,1)S(1)}, u32[]{:S(2)}, u32[]{:S(2)}) collective-permute-start(bf16[512,256]{0,1:T(8,128)(2,1)S(1)} %fusion.36), channel_id=1, source_target_pairs={{0,8},{8,0},{16,24},{24,16},{1,9},{9,1},{17,25},{25,17},{2,10},{10... | collective-permute-start | bytes 786440 | tf_op jit(solution)/shard_map/ppermute | solution.py:55
  106.4 2.1 %collective-permute-start.4 = (bf16[512,256]{0,1:T(8,128)(2,1)S(1)}, bf16[512,256]{0,1:T(8,128)(2,1)S(1)}, u32[]{:S(2)}, u32[]{:S(2)}) collective-permute-start(bf16[512,256]{0,1:T(8,128)(2,1)S(1)} %fusion.36), channel_id=1, source_target_pairs={{0,24},{8,16},{16,8},{24,0},{1,25},{9,17},{17,9},{25,1},{2,26},{10... | collective-permute-start | bytes 786440 | tf_op jit(solution)/shard_map/ppermute | solution.py:55
  109.6 3.9 %collective-permute-done.2 = bf16[512,256]{0,1:T(8,128)(2,1)S(1)} collective-permute-done((bf16[512,256]{0,1:T(8,128)(2,1)S(1)}, bf16[512,256]{0,1:T(8,128)(2,1)S(1)}, u32[]{:S(2)}, u32[]{:S(2)}) %collective-permute-start.2) | collective-permute-done | bytes 262176 | tf_op jit(solution)/shard_map/ppermute | solution.py:55
  114.7 5.3 %collective-permute-done.3 = bf16[512,256]{0,1:T(8,128)(2,1)S(1)} collective-permute-done((bf16[512,256]{0,1:T(8,128)(2,1)S(1)}, bf16[512,256]{0,1:T(8,128)(2,1)S(1)}, u32[]{:S(2)}, u32[]{:S(2)}) %collective-permute-start.3) | collective-permute-done | bytes 262176 | tf_op jit(solution)/shard_map/ppermute | solution.py:55
  133.9 1.9 fusion.38
  135.8 41.0 %reduce-scatter.2.cloned.1.call-done = f32[512,256]{0,1:T(8,128)} async-done(((f32[4096,256]{0,1:T(8,128)}), f32[512,256]{0,1:T(8,128)}) %reduce-scatter.2.cloned.1.call-update) | async-done | bytes 524304 | tf_op jit(solution)/shard_map/reduce_scatter | solution.py:121
  177.9 2.8 %collective-permute-start.5 = (bf16[512,256]{0,1:T(8,128)(2,1)S(1)}, bf16[512,256]{0,1:T(8,128)(2,1)S(1)}, u32[]{:S(2)}, u32[]{:S(2)}) collective-permute-start(bf16[512,256]{0,1:T(8,128)(2,1)S(1)} %convert_element_type.21), channel_id=1, source_target_pairs={{0,0},{1,8},{2,16},{3,24},{4,1},{5,9},{6,17},{7,25},{8,10},{9,2},{... | collective-permute-start | bytes 786440 | tf_op jit(solution)/shard_map/ppermute | solution.py:127
  180.7 4.3 %add_convert_fusion = bf16[512,1024]{1,0:T(8,128)(2,1)} fusion(f32[512,1024]{1,0:T(8,128)} %fusion.38, f32[512,1024]{1,0:T(8,128)} %fusion.40, f32[512,1024]{1,0:T(8,128)S(1)} %fusion.42, bf16[512,256]{0,1:T(8,128)(2,1)S(1)} %collective-permute-done.4, bf16[1024,1024]{0,1:T(8,128)(2,1)} %all-gather.2.cloned.1.call-done, s32[]{:T(128)S(6)} %select_n.19), kind=kOutput, calls=%fused_computation | convolution fusion | flops 274726912 | bytes 8126468 | tf_op jit(solution)/shard_map/dot_general | solution.py:134
  185.0 13.7 %collective-permute-done.5 = bf16[512,256]{0,1:T(8,128)(2,1)S(1)} collective-permute-done((bf16[512,256]{0,1:T(8,128)(2,1)S(1)}, bf16[512,256]{0,1:T(8,128)(2,1)S(1)}, u32[]{:S(2)}, u32[]{:S(2)}) %collective-permute-start.5) | collective-permute-done | bytes 262176 | tf_op jit(solution)/shard_map/ppermute | solution.py:127
  (82 shorter events, 29.9 us)
Async XLA Ops:
  7.2 54.8 %all-gather.2.cloned.1.call-start = ((), (), s32[]{:S(2)}) async-start(), calls=%async_computation.3 | async-start | bytes 2359296 | tf_op jit(solution)/shard_map/all_gather | solution.py:70
  15.1 23.4 %slice-start = ((f32[3,512,7]{1,2,0:T(8,128)}), f32[1,512,7]{1,2,0:T(8,128)S(1)}, s32[]{:S(2)}) async-start(f32[3,512,7]{1,2,0:T(8,128)} %param.7), calls=%async_computation.4 | async-start | bytes 32768 | tf_op jit(solution)/shard_map/slice | solution.py:102
  15.1 23.5 %copy-start.10 = (f32[3,512,7]{1,2,0:T(8,128)S(1)}, f32[3,512,7]{1,2,0:T(8,128)}, u32[]{:S(2)}) copy-start(f32[3,512,7]{1,2,0:T(8,128)} %param.7) | copy-start | bytes 129028
  15.1 23.6 %copy-start.5 = (f32[512,128]{1,0:T(8,128)S(1)}, f32[512,128]{1,0:T(8,128)}, u32[]{:S(2)}) copy-start(f32[512,128]{1,0:T(8,128)} %param.8) | copy-start | bytes 786436
  15.3 14.3 %collective-permute-start.6 = (bf16[128,1024]{0,1:T(8,128)(2,1)S(1)}, bf16[128,1024]{0,1:T(8,128)(2,1)S(1)}, u32[]{:S(2)}, u32[]{:S(2)}) collective-permute-start(bf16[128,1024]{0,1:T(8,128)(2,1)S(1)} %bitcast.118), channel_id=1, source_target_pairs={{0,0},{1,4},{2,8},{3,12},{4,16},{5,20},{6,24},{7,28},{8,1},{9,5},{... | collective-permute-start | bytes 786440 | tf_op jit(solution)/shard_map/ppermute | solution.py:69
  30.4 146.4 %reduce-scatter.2.cloned.1.call-start = ((), (), s32[]{:S(2)}) async-start(), calls=%async_computation.2 | async-start | bytes 4718592 | tf_op jit(solution)/shard_map/reduce_scatter | solution.py:121
  31.8 14.5 %copy-start.1 = (bf16[3,512,256]{1,2,0:T(8,128)(2,1)}, bf16[3,512,256]{1,2,0:T(8,128)(2,1)S(1)}, u32[]{:S(2)}) copy-start(bf16[3,512,256]{1,2,0:T(8,128)(2,1)S(1)} %copy.35) | copy-start | bytes 2359300
  32.0 14.4 %collective-permute-start = (bf16[3,512,133]{1,2,0:T(8,128)(2,1)S(1)}, bf16[3,512,133]{1,2,0:T(8,128)(2,1)S(1)}, u32[]{:S(2)}, u32[]{:S(2)}) collective-permute-start(bf16[3,512,133]{1,2,0:T(8,128)(2,1)S(1)} %get-tuple-element.26), channel_id=1, source_target_pairs={{0,8},{8,16},{16,24},{1,9},{9,17},{17,25},{2,10},{10,18},{18,26},{... | collective-permute-start | bytes 1225736 | tf_op jit(solution)/shard_map/ppermute | solution.py:13
  33.3 13.9 %collective-permute-start.1 = (bf16[3,512,133]{1,2,0:T(8,128)(2,1)S(1)}, bf16[3,512,133]{1,2,0:T(8,128)(2,1)}, u32[]{:S(2)}, u32[]{:S(2)}) collective-permute-start(bf16[3,512,133]{1,2,0:T(8,128)(2,1)S(1)} %get-tuple-element.27), channel_id=1, source_target_pairs={{8,0},{16,8},{24,16},{9,1},{17,9},{25,17},{10,2},{18,10},{26,18},{... | collective-permute-start | bytes 1225736 | tf_op jit(solution)/shard_map/ppermute | solution.py:14
  65.1 3.7 %copy-start.6 = (f32[1,512,389]{1,2,0:T(8,128)S(1)}, f32[1,512,389]{1,2,0:T(8,128)}, u32[]{:S(2)}) copy-start(f32[1,512,389]{1,2,0:T(8,128)} %get-tuple-element.19) | copy-start | bytes 2390020
  65.2 3.7 %copy-start.9 = (f32[512,1,128]{0,1,2:T(1,128)S(1)}, f32[512,1,128]{0,1,2:T(1,128)}, u32[]{:S(2)}) copy-start(f32[512,1,128]{0,1,2:T(1,128)} %copy.39) | copy-start | bytes 786436
  65.3 14.9 %collective-permute-start.7 = (f32[512,256]{0,1:T(8,128)S(1)}, f32[512,256]{0,1:T(8,128)S(1)}, u32[]{:S(2)}, u32[]{:S(2)}) collective-permute-start(f32[512,256]{0,1:T(8,128)S(1)} %get-tuple-element.16), channel_id=1, source_target_pairs={{0,8},{8,0},{16,24},{24,16},{1,9},{9,1},{17,25},{25,17},{2,10},{10... | collective-permute-start | bytes 1572872 | tf_op jit(solution)/shard_map/ppermute | solution.py:55
  65.9 25.0 %collective-permute-start.8 = (f32[512,256]{0,1:T(8,128)S(1)}, f32[512,256]{0,1:T(8,128)S(1)}, u32[]{:S(2)}, u32[]{:S(2)}) collective-permute-start(f32[512,256]{0,1:T(8,128)S(1)} %get-tuple-element.17), channel_id=1, source_target_pairs={{0,16},{8,24},{16,0},{24,8},{1,17},{9,25},{17,1},{25,9},{2,18},{10... | collective-permute-start | bytes 1572872 | tf_op jit(solution)/shard_map/ppermute | solution.py:55
  66.5 24.4 %collective-permute-start.9 = (f32[512,256]{0,1:T(8,128)S(1)}, f32[512,256]{0,1:T(8,128)S(1)}, u32[]{:S(2)}, u32[]{:S(2)}) collective-permute-start(f32[512,256]{0,1:T(8,128)S(1)} %get-tuple-element.18), channel_id=1, source_target_pairs={{0,24},{8,16},{16,8},{24,0},{1,25},{9,17},{17,9},{25,1},{2,26},{10... | collective-permute-start | bytes 1572872 | tf_op jit(solution)/shard_map/ppermute | solution.py:55
  91.2 6.0 %collective-permute-start.10 = (bf16[512,133]{0,1:T(8,128)(2,1)S(1)}, bf16[512,133]{0,1:T(8,128)(2,1)S(1)}, u32[]{:S(2)}, u32[]{:S(2)}) collective-permute-start(bf16[512,133]{0,1:T(8,128)(2,1)S(1)} %slice.441), channel_id=1, source_target_pairs={{8,0},{16,8},{24,16},{9,1},{17,9},{25,17},{10,2},{18,10},{26,18},{... | collective-permute-start | bytes 408584 | tf_op jit(solution)/shard_map/ppermute | solution.py:21
  97.9 5.5 %copy-start.2 = (f32[512,389]{0,1:T(8,128)S(1)}, f32[512,389]{0,1:T(8,128)}, u32[]{:S(2)}) copy-start(f32[512,389]{0,1:T(8,128)} %get-tuple-element.20) | copy-start | bytes 2390020
  97.9 5.5 %copy-start.3 = (f32[512,389]{0,1:T(8,128)S(1)}, f32[512,389]{0,1:T(8,128)}, u32[]{:S(2)}) copy-start(f32[512,389]{0,1:T(8,128)} %get-tuple-element.21) | copy-start | bytes 2390020
  97.9 5.5 %copy-start.12 = (f32[512]{0:T(512)S(1)}, f32[512]{0:T(512)}, u32[]{:S(2)}) copy-start(f32[512]{0:T(512)} %param.9) | copy-start | bytes 6148
  103.4 5.1 %copy-start = (bf16[512,1024]{1,0:T(8,128)(2,1)S(1)}, bf16[512,1024]{1,0:T(8,128)(2,1)}, u32[]{:S(2)}) copy-start(bf16[512,1024]{1,0:T(8,128)(2,1)} %param.10) | copy-start | bytes 3145732
  103.9 9.7 %collective-permute-start.2 = (bf16[512,256]{0,1:T(8,128)(2,1)S(1)}, bf16[512,256]{0,1:T(8,128)(2,1)S(1)}, u32[]{:S(2)}, u32[]{:S(2)}) collective-permute-start(bf16[512,256]{0,1:T(8,128)(2,1)S(1)} %fusion.36), channel_id=1, source_target_pairs={{0,8},{8,0},{16,24},{24,16},{1,9},{9,1},{17,25},{25,17},{2,10},{10... | collective-permute-start | bytes 786440 | tf_op jit(solution)/shard_map/ppermute | solution.py:55
  106.4 14.7 %collective-permute-start.4 = (bf16[512,256]{0,1:T(8,128)(2,1)S(1)}, bf16[512,256]{0,1:T(8,128)(2,1)S(1)}, u32[]{:S(2)}, u32[]{:S(2)}) collective-permute-start(bf16[512,256]{0,1:T(8,128)(2,1)S(1)} %fusion.36), channel_id=1, source_target_pairs={{0,24},{8,16},{16,8},{24,0},{1,25},{9,17},{17,9},{25,1},{2,26},{10... | collective-permute-start | bytes 786440 | tf_op jit(solution)/shard_map/ppermute | solution.py:55
  108.5 11.5 %collective-permute-start.3 = (bf16[512,256]{0,1:T(8,128)(2,1)S(1)}, bf16[512,256]{0,1:T(8,128)(2,1)S(1)}, u32[]{:S(2)}, u32[]{:S(2)}) collective-permute-start(bf16[512,256]{0,1:T(8,128)(2,1)S(1)} %fusion.36), channel_id=1, source_target_pairs={{0,16},{8,24},{16,0},{24,8},{1,17},{9,25},{17,1},{25,9},{2,18},{10... | collective-permute-start | bytes 786440 | tf_op jit(solution)/shard_map/ppermute | solution.py:55
  130.4 1.7 copy-start.4
  177.9 20.8 %collective-permute-start.5 = (bf16[512,256]{0,1:T(8,128)(2,1)S(1)}, bf16[512,256]{0,1:T(8,128)(2,1)S(1)}, u32[]{:S(2)}, u32[]{:S(2)}) collective-permute-start(bf16[512,256]{0,1:T(8,128)(2,1)S(1)} %convert_element_type.21), channel_id=1, source_target_pairs={{0,0},{1,8},{2,16},{3,24},{4,1},{5,9},{6,17},{7,25},{8,10},{9,2},{... | collective-permute-start | bytes 786440 | tf_op jit(solution)/shard_map/ppermute | solution.py:127
  (3 other events, 2.3 us)
Sparse Core Ops, SparseCore 0:
  30.5 31.4 all-gather.1
  127.0 49.7 reduce-scatter.1

commit v3 on v2

--- a/solution.py
+++ b/solution.py
@@ -47,6 +47,12 @@
     return (index + step) % count
 
 
+def source(index, step, count):
+    if count & (count - 1) == 0:
+        return index ^ step
+    return (index - step) % count
+
+
 def exchange(block_of, axis):
     count = lax.axis_size(axis)
     got = []
@@ -59,7 +65,16 @@
 def rows_of_slab(out_grad, n_seq, n_tp):
     rows, length = out_grad.shape
     piece = rows // n_seq
-    mine = lax.all_to_all(out_grad.reshape(n_seq, piece, length), "seq", 0, 0)
+    me = lax.axis_index("seq")
+    split = out_grad.reshape(n_seq, piece, length)
+    got = exchange(lambda step: split[partner(me, step, n_seq)], "seq")
+    stacked = jnp.stack([split[me]] + got)
+    index = jnp.zeros((n_seq,), jnp.int32)
+    for step in range(1, n_seq):
+        index = index + jnp.where(
+            jnp.arange(n_seq) == source(me, step, n_seq), step, 0
+        ).astype(jnp.int32)
+    mine = jnp.take(stacked, index, axis=0)
     mine = jnp.transpose(mine, (1, 0, 2)).reshape(piece, n_seq * length)
     route = []
     for a in range(n_seq):
@@ -81,20 +96,10 @@
     reach = taps_long + taps_short - 2
     keep = length + taps_short - 1
 
+    widened = extended(streams, "seq", reach).astype(jnp.float32)
     slab_grad = rows_of_slab(out_grad, n_seq, n_tp)
     slab_width = slab_grad.shape[0]
-    partial_grad = jnp.dot(out_weight, slab_grad, preferred_element_type=jnp.float32)
 
-    def grad_block(step):
-        start = partner(me, step, n_seq) * length
-        return lax.dynamic_slice_in_dim(partial_grad, start, length, axis=1)
-
-    arrived = exchange(grad_block, "seq")
-    gated_grad = lax.dynamic_slice_in_dim(partial_grad, me * length, length, axis=1)
-    for block in arrived:
-        gated_grad = gated_grad + block
-
-    widened = extended(streams, "seq", reach).astype(jnp.float32)
     key_value = short_correlate(
         widened[1:, :, : taps_long - 1 + keep + taps_short - 1], feat_weight[1:, :, ::-1]
     )
@@ -122,15 +127,28 @@
     route = []
     for s in range(n_seq):
         for p in range(n_tp):
-            target = partner(s, p % n_seq, n_seq) if p % n_seq else s
+            target = source(s, p % n_seq, n_seq) if p % n_seq else s
             route.append((s * n_tp + p, target * n_tp + group * s + p // n_seq))
     mixed = lax.ppermute(output_sum.astype(jnp.bfloat16), ("seq", "tp"), route)
+
+    slab_grad, gated_blocks = lax.optimization_barrier((slab_grad, gated_blocks))
+    partial_grad = jnp.dot(out_weight, slab_grad, preferred_element_type=jnp.float32)
+
+    def grad_block(step):
+        start = partner(me, step, n_seq) * length
+        block = lax.dynamic_slice_in_dim(partial_grad, start, length, axis=1)
+        return block.astype(jnp.bfloat16)
+
+    arrived = exchange(grad_block, "seq")
+    gated_grad = lax.dynamic_slice_in_dim(partial_grad, me * length, length, axis=1)
+    for block in arrived:
+        gated_grad = gated_grad + block.astype(jnp.float32)
 
     scale = 1.0 / math.sqrt(length * n_seq)
     weight_sum = None
     for step, block in enumerate(gated_blocks):
-        source = partner(me, step, n_seq) if step else me
-        grad_part = lax.dynamic_slice_in_dim(slab_grad, source * length, length, axis=1)
+        origin = source(me, step, n_seq) if step else me
+        grad_part = lax.dynamic_slice_in_dim(slab_grad, origin * length, length, axis=1)
         term = lax.dot_general(
             block, grad_part, (((1,), (1,)), ((), ())), preferred_element_type=jnp.float32
         )

time: 207 us -> 156 us (0.75)
  the two profiles are of different devices: /device:TPU:6 before, /device:TPU:4 now
where the time goes in v3:
time: 156 us
  waiting for transfers between devices  63.1 us (40%)
  starting transfers between devices  27.3 us (18%)
  matrix products  26.4 us (17%)
  local copies, waits for them, and re-layouts  17.3 us (11%)
  between operations  14.7 us (9%)
  other arithmetic  6.81 us (4%)
    ppermute x9, waiting for transfers between devices, exchange(): got.append(lax.ppermute(block_of(step), axis, route))  22.6 us
    reduce_scatter x1, waiting for transfers between devices, shards(): lax.psum_scatter(partial_out, 'tp', scatter_dimension=0, tiled=True)  16.7 us
    ppermute x1, waiting for transfers between devices, shards(): mixed = lax.ppermute(output_sum.astype(jnp.bfloat16), ('seq', 'tp'), route)  16.4 us
    ppermute x9, starting transfers between devices, exchange(): got.append(lax.ppermute(block_of(step), axis, route))  13.2 us
    conv_general_dilated x2, matrix products, correlate(): lax.conv_general_dilated(signal[None], taps[:, None, :], (1,), 'VALID', d...  10.9 us
    dot_general x8, matrix products, shards(): lax.dot_general(rows, block, (((0,), (0,)), ((), ())), preferred_element_...  9.11 us
    unnamed x85, local copies, waits for them, and re-layouts  8.77 us
    ppermute x1, waiting for transfers between devices, rows_of_slab(): moved = lax.ppermute(mine, ('seq', 'tp'), route)  5.93 us
  transfers between devices with their start and end apart: 16, of which 9 were waited for; matrix products, arithmetic and copies ran while one was open for 30% of the time, Pallas kernels for 0%

profile of v3, /device:TPU:4, one launch (start us, length us, event | category | flops | bytes accessed | tf_op | source)
XLA Modules:
  0.0 155.6 jit_solution(11315247083268115491)
XLA Ops:
  8.2 1.5 collective-permute-start.8
  9.7 1.5 collective-permute-start.7
  11.8 1.4 copy.27
  13.3 3.4 %collective-permute-start = (bf16[3,512,133]{1,2,0:T(8,128)(2,1)S(1)}, bf16[3,512,133]{1,2,0:T(8,128)(2,1)S(1)}, u32[]{:S(2)}, u32[]{:S(2)}) collective-permute-start(bf16[3,512,133]{1,2,0:T(8,128)(2,1)S(1)} %get-tuple-element.30), channel_id=1, source_target_pairs={{0,8},{8,16},{16,24},{1,9},{9,17},{17,25},{2,10},{10,18},{18,26},{... | collective-permute-start | bytes 1225736 | tf_op jit(solution)/shard_map/ppermute | solution.py:13
  16.7 3.3 %collective-permute-start.1 = (bf16[3,512,133]{1,2,0:T(8,128)(2,1)S(1)}, bf16[3,512,133]{1,2,0:T(8,128)(2,1)S(1)}, u32[]{:S(2)}, u32[]{:S(2)}) collective-permute-start(bf16[3,512,133]{1,2,0:T(8,128)(2,1)S(1)} %get-tuple-element.31), channel_id=1, source_target_pairs={{8,0},{16,8},{24,16},{9,1},{17,9},{25,17},{10,2},{18,10},{26,18},{... | collective-permute-start | bytes 1225736 | tf_op jit(solution)/shard_map/ppermute | solution.py:14
  22.9 1.9 %collective-permute-start.9 = (bf16[128,1024]{0,1:T(8,128)(2,1)}, bf16[128,1024]{0,1:T(8,128)(2,1)S(1)}, u32[]{:S(2)}, u32[]{:S(2)}) collective-permute-start(bf16[128,1024]{0,1:T(8,128)(2,1)} %bitcast.29), channel_id=1, source_target_pairs={{0,0},{1,4},{2,8},{3,12},{4,16},{5,20},{6,24},{7,28},{8,1},{9,5},{... | collective-permute-start | bytes 786440 | tf_op jit(solution)/shard_map/ppermute | solution.py:84
  27.8 1.7 %fusion.69 = (f32[512,1]{0,1:T(1,128)}, f32[512,1]{0,1:T(1,128)}, f32[512,1]{0,1:T(1,128)}, f32[512,1]{0,1:T(1,128)}, f32[512,1]{0,1:T(1,128)}, /*index=5*/f32[512,1]{0,1:T(1,128)}, f32[512,1]{0,1:T(1,128)}) fusion(f32[512,7]{0,1:T(8,128)} %bitcast.143), kind=kLoop, calls=%fused_computation.149 | loop fusion | bytes 28672 | tf_op jit(solution)/shard_map/slice | solution.py:38
  29.5 5.9 %collective-permute-done.9 = bf16[128,1024]{0,1:T(8,128)(2,1)S(1)} collective-permute-done((bf16[128,1024]{0,1:T(8,128)(2,1)}, bf16[128,1024]{0,1:T(8,128)(2,1)S(1)}, u32[]{:S(2)}, u32[]{:S(2)}) %collective-permute-start.9) | collective-permute-done | bytes 262176 | tf_op jit(solution)/shard_map/ppermute | solution.py:84
  38.4 5.4 %fusion.30 = f32[1,512,262]{1,0,2:T(1,128)S(1)} fusion(f32[512,1,128]{0,1,2:T(1,128)S(1)} %copy.31, f32[1,512,389]{1,2,0:T(8,128)S(1)} %get-tuple-element.27), kind=kOutput, calls=%fused_computation.67 | convolution fusion | flops 206045184 | bytes 1595392 | tf_op jit(solution)/shard_map/conv_general_dilated | solution.py:25
  45.4 2.7 %collective-permute-start.2 = (bf16[512,256]{0,1:T(8,128)(2,1)S(1)}, bf16[512,256]{0,1:T(8,128)(2,1)S(1)}, u32[]{:S(2)}, u32[]{:S(2)}) collective-permute-start(bf16[512,256]{0,1:T(8,128)(2,1)S(1)} %fusion.36), channel_id=1, source_target_pairs={{0,8},{8,0},{16,24},{24,16},{1,9},{9,1},{17,25},{25,17},{2,10},{10... | collective-permute-start | bytes 786440 | tf_op jit(solution)/shard_map/ppermute | solution.py:61
  48.1 2.9 %collective-permute-start.4 = (bf16[512,256]{0,1:T(8,128)(2,1)S(1)}, bf16[512,256]{0,1:T(8,128)(2,1)S(1)}, u32[]{:S(2)}, u32[]{:S(2)}) collective-permute-start(bf16[512,256]{0,1:T(8,128)(2,1)S(1)} %fusion.36), channel_id=1, source_target_pairs={{0,24},{8,16},{16,8},{24,0},{1,25},{9,17},{17,9},{25,1},{2,26},{10... | collective-permute-start | bytes 786440 | tf_op jit(solution)/shard_map/ppermute | solution.py:61
  54.6 10.6 %collective-permute-done.3 = bf16[512,256]{0,1:T(8,128)(2,1)S(1)} collective-permute-done((bf16[512,256]{0,1:T(8,128)(2,1)S(1)}, bf16[512,256]{0,1:T(8,128)(2,1)S(1)}, u32[]{:S(2)}, u32[]{:S(2)}) %collective-permute-start.3) | collective-permute-done | bytes 262176 | tf_op jit(solution)/shard_map/ppermute | solution.py:61
  72.7 1.8 %copy.34 = f32[512,1,128]{0,1,2:T(1,128)} copy(f32[512,1,128]{2,0,1:T(8,128)} %bitcast.137) | data formatting | bytes 524288 | tf_op jit(solution)/shard_map/broadcast_in_dim | solution.py:27
  76.0 3.0 %fusion.70 = f32[1024,512]{1,0:T(8,128)S(1)} fusion(bf16[1024,1024]{0,1:T(8,128)(2,1)} %all-gather.2.cloned.1.call-done, bf16[512,1024]{1,0:T(8,128)(2,1)S(1)} %copy-done), kind=kOutput, calls=%fused_computation.150 | convolution fusion | flops 1073741824 | bytes 5242880 | tf_op jit(solution)/shard_map/dot_general | solution.py:135
  79.1 1.6 %collective-permute-start.10 = (bf16[512,256]{0,1:T(8,128)(2,1)S(1)}, bf16[512,256]{0,1:T(8,128)(2,1)S(1)}, u32[]{:S(2)}, u32[]{:S(2)}) collective-permute-start(bf16[512,256]{0,1:T(8,128)(2,1)S(1)} %get-tuple-element.22), channel_id=1, source_target_pairs={{0,8},{8,0},{16,24},{24,16},{1,9},{9,1},{17,25},{25,17},{2,10},{10... | collective-permute-start | bytes 786440 | tf_op jit(solution)/shard_map/ppermute | solution.py:61
  84.1 4.3 %collective-permute-done.10 = bf16[512,256]{0,1:T(8,128)(2,1)S(1)} collective-permute-done((bf16[512,256]{0,1:T(8,128)(2,1)S(1)}, bf16[512,256]{0,1:T(8,128)(2,1)S(1)}, u32[]{:S(2)}, u32[]{:S(2)}) %collective-permute-start.10) | collective-permute-done | bytes 262176 | tf_op jit(solution)/shard_map/ppermute | solution.py:61
  88.4 5.5 %collective-permute-done.12 = bf16[512,256]{0,1:T(8,128)(2,1)S(1)} collective-permute-done((bf16[512,256]{0,1:T(8,128)(2,1)S(1)}, bf16[512,256]{0,1:T(8,128)(2,1)S(1)}, u32[]{:S(2)}, u32[]{:S(2)}) %collective-permute-start.12) | collective-permute-done | bytes 262176 | tf_op jit(solution)/shard_map/ppermute | solution.py:61
  95.4 3.4 %collective-permute-start.13 = (bf16[512,133]{0,1:T(8,128)(2,1)S(1)}, bf16[512,133]{0,1:T(8,128)(2,1)S(1)}, u32[]{:S(2)}, u32[]{:S(2)}) collective-permute-start(bf16[512,133]{0,1:T(8,128)(2,1)S(1)} %slice.443), channel_id=1, source_target_pairs={{8,0},{16,8},{24,16},{9,1},{17,9},{25,17},{10,2},{18,10},{26,18},{... | collective-permute-start | bytes 408584 | tf_op jit(solution)/shard_map/ppermute | solution.py:21
  98.9 1.9 %add_convert_fusion = bf16[512,1024]{1,0:T(8,128)(2,1)} fusion(f32[512,1024]{1,0:T(8,128)S(1)} %fusion.40, f32[512,1024]{1,0:T(8,128)S(1)} %fusion.42, f32[512,1024]{1,0:T(8,128)S(1)} %fusion.44, bf16[512,256]{0,1:T(8,128)(2,1)S(1)} %copy-done.4, bf16[1024,1024]{0,1:T(8,128)(2,1)S(1)} %copy-done.9, s32[]{:T(128)S(6)} %select_n.112), kind=kOutput, calls=%fused_computation.1 | convolution fusion | flops 274726912 | bytes 8126468 | tf_op jit(solution)/shard_map/dot_general | solution.py:152
  100.8 1.5 collective-permute-done.13
  103.5 5.5 %fusion.28 = f32[1,512,262]{1,0,2:T(1,128)S(1)} fusion(f32[512,1,128]{0,1,2:T(1,128)S(1)} %copy-done.12, f32[1,512,389]{1,2,0:T(8,128)S(1)} %bitcast.136), kind=kOutput, calls=%fused_computation.65 | convolution fusion | flops 206045184 | bytes 1595392 | tf_op jit(solution)/shard_map/conv_general_dilated | solution.py:25
  109.5 16.7 %reduce-scatter.2.cloned.1.call-done = f32[512,256]{0,1:T(8,128)} async-done(((f32[4096,256]{0,1:T(8,128)}), f32[512,256]{0,1:T(8,128)}) %reduce-scatter.2.cloned.1.call-update) | async-done | bytes 524304 | tf_op jit(solution)/shard_map/reduce_scatter | solution.py:126
  127.2 1.9 %collective-permute-start.5 = (bf16[512,256]{0,1:T(8,128)(2,1)S(1)}, bf16[512,256]{0,1:T(8,128)(2,1)S(1)}, u32[]{:S(2)}, u32[]{:S(2)}) collective-permute-start(bf16[512,256]{0,1:T(8,128)(2,1)S(1)} %convert_element_type.48), channel_id=1, source_target_pairs={{0,0},{1,8},{2,16},{3,24},{4,1},{5,9},{6,17},{7,25},{8,10},{9,2},{... | collective-permute-start | bytes 786440 | tf_op jit(solution)/shard_map/ppermute | solution.py:132
  131.6 16.4 %collective-permute-done.5 = bf16[512,256]{0,1:T(8,128)(2,1)S(1)} collective-permute-done((bf16[512,256]{0,1:T(8,128)(2,1)S(1)}, bf16[512,256]{0,1:T(8,128)(2,1)S(1)}, u32[]{:S(2)}, u32[]{:S(2)}) %collective-permute-start.5) | collective-permute-done | bytes 262176 | tf_op jit(solution)/shard_map/ppermute | solution.py:132
  (145 shorter events, 35.1 us)
Async XLA Ops:
  7.2 12.9 %copy-start.13 = (f32[3,512,7]{1,2,0:T(8,128)S(1)}, f32[3,512,7]{1,2,0:T(8,128)}, u32[]{:S(2)}) copy-start(f32[3,512,7]{1,2,0:T(8,128)} %param.7) | copy-start | bytes 129028
  7.2 68.8 %all-gather.2.cloned.1.call-start = ((), (), s32[]{:S(2)}) async-start(), calls=%async_computation.2 | async-start | bytes 2359296 | tf_op jit(solution)/shard_map/all_gather | solution.py:85
  8.2 13.1 %collective-permute-start.8 = (bf16[128,256]{1,0:T(8,128)(2,1)S(1)}, bf16[128,256]{1,0:T(8,128)(2,1)S(1)}, u32[]{:S(2)}, u32[]{:S(2)}) collective-permute-start(bf16[128,256]{1,0:T(8,128)(2,1)S(1)} %get-tuple-element.33), channel_id=1, source_target_pairs={{0,24},{8,16},{16,8},{24,0},{1,25},{9,17},{17,9},{25,1},{2,26},{10... | collective-permute-start | bytes 196616 | tf_op jit(solution)/shard_map/ppermute | solution.py:61
  9.7 11.7 %collective-permute-start.7 = (bf16[128,256]{1,0:T(8,128)(2,1)S(1)}, bf16[128,256]{1,0:T(8,128)(2,1)S(1)}, u32[]{:S(2)}, u32[]{:S(2)}) collective-permute-start(bf16[128,256]{1,0:T(8,128)(2,1)S(1)} %get-tuple-element.34), channel_id=1, source_target_pairs={{0,16},{8,24},{16,0},{24,8},{1,17},{9,25},{17,1},{25,9},{2,18},{10... | collective-permute-start | bytes 196616 | tf_op jit(solution)/shard_map/ppermute | solution.py:61
  11.2 10.1 %collective-permute-start.6 = (bf16[128,256]{1,0:T(8,128)(2,1)S(1)}, bf16[128,256]{1,0:T(8,128)(2,1)S(1)}, u32[]{:S(2)}, u32[]{:S(2)}) collective-permute-start(bf16[128,256]{1,0:T(8,128)(2,1)S(1)} %get-tuple-element.35), channel_id=1, source_target_pairs={{0,8},{8,0},{16,24},{24,16},{1,9},{9,1},{17,25},{25,17},{2,10},{10... | collective-permute-start | bytes 196616 | tf_op jit(solution)/shard_map/ppermute | solution.py:61
  13.2 12.3 %slice-start = ((f32[3,512,7]{1,2,0:T(8,128)}), f32[1,512,7]{1,2,0:T(8,128)S(1)}, s32[]{:S(2)}) async-start(f32[3,512,7]{1,2,0:T(8,128)} %param.7), calls=%async_computation.3 | async-start | bytes 32768 | tf_op jit(solution)/shard_map/slice | solution.py:107
  13.2 14.1 %copy-start.10 = (f32[512,128]{1,0:T(8,128)S(1)}, f32[512,128]{1,0:T(8,128)}, u32[]{:S(2)}) copy-start(f32[512,128]{1,0:T(8,128)} %param.8) | copy-start | bytes 786436
  13.3 22.9 %collective-permute-start = (bf16[3,512,133]{1,2,0:T(8,128)(2,1)S(1)}, bf16[3,512,133]{1,2,0:T(8,128)(2,1)S(1)}, u32[]{:S(2)}, u32[]{:S(2)}) collective-permute-start(bf16[3,512,133]{1,2,0:T(8,128)(2,1)S(1)} %get-tuple-element.30), channel_id=1, source_target_pairs={{0,8},{8,16},{16,24},{1,9},{9,17},{17,25},{2,10},{10,18},{18,26},{... | collective-permute-start | bytes 1225736 | tf_op jit(solution)/shard_map/ppermute | solution.py:13
  16.7 19.5 %collective-permute-start.1 = (bf16[3,512,133]{1,2,0:T(8,128)(2,1)S(1)}, bf16[3,512,133]{1,2,0:T(8,128)(2,1)S(1)}, u32[]{:S(2)}, u32[]{:S(2)}) collective-permute-start(bf16[3,512,133]{1,2,0:T(8,128)(2,1)S(1)} %get-tuple-element.31), channel_id=1, source_target_pairs={{8,0},{16,8},{24,16},{9,1},{17,9},{25,17},{10,2},{18,10},{26,18},{... | collective-permute-start | bytes 1225736 | tf_op jit(solution)/shard_map/ppermute | solution.py:14
  22.9 12.5 %collective-permute-start.9 = (bf16[128,1024]{0,1:T(8,128)(2,1)}, bf16[128,1024]{0,1:T(8,128)(2,1)S(1)}, u32[]{:S(2)}, u32[]{:S(2)}) collective-permute-start(bf16[128,1024]{0,1:T(8,128)(2,1)} %bitcast.29), channel_id=1, source_target_pairs={{0,0},{1,4},{2,8},{3,12},{4,16},{5,20},{6,24},{7,28},{8,1},{9,5},{... | collective-permute-start | bytes 786440 | tf_op jit(solution)/shard_map/ppermute | solution.py:84
  36.2 89.9 %reduce-scatter.2.cloned.1.call-start = ((), (), s32[]{:S(2)}) async-start(), calls=%async_computation.1 | async-start | bytes 4718592 | tf_op jit(solution)/shard_map/reduce_scatter | solution.py:126
  44.6 6.9 %copy-start = (bf16[512,1024]{1,0:T(8,128)(2,1)S(1)}, bf16[512,1024]{1,0:T(8,128)(2,1)}, u32[]{:S(2)}) copy-start(bf16[512,1024]{1,0:T(8,128)(2,1)} %param.10) | copy-start | bytes 3145732
  45.4 8.1 %collective-permute-start.2 = (bf16[512,256]{0,1:T(8,128)(2,1)S(1)}, bf16[512,256]{0,1:T(8,128)(2,1)S(1)}, u32[]{:S(2)}, u32[]{:S(2)}) collective-permute-start(bf16[512,256]{0,1:T(8,128)(2,1)S(1)} %fusion.36), channel_id=1, source_target_pairs={{0,8},{8,0},{16,24},{24,16},{1,9},{9,1},{17,25},{25,17},{2,10},{10... | collective-permute-start | bytes 786440 | tf_op jit(solution)/shard_map/ppermute | solution.py:61
  48.1 18.3 %collective-permute-start.4 = (bf16[512,256]{0,1:T(8,128)(2,1)S(1)}, bf16[512,256]{0,1:T(8,128)(2,1)S(1)}, u32[]{:S(2)}, u32[]{:S(2)}) collective-permute-start(bf16[512,256]{0,1:T(8,128)(2,1)S(1)} %fusion.36), channel_id=1, source_target_pairs={{0,24},{8,16},{16,8},{24,0},{1,25},{9,17},{17,9},{25,1},{2,26},{10... | collective-permute-start | bytes 786440 | tf_op jit(solution)/shard_map/ppermute | solution.py:61
  51.0 14.2 %collective-permute-start.3 = (bf16[512,256]{0,1:T(8,128)(2,1)S(1)}, bf16[512,256]{0,1:T(8,128)(2,1)S(1)}, u32[]{:S(2)}, u32[]{:S(2)}) collective-permute-start(bf16[512,256]{0,1:T(8,128)(2,1)S(1)} %fusion.36), channel_id=1, source_target_pairs={{0,16},{8,24},{16,0},{24,8},{1,17},{9,25},{17,1},{25,9},{2,18},{10... | collective-permute-start | bytes 786440 | tf_op jit(solution)/shard_map/ppermute | solution.py:61
  53.5 15.2 %copy-start.5 = (bf16[512,256]{0,1:T(8,128)(2,1)}, bf16[512,256]{0,1:T(8,128)(2,1)S(1)}, u32[]{:S(2)}) copy-start(bf16[512,256]{0,1:T(8,128)(2,1)S(1)} %collective-permute-done.2) | copy-start | bytes 786436
  76.0 6.7 %copy-start.8 = (bf16[512,256]{0,1:T(8,128)(2,1)S(1)}, bf16[512,256]{0,1:T(8,128)(2,1)}, u32[]{:S(2)}) copy-start(bf16[512,256]{0,1:T(8,128)(2,1)} %copy-done.7) | copy-start | bytes 786436
  76.0 6.7 %copy-start.9 = (bf16[1024,1024]{0,1:T(8,128)(2,1)S(1)}, bf16[1024,1024]{0,1:T(8,128)(2,1)}, u32[]{:S(2)}) copy-start(bf16[1024,1024]{0,1:T(8,128)(2,1)} %all-gather.2.cloned.1.call-done) | copy-start | bytes 6291460
  79.1 9.2 %collective-permute-start.10 = (bf16[512,256]{0,1:T(8,128)(2,1)S(1)}, bf16[512,256]{0,1:T(8,128)(2,1)S(1)}, u32[]{:S(2)}, u32[]{:S(2)}) collective-permute-start(bf16[512,256]{0,1:T(8,128)(2,1)S(1)} %get-tuple-element.22), channel_id=1, source_target_pairs={{0,8},{8,0},{16,24},{24,16},{1,9},{9,1},{17,25},{25,17},{2,10},{10... | collective-permute-start | bytes 786440 | tf_op jit(solution)/shard_map/ppermute | solution.py:61
  80.7 13.1 %collective-permute-start.12 = (bf16[512,256]{0,1:T(8,128)(2,1)S(1)}, bf16[512,256]{0,1:T(8,128)(2,1)S(1)}, u32[]{:S(2)}, u32[]{:S(2)}) collective-permute-start(bf16[512,256]{0,1:T(8,128)(2,1)S(1)} %get-tuple-element.23), channel_id=1, source_target_pairs={{0,24},{8,16},{16,8},{24,0},{1,25},{9,17},{17,9},{25,1},{2,26},{10... | collective-permute-start | bytes 786440 | tf_op jit(solution)/shard_map/ppermute | solution.py:61
  81.5 13.8 %collective-permute-start.11 = (bf16[512,256]{0,1:T(8,128)(2,1)S(1)}, bf16[512,256]{0,1:T(8,128)(2,1)S(1)}, u32[]{:S(2)}, u32[]{:S(2)}) collective-permute-start(bf16[512,256]{0,1:T(8,128)(2,1)S(1)} %get-tuple-element.24), channel_id=1, source_target_pairs={{0,16},{8,24},{16,0},{24,8},{1,17},{9,25},{17,1},{25,9},{2,18},{10... | collective-permute-start | bytes 786440 | tf_op jit(solution)/shard_map/ppermute | solution.py:61
  83.6 15.2 %copy-start.4 = (bf16[512,256]{0,1:T(8,128)(2,1)S(1)}, bf16[512,256]{0,1:T(8,128)(2,1)}, u32[]{:S(2)}) copy-start(bf16[512,256]{0,1:T(8,128)(2,1)} %copy-done.3) | copy-start | bytes 786436
  95.4 6.9 %collective-permute-start.13 = (bf16[512,133]{0,1:T(8,128)(2,1)S(1)}, bf16[512,133]{0,1:T(8,128)(2,1)S(1)}, u32[]{:S(2)}, u32[]{:S(2)}) collective-permute-start(bf16[512,133]{0,1:T(8,128)(2,1)S(1)} %slice.443), channel_id=1, source_target_pairs={{8,0},{16,8},{24,16},{9,1},{17,9},{25,17},{10,2},{18,10},{26,18},{... | collective-permute-start | bytes 408584 | tf_op jit(solution)/shard_map/ppermute | solution.py:21
  127.2 20.7 %collective-permute-start.5 = (bf16[512,256]{0,1:T(8,128)(2,1)S(1)}, bf16[512,256]{0,1:T(8,128)(2,1)S(1)}, u32[]{:S(2)}, u32[]{:S(2)}) collective-permute-start(bf16[512,256]{0,1:T(8,128)(2,1)S(1)} %convert_element_type.48), channel_id=1, source_target_pairs={{0,0},{1,8},{2,16},{3,24},{4,1},{5,9},{6,17},{7,25},{8,10},{9,2},{... | collective-permute-start | bytes 786440 | tf_op jit(solution)/shard_map/ppermute | solution.py:132
  (30 other events, 58.7 us)
Sparse Core Ops, SparseCore 0:
  36.2 38.6 all-gather.1
  77.2 48.8 reduce-scatter.1

commit v4 on v3

--- a/solution.py
+++ b/solution.py
@@ -6,13 +6,24 @@
 from jax.sharding import PartitionSpec as P
 
 
-def extended(block, axis, width):
+def halo(block, axis, width, short):
     count = lax.axis_size(axis)
     forward = [(i, i + 1) for i in range(count - 1)]
     backward = [(target, source) for source, target in forward]
-    low = lax.ppermute(block[..., block.shape[-1] - width :], axis, forward)
-    high = lax.ppermute(block[..., :width], axis, backward)
-    return jnp.concatenate([low, block, high], axis=-1)
+    length = block.shape[-1]
+    low = jnp.concatenate(
+        [block[1, :, length - width :], block[2, :, length - width :], block[0, :, length - short :]],
+        axis=-1,
+    )
+    high = jnp.concatenate([block[0, :, :width], block[1, :, :short], block[2, :, :short]], axis=-1)
+    low = lax.ppermute(low, axis, forward)
+    high = lax.ppermute(high, axis, backward)
+    query = jnp.concatenate([low[:, 2 * width :], block[0], high[:, :width]], axis=-1)
+    key = jnp.concatenate([low[:, :width], block[1], high[:, width : width + short]], axis=-1)
+    value = jnp.concatenate(
+        [low[:, width : 2 * width], block[2], high[:, width + short :]], axis=-1
+    )
+    return query, jnp.stack([key, value])
 
 
 def from_behind(block, axis, distance):
@@ -96,15 +107,13 @@
     reach = taps_long + taps_short - 2
     keep = length + taps_short - 1
 
-    widened = extended(streams, "seq", reach).astype(jnp.float32)
+    query_in, key_value_in = halo(streams, "seq", reach, taps_short - 1)
     slab_grad = rows_of_slab(out_grad, n_seq, n_tp)
     slab_width = slab_grad.shape[0]
 
-    key_value = short_correlate(
-        widened[1:, :, : taps_long - 1 + keep + taps_short - 1], feat_weight[1:, :, ::-1]
-    )
+    key_value = short_correlate(key_value_in.astype(jnp.float32), feat_weight[1:, :, ::-1])
     key_feat, value_feat = key_value[0], key_value[1]
-    query_tail = short_correlate(widened[0, :, taps_long - 1 :], feat_weight[0, :, ::-1])
+    query_tail = short_correlate(query_in.astype(jnp.float32), feat_weight[0, :, ::-1])
     product = key_feat * value_feat
     convolved = correlate(product, long_filter[:, ::-1])
     summed = convolved + skip_gain[:, None] * product[:, taps_long - 1 :]
@@ -120,7 +129,7 @@
             pieces.append(
                 lax.dot_general(
                     rows, block, (((0,), (0,)), ((), ())), preferred_element_type=jnp.float32
-                )
+                ).astype(jnp.bfloat16)
             )
     partial_out = jnp.concatenate(pieces, axis=0)
     output_sum = lax.psum_scatter(partial_out, "tp", scatter_dimension=0, tiled=True)
@@ -129,7 +138,7 @@
         for p in range(n_tp):
             target = source(s, p % n_seq, n_seq) if p % n_seq else s
             route.append((s * n_tp + p, target * n_tp + group * s + p // n_seq))
-    mixed = lax.ppermute(output_sum.astype(jnp.bfloat16), ("seq", "tp"), route)
+    mixed = lax.ppermute(output_sum, ("seq", "tp"), route)
 
     slab_grad, gated_blocks = lax.optimization_barrier((slab_grad, gated_blocks))
     partial_grad = jnp.dot(out_weight, slab_grad, preferred_element_type=jnp.float32)

time: 156 us -> 141 us (0.904)
  waiting for transfers between devices: 63.1 us -> 52 us
  local copies, waits for them, and re-layouts: 17.3 us -> 13.9 us
    reduce_scatter x1, waiting for transfers between devices: 16.7 us -> 4.13 us  [shards(): lax.psum_scatter(partial_out, 'tp', scatter_dimension=0, tiled=True)]
    slice x1 -> x8, local copies, waits for them, and re-layouts: 0.1 us -> 3.32 us  [the longest x1 1.37 us: halo(): block[1, :, length - width:]]
    unnamed x85 -> x83, local copies, waits for them, and re-layouts: 8.77 us -> 5.62 us
    ppermute x9, starting transfers between devices: 13.2 us -> 11.5 us  [exchange(): got.append(lax.ppermute(block_of(step), axis, route))]
    ppermute x1, starting transfers between devices: 1.91 us -> 3.51 us  [rows_of_slab(): moved = lax.ppermute(mine, ('seq', 'tp'), route)]
  transfers between devices with their start and end apart: 16 -> 16, of which waited for: 9 -> 11; matrix products, arithmetic and copies ran while one was open for 30% -> 29% of each run, Pallas kernels for 0% -> 0%
where the time goes in v4:
time: 141 us; the launch traced here: 140 us
  waiting for transfers between devices  52 us (37%)
  matrix products  26.7 us (19%)
  starting transfers between devices  26.4 us (19%)
  between operations  14.7 us (10%)
  local copies, waits for them, and re-layouts  13.9 us (10%)
  other arithmetic  6.44 us (5%)
    ppermute x9, waiting for transfers between devices, exchange(): got.append(lax.ppermute(block_of(step), axis, route))  22.9 us
    ppermute x1, waiting for transfers between devices, shards(): mixed = lax.ppermute(output_sum, ('seq', 'tp'), route)  15.6 us
    conv_general_dilated x2, matrix products, correlate(): lax.conv_general_dilated(signal[None], taps[:, None, :], (1,), 'VALID', d...  11.8 us
    ppermute x9, starting transfers between devices, exchange(): got.append(lax.ppermute(block_of(step), axis, route))  11.5 us
    dot_general x8, matrix products, shards(): lax.dot_general(rows, block, (((0,), (0,)), ((), ())), preferred_element_...  8.29 us
    ppermute x1, waiting for transfers between devices, rows_of_slab(): moved = lax.ppermute(mine, ('seq', 'tp'), route)  6.43 us
    unnamed x83, local copies, waits for them, and re-layouts  5.62 us
    reduce_scatter x1, waiting for transfers between devices, shards(): lax.psum_scatter(partial_out, 'tp', scatter_dimension=0, tiled=True)  4.13 us
  transfers between devices with their start and end apart: 16, of which 11 were waited for; matrix products, arithmetic and copies ran while one was open for 29% of the time, Pallas kernels for 0%

profile of v4, /device:TPU:4, one launch (start us, length us, event | category | flops | bytes accessed | tf_op | source)
XLA Modules:
  0.0 140.2 jit_solution(4943270358451238051)
XLA Ops:
  8.4 1.4 fusion.75
  10.8 3.3 %collective-permute-start.1 = (bf16[512,145]{0,1:T(8,128)(2,1)}, bf16[512,145]{0,1:T(8,128)(2,1)S(1)}, u32[]{:S(2)}, u32[]{:S(2)}) collective-permute-start(bf16[512,145]{0,1:T(8,128)(2,1)} %pad_maximum_fusion.4), channel_id=1, source_target_pairs={{8,0},{16,8},{24,16},{9,1},{17,9},{25,17},{10,2},{18,10},{26,18},{... | collective-permute-start | bytes 445448 | tf_op jit(solution)/shard_map/ppermute | solution.py:20
  14.5 2.5 %collective-permute-start = (bf16[512,272]{0,1:T(8,128)(2,1)S(1)}, bf16[512,272]{0,1:T(8,128)(2,1)S(1)}, u32[]{:S(2)}, u32[]{:S(2)}) collective-permute-start(bf16[512,272]{0,1:T(8,128)(2,1)S(1)} %pad_maximum_fusion.2), channel_id=1, source_target_pairs={{0,8},{8,16},{16,24},{1,9},{9,17},{17,25},{2,10},{10,18},{18,26},{... | collective-permute-start | bytes 835592 | tf_op jit(solution)/shard_map/ppermute | solution.py:19
  17.1 2.4 %collective-permute-start.8 = (bf16[128,256]{1,0:T(8,128)(2,1)S(1)}, bf16[128,256]{1,0:T(8,128)(2,1)S(1)}, u32[]{:S(2)}, u32[]{:S(2)}) collective-permute-start(bf16[128,256]{1,0:T(8,128)(2,1)S(1)} %get-tuple-element.42), channel_id=1, source_target_pairs={{0,24},{8,16},{16,8},{24,0},{1,25},{9,17},{17,9},{25,1},{2,26},{10... | collective-permute-start | bytes 196616 | tf_op jit(solution)/shard_map/ppermute | solution.py:72
  23.9 3.7 %collective-permute-done.8 = bf16[128,256]{1,0:T(8,128)(2,1)S(1)} collective-permute-done((bf16[128,256]{1,0:T(8,128)(2,1)S(1)}, bf16[128,256]{1,0:T(8,128)(2,1)S(1)}, u32[]{:S(2)}, u32[]{:S(2)}) %collective-permute-start.8) | collective-permute-done | bytes 65568 | tf_op jit(solution)/shard_map/ppermute | solution.py:72
  29.8 3.5 %collective-permute-start.9 = (bf16[128,1024]{0,1:T(8,128)(2,1)}, bf16[128,1024]{0,1:T(8,128)(2,1)S(1)}, u32[]{:S(2)}, u32[]{:S(2)}) collective-permute-start(bf16[128,1024]{0,1:T(8,128)(2,1)} %bitcast.39), channel_id=1, source_target_pairs={{0,0},{1,4},{2,8},{3,12},{4,16},{5,20},{6,24},{7,28},{8,1},{9,5},{... | collective-permute-start | bytes 786440 | tf_op jit(solution)/shard_map/ppermute | solution.py:95
  35.7 6.4 %collective-permute-done.9 = bf16[128,1024]{0,1:T(8,128)(2,1)S(1)} collective-permute-done((bf16[128,1024]{0,1:T(8,128)(2,1)}, bf16[128,1024]{0,1:T(8,128)(2,1)S(1)}, u32[]{:S(2)}, u32[]{:S(2)}) %collective-permute-start.9) | collective-permute-done | bytes 262176 | tf_op jit(solution)/shard_map/ppermute | solution.py:95
  43.1 6.3 %fusion.38 = f32[1,512,262]{1,0,2:T(1,128)S(1)} fusion(f32[512,1,128]{0,1,2:T(1,128)} %copy.49, f32[1,512,389]{1,2,0:T(8,128)S(1)} %get-tuple-element.27), kind=kOutput, calls=%fused_computation.74 | convolution fusion | flops 206045184 | bytes 1595392 | tf_op jit(solution)/shard_map/conv_general_dilated | solution.py:36
  51.6 2.9 %collective-permute-start.2 = (bf16[512,256]{0,1:T(8,128)(2,1)S(1)}, bf16[512,256]{0,1:T(8,128)(2,1)S(1)}, u32[]{:S(2)}, u32[]{:S(2)}) collective-permute-start(bf16[512,256]{0,1:T(8,128)(2,1)S(1)} %fusion.44), channel_id=1, source_target_pairs={{0,8},{8,0},{16,24},{24,16},{1,9},{9,1},{17,25},{25,17},{2,10},{10... | collective-permute-start | bytes 786440 | tf_op jit(solution)/shard_map/ppermute | solution.py:72
  57.1 4.6 %collective-permute-done.2 = bf16[512,256]{0,1:T(8,128)(2,1)S(1)} collective-permute-done((bf16[512,256]{0,1:T(8,128)(2,1)S(1)}, bf16[512,256]{0,1:T(8,128)(2,1)S(1)}, u32[]{:S(2)}, u32[]{:S(2)}) %collective-permute-start.2) | collective-permute-done | bytes 262176 | tf_op jit(solution)/shard_map/ppermute | solution.py:72
  62.7 3.9 %collective-permute-done.3 = bf16[512,256]{0,1:T(8,128)(2,1)S(1)} collective-permute-done((bf16[512,256]{0,1:T(8,128)(2,1)S(1)}, bf16[512,256]{0,1:T(8,128)(2,1)S(1)}, u32[]{:S(2)}, u32[]{:S(2)}) %collective-permute-start.3) | collective-permute-done | bytes 262176 | tf_op jit(solution)/shard_map/ppermute | solution.py:72
  75.2 3.3 %fusion.82 = f32[1024,512]{1,0:T(8,128)S(1)} fusion(bf16[1024,1024]{0,1:T(8,128)(2,1)} %all-gather.2.cloned.1.call-done, bf16[512,1024]{1,0:T(8,128)(2,1)} %param.10), kind=kOutput, calls=%fused_computation.166 | convolution fusion | flops 1073741824 | bytes 5242880 | tf_op jit(solution)/shard_map/dot_general | solution.py:144
  78.6 1.5 %collective-permute-start.12 = (bf16[512,256]{0,1:T(8,128)(2,1)S(1)}, bf16[512,256]{0,1:T(8,128)(2,1)S(1)}, u32[]{:S(2)}, u32[]{:S(2)}) collective-permute-start(bf16[512,256]{0,1:T(8,128)(2,1)S(1)} %get-tuple-element.23), channel_id=1, source_target_pairs={{0,24},{8,16},{16,8},{24,0},{1,25},{9,17},{17,9},{25,1},{2,26},{10... | collective-permute-start | bytes 786440 | tf_op jit(solution)/shard_map/ppermute | solution.py:72
  80.1 1.5 %collective-permute-start.11 = (bf16[512,256]{0,1:T(8,128)(2,1)S(1)}, bf16[512,256]{0,1:T(8,128)(2,1)S(1)}, u32[]{:S(2)}, u32[]{:S(2)}) collective-permute-start(bf16[512,256]{0,1:T(8,128)(2,1)S(1)} %get-tuple-element.24), channel_id=1, source_target_pairs={{0,16},{8,24},{16,0},{24,8},{1,17},{9,25},{17,1},{25,9},{2,18},{10... | collective-permute-start | bytes 786440 | tf_op jit(solution)/shard_map/ppermute | solution.py:72
  83.6 5.2 %collective-permute-done.12 = bf16[512,256]{0,1:T(8,128)(2,1)S(1)} collective-permute-done((bf16[512,256]{0,1:T(8,128)(2,1)S(1)}, bf16[512,256]{0,1:T(8,128)(2,1)S(1)}, u32[]{:S(2)}, u32[]{:S(2)}) %collective-permute-start.12) | collective-permute-done | bytes 262176 | tf_op jit(solution)/shard_map/ppermute | solution.py:72
  88.8 4.8 %collective-permute-done.11 = bf16[512,256]{0,1:T(8,128)(2,1)S(1)} collective-permute-done((bf16[512,256]{0,1:T(8,128)(2,1)S(1)}, bf16[512,256]{0,1:T(8,128)(2,1)S(1)}, u32[]{:S(2)}, u32[]{:S(2)}) %collective-permute-start.11) | collective-permute-done | bytes 262176 | tf_op jit(solution)/shard_map/ppermute | solution.py:72
  93.8 3.4 %collective-permute-start.13 = (bf16[512,133]{0,1:T(8,128)(2,1)S(1)}, bf16[512,133]{0,1:T(8,128)(2,1)S(1)}, u32[]{:S(2)}, u32[]{:S(2)}) collective-permute-start(bf16[512,133]{0,1:T(8,128)(2,1)S(1)} %slice.485), channel_id=1, source_target_pairs={{8,0},{16,8},{24,16},{9,1},{17,9},{25,17},{10,2},{18,10},{26,18},{... | collective-permute-start | bytes 408584 | tf_op jit(solution)/shard_map/ppermute | solution.py:32
  97.2 1.9 %add_convert_fusion = bf16[512,1024]{1,0:T(8,128)(2,1)} fusion(f32[512,1024]{1,0:T(8,128)S(1)} %fusion.48, f32[512,1024]{1,0:T(8,128)S(1)} %fusion.50, f32[512,1024]{1,0:T(8,128)S(1)} %fusion.52, bf16[512,256]{0,1:T(8,128)(2,1)S(1)} %copy-done.6, bf16[1024,1024]{0,1:T(8,128)(2,1)S(1)} %copy-done.1, s32[]{:T(128)S(6)} %select_n.112), kind=kOutput, calls=%fused_computation.1 | convolution fusion | flops 274726912 | bytes 8126468 | tf_op jit(solution)/shard_map/dot_general | solution.py:161
  99.2 2.2 %collective-permute-done.13 = bf16[512,133]{0,1:T(8,128)(2,1)S(1)} collective-permute-done((bf16[512,133]{0,1:T(8,128)(2,1)S(1)}, bf16[512,133]{0,1:T(8,128)(2,1)S(1)}, u32[]{:S(2)}, u32[]{:S(2)}) %collective-permute-start.13) | collective-permute-done | bytes 136224 | tf_op jit(solution)/shard_map/ppermute | solution.py:32
  102.5 5.5 %fusion.36 = f32[1,512,262]{1,0,2:T(1,128)S(1)} fusion(f32[512,1,128]{0,1,2:T(1,128)S(1)} %copy-done.13, f32[1,512,389]{1,2,0:T(8,128)S(1)} %bitcast.147), kind=kOutput, calls=%fused_computation.72 | convolution fusion | flops 206045184 | bytes 1595392 | tf_op jit(solution)/shard_map/conv_general_dilated | solution.py:36
  108.5 4.1 %reduce-scatter.2.cloned.1.call-done = bf16[512,256]{0,1:T(8,128)(2,1)} async-done(((bf16[4096,256]{0,1:T(8,128)(2,1)}), bf16[512,256]{0,1:T(8,128)(2,1)}) %reduce-scatter.2.cloned.1.call-update) | async-done | bytes 262160 | tf_op jit(solution)/shard_map/reduce_scatter | solution.py:135
  112.6 1.9 %collective-permute-start.5 = (bf16[512,256]{0,1:T(8,128)(2,1)}, bf16[512,256]{0,1:T(8,128)(2,1)S(1)}, u32[]{:S(2)}, u32[]{:S(2)}) collective-permute-start(bf16[512,256]{0,1:T(8,128)(2,1)} %reduce-scatter.2.cloned.1.call-done), channel_id=1, source_target_pairs={{0,0},{1,8},{2,16},{3,24},{4,1},{5,9},{6,17},{7,25},{8,10},{9,2},{... | collective-permute-start | bytes 786440 | tf_op jit(solution)/shard_map/ppermute | solution.py:141
  114.5 1.3 fusion.7
  117.0 15.6 %collective-permute-done.5 = bf16[512,256]{0,1:T(8,128)(2,1)S(1)} collective-permute-done((bf16[512,256]{0,1:T(8,128)(2,1)}, bf16[512,256]{0,1:T(8,128)(2,1)S(1)}, u32[]{:S(2)}, u32[]{:S(2)}) %collective-permute-start.5) | collective-permute-done | bytes 262176 | tf_op jit(solution)/shard_map/ppermute | solution.py:141
  (152 shorter events, 32.4 us)
Async XLA Ops:
  7.2 68.0 %all-gather.2.cloned.1.call-start = ((), (), s32[]{:S(2)}) async-start(), calls=%async_computation.2 | async-start | bytes 2359296 | tf_op jit(solution)/shard_map/all_gather | solution.py:96
  9.7 7.3 %copy-start.11 = (bf16[512,256]{1,0:T(8,128)(2,1)S(1)}, bf16[512,256]{1,0:T(8,128)(2,1)}, u32[]{:S(2)}) copy-start(bf16[512,256]{1,0:T(8,128)(2,1)} %param.11) | copy-start | bytes 786436
  9.7 10.9 %copy-start = (bf16[3,512,256]{2,1,0:T(8,128)(2,1)S(1)}, bf16[3,512,256]{2,1,0:T(8,128)(2,1)}, u32[]{:S(2)}) copy-start(bf16[3,512,256]{2,1,0:T(8,128)(2,1)} %param.6) | copy-start | bytes 2359300
  10.8 22.6 %collective-permute-start.1 = (bf16[512,145]{0,1:T(8,128)(2,1)}, bf16[512,145]{0,1:T(8,128)(2,1)S(1)}, u32[]{:S(2)}, u32[]{:S(2)}) collective-permute-start(bf16[512,145]{0,1:T(8,128)(2,1)} %pad_maximum_fusion.4), channel_id=1, source_target_pairs={{8,0},{16,8},{24,16},{9,1},{17,9},{25,17},{10,2},{18,10},{26,18},{... | collective-permute-start | bytes 445448 | tf_op jit(solution)/shard_map/ppermute | solution.py:20
  14.4 7.1 %copy-start.2 = (f32[512,128]{1,0:T(8,128)S(1)}, f32[512,128]{1,0:T(8,128)}, u32[]{:S(2)}) copy-start(f32[512,128]{1,0:T(8,128)} %param.8) | copy-start | bytes 786436
  14.5 18.8 %collective-permute-start = (bf16[512,272]{0,1:T(8,128)(2,1)S(1)}, bf16[512,272]{0,1:T(8,128)(2,1)S(1)}, u32[]{:S(2)}, u32[]{:S(2)}) collective-permute-start(bf16[512,272]{0,1:T(8,128)(2,1)S(1)} %pad_maximum_fusion.2), channel_id=1, source_target_pairs={{0,8},{8,16},{16,24},{1,9},{9,17},{17,25},{2,10},{10,18},{18,26},{... | collective-permute-start | bytes 835592 | tf_op jit(solution)/shard_map/ppermute | solution.py:19
  17.1 10.5 %collective-permute-start.8 = (bf16[128,256]{1,0:T(8,128)(2,1)S(1)}, bf16[128,256]{1,0:T(8,128)(2,1)S(1)}, u32[]{:S(2)}, u32[]{:S(2)}) collective-permute-start(bf16[128,256]{1,0:T(8,128)(2,1)S(1)} %get-tuple-element.42), channel_id=1, source_target_pairs={{0,24},{8,16},{16,8},{24,0},{1,25},{9,17},{17,9},{25,1},{2,26},{10... | collective-permute-start | bytes 196616 | tf_op jit(solution)/shard_map/ppermute | solution.py:72
  19.5 8.7 %collective-permute-start.7 = (bf16[128,256]{1,0:T(8,128)(2,1)S(1)}, bf16[128,256]{1,0:T(8,128)(2,1)S(1)}, u32[]{:S(2)}, u32[]{:S(2)}) collective-permute-start(bf16[128,256]{1,0:T(8,128)(2,1)S(1)} %get-tuple-element.43), channel_id=1, source_target_pairs={{0,16},{8,24},{16,0},{24,8},{1,17},{9,25},{17,1},{25,9},{2,18},{10... | collective-permute-start | bytes 196616 | tf_op jit(solution)/shard_map/ppermute | solution.py:72
  19.5 8.7 %collective-permute-start.6 = (bf16[128,256]{1,0:T(8,128)(2,1)S(1)}, bf16[128,256]{1,0:T(8,128)(2,1)S(1)}, u32[]{:S(2)}, u32[]{:S(2)}) collective-permute-start(bf16[128,256]{1,0:T(8,128)(2,1)S(1)} %get-tuple-element.44), channel_id=1, source_target_pairs={{0,8},{8,0},{16,24},{24,16},{1,9},{9,1},{17,25},{25,17},{2,10},{10... | collective-permute-start | bytes 196616 | tf_op jit(solution)/shard_map/ppermute | solution.py:72
  29.8 12.3 %collective-permute-start.9 = (bf16[128,1024]{0,1:T(8,128)(2,1)}, bf16[128,1024]{0,1:T(8,128)(2,1)S(1)}, u32[]{:S(2)}, u32[]{:S(2)}) collective-permute-start(bf16[128,1024]{0,1:T(8,128)(2,1)} %bitcast.39), channel_id=1, source_target_pairs={{0,0},{1,4},{2,8},{3,12},{4,16},{5,20},{6,24},{7,28},{8,1},{9,5},{... | collective-permute-start | bytes 786440 | tf_op jit(solution)/shard_map/ppermute | solution.py:95
  42.9 69.7 %reduce-scatter.2.cloned.1.call-start = ((), (), s32[]{:S(2)}) async-start(), calls=%async_computation.1 | async-start | bytes 2359296 | tf_op jit(solution)/shard_map/reduce_scatter | solution.py:135
  43.1 7.1 %slice-start = ((bf16[512,145]{0,1:T(8,128)(2,1)}), bf16[512,133]{0,1:T(8,128)(2,1)S(1)}, s32[]{:S(2)}) async-start(bf16[512,145]{0,1:T(8,128)(2,1)} %copy-done.3), calls=%async_computation.3 | async-start | bytes 278528 | tf_op jit(solution)/shard_map/slice | solution.py:21
  43.1 7.2 %copy-start.29 = (f32[512]{0:T(512)S(1)}, f32[512]{0:T(512)}, u32[]{:S(2)}) copy-start(f32[512]{0:T(512)} %param.9) | copy-start | bytes 6148
  51.6 10.0 %collective-permute-start.2 = (bf16[512,256]{0,1:T(8,128)(2,1)S(1)}, bf16[512,256]{0,1:T(8,128)(2,1)S(1)}, u32[]{:S(2)}, u32[]{:S(2)}) collective-permute-start(bf16[512,256]{0,1:T(8,128)(2,1)S(1)} %fusion.44), channel_id=1, source_target_pairs={{0,8},{8,0},{16,24},{24,16},{1,9},{9,1},{17,25},{25,17},{2,10},{10... | collective-permute-start | bytes 786440 | tf_op jit(solution)/shard_map/ppermute | solution.py:72
  54.5 12.1 %collective-permute-start.3 = (bf16[512,256]{0,1:T(8,128)(2,1)S(1)}, bf16[512,256]{0,1:T(8,128)(2,1)S(1)}, u32[]{:S(2)}, u32[]{:S(2)}) collective-permute-start(bf16[512,256]{0,1:T(8,128)(2,1)S(1)} %fusion.44), channel_id=1, source_target_pairs={{0,16},{8,24},{16,0},{24,8},{1,17},{9,25},{17,1},{25,9},{2,18},{10... | collective-permute-start | bytes 786440 | tf_op jit(solution)/shard_map/ppermute | solution.py:72
  55.7 11.9 %collective-permute-start.4 = (bf16[512,256]{0,1:T(8,128)(2,1)S(1)}, bf16[512,256]{0,1:T(8,128)(2,1)S(1)}, u32[]{:S(2)}, u32[]{:S(2)}) collective-permute-start(bf16[512,256]{0,1:T(8,128)(2,1)S(1)} %fusion.44), channel_id=1, source_target_pairs={{0,24},{8,16},{16,8},{24,0},{1,25},{9,17},{17,9},{25,1},{2,26},{10... | collective-permute-start | bytes 786440 | tf_op jit(solution)/shard_map/ppermute | solution.py:72
  61.7 8.1 %copy-start.7 = (bf16[512,256]{0,1:T(8,128)(2,1)}, bf16[512,256]{0,1:T(8,128)(2,1)S(1)}, u32[]{:S(2)}) copy-start(bf16[512,256]{0,1:T(8,128)(2,1)S(1)} %collective-permute-done.2) | copy-start | bytes 786436
  75.1 7.0 %copy-start.1 = (bf16[1024,1024]{0,1:T(8,128)(2,1)S(1)}, bf16[1024,1024]{0,1:T(8,128)(2,1)}, u32[]{:S(2)}) copy-start(bf16[1024,1024]{0,1:T(8,128)(2,1)} %all-gather.2.cloned.1.call-done) | copy-start | bytes 6291460
  78.6 10.2 %collective-permute-start.12 = (bf16[512,256]{0,1:T(8,128)(2,1)S(1)}, bf16[512,256]{0,1:T(8,128)(2,1)S(1)}, u32[]{:S(2)}, u32[]{:S(2)}) collective-permute-start(bf16[512,256]{0,1:T(8,128)(2,1)S(1)} %get-tuple-element.23), channel_id=1, source_target_pairs={{0,24},{8,16},{16,8},{24,0},{1,25},{9,17},{17,9},{25,1},{2,26},{10... | collective-permute-start | bytes 786440 | tf_op jit(solution)/shard_map/ppermute | solution.py:72
  80.1 13.5 %collective-permute-start.11 = (bf16[512,256]{0,1:T(8,128)(2,1)S(1)}, bf16[512,256]{0,1:T(8,128)(2,1)S(1)}, u32[]{:S(2)}, u32[]{:S(2)}) collective-permute-start(bf16[512,256]{0,1:T(8,128)(2,1)S(1)} %get-tuple-element.24), channel_id=1, source_target_pairs={{0,16},{8,24},{16,0},{24,8},{1,17},{9,25},{17,1},{25,9},{2,18},{10... | collective-permute-start | bytes 786440 | tf_op jit(solution)/shard_map/ppermute | solution.py:72
  81.6 12.1 %collective-permute-start.10 = (bf16[512,256]{0,1:T(8,128)(2,1)S(1)}, bf16[512,256]{0,1:T(8,128)(2,1)S(1)}, u32[]{:S(2)}, u32[]{:S(2)}) collective-permute-start(bf16[512,256]{0,1:T(8,128)(2,1)S(1)} %get-tuple-element.22), channel_id=1, source_target_pairs={{0,8},{8,0},{16,24},{24,16},{1,9},{9,1},{17,25},{25,17},{2,10},{10... | collective-permute-start | bytes 786440 | tf_op jit(solution)/shard_map/ppermute | solution.py:72
  83.6 13.6 %copy-start.6 = (bf16[512,256]{0,1:T(8,128)(2,1)S(1)}, bf16[512,256]{0,1:T(8,128)(2,1)}, u32[]{:S(2)}) copy-start(bf16[512,256]{0,1:T(8,128)(2,1)} %copy-done.5) | copy-start | bytes 786436
  93.8 7.6 %collective-permute-start.13 = (bf16[512,133]{0,1:T(8,128)(2,1)S(1)}, bf16[512,133]{0,1:T(8,128)(2,1)S(1)}, u32[]{:S(2)}, u32[]{:S(2)}) collective-permute-start(bf16[512,133]{0,1:T(8,128)(2,1)S(1)} %slice.485), channel_id=1, source_target_pairs={{8,0},{16,8},{24,16},{9,1},{17,9},{25,17},{10,2},{18,10},{26,18},{... | collective-permute-start | bytes 408584 | tf_op jit(solution)/shard_map/ppermute | solution.py:32
  112.6 19.9 %collective-permute-start.5 = (bf16[512,256]{0,1:T(8,128)(2,1)}, bf16[512,256]{0,1:T(8,128)(2,1)S(1)}, u32[]{:S(2)}, u32[]{:S(2)}) collective-permute-start(bf16[512,256]{0,1:T(8,128)(2,1)} %reduce-scatter.2.cloned.1.call-done), channel_id=1, source_target_pairs={{0,0},{1,8},{2,16},{3,24},{4,1},{5,9},{6,17},{7,25},{8,10},{9,2},{... | collective-permute-start | bytes 786440 | tf_op jit(solution)/shard_map/ppermute | solution.py:141
  (26 other events, 60.2 us)
Sparse Core Ops, SparseCore 0:
  43.0 32.1 all-gather.1
  77.4 35.1 reduce-scatter.1

commit v5 on v4

--- a/solution.py
+++ b/solution.py
@@ -121,23 +121,19 @@
 
     gated_blocks = [gated] + exchange(lambda step: gated, "seq")
     group = n_tp // n_seq
-    out_rows = slab_width // group
-    pieces = []
-    for j in range(group):
-        rows = out_weight[:, j * out_rows : (j + 1) * out_rows]
-        for block in gated_blocks:
-            pieces.append(
-                lax.dot_general(
-                    rows, block, (((0,), (0,)), ((), ())), preferred_element_type=jnp.float32
-                ).astype(jnp.bfloat16)
-            )
+    weight_t = out_weight.T
+    pieces = [
+        jnp.dot(weight_t, block, preferred_element_type=jnp.float32).astype(jnp.bfloat16)
+        for block in gated_blocks
+    ]
     partial_out = jnp.concatenate(pieces, axis=0)
     output_sum = lax.psum_scatter(partial_out, "tp", scatter_dimension=0, tiled=True)
     route = []
     for s in range(n_seq):
         for p in range(n_tp):
-            target = source(s, p % n_seq, n_seq) if p % n_seq else s
-            route.append((s * n_tp + p, target * n_tp + group * s + p // n_seq))
+            step = p // group
+            target = source(s, step, n_seq) if step else s
+            route.append((s * n_tp + p, target * n_tp + group * s + p % group))
     mixed = lax.ppermute(output_sum, ("seq", "tp"), route)
 
     slab_grad, gated_blocks = lax.optimization_barrier((slab_grad, gated_blocks))

time: 141 us -> 143 us (1.014)
  the two profiles are of different devices: /device:TPU:4 before, /device:TPU:27 now
where the time goes in v5:
time: 143 us; the launch traced here: 142 us
  waiting for transfers between devices  58 us (41%)
  local copies, waits for them, and re-layouts  20.5 us (14%)
  starting transfers between devices  20.4 us (14%)
  matrix products  19.1 us (13%)
  between operations  14.9 us (10%)
  other arithmetic  9.47 us (7%)
    ppermute x9, waiting for transfers between devices, exchange(): got.append(lax.ppermute(block_of(step), axis, route))  21.9 us
    ppermute x1, waiting for transfers between devices, shards(): mixed = lax.ppermute(output_sum, ('seq', 'tp'), route)  17 us
    conv_general_dilated x2, matrix products, correlate(): lax.conv_general_dilated(signal[None], taps[:, None, :], (1,), 'VALID', d...  11 us
    unnamed x111, local copies, waits for them, and re-layouts  9.98 us
    ppermute x1, waiting for transfers between devices, rows_of_slab(): moved = lax.ppermute(mine, ('seq', 'tp'), route)  8.39 us
    ppermute x9, starting transfers between devices, exchange(): got.append(lax.ppermute(block_of(step), axis, route))  8.07 us
    reduce_scatter x1, waiting for transfers between devices, shards(): lax.psum_scatter(partial_out, 'tp', scatter_dimension=0, tiled=True)  5.11 us
    ppermute x1, starting transfers between devices, halo(): low = lax.ppermute(low, axis, forward)  4.01 us
  transfers between devices with their start and end apart: 16, of which 10 were waited for; matrix products, arithmetic and copies ran while one was open for 30% of the time, Pallas kernels for 0%

profile of v5, /device:TPU:27, one launch (start us, length us, event | category | flops | bytes accessed | tf_op | source)
XLA Modules:
  0.0 142.4 jit_solution(8126126277111051743)
XLA Ops:
  7.3 1.8 %constant_dynamic-slice_fusion = (bf16[1,128,256]{2,1,0:T(8,128)(2,1)S(1)}, bf16[128,256]{1,0:T(8,128)(2,1)}, bf16[128,256]{1,0:T(8,128)(2,1)}, bf16[128,256]{1,0:T(8,128)(2,1)S(1)}) fusion(bf16[4,128,256]{2,1,0:T(8,128)(2,1)} %bitcast.132, s32[]{:T(128)S(6)} %select_n.99, s32[]{:T(128)S(6)} %select_n.102, s32[]{:T(128)S(6)} %select_n.101, s32[]{:T(128)S(6)} %select_n.100), kind=kLoop, calls=%fused_computation.120 | loop fusion | bytes 524304 | tf_op jit(solution)/shard_map/dynamic_slice | solution.py:82
  14.1 2.2 %collective-permute-start.1 = (bf16[512,145]{0,1:T(8,128)(2,1)}, bf16[512,145]{0,1:T(8,128)(2,1)S(1)}, u32[]{:S(2)}, u32[]{:S(2)}) collective-permute-start(bf16[512,145]{0,1:T(8,128)(2,1)} %pad_maximum_fusion.5), channel_id=1, source_target_pairs={{8,0},{16,8},{24,16},{9,1},{17,9},{25,17},{10,2},{18,10},{26,18},{... | collective-permute-start | bytes 445448 | tf_op jit(solution)/shard_map/ppermute | solution.py:20
  17.4 4.0 %collective-permute-start = (bf16[512,272]{0,1:T(8,128)(2,1)}, bf16[512,272]{0,1:T(8,128)(2,1)S(1)}, u32[]{:S(2)}, u32[]{:S(2)}) collective-permute-start(bf16[512,272]{0,1:T(8,128)(2,1)} %pad_maximum_fusion.3), channel_id=1, source_target_pairs={{0,8},{8,16},{16,24},{1,9},{9,17},{17,25},{2,10},{10,18},{18,26},{... | collective-permute-start | bytes 835592 | tf_op jit(solution)/shard_map/ppermute | solution.py:19
  30.9 1.9 %collective-permute-start.9 = (bf16[128,1024]{0,1:T(8,128)(2,1)}, bf16[128,1024]{0,1:T(8,128)(2,1)}, u32[]{:S(2)}, u32[]{:S(2)}) collective-permute-start(bf16[128,1024]{0,1:T(8,128)(2,1)} %bitcast.35), channel_id=1, source_target_pairs={{0,0},{1,4},{2,8},{3,12},{4,16},{5,20},{6,24},{7,28},{8,1},{9,5},{... | collective-permute-start | bytes 786440 | tf_op jit(solution)/shard_map/ppermute | solution.py:95
  35.1 8.4 %collective-permute-done.9 = bf16[128,1024]{0,1:T(8,128)(2,1)} collective-permute-done((bf16[128,1024]{0,1:T(8,128)(2,1)}, bf16[128,1024]{0,1:T(8,128)(2,1)}, u32[]{:S(2)}, u32[]{:S(2)}) %collective-permute-start.9) | collective-permute-done | bytes 262176 | tf_op jit(solution)/shard_map/ppermute | solution.py:95
  44.9 5.5 %fusion.26 = f32[1,512,262]{1,0,2:T(1,128)S(1)} fusion(f32[512,1,128]{0,1,2:T(1,128)S(1)} %copy-done.15, f32[1,512,389]{1,2,0:T(8,128)S(1)} %get-tuple-element.27), kind=kOutput, calls=%fused_computation.59 | convolution fusion | flops 206045184 | bytes 1595392 | tf_op jit(solution)/shard_map/conv_general_dilated | solution.py:36
  52.0 1.7 %collective-permute-start.4 = (bf16[512,256]{0,1:T(8,128)(2,1)S(1)}, bf16[512,256]{0,1:T(8,128)(2,1)S(1)}, u32[]{:S(2)}, u32[]{:S(2)}) collective-permute-start(bf16[512,256]{0,1:T(8,128)(2,1)S(1)} %fusion.32), channel_id=1, source_target_pairs={{0,24},{8,16},{16,8},{24,0},{1,25},{9,17},{17,9},{25,1},{2,26},{10... | collective-permute-start | bytes 786440 | tf_op jit(solution)/shard_map/ppermute | solution.py:72
  55.1 8.6 %collective-permute-done.2 = bf16[512,256]{0,1:T(8,128)(2,1)S(1)} collective-permute-done((bf16[512,256]{0,1:T(8,128)(2,1)S(1)}, bf16[512,256]{0,1:T(8,128)(2,1)S(1)}, u32[]{:S(2)}, u32[]{:S(2)}) %collective-permute-start.2) | collective-permute-done | bytes 262176 | tf_op jit(solution)/shard_map/ppermute | solution.py:72
  64.2 2.7 %collective-permute-done.3 = bf16[512,256]{0,1:T(8,128)(2,1)S(1)} collective-permute-done((bf16[512,256]{0,1:T(8,128)(2,1)S(1)}, bf16[512,256]{0,1:T(8,128)(2,1)S(1)}, u32[]{:S(2)}, u32[]{:S(2)}) %collective-permute-start.3) | collective-permute-done | bytes 262176 | tf_op jit(solution)/shard_map/ppermute | solution.py:72
  68.0 1.5 %pad_maximum_fusion = bf16[4096,256]{0,1:T(8,128)(2,1)} fusion(bf16[1024,256]{0,1:T(8,128)(2,1)S(1)} %fusion.16, bf16[1024,256]{0,1:T(8,128)(2,1)S(1)} %fusion.15, bf16[1024,256]{0,1:T(8,128)(2,1)S(1)} %fusion.14, bf16[1024,256]{0,1:T(8,128)(2,1)S(1)} %fusion.13), kind=kLoop, calls=%fused_computation.1 | loop fusion | flops 8388608 | bytes 4194304 | tf_op jit(solution)/shard_map/concatenate | solution.py:129
  70.2 1.8 %copy.52 = f32[512,1,128]{0,1,2:T(1,128)} copy(f32[512,1,128]{2,0,1:T(8,128)} %bitcast.127) | data formatting | bytes 524288 | tf_op jit(solution)/shard_map/broadcast_in_dim | solution.py:38
  72.0 2.9 %all-gather.2.cloned.1.call-done = bf16[1024,1024]{0,1:T(8,128)(2,1)} async-done(((bf16[128,1024]{0,1:T(8,128)(2,1)}), bf16[1024,1024]{0,1:T(8,128)(2,1)}) %all-gather.2.cloned.1.call-update) | async-done | bytes 2097168 | tf_op jit(solution)/shard_map/all_gather | solution.py:96
  74.9 3.0 %fusion.62 = f32[1024,512]{1,0:T(8,128)S(1)} fusion(bf16[1024,1024]{0,1:T(8,128)(2,1)} %all-gather.2.cloned.1.call-done, bf16[512,1024]{1,0:T(8,128)(2,1)S(1)} %copy-done), kind=kOutput, calls=%fused_computation.143 | convolution fusion | flops 1073741824 | bytes 5242880 | tf_op jit(solution)/shard_map/dot_general | solution.py:140
  78.5 2.1 %collective-permute-start.12 = (bf16[512,256]{0,1:T(8,128)(2,1)S(1)}, bf16[512,256]{0,1:T(8,128)(2,1)S(1)}, u32[]{:S(2)}, u32[]{:S(2)}) collective-permute-start(bf16[512,256]{0,1:T(8,128)(2,1)S(1)} %get-tuple-element.23), channel_id=1, source_target_pairs={{0,24},{8,16},{16,8},{24,0},{1,25},{9,17},{17,9},{25,1},{2,26},{10... | collective-permute-start | bytes 786440 | tf_op jit(solution)/shard_map/ppermute | solution.py:72
  82.7 3.2 %collective-permute-done.10 = bf16[512,256]{0,1:T(8,128)(2,1)S(1)} collective-permute-done((bf16[512,256]{0,1:T(8,128)(2,1)S(1)}, bf16[512,256]{0,1:T(8,128)(2,1)S(1)}, u32[]{:S(2)}, u32[]{:S(2)}) %collective-permute-start.10) | collective-permute-done | bytes 262176 | tf_op jit(solution)/shard_map/ppermute | solution.py:72
  85.8 6.5 %collective-permute-done.12 = bf16[512,256]{0,1:T(8,128)(2,1)S(1)} collective-permute-done((bf16[512,256]{0,1:T(8,128)(2,1)S(1)}, bf16[512,256]{0,1:T(8,128)(2,1)S(1)}, u32[]{:S(2)}, u32[]{:S(2)}) %collective-permute-start.12) | collective-permute-done | bytes 262176 | tf_op jit(solution)/shard_map/ppermute | solution.py:72
  93.5 2.1 %collective-permute-start.13 = (bf16[512,133]{0,1:T(8,128)(2,1)S(1)}, bf16[512,133]{0,1:T(8,128)(2,1)S(1)}, u32[]{:S(2)}, u32[]{:S(2)}) collective-permute-start(bf16[512,133]{0,1:T(8,128)(2,1)S(1)} %slice.461), channel_id=1, source_target_pairs={{8,0},{16,8},{24,16},{9,1},{17,9},{25,17},{10,2},{18,10},{26,18},{... | collective-permute-start | bytes 408584 | tf_op jit(solution)/shard_map/ppermute | solution.py:32
  95.6 1.9 %add_convert_fusion = bf16[512,1024]{1,0:T(8,128)(2,1)} fusion(f32[512,1024]{1,0:T(8,128)S(1)} %fusion.36, f32[512,1024]{1,0:T(8,128)S(1)} %fusion.38, f32[512,1024]{1,0:T(8,128)S(1)} %fusion.40, bf16[512,256]{0,1:T(8,128)(2,1)S(1)} %collective-permute-done.4, bf16[1024,1024]{0,1:T(8,128)(2,1)S(1)} %copy-done.6, s32[]{:T(128)S(6)} %select_n.112), kind=kOutput, calls=%fused_computation.2 | convolution fusion | flops 274726912 | bytes 8126468 | tf_op jit(solution)/shard_map/dot_general | solution.py:157
  97.5 2.6 %collective-permute-done.13 = bf16[512,133]{0,1:T(8,128)(2,1)S(1)} collective-permute-done((bf16[512,133]{0,1:T(8,128)(2,1)S(1)}, bf16[512,133]{0,1:T(8,128)(2,1)S(1)}, u32[]{:S(2)}, u32[]{:S(2)}) %collective-permute-start.13) | collective-permute-done | bytes 136224 | tf_op jit(solution)/shard_map/ppermute | solution.py:32
  101.3 5.5 %fusion.24 = f32[1,512,262]{1,0,2:T(1,128)S(1)} fusion(f32[512,1,128]{0,1,2:T(1,128)S(1)} %copy-done.16, f32[1,512,389]{1,2,0:T(8,128)S(1)} %bitcast.123), kind=kOutput, calls=%fused_computation.57 | convolution fusion | flops 206045184 | bytes 1595392 | tf_op jit(solution)/shard_map/conv_general_dilated | solution.py:36
  107.2 5.1 %reduce-scatter.2.cloned.1.call-done = bf16[512,256]{0,1:T(8,128)(2,1)} async-done(((bf16[4096,256]{0,1:T(8,128)(2,1)}), bf16[512,256]{0,1:T(8,128)(2,1)}) %reduce-scatter.2.cloned.1.call-update) | async-done | bytes 262160 | tf_op jit(solution)/shard_map/reduce_scatter | solution.py:130
  112.3 1.9 %collective-permute-start.5 = (bf16[512,256]{0,1:T(8,128)(2,1)}, bf16[512,256]{0,1:T(8,128)(2,1)}, u32[]{:S(2)}, u32[]{:S(2)}) collective-permute-start(bf16[512,256]{0,1:T(8,128)(2,1)} %reduce-scatter.2.cloned.1.call-done), channel_id=1, source_target_pairs={{0,0},{1,1},{2,8},{3,9},{4,16},{5,17},{6,24},{7,25},{8,10},{9,11},... | collective-permute-start | bytes 786440 | tf_op jit(solution)/shard_map/ppermute | solution.py:137
  116.7 17.0 %collective-permute-done.5 = bf16[512,256]{0,1:T(8,128)(2,1)} collective-permute-done((bf16[512,256]{0,1:T(8,128)(2,1)}, bf16[512,256]{0,1:T(8,128)(2,1)}, u32[]{:S(2)}, u32[]{:S(2)}) %collective-permute-start.5) | collective-permute-done | bytes 262176 | tf_op jit(solution)/shard_map/ppermute | solution.py:137
  133.8 1.8 %copy.53 = bf16[512,256]{1,0:T(8,128)(2,1)} copy(bf16[512,256]{0,1:T(8,128)(2,1)} %collective-permute-done.5) | data formatting | bytes 524288
  (177 shorter events, 31.9 us)
Async XLA Ops:
  7.2 47.5 %copy-start = (bf16[512,1024]{1,0:T(8,128)(2,1)S(1)}, bf16[512,1024]{1,0:T(8,128)(2,1)}, u32[]{:S(2)}) copy-start(bf16[512,1024]{1,0:T(8,128)(2,1)} %param.10) | copy-start | bytes 3145732
  7.2 5.6 %copy-start.1 = (bf16[3,512,256]{2,1,0:T(8,128)(2,1)S(1)}, bf16[3,512,256]{2,1,0:T(8,128)(2,1)}, u32[]{:S(2)}) copy-start(bf16[3,512,256]{2,1,0:T(8,128)(2,1)} %param.6) | copy-start | bytes 2359300
  7.2 67.7 %all-gather.2.cloned.1.call-start = ((), (), s32[]{:S(2)}) async-start(), calls=%async_computation.2 | async-start | bytes 2359296 | tf_op jit(solution)/shard_map/all_gather | solution.py:96
  9.0 19.4 %collective-permute-start.8 = (bf16[128,256]{1,0:T(8,128)(2,1)}, bf16[128,256]{1,0:T(8,128)(2,1)}, u32[]{:S(2)}, u32[]{:S(2)}) collective-permute-start(bf16[128,256]{1,0:T(8,128)(2,1)} %get-tuple-element.42), channel_id=1, source_target_pairs={{0,24},{8,16},{16,8},{24,0},{1,25},{9,17},{17,9},{25,1},{2,26},{10... | collective-permute-start | bytes 196616 | tf_op jit(solution)/shard_map/ppermute | solution.py:72
  10.2 18.2 %collective-permute-start.7 = (bf16[128,256]{1,0:T(8,128)(2,1)}, bf16[128,256]{1,0:T(8,128)(2,1)}, u32[]{:S(2)}, u32[]{:S(2)}) collective-permute-start(bf16[128,256]{1,0:T(8,128)(2,1)} %get-tuple-element.43), channel_id=1, source_target_pairs={{0,16},{8,24},{16,0},{24,8},{1,17},{9,25},{17,1},{25,9},{2,18},{10... | collective-permute-start | bytes 196616 | tf_op jit(solution)/shard_map/ppermute | solution.py:72
  10.5 18.0 %collective-permute-start.6 = (bf16[128,256]{1,0:T(8,128)(2,1)S(1)}, bf16[128,256]{1,0:T(8,128)(2,1)}, u32[]{:S(2)}, u32[]{:S(2)}) collective-permute-start(bf16[128,256]{1,0:T(8,128)(2,1)S(1)} %get-tuple-element.44), channel_id=1, source_target_pairs={{0,8},{8,0},{16,24},{24,16},{1,9},{9,1},{17,25},{25,17},{2,10},{10... | collective-permute-start | bytes 196616 | tf_op jit(solution)/shard_map/ppermute | solution.py:72
  13.1 8.3 %copy-start.17 = (f32[3,512,7]{1,2,0:T(8,128)S(1)}, f32[3,512,7]{1,2,0:T(8,128)}, u32[]{:S(2)}) copy-start(f32[3,512,7]{1,2,0:T(8,128)} %param.7) | copy-start | bytes 129028
  14.1 18.7 %collective-permute-start.1 = (bf16[512,145]{0,1:T(8,128)(2,1)}, bf16[512,145]{0,1:T(8,128)(2,1)S(1)}, u32[]{:S(2)}, u32[]{:S(2)}) collective-permute-start(bf16[512,145]{0,1:T(8,128)(2,1)} %pad_maximum_fusion.5), channel_id=1, source_target_pairs={{8,0},{16,8},{24,16},{9,1},{17,9},{25,17},{10,2},{18,10},{26,18},{... | collective-permute-start | bytes 445448 | tf_op jit(solution)/shard_map/ppermute | solution.py:20
  16.3 6.5 %slice-start.1 = ((f32[3,512,7]{1,2,0:T(8,128)}), f32[1,512,7]{1,2,0:T(8,128)S(1)}, s32[]{:S(2)}) async-start(f32[3,512,7]{1,2,0:T(8,128)} %param.7), calls=%async_computation.4 | async-start | bytes 32768 | tf_op jit(solution)/shard_map/slice | solution.py:116
  16.4 7.8 %copy-start.12 = (f32[512,128]{1,0:T(8,128)S(1)}, f32[512,128]{1,0:T(8,128)}, u32[]{:S(2)}) copy-start(f32[512,128]{1,0:T(8,128)} %param.8) | copy-start | bytes 786436
  17.4 15.4 %collective-permute-start = (bf16[512,272]{0,1:T(8,128)(2,1)}, bf16[512,272]{0,1:T(8,128)(2,1)S(1)}, u32[]{:S(2)}, u32[]{:S(2)}) collective-permute-start(bf16[512,272]{0,1:T(8,128)(2,1)} %pad_maximum_fusion.3), channel_id=1, source_target_pairs={{0,8},{8,16},{16,24},{1,9},{9,17},{17,25},{2,10},{10,18},{18,26},{... | collective-permute-start | bytes 835592 | tf_op jit(solution)/shard_map/ppermute | solution.py:19
  30.9 12.6 %collective-permute-start.9 = (bf16[128,1024]{0,1:T(8,128)(2,1)}, bf16[128,1024]{0,1:T(8,128)(2,1)}, u32[]{:S(2)}, u32[]{:S(2)}) collective-permute-start(bf16[128,1024]{0,1:T(8,128)(2,1)} %bitcast.35), channel_id=1, source_target_pairs={{0,0},{1,4},{2,8},{3,12},{4,16},{5,20},{6,24},{7,28},{8,1},{9,5},{... | collective-permute-start | bytes 786440 | tf_op jit(solution)/shard_map/ppermute | solution.py:95
  43.5 68.8 %reduce-scatter.2.cloned.1.call-start = ((), (), s32[]{:S(2)}) async-start(), calls=%async_computation.1 | async-start | bytes 2359296 | tf_op jit(solution)/shard_map/reduce_scatter | solution.py:130
  44.0 6.6 %copy-start.2 = (f32[512,389]{0,1:T(8,128)}, f32[512,389]{0,1:T(8,128)S(1)}, u32[]{:S(2)}) copy-start(f32[512,389]{0,1:T(8,128)S(1)} %get-tuple-element.26) | copy-start | bytes 2390020
  52.0 12.2 %copy-start.4 = (bf16[512,256]{0,1:T(8,128)(2,1)}, bf16[512,256]{0,1:T(8,128)(2,1)S(1)}, u32[]{:S(2)}) copy-start(bf16[512,256]{0,1:T(8,128)(2,1)S(1)} %fusion.32) | copy-start | bytes 786436
  52.0 15.4 %collective-permute-start.4 = (bf16[512,256]{0,1:T(8,128)(2,1)S(1)}, bf16[512,256]{0,1:T(8,128)(2,1)S(1)}, u32[]{:S(2)}, u32[]{:S(2)}) collective-permute-start(bf16[512,256]{0,1:T(8,128)(2,1)S(1)} %fusion.32), channel_id=1, source_target_pairs={{0,24},{8,16},{16,8},{24,0},{1,25},{9,17},{17,9},{25,1},{2,26},{10... | collective-permute-start | bytes 786440 | tf_op jit(solution)/shard_map/ppermute | solution.py:72
  53.7 13.2 %collective-permute-start.3 = (bf16[512,256]{0,1:T(8,128)(2,1)S(1)}, bf16[512,256]{0,1:T(8,128)(2,1)S(1)}, u32[]{:S(2)}, u32[]{:S(2)}) collective-permute-start(bf16[512,256]{0,1:T(8,128)(2,1)S(1)} %fusion.32), channel_id=1, source_target_pairs={{0,16},{8,24},{16,0},{24,8},{1,17},{9,25},{17,1},{25,9},{2,18},{10... | collective-permute-start | bytes 786440 | tf_op jit(solution)/shard_map/ppermute | solution.py:72
  53.7 10.1 %collective-permute-start.2 = (bf16[512,256]{0,1:T(8,128)(2,1)S(1)}, bf16[512,256]{0,1:T(8,128)(2,1)S(1)}, u32[]{:S(2)}, u32[]{:S(2)}) collective-permute-start(bf16[512,256]{0,1:T(8,128)(2,1)S(1)} %fusion.32), channel_id=1, source_target_pairs={{0,8},{8,0},{16,24},{24,16},{1,9},{9,1},{17,25},{25,17},{2,10},{10... | collective-permute-start | bytes 786440 | tf_op jit(solution)/shard_map/ppermute | solution.py:72
  74.9 5.9 %copy-start.6 = (bf16[1024,1024]{0,1:T(8,128)(2,1)S(1)}, bf16[1024,1024]{0,1:T(8,128)(2,1)}, u32[]{:S(2)}) copy-start(bf16[1024,1024]{0,1:T(8,128)(2,1)} %all-gather.2.cloned.1.call-done) | copy-start | bytes 6291460
  78.1 7.8 %collective-permute-start.10 = (bf16[512,256]{0,1:T(8,128)(2,1)S(1)}, bf16[512,256]{0,1:T(8,128)(2,1)S(1)}, u32[]{:S(2)}, u32[]{:S(2)}) collective-permute-start(bf16[512,256]{0,1:T(8,128)(2,1)S(1)} %get-tuple-element.22), channel_id=1, source_target_pairs={{0,8},{8,0},{16,24},{24,16},{1,9},{9,1},{17,25},{25,17},{2,10},{10... | collective-permute-start | bytes 786440 | tf_op jit(solution)/shard_map/ppermute | solution.py:72
  78.5 13.8 %collective-permute-start.12 = (bf16[512,256]{0,1:T(8,128)(2,1)S(1)}, bf16[512,256]{0,1:T(8,128)(2,1)S(1)}, u32[]{:S(2)}, u32[]{:S(2)}) collective-permute-start(bf16[512,256]{0,1:T(8,128)(2,1)S(1)} %get-tuple-element.23), channel_id=1, source_target_pairs={{0,24},{8,16},{16,8},{24,0},{1,25},{9,17},{17,9},{25,1},{2,26},{10... | collective-permute-start | bytes 786440 | tf_op jit(solution)/shard_map/ppermute | solution.py:72
  80.5 12.8 %collective-permute-start.11 = (bf16[512,256]{0,1:T(8,128)(2,1)S(1)}, bf16[512,256]{0,1:T(8,128)(2,1)S(1)}, u32[]{:S(2)}, u32[]{:S(2)}) collective-permute-start(bf16[512,256]{0,1:T(8,128)(2,1)S(1)} %get-tuple-element.24), channel_id=1, source_target_pairs={{0,16},{8,24},{16,0},{24,8},{1,17},{9,25},{17,1},{25,9},{2,18},{10... | collective-permute-start | bytes 786440 | tf_op jit(solution)/shard_map/ppermute | solution.py:72
  93.5 6.7 %collective-permute-start.13 = (bf16[512,133]{0,1:T(8,128)(2,1)S(1)}, bf16[512,133]{0,1:T(8,128)(2,1)S(1)}, u32[]{:S(2)}, u32[]{:S(2)}) collective-permute-start(bf16[512,133]{0,1:T(8,128)(2,1)S(1)} %slice.461), channel_id=1, source_target_pairs={{8,0},{16,8},{24,16},{9,1},{17,9},{25,17},{10,2},{18,10},{26,18},{... | collective-permute-start | bytes 408584 | tf_op jit(solution)/shard_map/ppermute | solution.py:32
  112.3 21.4 %collective-permute-start.5 = (bf16[512,256]{0,1:T(8,128)(2,1)}, bf16[512,256]{0,1:T(8,128)(2,1)}, u32[]{:S(2)}, u32[]{:S(2)}) collective-permute-start(bf16[512,256]{0,1:T(8,128)(2,1)} %reduce-scatter.2.cloned.1.call-done), channel_id=1, source_target_pairs={{0,0},{1,1},{2,8},{3,9},{4,16},{5,17},{6,24},{7,25},{8,10},{9,11},... | collective-permute-start | bytes 786440 | tf_op jit(solution)/shard_map/ppermute | solution.py:137
  (40 other events, 81.5 us)
Sparse Core Ops, SparseCore 0:
  43.6 31.2 all-gather.1
  77.2 35.0 reduce-scatter.1

commit v6 on v5

--- a/solution.py
+++ b/solution.py
@@ -96,6 +96,25 @@
     return lax.all_gather(moved, "tp", axis=0, tiled=True)
 
 
+def halving_scatter(total, axis):
+    count = lax.axis_size(axis)
+    if count & (count - 1):
+        return lax.psum_scatter(total, axis, scatter_dimension=0, tiled=True)
+    bits = count.bit_length() - 1
+    me = lax.axis_index(axis)
+    rows = total.shape[0] // count
+    total = total.reshape([2] * bits + [rows, total.shape[1]])
+    for level in range(bits):
+        mask = 1 << level
+        at = bits - 1 - level
+        mine = (me // mask) % 2
+        keep = lax.dynamic_index_in_dim(total, mine, at, keepdims=False)
+        send = lax.dynamic_index_in_dim(total, 1 - mine, at, keepdims=False)
+        route = [(i, i ^ mask) for i in range(count)]
+        total = keep + lax.ppermute(send.astype(jnp.bfloat16), axis, route).astype(jnp.float32)
+    return total
+
+
 def shards(streams, feat_weight, long_filter, skip_gain, out_weight, out_grad):
     channels = streams.shape[1]
     length = streams.shape[2]
@@ -122,12 +141,9 @@
     gated_blocks = [gated] + exchange(lambda step: gated, "seq")
     group = n_tp // n_seq
     weight_t = out_weight.T
-    pieces = [
-        jnp.dot(weight_t, block, preferred_element_type=jnp.float32).astype(jnp.bfloat16)
-        for block in gated_blocks
-    ]
+    pieces = [jnp.dot(weight_t, block, preferred_element_type=jnp.float32) for block in gated_blocks]
     partial_out = jnp.concatenate(pieces, axis=0)
-    output_sum = lax.psum_scatter(partial_out, "tp", scatter_dimension=0, tiled=True)
+    output_sum = halving_scatter(partial_out, "tp").astype(jnp.bfloat16)
     route = []
     for s in range(n_seq):
         for p in range(n_tp):

time: 143 us -> 202 us (1.41)
  the two profiles are of different devices: /device:TPU:27 before, /device:TPU:0 now
where the time goes in v6:
time: 202 us; the launch traced here: 200 us
  local copies, waits for them, and re-layouts  51.6 us (26%)
  waiting for transfers between devices  47.4 us (23%)
  starting transfers between devices  44.4 us (22%)
  matrix products  25.8 us (13%)
  other arithmetic  15.9 us (8%)
  between operations  14.9 us (7%)
    ppermute x9, starting transfers between devices, exchange(): got.append(lax.ppermute(block_of(step), axis, route))  26.7 us
    ppermute x3, waiting for transfers between devices, halving_scatter(): lax.ppermute(send.astype(jnp.bfloat16), axis, route).astype(jnp.float32)  25.2 us
    ppermute x9, waiting for transfers between devices, exchange(): got.append(lax.ppermute(block_of(step), axis, route))  19.4 us
    unnamed x80, local copies, waits for them, and re-layouts  15.6 us
    dynamic_slice x2, local copies, waits for them, and re-layouts, halving_scatter(): keep = lax.dynamic_index_in_dim(total, mine, at, keepdims=False)  11.7 us
    conv_general_dilated x2, matrix products, correlate(): lax.conv_general_dilated(signal[None], taps[:, None, :], (1,), 'VALID', d...  11 us
    reshape x1, local copies, waits for them, and re-layouts, halving_scatter(): total = total.reshape([2] * bits + [rows, total.shape[1]])  6.68 us
    dot_general x4, matrix products, shards(): lax.dot_general(block, grad_part, (((1,), (1,)), ((), ())), preferred_ele...  6.14 us
  transfers between devices with their start and end apart: 18, of which 10 were waited for; matrix products, arithmetic and copies ran while one was open for 36% of the time, Pallas kernels for 0%

profile of v6, /device:TPU:0, one launch (start us, length us, event | category | flops | bytes accessed | tf_op | source)
XLA Modules:
  0.0 200.0 jit_solution(4628221109324535184)
XLA Ops:
  13.3 5.5 %collective-permute-start = (bf16[512,272]{0,1:T(8,128)(2,1)}, bf16[512,272]{0,1:T(8,128)(2,1)S(1)}, u32[]{:S(2)}, u32[]{:S(2)}) collective-permute-start(bf16[512,272]{0,1:T(8,128)(2,1)} %pad_maximum_fusion.3), channel_id=1, source_target_pairs={{0,8},{8,16},{16,24},{1,9},{9,17},{17,25},{2,10},{10,18},{18,26},{... | collective-permute-start | bytes 835592 | tf_op jit(solution)/shard_map/ppermute | solution.py:19
  21.3 3.5 %collective-permute-start.10 = (bf16[128,256]{1,0:T(8,128)(2,1)}, bf16[128,256]{1,0:T(8,128)(2,1)}, u32[]{:S(2)}, u32[]{:S(2)}) collective-permute-start(bf16[128,256]{1,0:T(8,128)(2,1)} %get-tuple-element.43), channel_id=1, source_target_pairs={{0,16},{8,24},{16,0},{24,8},{1,17},{9,25},{17,1},{25,9},{2,18},{10... | collective-permute-start | bytes 196616 | tf_op jit(solution)/shard_map/ppermute | solution.py:72
  27.1 2.8 %collective-permute-done.10 = bf16[128,256]{1,0:T(8,128)(2,1)} collective-permute-done((bf16[128,256]{1,0:T(8,128)(2,1)}, bf16[128,256]{1,0:T(8,128)(2,1)}, u32[]{:S(2)}, u32[]{:S(2)}) %collective-permute-start.10) | collective-permute-done | bytes 65568 | tf_op jit(solution)/shard_map/ppermute | solution.py:72
  33.4 3.6 %collective-permute-start.12 = (bf16[128,1024]{0,1:T(8,128)(2,1)}, bf16[128,1024]{0,1:T(8,128)(2,1)}, u32[]{:S(2)}, u32[]{:S(2)}) collective-permute-start(bf16[128,1024]{0,1:T(8,128)(2,1)} %bitcast.41), channel_id=1, source_target_pairs={{0,0},{1,4},{2,8},{3,12},{4,16},{5,20},{6,24},{7,28},{8,1},{9,5},{... | collective-permute-start | bytes 786440 | tf_op jit(solution)/shard_map/ppermute | solution.py:95
  40.0 5.5 %fusion.22 = f32[1,512,262]{1,0,2:T(1,128)S(1)} fusion(f32[512,1,128]{0,1,2:T(1,128)S(1)} %copy-done.11, f32[1,512,389]{1,2,0:T(8,128)S(1)} %get-tuple-element.27), kind=kOutput, calls=%fused_computation.59 | convolution fusion | flops 206045184 | bytes 1595392 | tf_op jit(solution)/shard_map/conv_general_dilated | solution.py:36
  52.4 5.3 %collective-permute-done.4 = bf16[512,256]{0,1:T(8,128)(2,1)} collective-permute-done((bf16[512,256]{0,1:T(8,128)(2,1)S(1)}, bf16[512,256]{0,1:T(8,128)(2,1)}, u32[]{:S(2)}, u32[]{:S(2)}) %collective-permute-start.4) | collective-permute-done | bytes 262176 | tf_op jit(solution)/shard_map/ppermute | solution.py:72
  59.1 3.7 %collective-permute-done.3 = bf16[512,256]{0,1:T(8,128)(2,1)} collective-permute-done((bf16[512,256]{0,1:T(8,128)(2,1)S(1)}, bf16[512,256]{0,1:T(8,128)(2,1)}, u32[]{:S(2)}, u32[]{:S(2)}) %collective-permute-start.3) | collective-permute-done | bytes 262176 | tf_op jit(solution)/shard_map/ppermute | solution.py:72
  65.7 2.5 %pad_maximum_fusion = f32[4096,256]{0,1:T(8,128)} fusion(f32[1024,256]{0,1:T(8,128)S(1)} %convolution_bitcast_fusion, f32[1024,256]{0,1:T(8,128)S(1)} %convolution_bitcast_fusion.1, f32[1024,256]{0,1:T(8,128)S(1)} %convolution_bitcast_fusion.2, f32[1024,256]{0,1:T(8,128)S(1)} %copy-done.5), kind=kLoop, calls=%fused_computation.1 | loop fusion | flops 3145728 | bytes 8388608 | tf_op jit(solution)/shard_map/concatenate | solution.py:145
  68.2 6.7 %reshape.71 = f32[2,2,2,512,256]{3,2,1,0,4:T(2,128)} reshape(f32[4096,256]{0,1:T(8,128)} %pad_maximum_fusion) | data formatting | bytes 8388608 | tf_op jit(solution)/shard_map/reshape | solution.py:106
  74.9 5.7 %constant_dynamic-slice_fusion.1 = bf16[2,2,1,512,256]{3,2,1,0,4:T(2,128)(2,1)} fusion(f32[2,2,2,512,256]{3,2,1,0,4:T(2,128)} %reshape.71, s32[]{:T(128)S(6)} %select_n.141), kind=kLoop, calls=%fused_computation.118 | loop fusion | bytes 2097156 | tf_op jit(solution)/shard_map/jit(dynamic_index_in_dim)/dynamic_slice | solution.py:112
  80.5 5.8 %copy.83 = bf16[2,2,1,512,256]{4,3,0,1,2:T(8,128)(2,1)} copy(bf16[2,2,1,512,256]{3,2,1,0,4:T(2,128)(2,1)} %constant_dynamic-slice_fusion.1) | data formatting | bytes 2097152
  86.7 5.7 %constant_dynamic-slice_fusion.2 = f32[2,2,1,512,256]{3,2,1,0,4:T(1,128)} fusion(f32[2,2,2,512,256]{3,2,1,0,4:T(2,128)} %reshape.71, s32[]{:T(128)S(6)} %select_n.140), kind=kLoop, calls=%fused_computation.119 | loop fusion | bytes 4194308 | tf_op jit(solution)/shard_map/jit(dynamic_index_in_dim)/dynamic_slice | solution.py:111
  92.4 6.1 %copy.52 = f32[2,2,1,512,256]{4,3,0,1,2:T(8,128)} copy(f32[2,2,1,512,256]{3,2,1,0,4:T(1,128)} %constant_dynamic-slice_fusion.2) | data formatting | bytes 4194304 | tf_op jit(solution)/shard_map/jit(dynamic_index_in_dim)/dynamic_slice | solution.py:111
  98.5 2.1 %bitcast_add_fusion = f32[2,2,512,256]{3,2,0,1:T(8,128)S(1)} fusion(f32[2,2,1,512,256]{4,3,0,1,2:T(8,128)} %copy.52, bf16[2,2,512,256]{3,2,0,1:T(8,128)(2,1)} %collective-permute-done.5), kind=kLoop, calls=%fused_computation.2 | loop fusion | flops 1048576 | bytes 5242880 | tf_op jit(solution)/shard_map/add | solution.py:114
  102.8 14.3 %collective-permute-done.6 = bf16[2,512,256]{2,1,0:T(8,128)(2,1)} collective-permute-done((bf16[2,512,256]{2,1,0:T(8,128)(2,1)}, bf16[2,512,256]{2,1,0:T(8,128)(2,1)}, u32[]{:S(2)}, u32[]{:S(2)}) %collective-permute-start.6) | collective-permute-done | bytes 524320 | tf_op jit(solution)/shard_map/ppermute | solution.py:114
  123.6 10.9 %collective-permute-done.7 = bf16[512,256]{1,0:T(8,128)(2,1)} collective-permute-done((bf16[512,256]{1,0:T(8,128)(2,1)}, bf16[512,256]{1,0:T(8,128)(2,1)}, u32[]{:S(2)}, u32[]{:S(2)}) %collective-permute-start.7) | collective-permute-done | bytes 262176 | tf_op jit(solution)/shard_map/ppermute | solution.py:114
  136.4 3.6 %collective-permute-start.8 = (bf16[512,256]{1,0:T(8,128)(2,1)}, bf16[512,256]{1,0:T(8,128)(2,1)}, u32[]{:S(2)}, u32[]{:S(2)}) collective-permute-start(bf16[512,256]{1,0:T(8,128)(2,1)} %fusion.32), channel_id=1, source_target_pairs={{0,0},{1,1},{2,8},{3,9},{4,16},{5,17},{6,24},{7,25},{8,10},{9,11},... | collective-permute-start | bytes 786440 | tf_op jit(solution)/shard_map/ppermute | solution.py:153
  142.6 3.0 %fusion.61 = f32[1024,512]{1,0:T(8,128)S(1)} fusion(bf16[1024,1024]{0,1:T(8,128)(2,1)} %all-gather.2.cloned.1.call-done, bf16[512,1024]{1,0:T(8,128)(2,1)S(1)} %copy-done), kind=kOutput, calls=%fused_computation.150 | convolution fusion | flops 1073741824 | bytes 5242880 | tf_op jit(solution)/shard_map/dot_general | solution.py:156
  145.7 9.6 %collective-permute-start.15 = (bf16[512,256]{0,1:T(8,128)(2,1)S(1)}, bf16[512,256]{0,1:T(8,128)(2,1)S(1)}, u32[]{:S(2)}, u32[]{:S(2)}) collective-permute-start(bf16[512,256]{0,1:T(8,128)(2,1)S(1)} %get-tuple-element.23), channel_id=1, source_target_pairs={{0,24},{8,16},{16,8},{24,0},{1,25},{9,17},{17,9},{25,1},{2,26},{10... | collective-permute-start | bytes 786440 | tf_op jit(solution)/shard_map/ppermute | solution.py:72
  155.3 9.1 %collective-permute-start.14 = (bf16[512,256]{0,1:T(8,128)(2,1)S(1)}, bf16[512,256]{0,1:T(8,128)(2,1)S(1)}, u32[]{:S(2)}, u32[]{:S(2)}) collective-permute-start(bf16[512,256]{0,1:T(8,128)(2,1)S(1)} %get-tuple-element.24), channel_id=1, source_target_pairs={{0,16},{8,24},{16,0},{24,8},{1,17},{9,25},{17,1},{25,9},{2,18},{10... | collective-permute-start | bytes 786440 | tf_op jit(solution)/shard_map/ppermute | solution.py:72
  167.8 5.4 %collective-permute-done.14 = bf16[512,256]{0,1:T(8,128)(2,1)S(1)} collective-permute-done((bf16[512,256]{0,1:T(8,128)(2,1)S(1)}, bf16[512,256]{0,1:T(8,128)(2,1)S(1)}, u32[]{:S(2)}, u32[]{:S(2)}) %collective-permute-start.14) | collective-permute-done | bytes 262176 | tf_op jit(solution)/shard_map/ppermute | solution.py:72
  175.7 2.9 %add_convert_fusion = bf16[512,1024]{1,0:T(8,128)(2,1)} fusion(f32[512,1024]{1,0:T(8,128)S(1)} %fusion.34, f32[512,1024]{1,0:T(8,128)S(1)} %fusion.36, f32[512,1024]{1,0:T(8,128)S(1)} %fusion.38, bf16[512,256]{0,1:T(8,128)(2,1)} %collective-permute-done.4, bf16[1024,1024]{0,1:T(8,128)(2,1)S(1)} %copy-done.7, s32[]{:T(128)S(6)} %select_n.167), kind=kOutput, calls=%fused_computation.3 | convolution fusion | flops 274726912 | bytes 8126468 | tf_op jit(solution)/shard_map/dot_general | solution.py:173
  178.6 2.8 %collective-permute-done.16 = bf16[512,133]{0,1:T(8,128)(2,1)S(1)} collective-permute-done((bf16[512,133]{0,1:T(8,128)(2,1)S(1)}, bf16[512,133]{0,1:T(8,128)(2,1)S(1)}, u32[]{:S(2)}, u32[]{:S(2)}) %collective-permute-start.16) | collective-permute-done | bytes 136224 | tf_op jit(solution)/shard_map/ppermute | solution.py:32
  183.1 5.5 %fusion.20 = f32[1,512,262]{1,0,2:T(1,128)S(1)} fusion(f32[512,1,128]{0,1,2:T(1,128)S(1)} %copy-done.12, f32[1,512,389]{1,2,0:T(8,128)S(1)} %bitcast.140), kind=kOutput, calls=%fused_computation.57 | convolution fusion | flops 206045184 | bytes 1595392 | tf_op jit(solution)/shard_map/conv_general_dilated | solution.py:36
  (158 shorter events, 53.7 us)
Async XLA Ops:
  7.2 43.8 %copy-start = (bf16[512,1024]{1,0:T(8,128)(2,1)S(1)}, bf16[512,1024]{1,0:T(8,128)(2,1)}, u32[]{:S(2)}) copy-start(bf16[512,1024]{1,0:T(8,128)(2,1)} %param.10) | copy-start | bytes 3145732
  7.2 135.4 %all-gather.2.cloned.1.call-start = ((), (), s32[]{:S(2)}) async-start(), calls=%async_computation | async-start | bytes 2359296 | tf_op jit(solution)/shard_map/all_gather | solution.py:96
  10.9 26.1 %collective-permute-start.1 = (bf16[512,145]{0,1:T(8,128)(2,1)}, bf16[512,145]{0,1:T(8,128)(2,1)S(1)}, u32[]{:S(2)}, u32[]{:S(2)}) collective-permute-start(bf16[512,145]{0,1:T(8,128)(2,1)} %pad_maximum_fusion.5), channel_id=1, source_target_pairs={{8,0},{16,8},{24,16},{9,1},{17,9},{25,17},{10,2},{18,10},{26,18},{... | collective-permute-start | bytes 445448 | tf_op jit(solution)/shard_map/ppermute | solution.py:20
  13.3 23.7 %collective-permute-start = (bf16[512,272]{0,1:T(8,128)(2,1)}, bf16[512,272]{0,1:T(8,128)(2,1)S(1)}, u32[]{:S(2)}, u32[]{:S(2)}) collective-permute-start(bf16[512,272]{0,1:T(8,128)(2,1)} %pad_maximum_fusion.3), channel_id=1, source_target_pairs={{0,8},{8,16},{16,24},{1,9},{9,17},{17,25},{2,10},{10,18},{18,26},{... | collective-permute-start | bytes 835592 | tf_op jit(solution)/shard_map/ppermute | solution.py:19
  20.4 6.7 %collective-permute-start.11 = (bf16[128,256]{1,0:T(8,128)(2,1)}, bf16[128,256]{1,0:T(8,128)(2,1)}, u32[]{:S(2)}, u32[]{:S(2)}) collective-permute-start(bf16[128,256]{1,0:T(8,128)(2,1)} %get-tuple-element.42), channel_id=1, source_target_pairs={{0,24},{8,16},{16,8},{24,0},{1,25},{9,17},{17,9},{25,1},{2,26},{10... | collective-permute-start | bytes 196616 | tf_op jit(solution)/shard_map/ppermute | solution.py:72
  21.3 8.6 %collective-permute-start.10 = (bf16[128,256]{1,0:T(8,128)(2,1)}, bf16[128,256]{1,0:T(8,128)(2,1)}, u32[]{:S(2)}, u32[]{:S(2)}) collective-permute-start(bf16[128,256]{1,0:T(8,128)(2,1)} %get-tuple-element.43), channel_id=1, source_target_pairs={{0,16},{8,24},{16,0},{24,8},{1,17},{9,25},{17,1},{25,9},{2,18},{10... | collective-permute-start | bytes 196616 | tf_op jit(solution)/shard_map/ppermute | solution.py:72
  24.8 6.1 %collective-permute-start.9 = (bf16[128,256]{1,0:T(8,128)(2,1)}, bf16[128,256]{1,0:T(8,128)(2,1)}, u32[]{:S(2)}, u32[]{:S(2)}) collective-permute-start(bf16[128,256]{1,0:T(8,128)(2,1)} %get-tuple-element.44), channel_id=1, source_target_pairs={{0,8},{8,0},{16,24},{24,16},{1,9},{9,1},{17,25},{25,17},{2,10},{10... | collective-permute-start | bytes 196616 | tf_op jit(solution)/shard_map/ppermute | solution.py:72
  26.8 19.8 %copy-start.14 = (f32[512,1]{0,1:T(1,128)}, f32[512,1]{0,1:T(1,128)S(1)}, u32[]{:S(2)}) copy-start(f32[512,1]{0,1:T(1,128)S(1)} %get-tuple-element.61) | copy-start | bytes 6148
  26.8 19.8 %copy-start.16 = (f32[512,1]{0,1:T(1,128)}, f32[512,1]{0,1:T(1,128)S(1)}, u32[]{:S(2)}) copy-start(f32[512,1]{0,1:T(1,128)S(1)} %get-tuple-element.62) | copy-start | bytes 6148
  26.8 19.8 %copy-start.18 = (f32[512,1]{0,1:T(1,128)}, f32[512,1]{0,1:T(1,128)S(1)}, u32[]{:S(2)}) copy-start(f32[512,1]{0,1:T(1,128)S(1)} %get-tuple-element.63) | copy-start | bytes 6148
  26.8 19.8 %copy-start.20 = (f32[512,1]{0,1:T(1,128)}, f32[512,1]{0,1:T(1,128)S(1)}, u32[]{:S(2)}) copy-start(f32[512,1]{0,1:T(1,128)S(1)} %get-tuple-element.64) | copy-start | bytes 6148
  33.4 19.0 %collective-permute-start.12 = (bf16[128,1024]{0,1:T(8,128)(2,1)}, bf16[128,1024]{0,1:T(8,128)(2,1)}, u32[]{:S(2)}, u32[]{:S(2)}) collective-permute-start(bf16[128,1024]{0,1:T(8,128)(2,1)} %bitcast.41), channel_id=1, source_target_pairs={{0,0},{1,4},{2,8},{3,12},{4,16},{5,20},{6,24},{7,28},{8,1},{9,5},{... | collective-permute-start | bytes 786440 | tf_op jit(solution)/shard_map/ppermute | solution.py:95
  47.4 10.3 %collective-permute-start.4 = (bf16[512,256]{0,1:T(8,128)(2,1)S(1)}, bf16[512,256]{0,1:T(8,128)(2,1)}, u32[]{:S(2)}, u32[]{:S(2)}) collective-permute-start(bf16[512,256]{0,1:T(8,128)(2,1)S(1)} %fusion.29), channel_id=1, source_target_pairs={{0,24},{8,16},{16,8},{24,0},{1,25},{9,17},{17,9},{25,1},{2,26},{10... | collective-permute-start | bytes 786440 | tf_op jit(solution)/shard_map/ppermute | solution.py:72
  48.2 14.6 %collective-permute-start.3 = (bf16[512,256]{0,1:T(8,128)(2,1)S(1)}, bf16[512,256]{0,1:T(8,128)(2,1)}, u32[]{:S(2)}, u32[]{:S(2)}) collective-permute-start(bf16[512,256]{0,1:T(8,128)(2,1)S(1)} %fusion.29), channel_id=1, source_target_pairs={{0,16},{8,24},{16,0},{24,8},{1,17},{9,25},{17,1},{25,9},{2,18},{10... | collective-permute-start | bytes 786440 | tf_op jit(solution)/shard_map/ppermute | solution.py:72
  48.9 15.2 %collective-permute-start.2 = (bf16[512,256]{0,1:T(8,128)(2,1)S(1)}, bf16[512,256]{0,1:T(8,128)(2,1)}, u32[]{:S(2)}, u32[]{:S(2)}) collective-permute-start(bf16[512,256]{0,1:T(8,128)(2,1)S(1)} %fusion.29), channel_id=1, source_target_pairs={{0,8},{8,0},{16,24},{24,16},{1,9},{9,1},{17,25},{25,17},{2,10},{10... | collective-permute-start | bytes 786440 | tf_op jit(solution)/shard_map/ppermute | solution.py:72
  86.3 12.1 %collective-permute-start.5 = (bf16[2,2,512,256]{3,2,0,1:T(8,128)(2,1)}, bf16[2,2,512,256]{3,2,0,1:T(8,128)(2,1)}, u32[]{:S(2)}, u32[]{:S(2)}) collective-permute-start(bf16[2,2,512,256]{3,2,0,1:T(8,128)(2,1)} %bitcast.141), channel_id=1, source_target_pairs={{0,1},{1,0},{2,3},{3,2},{4,5},{5,4},{6,7},{7,6},{8,9},{9,8},{10,11... | collective-permute-start | bytes 3145736 | tf_op jit(solution)/shard_map/ppermute | solution.py:114
  102.8 14.3 %collective-permute-start.6 = (bf16[2,512,256]{2,1,0:T(8,128)(2,1)}, bf16[2,512,256]{2,1,0:T(8,128)(2,1)}, u32[]{:S(2)}, u32[]{:S(2)}) collective-permute-start(bf16[2,512,256]{2,1,0:T(8,128)(2,1)} %fusion.28), channel_id=1, source_target_pairs={{0,2},{1,3},{2,0},{3,1},{4,6},{5,7},{6,4},{7,5},{8,10},{9,11},{10,... | collective-permute-start | bytes 1572872 | tf_op jit(solution)/shard_map/ppermute | solution.py:114
  120.2 14.3 %collective-permute-start.7 = (bf16[512,256]{1,0:T(8,128)(2,1)}, bf16[512,256]{1,0:T(8,128)(2,1)}, u32[]{:S(2)}, u32[]{:S(2)}) collective-permute-start(bf16[512,256]{1,0:T(8,128)(2,1)} %fusion.40), channel_id=1, source_target_pairs={{0,4},{1,5},{2,6},{3,7},{4,0},{5,1},{6,2},{7,3},{8,12},{9,13},{10,... | collective-permute-start | bytes 786440 | tf_op jit(solution)/shard_map/ppermute | solution.py:114
  136.4 6.1 %collective-permute-start.8 = (bf16[512,256]{1,0:T(8,128)(2,1)}, bf16[512,256]{1,0:T(8,128)(2,1)}, u32[]{:S(2)}, u32[]{:S(2)}) collective-permute-start(bf16[512,256]{1,0:T(8,128)(2,1)} %fusion.32), channel_id=1, source_target_pairs={{0,0},{1,1},{2,8},{3,9},{4,16},{5,17},{6,24},{7,25},{8,10},{9,11},... | collective-permute-start | bytes 786440 | tf_op jit(solution)/shard_map/ppermute | solution.py:153
  142.6 21.9 %copy-start.7 = (bf16[1024,1024]{0,1:T(8,128)(2,1)S(1)}, bf16[1024,1024]{0,1:T(8,128)(2,1)}, u32[]{:S(2)}) copy-start(bf16[1024,1024]{0,1:T(8,128)(2,1)} %all-gather.2.cloned.1.call-done) | copy-start | bytes 6291460
  145.7 22.0 %collective-permute-start.15 = (bf16[512,256]{0,1:T(8,128)(2,1)S(1)}, bf16[512,256]{0,1:T(8,128)(2,1)S(1)}, u32[]{:S(2)}, u32[]{:S(2)}) collective-permute-start(bf16[512,256]{0,1:T(8,128)(2,1)S(1)} %get-tuple-element.23), channel_id=1, source_target_pairs={{0,24},{8,16},{16,8},{24,0},{1,25},{9,17},{17,9},{25,1},{2,26},{10... | collective-permute-start | bytes 786440 | tf_op jit(solution)/shard_map/ppermute | solution.py:72
  155.3 17.8 %collective-permute-start.14 = (bf16[512,256]{0,1:T(8,128)(2,1)S(1)}, bf16[512,256]{0,1:T(8,128)(2,1)S(1)}, u32[]{:S(2)}, u32[]{:S(2)}) collective-permute-start(bf16[512,256]{0,1:T(8,128)(2,1)S(1)} %get-tuple-element.24), channel_id=1, source_target_pairs={{0,16},{8,24},{16,0},{24,8},{1,17},{9,25},{17,1},{25,9},{2,18},{10... | collective-permute-start | bytes 786440 | tf_op jit(solution)/shard_map/ppermute | solution.py:72
  164.5 9.8 %collective-permute-start.13 = (bf16[512,256]{0,1:T(8,128)(2,1)S(1)}, bf16[512,256]{0,1:T(8,128)(2,1)S(1)}, u32[]{:S(2)}, u32[]{:S(2)}) collective-permute-start(bf16[512,256]{0,1:T(8,128)(2,1)S(1)} %get-tuple-element.22), channel_id=1, source_target_pairs={{0,8},{8,0},{16,24},{24,16},{1,9},{9,1},{17,25},{25,17},{2,10},{10... | collective-permute-start | bytes 786440 | tf_op jit(solution)/shard_map/ppermute | solution.py:72
  174.4 6.9 %collective-permute-start.16 = (bf16[512,133]{0,1:T(8,128)(2,1)S(1)}, bf16[512,133]{0,1:T(8,128)(2,1)S(1)}, u32[]{:S(2)}, u32[]{:S(2)}) collective-permute-start(bf16[512,133]{0,1:T(8,128)(2,1)S(1)} %slice.461), channel_id=1, source_target_pairs={{8,0},{16,8},{24,16},{9,1},{17,9},{25,17},{10,2},{18,10},{26,18},{... | collective-permute-start | bytes 408584 | tf_op jit(solution)/shard_map/ppermute | solution.py:32
  (26 other events, 188.3 us)
Sparse Core Ops, SparseCore 0:
  52.5 29.1 all-gather.1

commit v7 on v4

--- a/solution.py
+++ b/solution.py
@@ -138,7 +138,7 @@
         for p in range(n_tp):
             target = source(s, p % n_seq, n_seq) if p % n_seq else s
             route.append((s * n_tp + p, target * n_tp + group * s + p // n_seq))
-    mixed = lax.ppermute(output_sum, ("seq", "tp"), route)
+    mixed_route = route
 
     slab_grad, gated_blocks = lax.optimization_barrier((slab_grad, gated_blocks))
     partial_grad = jnp.dot(out_weight, slab_grad, preferred_element_type=jnp.float32)
@@ -176,6 +176,10 @@
     value_grad = prod_grad * key_feat[:, taps_long - 1 : taps_long - 1 + keep]
     feat_grad = jnp.stack([query_grad, key_grad, value_grad])
     stream_grad = short_correlate(feat_grad, feat_weight).astype(jnp.bfloat16)
+    output_sum, stream_grad, weight_grad = lax.optimization_barrier(
+        (output_sum, stream_grad, weight_grad)
+    )
+    mixed = lax.ppermute(output_sum, ("seq", "tp"), mixed_route)
     return (mixed, stream_grad, weight_grad)
 
 

time: 141 us -> 141 us (level)
  matrix products: 26.7 us -> 30.7 us
  waiting for transfers between devices: 52 us -> 48.7 us
    ppermute x9, waiting for transfers between devices: 22.9 us -> 19.8 us  [exchange(): got.append(lax.ppermute(block_of(step), axis, route))]
    dot_general x8, matrix products: 8.29 us -> 11.4 us  [shards(): lax.dot_general(rows, block, (((0,), (0,)), ((), ())), preferred_element_...]
    unnamed x83 -> x77, local copies, waits for them, and re-layouts: 5.62 us -> 4.93 us
  transfers between devices with their start and end apart: 16 -> 16, of which waited for: 11 -> 11; matrix products, arithmetic and copies ran while one was open for 29% -> 32% of each run, Pallas kernels for 0% -> 0%
where the time goes in v7:
time: 141 us; the launch traced here: 140 us
  waiting for transfers between devices  48.7 us (35%)
  matrix products  30.7 us (22%)
  starting transfers between devices  26.4 us (19%)
  between operations  14.7 us (10%)
  local copies, waits for them, and re-layouts  13.3 us (9%)
  other arithmetic  6.44 us (5%)
    ppermute x9, waiting for transfers between devices, exchange(): got.append(lax.ppermute(block_of(step), axis, route))  19.8 us
    ppermute x1, waiting for transfers between devices, shards(): mixed = lax.ppermute(output_sum, ('seq', 'tp'), mixed_route)  16.9 us
    conv_general_dilated x2, matrix products, correlate(): lax.conv_general_dilated(signal[None], taps[:, None, :], (1,), 'VALID', d...  11.8 us
    ppermute x9, starting transfers between devices, exchange(): got.append(lax.ppermute(block_of(step), axis, route))  11.5 us
    dot_general x8, matrix products, shards(): lax.dot_general(rows, block, (((0,), (0,)), ((), ())), preferred_element_...  11.4 us
    ppermute x1, waiting for transfers between devices, rows_of_slab(): moved = lax.ppermute(mine, ('seq', 'tp'), route)  6.43 us
    unnamed x77, local copies, waits for them, and re-layouts  4.93 us
    dot_general x4, matrix products, shards(): lax.dot_general(block, grad_part, (((1,), (1,)), ((), ())), preferred_ele...  4.25 us
  transfers between devices with their start and end apart: 16, of which 11 were waited for; matrix products, arithmetic and copies ran while one was open for 32% of the time, Pallas kernels for 0%

profile of v7, /device:TPU:4, one launch (start us, length us, event | category | flops | bytes accessed | tf_op | source)
XLA Modules:
  0.0 140.2 jit_solution(1679421108061422768)
XLA Ops:
  10.8 3.3 %collective-permute-start.1 = (bf16[512,145]{0,1:T(8,128)(2,1)}, bf16[512,145]{0,1:T(8,128)(2,1)S(1)}, u32[]{:S(2)}, u32[]{:S(2)}) collective-permute-start(bf16[512,145]{0,1:T(8,128)(2,1)} %pad_maximum_fusion.4), channel_id=1, source_target_pairs={{8,0},{16,8},{24,16},{9,1},{17,9},{25,17},{10,2},{18,10},{26,18},{... | collective-permute-start | bytes 445448 | tf_op jit(solution)/shard_map/ppermute | solution.py:20
  14.5 2.5 %collective-permute-start = (bf16[512,272]{0,1:T(8,128)(2,1)S(1)}, bf16[512,272]{0,1:T(8,128)(2,1)S(1)}, u32[]{:S(2)}, u32[]{:S(2)}) collective-permute-start(bf16[512,272]{0,1:T(8,128)(2,1)S(1)} %pad_maximum_fusion.2), channel_id=1, source_target_pairs={{0,8},{8,16},{16,24},{1,9},{9,17},{17,25},{2,10},{10,18},{18,26},{... | collective-permute-start | bytes 835592 | tf_op jit(solution)/shard_map/ppermute | solution.py:19
  17.1 2.4 %collective-permute-start.7 = (bf16[128,256]{1,0:T(8,128)(2,1)S(1)}, bf16[128,256]{1,0:T(8,128)(2,1)S(1)}, u32[]{:S(2)}, u32[]{:S(2)}) collective-permute-start(bf16[128,256]{1,0:T(8,128)(2,1)S(1)} %get-tuple-element.48), channel_id=1, source_target_pairs={{0,24},{8,16},{16,8},{24,0},{1,25},{9,17},{17,9},{25,1},{2,26},{10... | collective-permute-start | bytes 196616 | tf_op jit(solution)/shard_map/ppermute | solution.py:72
  23.9 3.6 %collective-permute-done.7 = bf16[128,256]{1,0:T(8,128)(2,1)S(1)} collective-permute-done((bf16[128,256]{1,0:T(8,128)(2,1)S(1)}, bf16[128,256]{1,0:T(8,128)(2,1)S(1)}, u32[]{:S(2)}, u32[]{:S(2)}) %collective-permute-start.7) | collective-permute-done | bytes 65568 | tf_op jit(solution)/shard_map/ppermute | solution.py:72
  29.8 3.5 %collective-permute-start.8 = (bf16[128,1024]{0,1:T(8,128)(2,1)}, bf16[128,1024]{0,1:T(8,128)(2,1)S(1)}, u32[]{:S(2)}, u32[]{:S(2)}) collective-permute-start(bf16[128,1024]{0,1:T(8,128)(2,1)} %bitcast.39), channel_id=1, source_target_pairs={{0,0},{1,4},{2,8},{3,12},{4,16},{5,20},{6,24},{7,28},{8,1},{9,5},{... | collective-permute-start | bytes 786440 | tf_op jit(solution)/shard_map/ppermute | solution.py:95
  35.7 6.4 %collective-permute-done.8 = bf16[128,1024]{0,1:T(8,128)(2,1)S(1)} collective-permute-done((bf16[128,1024]{0,1:T(8,128)(2,1)}, bf16[128,1024]{0,1:T(8,128)(2,1)S(1)}, u32[]{:S(2)}, u32[]{:S(2)}) %collective-permute-start.8) | collective-permute-done | bytes 262176 | tf_op jit(solution)/shard_map/ppermute | solution.py:95
  42.9 6.3 %fusion.38 = f32[1,512,262]{1,0,2:T(1,128)S(1)} fusion(f32[512,1,128]{0,1,2:T(1,128)} %copy.49, f32[1,512,389]{1,2,0:T(8,128)S(1)} %get-tuple-element.33), kind=kOutput, calls=%fused_computation.74 | convolution fusion | flops 206045184 | bytes 1595392 | tf_op jit(solution)/shard_map/conv_general_dilated | solution.py:36
  51.5 2.8 %collective-permute-start.2 = (bf16[512,256]{0,1:T(8,128)(2,1)S(1)}, bf16[512,256]{0,1:T(8,128)(2,1)}, u32[]{:S(2)}, u32[]{:S(2)}) collective-permute-start(bf16[512,256]{0,1:T(8,128)(2,1)S(1)} %fusion.44), channel_id=1, source_target_pairs={{0,8},{8,0},{16,24},{24,16},{1,9},{9,1},{17,25},{25,17},{2,10},{10... | collective-permute-start | bytes 786440 | tf_op jit(solution)/shard_map/ppermute | solution.py:72
  56.7 2.1 %fusion.14 = bf16[4096,256]{0,1:T(8,128)(2,1)} fusion(bf16[512,256]{0,1:T(8,128)(2,1)S(1)} %fusion.44, bf16[512,1024]{1,0:T(8,128)(2,1)} %param.10), kind=kOutput, calls=%fused_computation.39 | convolution fusion | flops 134348800 | bytes 1048576 | tf_op jit(solution)/shard_map/dot_general | solution.py:130
  58.8 2.8 %collective-permute-done.2 = bf16[512,256]{0,1:T(8,128)(2,1)} collective-permute-done((bf16[512,256]{0,1:T(8,128)(2,1)S(1)}, bf16[512,256]{0,1:T(8,128)(2,1)}, u32[]{:S(2)}, u32[]{:S(2)}) %collective-permute-start.2) | collective-permute-done | bytes 262176 | tf_op jit(solution)/shard_map/ppermute | solution.py:72
  61.6 2.2 %fusion.16 = bf16[4096,256]{0,1:T(8,128)(2,1)} fusion(bf16[4096,256]{0,1:T(8,128)(2,1)} %fusion.14, bf16[512,256]{0,1:T(8,128)(2,1)} %collective-permute-done.2, bf16[512,1024]{1,0:T(8,128)(2,1)} %param.10), kind=kOutput, calls=%fused_computation.41 | convolution fusion | flops 134348800 | bytes 1048576 | tf_op jit(solution)/shard_map/dot_general | solution.py:130
  63.7 3.5 %collective-permute-done.3 = bf16[512,256]{0,1:T(8,128)(2,1)S(1)} collective-permute-done((bf16[512,256]{0,1:T(8,128)(2,1)S(1)}, bf16[512,256]{0,1:T(8,128)(2,1)S(1)}, u32[]{:S(2)}, u32[]{:S(2)}) %collective-permute-start.3) | collective-permute-done | bytes 262176 | tf_op jit(solution)/shard_map/ppermute | solution.py:72
  70.3 2.0 %fusion.24 = bf16[4096,256]{0,1:T(8,128)(2,1)} fusion(bf16[4096,256]{0,1:T(8,128)(2,1)} %fusion.22, bf16[512,256]{0,1:T(8,128)(2,1)} %collective-permute-done.2, bf16[512,1024]{1,0:T(8,128)(2,1)S(1)} %copy-done.28), kind=kOutput, calls=%fused_computation.49 | convolution fusion | flops 134348800 | bytes 1048576 | tf_op jit(solution)/shard_map/dot_general | solution.py:130
  75.1 3.3 %fusion.82 = f32[1024,512]{1,0:T(8,128)S(1)} fusion(bf16[1024,1024]{0,1:T(8,128)(2,1)} %all-gather.2.cloned.1.call-done, bf16[512,1024]{1,0:T(8,128)(2,1)} %param.10), kind=kOutput, calls=%fused_computation.166 | convolution fusion | flops 1073741824 | bytes 5242880 | tf_op jit(solution)/shard_map/dot_general | solution.py:144
  78.6 1.5 %collective-permute-start.11 = (bf16[512,256]{0,1:T(8,128)(2,1)S(1)}, bf16[512,256]{0,1:T(8,128)(2,1)S(1)}, u32[]{:S(2)}, u32[]{:S(2)}) collective-permute-start(bf16[512,256]{0,1:T(8,128)(2,1)S(1)} %get-tuple-element.29), channel_id=1, source_target_pairs={{0,24},{8,16},{16,8},{24,0},{1,25},{9,17},{17,9},{25,1},{2,26},{10... | collective-permute-start | bytes 786440 | tf_op jit(solution)/shard_map/ppermute | solution.py:72
  84.5 4.3 %collective-permute-done.11 = bf16[512,256]{0,1:T(8,128)(2,1)S(1)} collective-permute-done((bf16[512,256]{0,1:T(8,128)(2,1)S(1)}, bf16[512,256]{0,1:T(8,128)(2,1)S(1)}, u32[]{:S(2)}, u32[]{:S(2)}) %collective-permute-start.11) | collective-permute-done | bytes 262176 | tf_op jit(solution)/shard_map/ppermute | solution.py:72
  88.7 4.8 %collective-permute-done.10 = bf16[512,256]{0,1:T(8,128)(2,1)S(1)} collective-permute-done((bf16[512,256]{0,1:T(8,128)(2,1)S(1)}, bf16[512,256]{0,1:T(8,128)(2,1)S(1)}, u32[]{:S(2)}, u32[]{:S(2)}) %collective-permute-start.10) | collective-permute-done | bytes 262176 | tf_op jit(solution)/shard_map/ppermute | solution.py:72
  93.8 3.6 %collective-permute-start.12 = (bf16[512,133]{0,1:T(8,128)(2,1)S(1)}, bf16[512,133]{0,1:T(8,128)(2,1)S(1)}, u32[]{:S(2)}, u32[]{:S(2)}) collective-permute-start(bf16[512,133]{0,1:T(8,128)(2,1)S(1)} %slice.485), channel_id=1, source_target_pairs={{8,0},{16,8},{24,16},{9,1},{17,9},{25,17},{10,2},{18,10},{26,18},{... | collective-permute-start | bytes 408584 | tf_op jit(solution)/shard_map/ppermute | solution.py:32
  97.4 1.9 %add_convert_fusion = bf16[512,1024]{1,0:T(8,128)(2,1)} fusion(f32[512,1024]{1,0:T(8,128)S(1)} %fusion.48, f32[512,1024]{1,0:T(8,128)S(1)} %fusion.50, f32[512,1024]{1,0:T(8,128)S(1)} %fusion.52, bf16[512,256]{0,1:T(8,128)(2,1)S(1)} %collective-permute-done.4, bf16[1024,1024]{0,1:T(8,128)(2,1)S(1)} %copy-done.1, s32[]{:T(128)S(6)} %select_n.112), kind=kOutput, calls=%fused_computation.1 | convolution fusion | flops 274726912 | bytes 8126468 | tf_op jit(solution)/shard_map/dot_general | solution.py:161
  99.3 2.0 %collective-permute-done.12 = bf16[512,133]{0,1:T(8,128)(2,1)S(1)} collective-permute-done((bf16[512,133]{0,1:T(8,128)(2,1)S(1)}, bf16[512,133]{0,1:T(8,128)(2,1)S(1)}, u32[]{:S(2)}, u32[]{:S(2)}) %collective-permute-start.12) | collective-permute-done | bytes 136224 | tf_op jit(solution)/shard_map/ppermute | solution.py:32
  102.5 5.5 %fusion.36 = f32[1,512,262]{1,0,2:T(1,128)S(1)} fusion(f32[512,1,128]{0,1,2:T(1,128)S(1)} %copy-done.9, f32[1,512,389]{1,2,0:T(8,128)S(1)} %bitcast.147), kind=kOutput, calls=%fused_computation.72 | convolution fusion | flops 206045184 | bytes 1595392 | tf_op jit(solution)/shard_map/conv_general_dilated | solution.py:36
  109.7 2.8 %reduce-scatter.2.cloned.1.call-done = bf16[512,256]{0,1:T(8,128)(2,1)} async-done(((bf16[4096,256]{0,1:T(8,128)(2,1)}), bf16[512,256]{0,1:T(8,128)(2,1)}) %reduce-scatter.2.cloned.1.call-update) | async-done | bytes 262160 | tf_op jit(solution)/shard_map/reduce_scatter | solution.py:135
  112.6 1.9 %collective-permute-start.13 = (bf16[512,256]{0,1:T(8,128)(2,1)}, bf16[512,256]{0,1:T(8,128)(2,1)S(1)}, u32[]{:S(2)}, u32[]{:S(2)}) collective-permute-start(bf16[512,256]{0,1:T(8,128)(2,1)} %reduce-scatter.2.cloned.1.call-done), channel_id=1, source_target_pairs={{0,0},{1,8},{2,16},{3,24},{4,1},{5,9},{6,17},{7,25},{8,10},{9,2},{... | collective-permute-start | bytes 786440 | tf_op jit(solution)/shard_map/ppermute | solution.py:182
  115.6 16.9 %collective-permute-done.13 = bf16[512,256]{0,1:T(8,128)(2,1)S(1)} collective-permute-done((bf16[512,256]{0,1:T(8,128)(2,1)}, bf16[512,256]{0,1:T(8,128)(2,1)S(1)}, u32[]{:S(2)}, u32[]{:S(2)}) %collective-permute-start.13) | collective-permute-done | bytes 262176 | tf_op jit(solution)/shard_map/ppermute | solution.py:182
  (146 shorter events, 33.4 us)
Async XLA Ops:
  7.2 68.0 %all-gather.2.cloned.1.call-start = ((), (), s32[]{:S(2)}) async-start(), calls=%async_computation.2 | async-start | bytes 2359296 | tf_op jit(solution)/shard_map/all_gather | solution.py:96
  9.7 7.3 %copy-start.7 = (bf16[512,256]{1,0:T(8,128)(2,1)S(1)}, bf16[512,256]{1,0:T(8,128)(2,1)}, u32[]{:S(2)}) copy-start(bf16[512,256]{1,0:T(8,128)(2,1)} %param.11) | copy-start | bytes 786436
  9.7 10.9 %copy-start = (bf16[3,512,256]{2,1,0:T(8,128)(2,1)S(1)}, bf16[3,512,256]{2,1,0:T(8,128)(2,1)}, u32[]{:S(2)}) copy-start(bf16[3,512,256]{2,1,0:T(8,128)(2,1)} %param.6) | copy-start | bytes 2359300
  10.8 22.6 %collective-permute-start.1 = (bf16[512,145]{0,1:T(8,128)(2,1)}, bf16[512,145]{0,1:T(8,128)(2,1)S(1)}, u32[]{:S(2)}, u32[]{:S(2)}) collective-permute-start(bf16[512,145]{0,1:T(8,128)(2,1)} %pad_maximum_fusion.4), channel_id=1, source_target_pairs={{8,0},{16,8},{24,16},{9,1},{17,9},{25,17},{10,2},{18,10},{26,18},{... | collective-permute-start | bytes 445448 | tf_op jit(solution)/shard_map/ppermute | solution.py:20
  14.3 6.4 %copy-start.10 = (f32[3,512,7]{1,2,0:T(8,128)S(1)}, f32[3,512,7]{1,2,0:T(8,128)}, u32[]{:S(2)}) copy-start(f32[3,512,7]{1,2,0:T(8,128)} %param.7) | copy-start | bytes 129028
  14.4 7.1 %copy-start.2 = (f32[512,128]{1,0:T(8,128)S(1)}, f32[512,128]{1,0:T(8,128)}, u32[]{:S(2)}) copy-start(f32[512,128]{1,0:T(8,128)} %param.8) | copy-start | bytes 786436
  14.5 18.8 %collective-permute-start = (bf16[512,272]{0,1:T(8,128)(2,1)S(1)}, bf16[512,272]{0,1:T(8,128)(2,1)S(1)}, u32[]{:S(2)}, u32[]{:S(2)}) collective-permute-start(bf16[512,272]{0,1:T(8,128)(2,1)S(1)} %pad_maximum_fusion.2), channel_id=1, source_target_pairs={{0,8},{8,16},{16,24},{1,9},{9,17},{17,25},{2,10},{10,18},{18,26},{... | collective-permute-start | bytes 835592 | tf_op jit(solution)/shard_map/ppermute | solution.py:19
  17.1 10.5 %collective-permute-start.7 = (bf16[128,256]{1,0:T(8,128)(2,1)S(1)}, bf16[128,256]{1,0:T(8,128)(2,1)S(1)}, u32[]{:S(2)}, u32[]{:S(2)}) collective-permute-start(bf16[128,256]{1,0:T(8,128)(2,1)S(1)} %get-tuple-element.48), channel_id=1, source_target_pairs={{0,24},{8,16},{16,8},{24,0},{1,25},{9,17},{17,9},{25,1},{2,26},{10... | collective-permute-start | bytes 196616 | tf_op jit(solution)/shard_map/ppermute | solution.py:72
  19.5 8.7 %collective-permute-start.6 = (bf16[128,256]{1,0:T(8,128)(2,1)S(1)}, bf16[128,256]{1,0:T(8,128)(2,1)S(1)}, u32[]{:S(2)}, u32[]{:S(2)}) collective-permute-start(bf16[128,256]{1,0:T(8,128)(2,1)S(1)} %get-tuple-element.49), channel_id=1, source_target_pairs={{0,16},{8,24},{16,0},{24,8},{1,17},{9,25},{17,1},{25,9},{2,18},{10... | collective-permute-start | bytes 196616 | tf_op jit(solution)/shard_map/ppermute | solution.py:72
  19.5 8.7 %collective-permute-start.5 = (bf16[128,256]{1,0:T(8,128)(2,1)S(1)}, bf16[128,256]{1,0:T(8,128)(2,1)S(1)}, u32[]{:S(2)}, u32[]{:S(2)}) collective-permute-start(bf16[128,256]{1,0:T(8,128)(2,1)S(1)} %get-tuple-element.50), channel_id=1, source_target_pairs={{0,8},{8,0},{16,24},{24,16},{1,9},{9,1},{17,25},{25,17},{2,10},{10... | collective-permute-start | bytes 196616 | tf_op jit(solution)/shard_map/ppermute | solution.py:72
  29.8 12.3 %collective-permute-start.8 = (bf16[128,1024]{0,1:T(8,128)(2,1)}, bf16[128,1024]{0,1:T(8,128)(2,1)S(1)}, u32[]{:S(2)}, u32[]{:S(2)}) collective-permute-start(bf16[128,1024]{0,1:T(8,128)(2,1)} %bitcast.39), channel_id=1, source_target_pairs={{0,0},{1,4},{2,8},{3,12},{4,16},{5,20},{6,24},{7,28},{8,1},{9,5},{... | collective-permute-start | bytes 786440 | tf_op jit(solution)/shard_map/ppermute | solution.py:95
  42.9 69.7 %reduce-scatter.2.cloned.1.call-start = ((), (), s32[]{:S(2)}) async-start(), calls=%async_computation.1 | async-start | bytes 2359296 | tf_op jit(solution)/shard_map/reduce_scatter | solution.py:135
  42.9 7.1 %slice-start = ((bf16[512,145]{0,1:T(8,128)(2,1)}), bf16[512,133]{0,1:T(8,128)(2,1)S(1)}, s32[]{:S(2)}) async-start(bf16[512,145]{0,1:T(8,128)(2,1)} %copy-done.3), calls=%async_computation.3 | async-start | bytes 278528 | tf_op jit(solution)/shard_map/slice | solution.py:21
  42.9 7.2 %copy-start.26 = (f32[512]{0:T(512)S(1)}, f32[512]{0:T(512)}, u32[]{:S(2)}) copy-start(f32[512]{0:T(512)} %param.9) | copy-start | bytes 6148
  51.5 10.1 %collective-permute-start.2 = (bf16[512,256]{0,1:T(8,128)(2,1)S(1)}, bf16[512,256]{0,1:T(8,128)(2,1)}, u32[]{:S(2)}, u32[]{:S(2)}) collective-permute-start(bf16[512,256]{0,1:T(8,128)(2,1)S(1)} %fusion.44), channel_id=1, source_target_pairs={{0,8},{8,0},{16,24},{24,16},{1,9},{9,1},{17,25},{25,17},{2,10},{10... | collective-permute-start | bytes 786440 | tf_op jit(solution)/shard_map/ppermute | solution.py:72
  55.2 12.1 %copy-start.28 = (bf16[512,1024]{1,0:T(8,128)(2,1)S(1)}, bf16[512,1024]{1,0:T(8,128)(2,1)}, u32[]{:S(2)}) copy-start(bf16[512,1024]{1,0:T(8,128)(2,1)} %param.10) | copy-start | bytes 3145732
  55.2 12.1 %collective-permute-start.3 = (bf16[512,256]{0,1:T(8,128)(2,1)S(1)}, bf16[512,256]{0,1:T(8,128)(2,1)S(1)}, u32[]{:S(2)}, u32[]{:S(2)}) collective-permute-start(bf16[512,256]{0,1:T(8,128)(2,1)S(1)} %fusion.44), channel_id=1, source_target_pairs={{0,16},{8,24},{16,0},{24,8},{1,17},{9,25},{17,1},{25,9},{2,18},{10... | collective-permute-start | bytes 786440 | tf_op jit(solution)/shard_map/ppermute | solution.py:72
  56.4 11.9 %collective-permute-start.4 = (bf16[512,256]{0,1:T(8,128)(2,1)S(1)}, bf16[512,256]{0,1:T(8,128)(2,1)S(1)}, u32[]{:S(2)}, u32[]{:S(2)}) collective-permute-start(bf16[512,256]{0,1:T(8,128)(2,1)S(1)} %fusion.44), channel_id=1, source_target_pairs={{0,24},{8,16},{16,8},{24,0},{1,25},{9,17},{17,9},{25,1},{2,26},{10... | collective-permute-start | bytes 786440 | tf_op jit(solution)/shard_map/ppermute | solution.py:72
  75.1 7.0 %copy-start.1 = (bf16[1024,1024]{0,1:T(8,128)(2,1)S(1)}, bf16[1024,1024]{0,1:T(8,128)(2,1)}, u32[]{:S(2)}) copy-start(bf16[1024,1024]{0,1:T(8,128)(2,1)} %all-gather.2.cloned.1.call-done) | copy-start | bytes 6291460
  78.6 10.2 %collective-permute-start.11 = (bf16[512,256]{0,1:T(8,128)(2,1)S(1)}, bf16[512,256]{0,1:T(8,128)(2,1)S(1)}, u32[]{:S(2)}, u32[]{:S(2)}) collective-permute-start(bf16[512,256]{0,1:T(8,128)(2,1)S(1)} %get-tuple-element.29), channel_id=1, source_target_pairs={{0,24},{8,16},{16,8},{24,0},{1,25},{9,17},{17,9},{25,1},{2,26},{10... | collective-permute-start | bytes 786440 | tf_op jit(solution)/shard_map/ppermute | solution.py:72
  80.1 13.5 %collective-permute-start.10 = (bf16[512,256]{0,1:T(8,128)(2,1)S(1)}, bf16[512,256]{0,1:T(8,128)(2,1)S(1)}, u32[]{:S(2)}, u32[]{:S(2)}) collective-permute-start(bf16[512,256]{0,1:T(8,128)(2,1)S(1)} %get-tuple-element.30), channel_id=1, source_target_pairs={{0,16},{8,24},{16,0},{24,8},{1,17},{9,25},{17,1},{25,9},{2,18},{10... | collective-permute-start | bytes 786440 | tf_op jit(solution)/shard_map/ppermute | solution.py:72
  81.5 12.1 %collective-permute-start.9 = (bf16[512,256]{0,1:T(8,128)(2,1)S(1)}, bf16[512,256]{0,1:T(8,128)(2,1)S(1)}, u32[]{:S(2)}, u32[]{:S(2)}) collective-permute-start(bf16[512,256]{0,1:T(8,128)(2,1)S(1)} %get-tuple-element.28), channel_id=1, source_target_pairs={{0,8},{8,0},{16,24},{24,16},{1,9},{9,1},{17,25},{25,17},{2,10},{10... | collective-permute-start | bytes 786440 | tf_op jit(solution)/shard_map/ppermute | solution.py:72
  93.8 7.6 %collective-permute-start.12 = (bf16[512,133]{0,1:T(8,128)(2,1)S(1)}, bf16[512,133]{0,1:T(8,128)(2,1)S(1)}, u32[]{:S(2)}, u32[]{:S(2)}) collective-permute-start(bf16[512,133]{0,1:T(8,128)(2,1)S(1)} %slice.485), channel_id=1, source_target_pairs={{8,0},{16,8},{24,16},{9,1},{17,9},{25,17},{10,2},{18,10},{26,18},{... | collective-permute-start | bytes 408584 | tf_op jit(solution)/shard_map/ppermute | solution.py:32
  112.6 20.0 %collective-permute-start.13 = (bf16[512,256]{0,1:T(8,128)(2,1)}, bf16[512,256]{0,1:T(8,128)(2,1)S(1)}, u32[]{:S(2)}, u32[]{:S(2)}) collective-permute-start(bf16[512,256]{0,1:T(8,128)(2,1)} %reduce-scatter.2.cloned.1.call-done), channel_id=1, source_target_pairs={{0,0},{1,8},{2,16},{3,24},{4,1},{5,9},{6,17},{7,25},{8,10},{9,2},{... | collective-permute-start | bytes 786440 | tf_op jit(solution)/shard_map/ppermute | solution.py:182
  (23 other events, 43.8 us)
Sparse Core Ops, SparseCore 0:
  43.0 32.1 all-gather.1
  77.4 35.0 reduce-scatter.1

commit v8 on v5

--- a/solution.py
+++ b/solution.py
@@ -134,7 +134,7 @@
             step = p // group
             target = source(s, step, n_seq) if step else s
             route.append((s * n_tp + p, target * n_tp + group * s + p % group))
-    mixed = lax.ppermute(output_sum, ("seq", "tp"), route)
+    mixed_route = route
 
     slab_grad, gated_blocks = lax.optimization_barrier((slab_grad, gated_blocks))
     partial_grad = jnp.dot(out_weight, slab_grad, preferred_element_type=jnp.float32)
@@ -172,6 +172,10 @@
     value_grad = prod_grad * key_feat[:, taps_long - 1 : taps_long - 1 + keep]
     feat_grad = jnp.stack([query_grad, key_grad, value_grad])
     stream_grad = short_correlate(feat_grad, feat_weight).astype(jnp.bfloat16)
+    output_sum, stream_grad, weight_grad = lax.optimization_barrier(
+        (output_sum, stream_grad, weight_grad)
+    )
+    mixed = lax.ppermute(output_sum, ("seq", "tp"), mixed_route)
     return (mixed, stream_grad, weight_grad)
 
 

time: 143 us -> 145 us (1.014)
  waiting for transfers between devices: 58 us -> 60.4 us
    all_gather x1, waiting for transfers between devices: 2.88 us -> 5.31 us  [rows_of_slab(): return lax.all_gather(moved, 'tp', axis=0, tiled=True)]
    ppermute x1, waiting for transfers between devices: 17 us -> 19 us  [shards(): mixed = lax.ppermute(output_sum, ('seq', 'tp'), mixed_route)]
    reduce_scatter x1, waiting for transfers between devices: 5.11 us -> 3.33 us  [shards(): lax.psum_scatter(partial_out, 'tp', scatter_dimension=0, tiled=True)]
    unnamed x111 -> x105, local copies, waits for them, and re-layouts: 9.98 us -> 10 us
where the time goes in v8:
time: 145 us
  waiting for transfers between devices  60.4 us (42%)
  starting transfers between devices  21 us (14%)
  local copies, waits for them, and re-layouts  19.7 us (14%)
  matrix products  19.1 us (13%)
  between operations  14.9 us (10%)
  other arithmetic  9.5 us (7%)
    ppermute x9, waiting for transfers between devices, exchange(): got.append(lax.ppermute(block_of(step), axis, route))  21.9 us
    ppermute x1, waiting for transfers between devices, shards(): mixed = lax.ppermute(output_sum, ('seq', 'tp'), mixed_route)  19 us
    conv_general_dilated x2, matrix products, correlate(): lax.conv_general_dilated(signal[None], taps[:, None, :], (1,), 'VALID', d...  11 us
    unnamed x105, local copies, waits for them, and re-layouts  10 us
    ppermute x1, waiting for transfers between devices, rows_of_slab(): moved = lax.ppermute(mine, ('seq', 'tp'), route)  8.39 us
    ppermute x9, starting transfers between devices, exchange(): got.append(lax.ppermute(block_of(step), axis, route))  8.07 us
    all_gather x1, waiting for transfers between devices, rows_of_slab(): return lax.all_gather(moved, 'tp', axis=0, tiled=True)  5.31 us
    ppermute x1, starting transfers between devices, halo(): low = lax.ppermute(low, axis, forward)  4.01 us
  transfers between devices with their start and end apart: 16, of which 10 were waited for; matrix products, arithmetic and copies ran while one was open for 30% of the time, Pallas kernels for 0%

profile of v8, /device:TPU:27, one launch (start us, length us, event | category | flops | bytes accessed | tf_op | source)
XLA Modules:
  0.0 144.6 jit_solution(14126449924190884627)
XLA Ops:
  7.3 1.8 %constant_dynamic-slice_fusion = (bf16[1,128,256]{2,1,0:T(8,128)(2,1)S(1)}, bf16[128,256]{1,0:T(8,128)(2,1)}, bf16[128,256]{1,0:T(8,128)(2,1)}, bf16[128,256]{1,0:T(8,128)(2,1)S(1)}) fusion(bf16[4,128,256]{2,1,0:T(8,128)(2,1)} %bitcast.132, s32[]{:T(128)S(6)} %select_n.99, s32[]{:T(128)S(6)} %select_n.102, s32[]{:T(128)S(6)} %select_n.101, s32[]{:T(128)S(6)} %select_n.100), kind=kLoop, calls=%fused_computation.120 | loop fusion | bytes 524304 | tf_op jit(solution)/shard_map/dynamic_slice | solution.py:82
  14.1 2.2 %collective-permute-start.1 = (bf16[512,145]{0,1:T(8,128)(2,1)}, bf16[512,145]{0,1:T(8,128)(2,1)S(1)}, u32[]{:S(2)}, u32[]{:S(2)}) collective-permute-start(bf16[512,145]{0,1:T(8,128)(2,1)} %pad_maximum_fusion.5), channel_id=1, source_target_pairs={{8,0},{16,8},{24,16},{9,1},{17,9},{25,17},{10,2},{18,10},{26,18},{... | collective-permute-start | bytes 445448 | tf_op jit(solution)/shard_map/ppermute | solution.py:20
  17.4 4.0 %collective-permute-start = (bf16[512,272]{0,1:T(8,128)(2,1)}, bf16[512,272]{0,1:T(8,128)(2,1)S(1)}, u32[]{:S(2)}, u32[]{:S(2)}) collective-permute-start(bf16[512,272]{0,1:T(8,128)(2,1)} %pad_maximum_fusion.3), channel_id=1, source_target_pairs={{0,8},{8,16},{16,24},{1,9},{9,17},{17,25},{2,10},{10,18},{18,26},{... | collective-permute-start | bytes 835592 | tf_op jit(solution)/shard_map/ppermute | solution.py:19
  33.0 1.9 %collective-permute-start.8 = (bf16[128,1024]{0,1:T(8,128)(2,1)}, bf16[128,1024]{0,1:T(8,128)(2,1)}, u32[]{:S(2)}, u32[]{:S(2)}) collective-permute-start(bf16[128,1024]{0,1:T(8,128)(2,1)} %bitcast.35), channel_id=1, source_target_pairs={{0,0},{1,4},{2,8},{3,12},{4,16},{5,20},{6,24},{7,28},{8,1},{9,5},{... | collective-permute-start | bytes 786440 | tf_op jit(solution)/shard_map/ppermute | solution.py:95
  35.9 1.3 fusion
  37.2 8.4 %collective-permute-done.8 = bf16[128,1024]{0,1:T(8,128)(2,1)} collective-permute-done((bf16[128,1024]{0,1:T(8,128)(2,1)}, bf16[128,1024]{0,1:T(8,128)(2,1)}, u32[]{:S(2)}, u32[]{:S(2)}) %collective-permute-start.8) | collective-permute-done | bytes 262176 | tf_op jit(solution)/shard_map/ppermute | solution.py:95
  47.0 5.5 %fusion.26 = f32[1,512,262]{1,0,2:T(1,128)S(1)} fusion(f32[512,1,128]{0,1,2:T(1,128)S(1)} %copy-done.16, f32[1,512,389]{1,2,0:T(8,128)S(1)} %get-tuple-element.33), kind=kOutput, calls=%fused_computation.59 | convolution fusion | flops 206045184 | bytes 1595392 | tf_op jit(solution)/shard_map/conv_general_dilated | solution.py:36
  54.1 1.7 %collective-permute-start.4 = (bf16[512,256]{0,1:T(8,128)(2,1)S(1)}, bf16[512,256]{0,1:T(8,128)(2,1)S(1)}, u32[]{:S(2)}, u32[]{:S(2)}) collective-permute-start(bf16[512,256]{0,1:T(8,128)(2,1)S(1)} %fusion.32), channel_id=1, source_target_pairs={{0,24},{8,16},{16,8},{24,0},{1,25},{9,17},{17,9},{25,1},{2,26},{10... | collective-permute-start | bytes 786440 | tf_op jit(solution)/shard_map/ppermute | solution.py:72
  57.2 8.6 %collective-permute-done.2 = bf16[512,256]{0,1:T(8,128)(2,1)S(1)} collective-permute-done((bf16[512,256]{0,1:T(8,128)(2,1)S(1)}, bf16[512,256]{0,1:T(8,128)(2,1)S(1)}, u32[]{:S(2)}, u32[]{:S(2)}) %collective-permute-start.2) | collective-permute-done | bytes 262176 | tf_op jit(solution)/shard_map/ppermute | solution.py:72
  66.3 2.7 %collective-permute-done.3 = bf16[512,256]{0,1:T(8,128)(2,1)S(1)} collective-permute-done((bf16[512,256]{0,1:T(8,128)(2,1)S(1)}, bf16[512,256]{0,1:T(8,128)(2,1)S(1)}, u32[]{:S(2)}, u32[]{:S(2)}) %collective-permute-start.3) | collective-permute-done | bytes 262176 | tf_op jit(solution)/shard_map/ppermute | solution.py:72
  70.1 1.5 %pad_maximum_fusion = bf16[4096,256]{0,1:T(8,128)(2,1)} fusion(bf16[1024,256]{0,1:T(8,128)(2,1)S(1)} %fusion.16, bf16[1024,256]{0,1:T(8,128)(2,1)S(1)} %fusion.15, bf16[1024,256]{0,1:T(8,128)(2,1)S(1)} %fusion.14, bf16[1024,256]{0,1:T(8,128)(2,1)S(1)} %fusion.13), kind=kLoop, calls=%fused_computation.1 | loop fusion | flops 8388608 | bytes 4194304 | tf_op jit(solution)/shard_map/concatenate | solution.py:129
  71.7 5.3 %all-gather.2.cloned.1.call-done = bf16[1024,1024]{0,1:T(8,128)(2,1)} async-done(((bf16[128,1024]{0,1:T(8,128)(2,1)}), bf16[1024,1024]{0,1:T(8,128)(2,1)}) %all-gather.2.cloned.1.call-update) | async-done | bytes 2097168 | tf_op jit(solution)/shard_map/all_gather | solution.py:96
  77.0 3.0 %fusion.62 = f32[1024,512]{1,0:T(8,128)S(1)} fusion(bf16[1024,1024]{0,1:T(8,128)(2,1)} %all-gather.2.cloned.1.call-done, bf16[512,1024]{1,0:T(8,128)(2,1)S(1)} %copy-done), kind=kOutput, calls=%fused_computation.143 | convolution fusion | flops 1073741824 | bytes 5242880 | tf_op jit(solution)/shard_map/dot_general | solution.py:140
  80.5 2.1 %collective-permute-start.11 = (bf16[512,256]{0,1:T(8,128)(2,1)S(1)}, bf16[512,256]{0,1:T(8,128)(2,1)S(1)}, u32[]{:S(2)}, u32[]{:S(2)}) collective-permute-start(bf16[512,256]{0,1:T(8,128)(2,1)S(1)} %get-tuple-element.29), channel_id=1, source_target_pairs={{0,24},{8,16},{16,8},{24,0},{1,25},{9,17},{17,9},{25,1},{2,26},{10... | collective-permute-start | bytes 786440 | tf_op jit(solution)/shard_map/ppermute | solution.py:72
  84.8 3.2 %collective-permute-done.9 = bf16[512,256]{0,1:T(8,128)(2,1)S(1)} collective-permute-done((bf16[512,256]{0,1:T(8,128)(2,1)S(1)}, bf16[512,256]{0,1:T(8,128)(2,1)S(1)}, u32[]{:S(2)}, u32[]{:S(2)}) %collective-permute-start.9) | collective-permute-done | bytes 262176 | tf_op jit(solution)/shard_map/ppermute | solution.py:72
  87.9 6.5 %collective-permute-done.11 = bf16[512,256]{0,1:T(8,128)(2,1)S(1)} collective-permute-done((bf16[512,256]{0,1:T(8,128)(2,1)S(1)}, bf16[512,256]{0,1:T(8,128)(2,1)S(1)}, u32[]{:S(2)}, u32[]{:S(2)}) %collective-permute-start.11) | collective-permute-done | bytes 262176 | tf_op jit(solution)/shard_map/ppermute | solution.py:72
  95.5 2.3 %collective-permute-start.12 = (bf16[512,133]{0,1:T(8,128)(2,1)S(1)}, bf16[512,133]{0,1:T(8,128)(2,1)S(1)}, u32[]{:S(2)}, u32[]{:S(2)}) collective-permute-start(bf16[512,133]{0,1:T(8,128)(2,1)S(1)} %slice.461), channel_id=1, source_target_pairs={{8,0},{16,8},{24,16},{9,1},{17,9},{25,17},{10,2},{18,10},{26,18},{... | collective-permute-start | bytes 408584 | tf_op jit(solution)/shard_map/ppermute | solution.py:32
  97.9 1.9 %add_convert_fusion = bf16[512,1024]{1,0:T(8,128)(2,1)} fusion(f32[512,1024]{1,0:T(8,128)S(1)} %fusion.36, f32[512,1024]{1,0:T(8,128)S(1)} %fusion.38, f32[512,1024]{1,0:T(8,128)S(1)} %fusion.40, bf16[512,256]{0,1:T(8,128)(2,1)S(1)} %collective-permute-done.4, bf16[1024,1024]{0,1:T(8,128)(2,1)S(1)} %copy-done.6, s32[]{:T(128)S(6)} %select_n.112), kind=kOutput, calls=%fused_computation.2 | convolution fusion | flops 274726912 | bytes 8126468 | tf_op jit(solution)/shard_map/dot_general | solution.py:157
  99.8 2.4 %collective-permute-done.12 = bf16[512,133]{0,1:T(8,128)(2,1)S(1)} collective-permute-done((bf16[512,133]{0,1:T(8,128)(2,1)S(1)}, bf16[512,133]{0,1:T(8,128)(2,1)S(1)}, u32[]{:S(2)}, u32[]{:S(2)}) %collective-permute-start.12) | collective-permute-done | bytes 136224 | tf_op jit(solution)/shard_map/ppermute | solution.py:32
  103.3 5.5 %fusion.24 = f32[1,512,262]{1,0,2:T(1,128)S(1)} fusion(f32[512,1,128]{0,1,2:T(1,128)S(1)} %copy-done.15, f32[1,512,389]{1,2,0:T(8,128)S(1)} %bitcast.123), kind=kOutput, calls=%fused_computation.57 | convolution fusion | flops 206045184 | bytes 1595392 | tf_op jit(solution)/shard_map/conv_general_dilated | solution.py:36
  109.8 1.3 fusion.7
  111.1 3.3 %reduce-scatter.2.cloned.1.call-done = bf16[512,256]{0,1:T(8,128)(2,1)} async-done(((bf16[4096,256]{0,1:T(8,128)(2,1)}), bf16[512,256]{0,1:T(8,128)(2,1)}) %reduce-scatter.2.cloned.1.call-update) | async-done | bytes 262160 | tf_op jit(solution)/shard_map/reduce_scatter | solution.py:130
  114.4 2.3 %collective-permute-start.13 = (bf16[512,256]{0,1:T(8,128)(2,1)}, bf16[512,256]{0,1:T(8,128)(2,1)S(1)}, u32[]{:S(2)}, u32[]{:S(2)}) collective-permute-start(bf16[512,256]{0,1:T(8,128)(2,1)} %reduce-scatter.2.cloned.1.call-done), channel_id=1, source_target_pairs={{0,0},{1,1},{2,8},{3,9},{4,16},{5,17},{6,24},{7,25},{8,10},{9,11},... | collective-permute-start | bytes 786440 | tf_op jit(solution)/shard_map/ppermute | solution.py:178
  117.9 19.0 %collective-permute-done.13 = bf16[512,256]{0,1:T(8,128)(2,1)S(1)} collective-permute-done((bf16[512,256]{0,1:T(8,128)(2,1)}, bf16[512,256]{0,1:T(8,128)(2,1)S(1)}, u32[]{:S(2)}, u32[]{:S(2)}) %collective-permute-start.13) | collective-permute-done | bytes 262176 | tf_op jit(solution)/shard_map/ppermute | solution.py:178
  (171 shorter events, 32.0 us)
Async XLA Ops:
  7.2 49.6 %copy-start = (bf16[512,1024]{1,0:T(8,128)(2,1)S(1)}, bf16[512,1024]{1,0:T(8,128)(2,1)}, u32[]{:S(2)}) copy-start(bf16[512,1024]{1,0:T(8,128)(2,1)} %param.10) | copy-start | bytes 3145732
  7.2 69.8 %all-gather.2.cloned.1.call-start = ((), (), s32[]{:S(2)}) async-start(), calls=%async_computation.2 | async-start | bytes 2359296 | tf_op jit(solution)/shard_map/all_gather | solution.py:96
  9.0 21.4 %collective-permute-start.7 = (bf16[128,256]{1,0:T(8,128)(2,1)}, bf16[128,256]{1,0:T(8,128)(2,1)}, u32[]{:S(2)}, u32[]{:S(2)}) collective-permute-start(bf16[128,256]{1,0:T(8,128)(2,1)} %get-tuple-element.48), channel_id=1, source_target_pairs={{0,24},{8,16},{16,8},{24,0},{1,25},{9,17},{17,9},{25,1},{2,26},{10... | collective-permute-start | bytes 196616 | tf_op jit(solution)/shard_map/ppermute | solution.py:72
  10.2 20.2 %collective-permute-start.6 = (bf16[128,256]{1,0:T(8,128)(2,1)}, bf16[128,256]{1,0:T(8,128)(2,1)}, u32[]{:S(2)}, u32[]{:S(2)}) collective-permute-start(bf16[128,256]{1,0:T(8,128)(2,1)} %get-tuple-element.49), channel_id=1, source_target_pairs={{0,16},{8,24},{16,0},{24,8},{1,17},{9,25},{17,1},{25,9},{2,18},{10... | collective-permute-start | bytes 196616 | tf_op jit(solution)/shard_map/ppermute | solution.py:72
  10.4 20.0 %collective-permute-start.5 = (bf16[128,256]{1,0:T(8,128)(2,1)S(1)}, bf16[128,256]{1,0:T(8,128)(2,1)}, u32[]{:S(2)}, u32[]{:S(2)}) collective-permute-start(bf16[128,256]{1,0:T(8,128)(2,1)S(1)} %get-tuple-element.50), channel_id=1, source_target_pairs={{0,8},{8,0},{16,24},{24,16},{1,9},{9,1},{17,25},{25,17},{2,10},{10... | collective-permute-start | bytes 196616 | tf_op jit(solution)/shard_map/ppermute | solution.py:72
  13.1 8.4 %copy-start.17 = (f32[3,512,7]{1,2,0:T(8,128)S(1)}, f32[3,512,7]{1,2,0:T(8,128)}, u32[]{:S(2)}) copy-start(f32[3,512,7]{1,2,0:T(8,128)} %param.7) | copy-start | bytes 129028
  14.1 20.8 %collective-permute-start.1 = (bf16[512,145]{0,1:T(8,128)(2,1)}, bf16[512,145]{0,1:T(8,128)(2,1)S(1)}, u32[]{:S(2)}, u32[]{:S(2)}) collective-permute-start(bf16[512,145]{0,1:T(8,128)(2,1)} %pad_maximum_fusion.5), channel_id=1, source_target_pairs={{8,0},{16,8},{24,16},{9,1},{17,9},{25,17},{10,2},{18,10},{26,18},{... | collective-permute-start | bytes 445448 | tf_op jit(solution)/shard_map/ppermute | solution.py:20
  16.3 6.5 %slice-start.1 = ((f32[3,512,7]{1,2,0:T(8,128)}), f32[1,512,7]{1,2,0:T(8,128)S(1)}, s32[]{:S(2)}) async-start(f32[3,512,7]{1,2,0:T(8,128)} %param.7), calls=%async_computation.4 | async-start | bytes 32768 | tf_op jit(solution)/shard_map/slice | solution.py:116
  16.4 8.4 %copy-start.12 = (f32[512,128]{1,0:T(8,128)S(1)}, f32[512,128]{1,0:T(8,128)}, u32[]{:S(2)}) copy-start(f32[512,128]{1,0:T(8,128)} %param.8) | copy-start | bytes 786436
  17.4 17.5 %collective-permute-start = (bf16[512,272]{0,1:T(8,128)(2,1)}, bf16[512,272]{0,1:T(8,128)(2,1)S(1)}, u32[]{:S(2)}, u32[]{:S(2)}) collective-permute-start(bf16[512,272]{0,1:T(8,128)(2,1)} %pad_maximum_fusion.3), channel_id=1, source_target_pairs={{0,8},{8,16},{16,24},{1,9},{9,17},{17,25},{2,10},{10,18},{18,26},{... | collective-permute-start | bytes 835592 | tf_op jit(solution)/shard_map/ppermute | solution.py:19
  22.9 5.7 %copy-start.38 = (f32[2,512,1]{1,2,0:T(1,128)S(1)}, f32[2,512,1]{1,2,0:T(1,128)}, u32[]{:S(2)}) copy-start(f32[2,512,1]{1,2,0:T(1,128)} %get-tuple-element.63) | copy-start | bytes 12292
  33.0 12.6 %collective-permute-start.8 = (bf16[128,1024]{0,1:T(8,128)(2,1)}, bf16[128,1024]{0,1:T(8,128)(2,1)}, u32[]{:S(2)}, u32[]{:S(2)}) collective-permute-start(bf16[128,1024]{0,1:T(8,128)(2,1)} %bitcast.35), channel_id=1, source_target_pairs={{0,0},{1,4},{2,8},{3,12},{4,16},{5,20},{6,24},{7,28},{8,1},{9,5},{... | collective-permute-start | bytes 786440 | tf_op jit(solution)/shard_map/ppermute | solution.py:95
  45.6 68.9 %reduce-scatter.2.cloned.1.call-start = ((), (), s32[]{:S(2)}) async-start(), calls=%async_computation.1 | async-start | bytes 2359296 | tf_op jit(solution)/shard_map/reduce_scatter | solution.py:130
  46.1 6.6 %copy-start.2 = (f32[512,389]{0,1:T(8,128)}, f32[512,389]{0,1:T(8,128)S(1)}, u32[]{:S(2)}) copy-start(f32[512,389]{0,1:T(8,128)S(1)} %get-tuple-element.32) | copy-start | bytes 2390020
  54.1 12.3 %copy-start.4 = (bf16[512,256]{0,1:T(8,128)(2,1)}, bf16[512,256]{0,1:T(8,128)(2,1)S(1)}, u32[]{:S(2)}) copy-start(bf16[512,256]{0,1:T(8,128)(2,1)S(1)} %fusion.32) | copy-start | bytes 786436
  54.1 15.4 %collective-permute-start.4 = (bf16[512,256]{0,1:T(8,128)(2,1)S(1)}, bf16[512,256]{0,1:T(8,128)(2,1)S(1)}, u32[]{:S(2)}, u32[]{:S(2)}) collective-permute-start(bf16[512,256]{0,1:T(8,128)(2,1)S(1)} %fusion.32), channel_id=1, source_target_pairs={{0,24},{8,16},{16,8},{24,0},{1,25},{9,17},{17,9},{25,1},{2,26},{10... | collective-permute-start | bytes 786440 | tf_op jit(solution)/shard_map/ppermute | solution.py:72
  55.8 13.2 %collective-permute-start.3 = (bf16[512,256]{0,1:T(8,128)(2,1)S(1)}, bf16[512,256]{0,1:T(8,128)(2,1)S(1)}, u32[]{:S(2)}, u32[]{:S(2)}) collective-permute-start(bf16[512,256]{0,1:T(8,128)(2,1)S(1)} %fusion.32), channel_id=1, source_target_pairs={{0,16},{8,24},{16,0},{24,8},{1,17},{9,25},{17,1},{25,9},{2,18},{10... | collective-permute-start | bytes 786440 | tf_op jit(solution)/shard_map/ppermute | solution.py:72
  55.8 10.1 %collective-permute-start.2 = (bf16[512,256]{0,1:T(8,128)(2,1)S(1)}, bf16[512,256]{0,1:T(8,128)(2,1)S(1)}, u32[]{:S(2)}, u32[]{:S(2)}) collective-permute-start(bf16[512,256]{0,1:T(8,128)(2,1)S(1)} %fusion.32), channel_id=1, source_target_pairs={{0,8},{8,0},{16,24},{24,16},{1,9},{9,1},{17,25},{25,17},{2,10},{10... | collective-permute-start | bytes 786440 | tf_op jit(solution)/shard_map/ppermute | solution.py:72
  77.0 5.9 %copy-start.6 = (bf16[1024,1024]{0,1:T(8,128)(2,1)S(1)}, bf16[1024,1024]{0,1:T(8,128)(2,1)}, u32[]{:S(2)}) copy-start(bf16[1024,1024]{0,1:T(8,128)(2,1)} %all-gather.2.cloned.1.call-done) | copy-start | bytes 6291460
  80.2 7.8 %collective-permute-start.9 = (bf16[512,256]{0,1:T(8,128)(2,1)S(1)}, bf16[512,256]{0,1:T(8,128)(2,1)S(1)}, u32[]{:S(2)}, u32[]{:S(2)}) collective-permute-start(bf16[512,256]{0,1:T(8,128)(2,1)S(1)} %get-tuple-element.28), channel_id=1, source_target_pairs={{0,8},{8,0},{16,24},{24,16},{1,9},{9,1},{17,25},{25,17},{2,10},{10... | collective-permute-start | bytes 786440 | tf_op jit(solution)/shard_map/ppermute | solution.py:72
  80.5 13.8 %collective-permute-start.11 = (bf16[512,256]{0,1:T(8,128)(2,1)S(1)}, bf16[512,256]{0,1:T(8,128)(2,1)S(1)}, u32[]{:S(2)}, u32[]{:S(2)}) collective-permute-start(bf16[512,256]{0,1:T(8,128)(2,1)S(1)} %get-tuple-element.29), channel_id=1, source_target_pairs={{0,24},{8,16},{16,8},{24,0},{1,25},{9,17},{17,9},{25,1},{2,26},{10... | collective-permute-start | bytes 786440 | tf_op jit(solution)/shard_map/ppermute | solution.py:72
  82.6 12.8 %collective-permute-start.10 = (bf16[512,256]{0,1:T(8,128)(2,1)S(1)}, bf16[512,256]{0,1:T(8,128)(2,1)S(1)}, u32[]{:S(2)}, u32[]{:S(2)}) collective-permute-start(bf16[512,256]{0,1:T(8,128)(2,1)S(1)} %get-tuple-element.30), channel_id=1, source_target_pairs={{0,16},{8,24},{16,0},{24,8},{1,17},{9,25},{17,1},{25,9},{2,18},{10... | collective-permute-start | bytes 786440 | tf_op jit(solution)/shard_map/ppermute | solution.py:72
  95.5 6.7 %collective-permute-start.12 = (bf16[512,133]{0,1:T(8,128)(2,1)S(1)}, bf16[512,133]{0,1:T(8,128)(2,1)S(1)}, u32[]{:S(2)}, u32[]{:S(2)}) collective-permute-start(bf16[512,133]{0,1:T(8,128)(2,1)S(1)} %slice.461), channel_id=1, source_target_pairs={{8,0},{16,8},{24,16},{9,1},{17,9},{25,17},{10,2},{18,10},{26,18},{... | collective-permute-start | bytes 408584 | tf_op jit(solution)/shard_map/ppermute | solution.py:32
  114.4 22.4 %collective-permute-start.13 = (bf16[512,256]{0,1:T(8,128)(2,1)}, bf16[512,256]{0,1:T(8,128)(2,1)S(1)}, u32[]{:S(2)}, u32[]{:S(2)}) collective-permute-start(bf16[512,256]{0,1:T(8,128)(2,1)} %reduce-scatter.2.cloned.1.call-done), channel_id=1, source_target_pairs={{0,0},{1,1},{2,8},{3,9},{4,16},{5,17},{6,24},{7,25},{8,10},{9,11},... | collective-permute-start | bytes 786440 | tf_op jit(solution)/shard_map/ppermute | solution.py:178
  (37 other events, 81.3 us)
Sparse Core Ops, SparseCore 0:
  45.7 31.2 all-gather.1
  79.3 35.1 reduce-scatter.1

commit v9 on v8

--- a/solution.py
+++ b/solution.py
@@ -86,7 +86,10 @@
             jnp.arange(n_seq) == source(me, step, n_seq), step, 0
         ).astype(jnp.int32)
     mine = jnp.take(stacked, index, axis=0)
-    mine = jnp.transpose(mine, (1, 0, 2)).reshape(piece, n_seq * length)
+    return jnp.transpose(mine, (1, 0, 2)).reshape(piece, n_seq * length)
+
+
+def rows_gathered(mine, n_seq, n_tp):
     route = []
     for a in range(n_seq):
         for b in range(n_tp):
@@ -107,8 +110,10 @@
     reach = taps_long + taps_short - 2
     keep = length + taps_short - 1
 
+    slab_piece = rows_of_slab(out_grad, n_seq, n_tp)
+    streams, slab_piece = lax.optimization_barrier((streams, slab_piece))
     query_in, key_value_in = halo(streams, "seq", reach, taps_short - 1)
-    slab_grad = rows_of_slab(out_grad, n_seq, n_tp)
+    slab_grad = rows_gathered(slab_piece, n_seq, n_tp)
     slab_width = slab_grad.shape[0]
 
     key_value = short_correlate(key_value_in.astype(jnp.float32), feat_weight[1:, :, ::-1])

time: 145 us -> 135 us (0.931)
  waiting for transfers between devices: 60.4 us -> 51.3 us
  starting transfers between devices: 21 us -> 26.5 us
  local copies, waits for them, and re-layouts: 19.7 us -> 15 us
  other arithmetic: 9.5 us -> 7.22 us
    ppermute x1, waiting for transfers between devices: 8.39 us -> 0.01 us  [rows_gathered(): moved = lax.ppermute(mine, ('seq', 'tp'), route)]
    ppermute x1, waiting for transfers between devices: 0.01 us -> 7.26 us  [halo(): high = lax.ppermute(high, axis, backward)]
    unnamed x105 -> x46, local copies, waits for them, and re-layouts: 10 us -> 3.36 us
    all_gather x1, waiting for transfers between devices: 5.31 us -> 0.02 us  [rows_gathered(): return lax.all_gather(moved, 'tp', axis=0, tiled=True)]
    ppermute x9, starting transfers between devices: 8.07 us -> 11.8 us  [exchange(): got.append(lax.ppermute(block_of(step), axis, route))]
    ppermute x1, starting transfers between devices: 2.15 us -> 4.49 us  [halo(): high = lax.ppermute(high, axis, backward)]
    ppermute x1, starting transfers between devices: 4.01 us -> 2.04 us  [halo(): low = lax.ppermute(low, axis, forward)]
    ppermute x9, waiting for transfers between devices: 21.9 us -> 20 us  [exchange(): got.append(lax.ppermute(block_of(step), axis, route))]
  transfers between devices with their start and end apart: 16 -> 16, of which waited for: 10 -> 8; matrix products, arithmetic and copies ran while one was open for 30% -> 27% of each run, Pallas kernels for 0% -> 0%
where the time goes in v9:
time: 135 us; the launch traced here: 134 us
  waiting for transfers between devices  51.3 us (38%)
  starting transfers between devices  26.5 us (20%)
  matrix products  19.1 us (14%)
  local copies, waits for them, and re-layouts  15 us (11%)
  between operations  14.7 us (11%)
  other arithmetic  7.22 us (5%)
    ppermute x9, waiting for transfers between devices, exchange(): got.append(lax.ppermute(block_of(step), axis, route))  20 us
    ppermute x1, waiting for transfers between devices, shards(): mixed = lax.ppermute(output_sum, ('seq', 'tp'), mixed_route)  18.4 us
    ppermute x9, starting transfers between devices, exchange(): got.append(lax.ppermute(block_of(step), axis, route))  11.8 us
    conv_general_dilated x2, matrix products, correlate(): lax.conv_general_dilated(signal[None], taps[:, None, :], (1,), 'VALID', d...  11 us
    ppermute x1, waiting for transfers between devices, halo(): high = lax.ppermute(high, axis, backward)  7.26 us
    ppermute x1, starting transfers between devices, halo(): high = lax.ppermute(high, axis, backward)  4.49 us
    reduce_scatter x1, waiting for transfers between devices, shards(): lax.psum_scatter(partial_out, 'tp', scatter_dimension=0, tiled=True)  3.69 us
    unnamed x46, local copies, waits for them, and re-layouts  3.36 us
  transfers between devices with their start and end apart: 16, of which 8 were waited for; matrix products, arithmetic and copies ran while one was open for 27% of the time, Pallas kernels for 0%

profile of v9, /device:TPU:27, one launch (start us, length us, event | category | flops | bytes accessed | tf_op | source)
XLA Modules:
  0.0 133.7 jit_solution(6931142709970769024)
XLA Ops:
  8.3 1.3 collective-permute-start.2
  14.3 1.9 %rev.8 = f32[512,128]{1,0:T(8,128)S(1)} reverse(f32[512,128]{1,0:T(8,128)} %param.8), dimensions={1} | reverse | bytes 524288 | tf_op jit(solution)/shard_map/rev | solution.py:123
  16.2 1.9 %copy.52 = f32[512,1,128]{0,1,2:T(1,128)} copy(f32[512,1,128]{2,0,1:T(8,128)} %bitcast.133) | data formatting | bytes 524288 | tf_op jit(solution)/shard_map/broadcast_in_dim | solution.py:38
  21.0 3.0 %collective-permute-start.8 = (bf16[128,1024]{0,1:T(8,128)(2,1)}, bf16[128,1024]{0,1:T(8,128)(2,1)}, u32[]{:S(2)}, u32[]{:S(2)}) collective-permute-start(bf16[128,1024]{0,1:T(8,128)(2,1)} %bitcast.11), channel_id=1, source_target_pairs={{0,0},{1,4},{2,8},{3,12},{4,16},{5,20},{6,24},{7,28},{8,1},{9,5},{... | collective-permute-start | bytes 786440 | tf_op jit(solution)/shard_map/ppermute | solution.py:98
  24.1 4.5 %collective-permute-start.4 = (bf16[512,145]{0,1:T(8,128)(2,1)S(1)}, bf16[512,145]{0,1:T(8,128)(2,1)S(1)}, u32[]{:S(2)}, u32[]{:S(2)}) collective-permute-start(bf16[512,145]{0,1:T(8,128)(2,1)S(1)} %pad_maximum_fusion.5), channel_id=1, source_target_pairs={{8,0},{16,8},{24,16},{9,1},{17,9},{25,17},{10,2},{18,10},{26,18},{... | collective-permute-start | bytes 445448 | tf_op jit(solution)/shard_map/ppermute | solution.py:20
  28.6 2.0 %collective-permute-start.3 = (bf16[512,272]{0,1:T(8,128)(2,1)S(1)}, bf16[512,272]{0,1:T(8,128)(2,1)S(1)}, u32[]{:S(2)}, u32[]{:S(2)}) collective-permute-start(bf16[512,272]{0,1:T(8,128)(2,1)S(1)} %pad_maximum_fusion.3), channel_id=1, source_target_pairs={{0,8},{8,16},{16,24},{1,9},{9,17},{17,25},{2,10},{10,18},{18,26},{... | collective-permute-start | bytes 835592 | tf_op jit(solution)/shard_map/ppermute | solution.py:19
  30.7 7.3 %collective-permute-done.4 = bf16[512,145]{0,1:T(8,128)(2,1)S(1)} collective-permute-done((bf16[512,145]{0,1:T(8,128)(2,1)S(1)}, bf16[512,145]{0,1:T(8,128)(2,1)S(1)}, u32[]{:S(2)}, u32[]{:S(2)}) %collective-permute-start.4) | collective-permute-done | bytes 148512 | tf_op jit(solution)/shard_map/ppermute | solution.py:20
  38.6 1.3 fusion
  41.1 5.5 %fusion.26 = f32[1,512,262]{1,0,2:T(1,128)S(1)} fusion(f32[512,1,128]{0,1,2:T(1,128)S(1)} %copy-done.13, f32[1,512,389]{1,2,0:T(8,128)S(1)} %get-tuple-element.37), kind=kOutput, calls=%fused_computation.59 | convolution fusion | flops 206045184 | bytes 1595392 | tf_op jit(solution)/shard_map/conv_general_dilated | solution.py:36
  47.6 4.5 %collective-permute-start.7 = (bf16[512,256]{0,1:T(8,128)(2,1)S(1)}, bf16[512,256]{0,1:T(8,128)(2,1)S(1)}, u32[]{:S(2)}, u32[]{:S(2)}) collective-permute-start(bf16[512,256]{0,1:T(8,128)(2,1)S(1)} %fusion.32), channel_id=1, source_target_pairs={{0,24},{8,16},{16,8},{24,0},{1,25},{9,17},{17,9},{25,1},{2,26},{10... | collective-permute-start | bytes 786440 | tf_op jit(solution)/shard_map/ppermute | solution.py:72
  54.5 11.7 %collective-permute-done.5 = bf16[512,256]{0,1:T(8,128)(2,1)S(1)} collective-permute-done((bf16[512,256]{0,1:T(8,128)(2,1)S(1)}, bf16[512,256]{0,1:T(8,128)(2,1)S(1)}, u32[]{:S(2)}, u32[]{:S(2)}) %collective-permute-start.5) | collective-permute-done | bytes 262176 | tf_op jit(solution)/shard_map/ppermute | solution.py:72
  68.5 1.5 %pad_maximum_fusion = bf16[4096,256]{0,1:T(8,128)(2,1)} fusion(bf16[1024,256]{0,1:T(8,128)(2,1)S(1)} %fusion.16, bf16[1024,256]{0,1:T(8,128)(2,1)S(1)} %fusion.15, bf16[1024,256]{0,1:T(8,128)(2,1)S(1)} %fusion.14, bf16[1024,256]{0,1:T(8,128)(2,1)S(1)} %fusion.13), kind=kLoop, calls=%fused_computation.1 | loop fusion | flops 8388608 | bytes 4194304 | tf_op jit(solution)/shard_map/concatenate | solution.py:134
  70.1 3.0 %fusion.59 = f32[1024,512]{1,0:T(8,128)S(1)} fusion(bf16[1024,1024]{0,1:T(8,128)(2,1)} %all-gather.2.cloned.1.call-done, bf16[512,1024]{1,0:T(8,128)(2,1)S(1)} %copy-done), kind=kOutput, calls=%fused_computation.149 | convolution fusion | flops 1073741824 | bytes 5242880 | tf_op jit(solution)/shard_map/dot_general | solution.py:145
  74.3 1.6 %collective-permute-start.10 = (bf16[512,256]{0,1:T(8,128)(2,1)S(1)}, bf16[512,256]{0,1:T(8,128)(2,1)S(1)}, u32[]{:S(2)}, u32[]{:S(2)}) collective-permute-start(bf16[512,256]{0,1:T(8,128)(2,1)S(1)} %get-tuple-element.34), channel_id=1, source_target_pairs={{0,16},{8,24},{16,0},{24,8},{1,17},{9,25},{17,1},{25,9},{2,18},{10... | collective-permute-start | bytes 786440 | tf_op jit(solution)/shard_map/ppermute | solution.py:72
  77.4 3.1 %collective-permute-done.9 = bf16[512,256]{0,1:T(8,128)(2,1)S(1)} collective-permute-done((bf16[512,256]{0,1:T(8,128)(2,1)S(1)}, bf16[512,256]{0,1:T(8,128)(2,1)S(1)}, u32[]{:S(2)}, u32[]{:S(2)}) %collective-permute-start.9) | collective-permute-done | bytes 262176 | tf_op jit(solution)/shard_map/ppermute | solution.py:72
  80.5 5.2 %collective-permute-done.11 = bf16[512,256]{0,1:T(8,128)(2,1)S(1)} collective-permute-done((bf16[512,256]{0,1:T(8,128)(2,1)S(1)}, bf16[512,256]{0,1:T(8,128)(2,1)S(1)}, u32[]{:S(2)}, u32[]{:S(2)}) %collective-permute-start.11) | collective-permute-done | bytes 262176 | tf_op jit(solution)/shard_map/ppermute | solution.py:72
  85.8 3.1 %collective-permute-start.12 = (bf16[512,133]{0,1:T(8,128)(2,1)S(1)}, bf16[512,133]{0,1:T(8,128)(2,1)S(1)}, u32[]{:S(2)}, u32[]{:S(2)}) collective-permute-start(bf16[512,133]{0,1:T(8,128)(2,1)S(1)} %slice.479), channel_id=1, source_target_pairs={{8,0},{16,8},{24,16},{9,1},{17,9},{25,17},{10,2},{18,10},{26,18},{... | collective-permute-start | bytes 408584 | tf_op jit(solution)/shard_map/ppermute | solution.py:32
  88.9 1.9 %add_convert_fusion = bf16[512,1024]{1,0:T(8,128)(2,1)} fusion(f32[512,1024]{1,0:T(8,128)S(1)} %fusion.36, f32[512,1024]{1,0:T(8,128)S(1)} %fusion.38, f32[512,1024]{1,0:T(8,128)S(1)} %fusion.40, bf16[512,256]{0,1:T(8,128)(2,1)S(1)} %copy-done.5, bf16[1024,1024]{0,1:T(8,128)(2,1)S(1)} %copy-done.3, s32[]{:T(128)S(6)} %select_n.112), kind=kOutput, calls=%fused_computation.2 | convolution fusion | flops 274726912 | bytes 8126468 | tf_op jit(solution)/shard_map/dot_general | solution.py:162
  90.8 1.7 %collective-permute-done.12 = bf16[512,133]{0,1:T(8,128)(2,1)S(1)} collective-permute-done((bf16[512,133]{0,1:T(8,128)(2,1)S(1)}, bf16[512,133]{0,1:T(8,128)(2,1)S(1)}, u32[]{:S(2)}, u32[]{:S(2)}) %collective-permute-start.12) | collective-permute-done | bytes 136224 | tf_op jit(solution)/shard_map/ppermute | solution.py:32
  93.6 5.5 %fusion.24 = f32[1,512,262]{1,0,2:T(1,128)S(1)} fusion(f32[512,1,128]{0,1,2:T(1,128)S(1)} %copy-done.12, f32[1,512,389]{1,2,0:T(8,128)S(1)} %bitcast.132), kind=kOutput, calls=%fused_computation.57 | convolution fusion | flops 206045184 | bytes 1595392 | tf_op jit(solution)/shard_map/conv_general_dilated | solution.py:36
  99.5 1.3 fusion.7
  100.8 3.7 %reduce-scatter.2.cloned.1.call-done = bf16[512,256]{0,1:T(8,128)(2,1)} async-done(((bf16[4096,256]{0,1:T(8,128)(2,1)}), bf16[512,256]{0,1:T(8,128)(2,1)}) %reduce-scatter.2.cloned.1.call-update) | async-done | bytes 262160 | tf_op jit(solution)/shard_map/reduce_scatter | solution.py:135
  104.5 1.9 %collective-permute-start.13 = (bf16[512,256]{0,1:T(8,128)(2,1)}, bf16[512,256]{0,1:T(8,128)(2,1)S(1)}, u32[]{:S(2)}, u32[]{:S(2)}) collective-permute-start(bf16[512,256]{0,1:T(8,128)(2,1)} %reduce-scatter.2.cloned.1.call-done), channel_id=1, source_target_pairs={{0,0},{1,1},{2,8},{3,9},{4,16},{5,17},{6,24},{7,25},{8,10},{9,11},... | collective-permute-start | bytes 786440 | tf_op jit(solution)/shard_map/ppermute | solution.py:183
  107.6 18.4 %collective-permute-done.13 = bf16[512,256]{0,1:T(8,128)(2,1)S(1)} collective-permute-done((bf16[512,256]{0,1:T(8,128)(2,1)}, bf16[512,256]{0,1:T(8,128)(2,1)S(1)}, u32[]{:S(2)}, u32[]{:S(2)}) %collective-permute-start.13) | collective-permute-done | bytes 262176 | tf_op jit(solution)/shard_map/ppermute | solution.py:183
  (112 shorter events, 22.2 us)
Async XLA Ops:
  7.2 46.9 %copy-start = (bf16[512,1024]{1,0:T(8,128)(2,1)S(1)}, bf16[512,1024]{1,0:T(8,128)(2,1)}, u32[]{:S(2)}) copy-start(bf16[512,1024]{1,0:T(8,128)(2,1)} %param.10) | copy-start | bytes 3145732
  7.2 62.9 %all-gather.2.cloned.1.call-start = ((), (), s32[]{:S(2)}) async-start(), calls=%async_computation.2 | async-start | bytes 2359296 | tf_op jit(solution)/shard_map/all_gather | solution.py:99
  8.3 10.7 %collective-permute-start.2 = (bf16[128,256]{1,0:T(8,128)(2,1)S(1)}, bf16[128,256]{1,0:T(8,128)(2,1)S(1)}, u32[]{:S(2)}, u32[]{:S(2)}) collective-permute-start(bf16[128,256]{1,0:T(8,128)(2,1)S(1)} %get-tuple-element.52), channel_id=1, source_target_pairs={{0,24},{8,16},{16,8},{24,0},{1,25},{9,17},{17,9},{25,1},{2,26},{10... | collective-permute-start | bytes 196616 | tf_op jit(solution)/shard_map/ppermute | solution.py:72
  9.6 9.5 %collective-permute-start.1 = (bf16[128,256]{1,0:T(8,128)(2,1)S(1)}, bf16[128,256]{1,0:T(8,128)(2,1)S(1)}, u32[]{:S(2)}, u32[]{:S(2)}) collective-permute-start(bf16[128,256]{1,0:T(8,128)(2,1)S(1)} %get-tuple-element.53), channel_id=1, source_target_pairs={{0,16},{8,24},{16,0},{24,8},{1,17},{9,25},{17,1},{25,9},{2,18},{10... | collective-permute-start | bytes 196616 | tf_op jit(solution)/shard_map/ppermute | solution.py:72
  9.8 9.3 %collective-permute-start = (bf16[128,256]{1,0:T(8,128)(2,1)S(1)}, bf16[128,256]{1,0:T(8,128)(2,1)S(1)}, u32[]{:S(2)}, u32[]{:S(2)}) collective-permute-start(bf16[128,256]{1,0:T(8,128)(2,1)S(1)} %get-tuple-element.54), channel_id=1, source_target_pairs={{0,8},{8,0},{16,24},{24,16},{1,9},{9,1},{17,25},{25,17},{2,10},{10... | collective-permute-start | bytes 196616 | tf_op jit(solution)/shard_map/ppermute | solution.py:72
  14.3 32.6 %copy-start.14 = (f32[512,1]{0,1:T(1,128)}, f32[512,1]{0,1:T(1,128)S(1)}, u32[]{:S(2)}) copy-start(f32[512,1]{0,1:T(1,128)S(1)} %get-tuple-element.77) | copy-start | bytes 6148
  21.0 17.0 %collective-permute-start.8 = (bf16[128,1024]{0,1:T(8,128)(2,1)}, bf16[128,1024]{0,1:T(8,128)(2,1)}, u32[]{:S(2)}, u32[]{:S(2)}) collective-permute-start(bf16[128,1024]{0,1:T(8,128)(2,1)} %bitcast.11), channel_id=1, source_target_pairs={{0,0},{1,4},{2,8},{3,12},{4,16},{5,20},{6,24},{7,28},{8,1},{9,5},{... | collective-permute-start | bytes 786440 | tf_op jit(solution)/shard_map/ppermute | solution.py:98
  24.1 13.9 %collective-permute-start.4 = (bf16[512,145]{0,1:T(8,128)(2,1)S(1)}, bf16[512,145]{0,1:T(8,128)(2,1)S(1)}, u32[]{:S(2)}, u32[]{:S(2)}) collective-permute-start(bf16[512,145]{0,1:T(8,128)(2,1)S(1)} %pad_maximum_fusion.5), channel_id=1, source_target_pairs={{8,0},{16,8},{24,16},{9,1},{17,9},{25,17},{10,2},{18,10},{26,18},{... | collective-permute-start | bytes 445448 | tf_op jit(solution)/shard_map/ppermute | solution.py:20
  28.6 9.7 %collective-permute-start.3 = (bf16[512,272]{0,1:T(8,128)(2,1)S(1)}, bf16[512,272]{0,1:T(8,128)(2,1)S(1)}, u32[]{:S(2)}, u32[]{:S(2)}) collective-permute-start(bf16[512,272]{0,1:T(8,128)(2,1)S(1)} %pad_maximum_fusion.3), channel_id=1, source_target_pairs={{0,8},{8,16},{16,24},{1,9},{9,17},{17,25},{2,10},{10,18},{18,26},{... | collective-permute-start | bytes 835592 | tf_op jit(solution)/shard_map/ppermute | solution.py:19
  38.0 66.5 %reduce-scatter.2.cloned.1.call-start = ((), (), s32[]{:S(2)}) async-start(), calls=%async_computation.1 | async-start | bytes 2359296 | tf_op jit(solution)/shard_map/reduce_scatter | solution.py:135
  40.2 6.4 %copy-start.1 = (f32[512,389]{0,1:T(8,128)}, f32[512,389]{0,1:T(8,128)S(1)}, u32[]{:S(2)}) copy-start(f32[512,389]{0,1:T(8,128)S(1)} %get-tuple-element.36) | copy-start | bytes 2390020
  41.1 5.5 %copy-start.16 = (f32[512]{0:T(512)S(1)}, f32[512]{0:T(512)}, u32[]{:S(2)}) copy-start(f32[512]{0:T(512)} %param.9) | copy-start | bytes 6148
  47.6 19.5 %collective-permute-start.7 = (bf16[512,256]{0,1:T(8,128)(2,1)S(1)}, bf16[512,256]{0,1:T(8,128)(2,1)S(1)}, u32[]{:S(2)}, u32[]{:S(2)}) collective-permute-start(bf16[512,256]{0,1:T(8,128)(2,1)S(1)} %fusion.32), channel_id=1, source_target_pairs={{0,24},{8,16},{16,8},{24,0},{1,25},{9,17},{17,9},{25,1},{2,26},{10... | collective-permute-start | bytes 786440 | tf_op jit(solution)/shard_map/ppermute | solution.py:72
  52.1 14.5 %collective-permute-start.6 = (bf16[512,256]{0,1:T(8,128)(2,1)S(1)}, bf16[512,256]{0,1:T(8,128)(2,1)S(1)}, u32[]{:S(2)}, u32[]{:S(2)}) collective-permute-start(bf16[512,256]{0,1:T(8,128)(2,1)S(1)} %fusion.32), channel_id=1, source_target_pairs={{0,16},{8,24},{16,0},{24,8},{1,17},{9,25},{17,1},{25,9},{2,18},{10... | collective-permute-start | bytes 786440 | tf_op jit(solution)/shard_map/ppermute | solution.py:72
  52.9 13.3 %collective-permute-start.5 = (bf16[512,256]{0,1:T(8,128)(2,1)S(1)}, bf16[512,256]{0,1:T(8,128)(2,1)S(1)}, u32[]{:S(2)}, u32[]{:S(2)}) collective-permute-start(bf16[512,256]{0,1:T(8,128)(2,1)S(1)} %fusion.32), channel_id=1, source_target_pairs={{0,8},{8,0},{16,24},{24,16},{1,9},{9,1},{17,25},{25,17},{2,10},{10... | collective-permute-start | bytes 786440 | tf_op jit(solution)/shard_map/ppermute | solution.py:72
  70.1 5.9 %copy-start.3 = (bf16[1024,1024]{0,1:T(8,128)(2,1)S(1)}, bf16[1024,1024]{0,1:T(8,128)(2,1)}, u32[]{:S(2)}) copy-start(bf16[1024,1024]{0,1:T(8,128)(2,1)} %all-gather.2.cloned.1.call-done) | copy-start | bytes 6291460
  73.2 7.2 %collective-permute-start.9 = (bf16[512,256]{0,1:T(8,128)(2,1)S(1)}, bf16[512,256]{0,1:T(8,128)(2,1)S(1)}, u32[]{:S(2)}, u32[]{:S(2)}) collective-permute-start(bf16[512,256]{0,1:T(8,128)(2,1)S(1)} %get-tuple-element.32), channel_id=1, source_target_pairs={{0,8},{8,0},{16,24},{24,16},{1,9},{9,1},{17,25},{25,17},{2,10},{10... | collective-permute-start | bytes 786440 | tf_op jit(solution)/shard_map/ppermute | solution.py:72
  73.3 12.3 %collective-permute-start.11 = (bf16[512,256]{0,1:T(8,128)(2,1)S(1)}, bf16[512,256]{0,1:T(8,128)(2,1)S(1)}, u32[]{:S(2)}, u32[]{:S(2)}) collective-permute-start(bf16[512,256]{0,1:T(8,128)(2,1)S(1)} %get-tuple-element.33), channel_id=1, source_target_pairs={{0,24},{8,16},{16,8},{24,0},{1,25},{9,17},{17,9},{25,1},{2,26},{10... | collective-permute-start | bytes 786440 | tf_op jit(solution)/shard_map/ppermute | solution.py:72
  74.3 11.3 %collective-permute-start.10 = (bf16[512,256]{0,1:T(8,128)(2,1)S(1)}, bf16[512,256]{0,1:T(8,128)(2,1)S(1)}, u32[]{:S(2)}, u32[]{:S(2)}) collective-permute-start(bf16[512,256]{0,1:T(8,128)(2,1)S(1)} %get-tuple-element.34), channel_id=1, source_target_pairs={{0,16},{8,24},{16,0},{24,8},{1,17},{9,25},{17,1},{25,9},{2,18},{10... | collective-permute-start | bytes 786440 | tf_op jit(solution)/shard_map/ppermute | solution.py:72
  77.4 11.5 %copy-start.5 = (bf16[512,256]{0,1:T(8,128)(2,1)S(1)}, bf16[512,256]{0,1:T(8,128)(2,1)}, u32[]{:S(2)}) copy-start(bf16[512,256]{0,1:T(8,128)(2,1)} %copy-done.4) | copy-start | bytes 786436
  85.8 6.7 %collective-permute-start.12 = (bf16[512,133]{0,1:T(8,128)(2,1)S(1)}, bf16[512,133]{0,1:T(8,128)(2,1)S(1)}, u32[]{:S(2)}, u32[]{:S(2)}) collective-permute-start(bf16[512,133]{0,1:T(8,128)(2,1)S(1)} %slice.479), channel_id=1, source_target_pairs={{8,0},{16,8},{24,16},{9,1},{17,9},{25,17},{10,2},{18,10},{26,18},{... | collective-permute-start | bytes 408584 | tf_op jit(solution)/shard_map/ppermute | solution.py:32
  93.6 5.5 %copy-start.2 = (f32[512,389]{0,1:T(8,128)S(1)}, f32[512,389]{0,1:T(8,128)}, u32[]{:S(2)}) copy-start(f32[512,389]{0,1:T(8,128)} %copy-done.1) | copy-start | bytes 2390020
  93.6 5.5 %copy-start.17 = (f32[512]{0:T(512)S(1)}, f32[512]{0:T(512)}, u32[]{:S(2)}) copy-start(f32[512]{0:T(512)} %param.9) | copy-start | bytes 6148
  104.5 21.5 %collective-permute-start.13 = (bf16[512,256]{0,1:T(8,128)(2,1)}, bf16[512,256]{0,1:T(8,128)(2,1)S(1)}, u32[]{:S(2)}, u32[]{:S(2)}) collective-permute-start(bf16[512,256]{0,1:T(8,128)(2,1)} %reduce-scatter.2.cloned.1.call-done), channel_id=1, source_target_pairs={{0,0},{1,1},{2,8},{3,9},{4,16},{5,17},{6,24},{7,25},{8,10},{9,11},... | collective-permute-start | bytes 786440 | tf_op jit(solution)/shard_map/ppermute | solution.py:183
  (11 other events, 18.3 us)
Sparse Core Ops, SparseCore 0:
  38.1 28.1 all-gather.1
  70.2 34.3 reduce-scatter.1

commit v10 on v9

--- a/solution.py
+++ b/solution.py
@@ -78,25 +78,22 @@
     piece = rows // n_seq
     me = lax.axis_index("seq")
     split = out_grad.reshape(n_seq, piece, length)
-    got = exchange(lambda step: split[partner(me, step, n_seq)], "seq")
-    stacked = jnp.stack([split[me]] + got)
-    index = jnp.zeros((n_seq,), jnp.int32)
-    for step in range(1, n_seq):
-        index = index + jnp.where(
-            jnp.arange(n_seq) == source(me, step, n_seq), step, 0
-        ).astype(jnp.int32)
+    got = []
+    for k in range(n_seq):
+        route = []
+        for r in range(n_seq):
+            for b in range(n_tp):
+                route.append((r * n_tp + b, n_seq * b + (r + k) % n_seq))
+        got.append(lax.ppermute(split[(me + k) % n_seq], ("seq", "tp"), route))
+    stacked = jnp.stack(got)
+    flat = me * n_tp + lax.axis_index("tp")
+    index = (flat % n_seq - jnp.arange(n_seq)) % n_seq
     mine = jnp.take(stacked, index, axis=0)
     return jnp.transpose(mine, (1, 0, 2)).reshape(piece, n_seq * length)
 
 
 def rows_gathered(mine, n_seq, n_tp):
-    route = []
-    for a in range(n_seq):
-        for b in range(n_tp):
-            flat = n_seq * b + a
-            route.append((a * n_tp + b, (flat // n_tp) * n_tp + flat % n_tp))
-    moved = lax.ppermute(mine, ("seq", "tp"), route)
-    return lax.all_gather(moved, "tp", axis=0, tiled=True)
+    return lax.all_gather(mine, "tp", axis=0, tiled=True)
 
 
 def shards(streams, feat_weight, long_filter, skip_gain, out_weight, out_grad):

time: 135 us -> 142 us (1.052)
  local copies, waits for them, and re-layouts: 15 us -> 19.7 us
  starting transfers between devices: 26.5 us -> 29.3 us
    ppermute x1 -> x4, starting transfers between devices: 3.04 us -> 13.1 us  [rows_of_slab(): got.append(lax.ppermute(split[(me + k) % n_seq], ('seq', 'tp'), route))]
    ppermute x9 -> x6, starting transfers between devices: 11.8 us -> 5.94 us  [exchange(): got.append(lax.ppermute(block_of(step), axis, route))]
    ppermute x1, waiting for transfers between devices: 7.26 us -> 2.16 us  [halo(): high = lax.ppermute(high, axis, backward)]
    unnamed x46 -> x76, local copies, waits for them, and re-layouts: 3.36 us -> 8.46 us
    ppermute x1, waiting for transfers between devices: 0.19 us -> 3.62 us  [halo(): low = lax.ppermute(low, axis, forward)]
    ppermute x1, starting transfers between devices: 4.49 us -> 1.92 us  [halo(): high = lax.ppermute(high, axis, backward)]
    ppermute x1, starting transfers between devices: 2.04 us -> 4.26 us  [halo(): low = lax.ppermute(low, axis, forward)]
    reduce_scatter x1, waiting for transfers between devices: 3.69 us -> 2.06 us  [shards(): lax.psum_scatter(partial_out, 'tp', scatter_dimension=0, tiled=True)]
where the time goes in v10:
time: 142 us; the launch traced here: 140 us
  waiting for transfers between devices  50.3 us (35%)
  starting transfers between devices  29.3 us (21%)
  local copies, waits for them, and re-layouts  19.7 us (14%)
  matrix products  19.1 us (13%)
  between operations  14.8 us (10%)
  other arithmetic  7.22 us (5%)
    ppermute x6, waiting for transfers between devices, exchange(): got.append(lax.ppermute(block_of(step), axis, route))  21.1 us
    ppermute x1, waiting for transfers between devices, shards(): mixed = lax.ppermute(output_sum, ('seq', 'tp'), mixed_route)  18.6 us
    ppermute x4, starting transfers between devices, rows_of_slab(): got.append(lax.ppermute(split[(me + k) % n_seq], ('seq', 'tp'), route))  13.1 us
    conv_general_dilated x2, matrix products, correlate(): lax.conv_general_dilated(signal[None], taps[:, None, :], (1,), 'VALID', d...  11 us
    unnamed x76, local copies, waits for them, and re-layouts  8.46 us
    ppermute x6, starting transfers between devices, exchange(): got.append(lax.ppermute(block_of(step), axis, route))  5.94 us
    ppermute x1, starting transfers between devices, halo(): low = lax.ppermute(low, axis, forward)  4.26 us
    ppermute x1, waiting for transfers between devices, halo(): low = lax.ppermute(low, axis, forward)  3.62 us
  transfers between devices with their start and end apart: 16, of which 8 were waited for; matrix products, arithmetic and copies ran while one was open for 27% of the time, Pallas kernels for 0%

profile of v10, /device:TPU:27, one launch (start us, length us, event | category | flops | bytes accessed | tf_op | source)
XLA Modules:
  0.0 140.4 jit_solution(11859294340483092277)
XLA Ops:
  8.3 3.0 %collective-permute-start = (bf16[128,256]{1,0:T(8,128)(2,1)S(1)}, bf16[128,256]{1,0:T(8,128)(2,1)S(1)}, u32[]{:S(2)}, u32[]{:S(2)}) collective-permute-start(bf16[128,256]{1,0:T(8,128)(2,1)S(1)} %get-tuple-element.51), channel_id=1, source_target_pairs={{0,0},{1,4},{2,8},{3,12},{4,16},{5,20},{6,24},{7,28},{8,1},{9,5},{... | collective-permute-start | bytes 196616 | tf_op jit(solution)/shard_map/ppermute | solution.py:87
  11.4 2.5 %collective-permute-start.3 = (bf16[128,256]{1,0:T(8,128)(2,1)S(1)}, bf16[128,256]{1,0:T(8,128)(2,1)S(1)}, u32[]{:S(2)}, u32[]{:S(2)}) collective-permute-start(bf16[128,256]{1,0:T(8,128)(2,1)S(1)} %get-tuple-element.52), channel_id=1, source_target_pairs={{0,3},{1,7},{2,11},{3,15},{4,19},{5,23},{6,27},{7,31},{8,0},{9,4},... | collective-permute-start | bytes 196616 | tf_op jit(solution)/shard_map/ppermute | solution.py:87
  14.2 7.3 %collective-permute-start.1 = (bf16[128,256]{1,0:T(8,128)(2,1)S(1)}, bf16[128,256]{1,0:T(8,128)(2,1)S(1)}, u32[]{:S(2)}, u32[]{:S(2)}) collective-permute-start(bf16[128,256]{1,0:T(8,128)(2,1)S(1)} %get-tuple-element.54), channel_id=1, source_target_pairs={{0,1},{1,5},{2,9},{3,13},{4,17},{5,21},{6,25},{7,29},{8,2},{9,6},{... | collective-permute-start | bytes 196616 | tf_op jit(solution)/shard_map/ppermute | solution.py:87
  26.6 1.9 %rev.8 = f32[512,128]{1,0:T(8,128)S(1)} reverse(f32[512,128]{1,0:T(8,128)} %param.8), dimensions={1} | reverse | bytes 524288 | tf_op jit(solution)/shard_map/rev | solution.py:120
  34.7 1.9 %collective-permute-start.5 = (bf16[512,145]{0,1:T(8,128)(2,1)S(1)}, bf16[512,145]{0,1:T(8,128)(2,1)S(1)}, u32[]{:S(2)}, u32[]{:S(2)}) collective-permute-start(bf16[512,145]{0,1:T(8,128)(2,1)S(1)} %pad_maximum_fusion.5), channel_id=1, source_target_pairs={{8,0},{16,8},{24,16},{9,1},{17,9},{25,17},{10,2},{18,10},{26,18},{... | collective-permute-start | bytes 445448 | tf_op jit(solution)/shard_map/ppermute | solution.py:20
  36.6 4.3 %collective-permute-start.4 = (bf16[512,272]{0,1:T(8,128)(2,1)S(1)}, bf16[512,272]{0,1:T(8,128)(2,1)S(1)}, u32[]{:S(2)}, u32[]{:S(2)}) collective-permute-start(bf16[512,272]{0,1:T(8,128)(2,1)S(1)} %pad_maximum_fusion.3), channel_id=1, source_target_pairs={{0,8},{8,16},{16,24},{1,9},{9,17},{17,25},{2,10},{10,18},{18,26},{... | collective-permute-start | bytes 835592 | tf_op jit(solution)/shard_map/ppermute | solution.py:19
  41.0 2.2 %collective-permute-done.5 = bf16[512,145]{0,1:T(8,128)(2,1)S(1)} collective-permute-done((bf16[512,145]{0,1:T(8,128)(2,1)S(1)}, bf16[512,145]{0,1:T(8,128)(2,1)S(1)}, u32[]{:S(2)}, u32[]{:S(2)}) %collective-permute-start.5) | collective-permute-done | bytes 148512 | tf_op jit(solution)/shard_map/ppermute | solution.py:20
  43.2 3.6 %collective-permute-done.4 = bf16[512,272]{0,1:T(8,128)(2,1)S(1)} collective-permute-done((bf16[512,272]{0,1:T(8,128)(2,1)S(1)}, bf16[512,272]{0,1:T(8,128)(2,1)S(1)}, u32[]{:S(2)}, u32[]{:S(2)}) %collective-permute-start.4) | collective-permute-done | bytes 278560 | tf_op jit(solution)/shard_map/ppermute | solution.py:19
  47.8 1.3 fusion
  50.2 5.5 %fusion.26 = f32[1,512,262]{1,0,2:T(1,128)S(1)} fusion(f32[512,1,128]{0,1,2:T(1,128)S(1)} %copy-done.14, f32[1,512,389]{1,2,0:T(8,128)S(1)} %get-tuple-element.37), kind=kOutput, calls=%fused_computation.59 | convolution fusion | flops 206045184 | bytes 1595392 | tf_op jit(solution)/shard_map/conv_general_dilated | solution.py:36
  57.3 2.9 %collective-permute-start.8 = (bf16[512,256]{0,1:T(8,128)(2,1)S(1)}, bf16[512,256]{0,1:T(8,128)(2,1)S(1)}, u32[]{:S(2)}, u32[]{:S(2)}) collective-permute-start(bf16[512,256]{0,1:T(8,128)(2,1)S(1)} %fusion.32), channel_id=1, source_target_pairs={{0,24},{8,16},{16,8},{24,0},{1,25},{9,17},{17,9},{25,1},{2,26},{10... | collective-permute-start | bytes 786440 | tf_op jit(solution)/shard_map/ppermute | solution.py:72
  60.9 11.6 %collective-permute-done.6 = bf16[512,256]{0,1:T(8,128)(2,1)S(1)} collective-permute-done((bf16[512,256]{0,1:T(8,128)(2,1)S(1)}, bf16[512,256]{0,1:T(8,128)(2,1)S(1)}, u32[]{:S(2)}, u32[]{:S(2)}) %collective-permute-start.6) | collective-permute-done | bytes 262176 | tf_op jit(solution)/shard_map/ppermute | solution.py:72
  74.8 1.5 %pad_maximum_fusion = bf16[4096,256]{0,1:T(8,128)(2,1)} fusion(bf16[1024,256]{0,1:T(8,128)(2,1)S(1)} %fusion.16, bf16[1024,256]{0,1:T(8,128)(2,1)S(1)} %fusion.15, bf16[1024,256]{0,1:T(8,128)(2,1)S(1)} %fusion.14, bf16[1024,256]{0,1:T(8,128)(2,1)S(1)} %fusion.13), kind=kLoop, calls=%fused_computation.1 | loop fusion | flops 8388608 | bytes 4194304 | tf_op jit(solution)/shard_map/concatenate | solution.py:131
  76.4 3.0 %fusion.57 = f32[1024,512]{1,0:T(8,128)S(1)} fusion(bf16[1024,1024]{0,1:T(8,128)(2,1)} %all-gather.2.cloned.1.call-done, bf16[512,1024]{1,0:T(8,128)(2,1)S(1)} %copy-done), kind=kOutput, calls=%fused_computation.147 | convolution fusion | flops 1073741824 | bytes 5242880 | tf_op jit(solution)/shard_map/dot_general | solution.py:142
  83.7 3.3 %collective-permute-done.9 = bf16[512,256]{0,1:T(8,128)(2,1)S(1)} collective-permute-done((bf16[512,256]{0,1:T(8,128)(2,1)S(1)}, bf16[512,256]{0,1:T(8,128)(2,1)S(1)}, u32[]{:S(2)}, u32[]{:S(2)}) %collective-permute-start.9) | collective-permute-done | bytes 262176 | tf_op jit(solution)/shard_map/ppermute | solution.py:72
  87.0 6.2 %collective-permute-done.11 = bf16[512,256]{0,1:T(8,128)(2,1)S(1)} collective-permute-done((bf16[512,256]{0,1:T(8,128)(2,1)S(1)}, bf16[512,256]{0,1:T(8,128)(2,1)S(1)}, u32[]{:S(2)}, u32[]{:S(2)}) %collective-permute-start.11) | collective-permute-done | bytes 262176 | tf_op jit(solution)/shard_map/ppermute | solution.py:72
  93.4 2.1 %collective-permute-start.12 = (bf16[512,133]{0,1:T(8,128)(2,1)S(1)}, bf16[512,133]{0,1:T(8,128)(2,1)S(1)}, u32[]{:S(2)}, u32[]{:S(2)}) collective-permute-start(bf16[512,133]{0,1:T(8,128)(2,1)S(1)} %slice.479), channel_id=1, source_target_pairs={{8,0},{16,8},{24,16},{9,1},{17,9},{25,17},{10,2},{18,10},{26,18},{... | collective-permute-start | bytes 408584 | tf_op jit(solution)/shard_map/ppermute | solution.py:32
  95.5 1.9 %add_convert_fusion = bf16[512,1024]{1,0:T(8,128)(2,1)} fusion(f32[512,1024]{1,0:T(8,128)S(1)} %fusion.36, f32[512,1024]{1,0:T(8,128)S(1)} %fusion.38, f32[512,1024]{1,0:T(8,128)S(1)} %fusion.40, bf16[512,256]{0,1:T(8,128)(2,1)S(1)} %copy-done.5, bf16[1024,1024]{0,1:T(8,128)(2,1)S(1)} %copy-done.3, s32[]{:T(128)S(6)} %select_n.110), kind=kOutput, calls=%fused_computation.2 | convolution fusion | flops 274726912 | bytes 8126468 | tf_op jit(solution)/shard_map/dot_general | solution.py:159
  97.4 2.7 %collective-permute-done.12 = bf16[512,133]{0,1:T(8,128)(2,1)S(1)} collective-permute-done((bf16[512,133]{0,1:T(8,128)(2,1)S(1)}, bf16[512,133]{0,1:T(8,128)(2,1)S(1)}, u32[]{:S(2)}, u32[]{:S(2)}) %collective-permute-start.12) | collective-permute-done | bytes 136224 | tf_op jit(solution)/shard_map/ppermute | solution.py:32
  101.2 5.5 %fusion.24 = f32[1,512,262]{1,0,2:T(1,128)S(1)} fusion(f32[512,1,128]{0,1,2:T(1,128)S(1)} %copy-done.13, f32[1,512,389]{1,2,0:T(8,128)S(1)} %bitcast.135), kind=kOutput, calls=%fused_computation.57 | convolution fusion | flops 206045184 | bytes 1595392 | tf_op jit(solution)/shard_map/conv_general_dilated | solution.py:36
  107.7 1.3 fusion.7
  109.0 2.1 %reduce-scatter.2.cloned.1.call-done = bf16[512,256]{0,1:T(8,128)(2,1)} async-done(((bf16[4096,256]{0,1:T(8,128)(2,1)}), bf16[512,256]{0,1:T(8,128)(2,1)}) %reduce-scatter.2.cloned.1.call-update) | async-done | bytes 262160 | tf_op jit(solution)/shard_map/reduce_scatter | solution.py:132
  111.1 1.9 %collective-permute-start.13 = (bf16[512,256]{0,1:T(8,128)(2,1)}, bf16[512,256]{0,1:T(8,128)(2,1)S(1)}, u32[]{:S(2)}, u32[]{:S(2)}) collective-permute-start(bf16[512,256]{0,1:T(8,128)(2,1)} %reduce-scatter.2.cloned.1.call-done), channel_id=1, source_target_pairs={{0,0},{1,1},{2,8},{3,9},{4,16},{5,17},{6,24},{7,25},{8,10},{9,11},... | collective-permute-start | bytes 786440 | tf_op jit(solution)/shard_map/ppermute | solution.py:180
  114.1 18.6 %collective-permute-done.13 = bf16[512,256]{0,1:T(8,128)(2,1)S(1)} collective-permute-done((bf16[512,256]{0,1:T(8,128)(2,1)}, bf16[512,256]{0,1:T(8,128)(2,1)S(1)}, u32[]{:S(2)}, u32[]{:S(2)}) %collective-permute-start.13) | collective-permute-done | bytes 262176 | tf_op jit(solution)/shard_map/ppermute | solution.py:180
  (142 shorter events, 27.5 us)
Async XLA Ops:
  7.2 53.3 %copy-start = (bf16[512,1024]{1,0:T(8,128)(2,1)S(1)}, bf16[512,1024]{1,0:T(8,128)(2,1)}, u32[]{:S(2)}) copy-start(bf16[512,1024]{1,0:T(8,128)(2,1)} %param.10) | copy-start | bytes 3145732
  7.2 21.4 %copy-start.10 = (f32[512,128]{1,0:T(8,128)S(1)}, f32[512,128]{1,0:T(8,128)}, u32[]{:S(2)}) copy-start(f32[512,128]{1,0:T(8,128)} %param.8) | copy-start | bytes 786436
  7.2 69.2 %all-gather.2.cloned.1.call-start = ((), (), s32[]{:S(2)}) async-start(), calls=%async_computation.2 | async-start | bytes 2359296 | tf_op jit(solution)/shard_map/all_gather | solution.py:96
  8.3 24.3 %collective-permute-start = (bf16[128,256]{1,0:T(8,128)(2,1)S(1)}, bf16[128,256]{1,0:T(8,128)(2,1)S(1)}, u32[]{:S(2)}, u32[]{:S(2)}) collective-permute-start(bf16[128,256]{1,0:T(8,128)(2,1)S(1)} %get-tuple-element.51), channel_id=1, source_target_pairs={{0,0},{1,4},{2,8},{3,12},{4,16},{5,20},{6,24},{7,28},{8,1},{9,5},{... | collective-permute-start | bytes 196616 | tf_op jit(solution)/shard_map/ppermute | solution.py:87
  11.4 21.3 %collective-permute-start.3 = (bf16[128,256]{1,0:T(8,128)(2,1)S(1)}, bf16[128,256]{1,0:T(8,128)(2,1)S(1)}, u32[]{:S(2)}, u32[]{:S(2)}) collective-permute-start(bf16[128,256]{1,0:T(8,128)(2,1)S(1)} %get-tuple-element.52), channel_id=1, source_target_pairs={{0,3},{1,7},{2,11},{3,15},{4,19},{5,23},{6,27},{7,31},{8,0},{9,4},... | collective-permute-start | bytes 196616 | tf_op jit(solution)/shard_map/ppermute | solution.py:87
  13.9 18.8 %collective-permute-start.2 = (bf16[128,256]{1,0:T(8,128)(2,1)S(1)}, bf16[128,256]{1,0:T(8,128)(2,1)S(1)}, u32[]{:S(2)}, u32[]{:S(2)}) collective-permute-start(bf16[128,256]{1,0:T(8,128)(2,1)S(1)} %get-tuple-element.53), channel_id=1, source_target_pairs={{0,2},{1,6},{2,10},{3,14},{4,18},{5,22},{6,26},{7,30},{8,3},{9,7},... | collective-permute-start | bytes 196616 | tf_op jit(solution)/shard_map/ppermute | solution.py:87
  14.2 18.5 %collective-permute-start.1 = (bf16[128,256]{1,0:T(8,128)(2,1)S(1)}, bf16[128,256]{1,0:T(8,128)(2,1)S(1)}, u32[]{:S(2)}, u32[]{:S(2)}) collective-permute-start(bf16[128,256]{1,0:T(8,128)(2,1)S(1)} %get-tuple-element.54), channel_id=1, source_target_pairs={{0,1},{1,5},{2,9},{3,13},{4,17},{5,21},{6,25},{7,29},{8,2},{9,6},{... | collective-permute-start | bytes 196616 | tf_op jit(solution)/shard_map/ppermute | solution.py:87
  28.5 5.7 %copy-start.11 = (bf16[3,512,256]{2,1,0:T(8,128)(2,1)S(1)}, bf16[3,512,256]{2,1,0:T(8,128)(2,1)}, u32[]{:S(2)}) copy-start(bf16[3,512,256]{2,1,0:T(8,128)(2,1)} %param.6) | copy-start | bytes 2359300
  34.7 8.5 %collective-permute-start.5 = (bf16[512,145]{0,1:T(8,128)(2,1)S(1)}, bf16[512,145]{0,1:T(8,128)(2,1)S(1)}, u32[]{:S(2)}, u32[]{:S(2)}) collective-permute-start(bf16[512,145]{0,1:T(8,128)(2,1)S(1)} %pad_maximum_fusion.5), channel_id=1, source_target_pairs={{8,0},{16,8},{24,16},{9,1},{17,9},{25,17},{10,2},{18,10},{26,18},{... | collective-permute-start | bytes 445448 | tf_op jit(solution)/shard_map/ppermute | solution.py:20
  36.6 10.2 %collective-permute-start.4 = (bf16[512,272]{0,1:T(8,128)(2,1)S(1)}, bf16[512,272]{0,1:T(8,128)(2,1)S(1)}, u32[]{:S(2)}, u32[]{:S(2)}) collective-permute-start(bf16[512,272]{0,1:T(8,128)(2,1)S(1)} %pad_maximum_fusion.3), channel_id=1, source_target_pairs={{0,8},{8,16},{16,24},{1,9},{9,17},{17,25},{2,10},{10,18},{18,26},{... | collective-permute-start | bytes 835592 | tf_op jit(solution)/shard_map/ppermute | solution.py:19
  41.0 70.1 %reduce-scatter.2.cloned.1.call-start = ((), (), s32[]{:S(2)}) async-start(), calls=%async_computation.1 | async-start | bytes 2359296 | tf_op jit(solution)/shard_map/reduce_scatter | solution.py:132
  49.3 6.5 %copy-start.1 = (f32[512,389]{0,1:T(8,128)}, f32[512,389]{0,1:T(8,128)S(1)}, u32[]{:S(2)}) copy-start(f32[512,389]{0,1:T(8,128)S(1)} %get-tuple-element.36) | copy-start | bytes 2390020
  50.2 5.6 %copy-start.32 = (f32[512]{0:T(512)S(1)}, f32[512]{0:T(512)}, u32[]{:S(2)}) copy-start(f32[512]{0:T(512)} %param.9) | copy-start | bytes 6148
  57.3 16.2 %collective-permute-start.8 = (bf16[512,256]{0,1:T(8,128)(2,1)S(1)}, bf16[512,256]{0,1:T(8,128)(2,1)S(1)}, u32[]{:S(2)}, u32[]{:S(2)}) collective-permute-start(bf16[512,256]{0,1:T(8,128)(2,1)S(1)} %fusion.32), channel_id=1, source_target_pairs={{0,24},{8,16},{16,8},{24,0},{1,25},{9,17},{17,9},{25,1},{2,26},{10... | collective-permute-start | bytes 786440 | tf_op jit(solution)/shard_map/ppermute | solution.py:72
  60.1 12.8 %collective-permute-start.7 = (bf16[512,256]{0,1:T(8,128)(2,1)S(1)}, bf16[512,256]{0,1:T(8,128)(2,1)S(1)}, u32[]{:S(2)}, u32[]{:S(2)}) collective-permute-start(bf16[512,256]{0,1:T(8,128)(2,1)S(1)} %fusion.32), channel_id=1, source_target_pairs={{0,16},{8,24},{16,0},{24,8},{1,17},{9,25},{17,1},{25,9},{2,18},{10... | collective-permute-start | bytes 786440 | tf_op jit(solution)/shard_map/ppermute | solution.py:72
  60.1 12.4 %collective-permute-start.6 = (bf16[512,256]{0,1:T(8,128)(2,1)S(1)}, bf16[512,256]{0,1:T(8,128)(2,1)S(1)}, u32[]{:S(2)}, u32[]{:S(2)}) collective-permute-start(bf16[512,256]{0,1:T(8,128)(2,1)S(1)} %fusion.32), channel_id=1, source_target_pairs={{0,8},{8,0},{16,24},{24,16},{1,9},{9,1},{17,25},{25,17},{2,10},{10... | collective-permute-start | bytes 786440 | tf_op jit(solution)/shard_map/ppermute | solution.py:72
  76.4 5.9 %copy-start.3 = (bf16[1024,1024]{0,1:T(8,128)(2,1)S(1)}, bf16[1024,1024]{0,1:T(8,128)(2,1)}, u32[]{:S(2)}) copy-start(bf16[1024,1024]{0,1:T(8,128)(2,1)} %all-gather.2.cloned.1.call-done) | copy-start | bytes 6291460
  79.6 7.4 %collective-permute-start.9 = (bf16[512,256]{0,1:T(8,128)(2,1)S(1)}, bf16[512,256]{0,1:T(8,128)(2,1)S(1)}, u32[]{:S(2)}, u32[]{:S(2)}) collective-permute-start(bf16[512,256]{0,1:T(8,128)(2,1)S(1)} %get-tuple-element.32), channel_id=1, source_target_pairs={{0,8},{8,0},{16,24},{24,16},{1,9},{9,1},{17,25},{25,17},{2,10},{10... | collective-permute-start | bytes 786440 | tf_op jit(solution)/shard_map/ppermute | solution.py:72
  80.6 12.6 %collective-permute-start.11 = (bf16[512,256]{0,1:T(8,128)(2,1)S(1)}, bf16[512,256]{0,1:T(8,128)(2,1)S(1)}, u32[]{:S(2)}, u32[]{:S(2)}) collective-permute-start(bf16[512,256]{0,1:T(8,128)(2,1)S(1)} %get-tuple-element.33), channel_id=1, source_target_pairs={{0,24},{8,16},{16,8},{24,0},{1,25},{9,17},{17,9},{25,1},{2,26},{10... | collective-permute-start | bytes 786440 | tf_op jit(solution)/shard_map/ppermute | solution.py:72
  81.6 11.6 %collective-permute-start.10 = (bf16[512,256]{0,1:T(8,128)(2,1)S(1)}, bf16[512,256]{0,1:T(8,128)(2,1)S(1)}, u32[]{:S(2)}, u32[]{:S(2)}) collective-permute-start(bf16[512,256]{0,1:T(8,128)(2,1)S(1)} %get-tuple-element.34), channel_id=1, source_target_pairs={{0,16},{8,24},{16,0},{24,8},{1,17},{9,25},{17,1},{25,9},{2,18},{10... | collective-permute-start | bytes 786440 | tf_op jit(solution)/shard_map/ppermute | solution.py:72
  83.7 11.8 %copy-start.5 = (bf16[512,256]{0,1:T(8,128)(2,1)S(1)}, bf16[512,256]{0,1:T(8,128)(2,1)}, u32[]{:S(2)}) copy-start(bf16[512,256]{0,1:T(8,128)(2,1)} %copy-done.4) | copy-start | bytes 786436
  93.4 6.7 %collective-permute-start.12 = (bf16[512,133]{0,1:T(8,128)(2,1)S(1)}, bf16[512,133]{0,1:T(8,128)(2,1)S(1)}, u32[]{:S(2)}, u32[]{:S(2)}) collective-permute-start(bf16[512,133]{0,1:T(8,128)(2,1)S(1)} %slice.479), channel_id=1, source_target_pairs={{8,0},{16,8},{24,16},{9,1},{17,9},{25,17},{10,2},{18,10},{26,18},{... | collective-permute-start | bytes 408584 | tf_op jit(solution)/shard_map/ppermute | solution.py:32
  101.2 5.5 %copy-start.2 = (f32[512,389]{0,1:T(8,128)S(1)}, f32[512,389]{0,1:T(8,128)}, u32[]{:S(2)}) copy-start(f32[512,389]{0,1:T(8,128)} %copy-done.1) | copy-start | bytes 2390020
  111.1 21.7 %collective-permute-start.13 = (bf16[512,256]{0,1:T(8,128)(2,1)}, bf16[512,256]{0,1:T(8,128)(2,1)S(1)}, u32[]{:S(2)}, u32[]{:S(2)}) collective-permute-start(bf16[512,256]{0,1:T(8,128)(2,1)} %reduce-scatter.2.cloned.1.call-done), channel_id=1, source_target_pairs={{0,0},{1,1},{2,8},{3,9},{4,16},{5,17},{6,24},{7,25},{8,10},{9,11},... | collective-permute-start | bytes 786440 | tf_op jit(solution)/shard_map/ppermute | solution.py:180
  (26 other events, 27.1 us)
Sparse Core Ops, SparseCore 0:
  41.1 28.1 all-gather.1
  76.5 34.5 reduce-scatter.1

commit v11 on v9

--- a/solution.py
+++ b/solution.py
@@ -18,12 +18,17 @@
     high = jnp.concatenate([block[0, :, :width], block[1, :, :short], block[2, :, :short]], axis=-1)
     low = lax.ppermute(low, axis, forward)
     high = lax.ppermute(high, axis, backward)
-    query = jnp.concatenate([low[:, 2 * width :], block[0], high[:, :width]], axis=-1)
-    key = jnp.concatenate([low[:, :width], block[1], high[:, width : width + short]], axis=-1)
-    value = jnp.concatenate(
-        [low[:, width : 2 * width], block[2], high[:, width + short :]], axis=-1
-    )
-    return query, jnp.stack([key, value])
+    query_head = jnp.concatenate([low[:, 2 * width :], block[0]], axis=-1)
+    key_value_head = jnp.stack(
+        [
+            jnp.concatenate([low[:, :width], block[1]], axis=-1),
+            jnp.concatenate([low[:, width : 2 * width], block[2]], axis=-1),
+        ]
+    )
+    query = jnp.concatenate([query_head, high[:, :width]], axis=-1)
+    key = jnp.concatenate([key_value_head[0], high[:, width : width + short]], axis=-1)
+    value = jnp.concatenate([key_value_head[1], high[:, width + short :]], axis=-1)
+    return query_head, key_value_head, query, jnp.stack([key, value])
 
 
 def from_behind(block, axis, distance):
@@ -112,17 +117,21 @@
 
     slab_piece = rows_of_slab(out_grad, n_seq, n_tp)
     streams, slab_piece = lax.optimization_barrier((streams, slab_piece))
-    query_in, key_value_in = halo(streams, "seq", reach, taps_short - 1)
+    query_head_in, key_value_head_in, query_in, key_value_in = halo(
+        streams, "seq", reach, taps_short - 1
+    )
     slab_grad = rows_gathered(slab_piece, n_seq, n_tp)
     slab_width = slab_grad.shape[0]
 
-    key_value = short_correlate(key_value_in.astype(jnp.float32), feat_weight[1:, :, ::-1])
-    key_feat, value_feat = key_value[0], key_value[1]
-    query_tail = short_correlate(query_in.astype(jnp.float32), feat_weight[0, :, ::-1])
-    product = key_feat * value_feat
-    convolved = correlate(product, long_filter[:, ::-1])
-    summed = convolved + skip_gain[:, None] * product[:, taps_long - 1 :]
-    gated = (query_tail[:, :length] * summed[:, :length]).astype(jnp.bfloat16)
+    key_value_head = short_correlate(
+        key_value_head_in.astype(jnp.float32), feat_weight[1:, :, ::-1]
+    )
+    query_head = short_correlate(query_head_in.astype(jnp.float32), feat_weight[0, :, ::-1])
+    product_head = key_value_head[0] * key_value_head[1]
+    summed_head = correlate(product_head, long_filter[:, ::-1]) + (
+        skip_gain[:, None] * product_head[:, taps_long - 1 :]
+    )
+    gated = (query_head * summed_head).astype(jnp.bfloat16)
 
     gated_blocks = [gated] + exchange(lambda step: gated, "seq")
     group = n_tp // n_seq
@@ -141,6 +150,16 @@
             route.append((s * n_tp + p, target * n_tp + group * s + p % group))
     mixed_route = route
 
+    key_value = short_correlate(key_value_in.astype(jnp.float32), feat_weight[1:, :, ::-1])
+    key_feat, value_feat = key_value[0], key_value[1]
+    query_tail = short_correlate(query_in.astype(jnp.float32), feat_weight[0, :, ::-1])
+    product = key_feat * value_feat
+    past = product[:, length:]
+    summed_next = correlate(past, long_filter[:, ::-1]) + (
+        skip_gain[:, None] * past[:, taps_long - 1 :]
+    )
+    summed = jnp.concatenate([summed_head, summed_next], axis=1)
+
     slab_grad, gated_blocks = lax.optimization_barrier((slab_grad, gated_blocks))
     partial_grad = jnp.dot(out_weight, slab_grad, preferred_element_type=jnp.float32)
 

time: 135 us -> 136 us (level)
  local copies, waits for them, and re-layouts: 15 us -> 18 us
  starting transfers between devices: 26.5 us -> 24.5 us
  other arithmetic: 7.22 us -> 8.65 us
    ppermute x9, waiting for transfers between devices: 20 us -> 17.5 us  [exchange(): got.append(lax.ppermute(block_of(step), axis, route))]
    unnamed x46 -> x60, local copies, waits for them, and re-layouts: 3.36 us -> 5.13 us
    conv_general_dilated x2 -> x3, matrix products: 11 us -> 11.6 us  [correlate(): lax.conv_general_dilated(signal[None], taps[:, None, :], (1,), 'VALID', d...]
  transfers between devices with their start and end apart: 16 -> 16, of which waited for: 8 -> 8; matrix products, arithmetic and copies ran while one was open for 27% -> 29% of each run, Pallas kernels for 0% -> 0%
where the time goes in v11:
time: 136 us
  waiting for transfers between devices  50.1 us (37%)
  starting transfers between devices  24.5 us (18%)
  matrix products  19.7 us (14%)
  local copies, waits for them, and re-layouts  18 us (13%)
  between operations  14.8 us (11%)
  other arithmetic  8.65 us (6%)
    ppermute x1, waiting for transfers between devices, shards(): mixed = lax.ppermute(output_sum, ('seq', 'tp'), mixed_route)  19.3 us
    ppermute x9, waiting for transfers between devices, exchange(): got.append(lax.ppermute(block_of(step), axis, route))  17.5 us
    conv_general_dilated x3, matrix products, correlate(): lax.conv_general_dilated(signal[None], taps[:, None, :], (1,), 'VALID', d...  11.6 us
    ppermute x9, starting transfers between devices, exchange(): got.append(lax.ppermute(block_of(step), axis, route))  10.7 us
    ppermute x1, waiting for transfers between devices, halo(): high = lax.ppermute(high, axis, backward)  7.26 us
    unnamed x60, local copies, waits for them, and re-layouts  5.13 us
    ppermute x1, starting transfers between devices, halo(): high = lax.ppermute(high, axis, backward)  4.49 us
    reduce_scatter x1, waiting for transfers between devices, shards(): lax.psum_scatter(partial_out, 'tp', scatter_dimension=0, tiled=True)  3.42 us
  transfers between devices with their start and end apart: 16, of which 8 were waited for; matrix products, arithmetic and copies ran while one was open for 29% of the time, Pallas kernels for 0%

profile of v11, /device:TPU:27, one launch (start us, length us, event | category | flops | bytes accessed | tf_op | source)
XLA Modules:
  0.0 135.7 jit_solution(7937834014326610628)
XLA Ops:
  14.9 1.9 %rev.5 = f32[512,128]{1,0:T(8,128)S(1)} reverse(f32[512,128]{1,0:T(8,128)} %param.8), dimensions={1} | reverse | bytes 524288 | tf_op jit(solution)/shard_map/rev | solution.py:131
  16.8 1.9 %copy.58 = f32[512,1,128]{0,1,2:T(1,128)} copy(f32[512,1,128]{2,0,1:T(8,128)} %bitcast.149) | data formatting | bytes 524288 | tf_op jit(solution)/shard_map/broadcast_in_dim | solution.py:43
  21.6 3.0 %collective-permute-start.7 = (bf16[128,1024]{0,1:T(8,128)(2,1)}, bf16[128,1024]{0,1:T(8,128)(2,1)S(1)}, u32[]{:S(2)}, u32[]{:S(2)}) collective-permute-start(bf16[128,1024]{0,1:T(8,128)(2,1)} %bitcast.11), channel_id=1, source_target_pairs={{0,0},{1,4},{2,8},{3,12},{4,16},{5,20},{6,24},{7,28},{8,1},{9,5},{... | collective-permute-start | bytes 786440 | tf_op jit(solution)/shard_map/ppermute | solution.py:103
  24.7 4.5 %collective-permute-start.12 = (bf16[512,145]{0,1:T(8,128)(2,1)S(1)}, bf16[512,145]{0,1:T(8,128)(2,1)S(1)}, u32[]{:S(2)}, u32[]{:S(2)}) collective-permute-start(bf16[512,145]{0,1:T(8,128)(2,1)S(1)} %pad_maximum_fusion.5), channel_id=1, source_target_pairs={{8,0},{16,8},{24,16},{9,1},{17,9},{25,17},{10,2},{18,10},{26,18},{... | collective-permute-start | bytes 445448 | tf_op jit(solution)/shard_map/ppermute | solution.py:20
  29.2 2.0 %collective-permute-start.3 = (bf16[512,272]{0,1:T(8,128)(2,1)S(1)}, bf16[512,272]{0,1:T(8,128)(2,1)S(1)}, u32[]{:S(2)}, u32[]{:S(2)}) collective-permute-start(bf16[512,272]{0,1:T(8,128)(2,1)S(1)} %pad_maximum_fusion.3), channel_id=1, source_target_pairs={{0,8},{8,16},{16,24},{1,9},{9,17},{17,25},{2,10},{10,18},{18,26},{... | collective-permute-start | bytes 835592 | tf_op jit(solution)/shard_map/ppermute | solution.py:19
  31.3 7.3 %collective-permute-done.12 = bf16[512,145]{0,1:T(8,128)(2,1)S(1)} collective-permute-done((bf16[512,145]{0,1:T(8,128)(2,1)S(1)}, bf16[512,145]{0,1:T(8,128)(2,1)S(1)}, u32[]{:S(2)}, u32[]{:S(2)}) %collective-permute-start.12) | collective-permute-done | bytes 148512 | tf_op jit(solution)/shard_map/ppermute | solution.py:20
  42.8 5.3 %fusion.32 = f32[1,512,256]{1,0,2:T(1,128)S(1)} fusion(f32[512,1,128]{0,1,2:T(1,128)S(1)} %copy-done.13, f32[1,512,383]{1,2,0:T(8,128)S(1)} %slice_multiply_fusion.28), kind=kOutput, calls=%fused_computation.76 | convolution fusion | flops 201326592 | bytes 1570816 | tf_op jit(solution)/shard_map/conv_general_dilated | solution.py:41
  48.7 3.4 %collective-permute-start.6 = (bf16[512,256]{0,1:T(8,128)(2,1)S(1)}, bf16[512,256]{0,1:T(8,128)(2,1)S(1)}, u32[]{:S(2)}, u32[]{:S(2)}) collective-permute-start(bf16[512,256]{0,1:T(8,128)(2,1)S(1)} %get-tuple-element.16), channel_id=1, source_target_pairs={{0,24},{8,16},{16,8},{24,0},{1,25},{9,17},{17,9},{25,1},{2,26},{10... | collective-permute-start | bytes 786440 | tf_op jit(solution)/shard_map/ppermute | solution.py:77
  56.6 1.3 slice_bitcast_fusion
  58.4 7.8 %collective-permute-done.4 = bf16[512,256]{0,1:T(8,128)(2,1)S(1)} collective-permute-done((bf16[512,256]{0,1:T(8,128)(2,1)S(1)}, bf16[512,256]{0,1:T(8,128)(2,1)S(1)}, u32[]{:S(2)}, u32[]{:S(2)}) %collective-permute-start.4) | collective-permute-done | bytes 262176 | tf_op jit(solution)/shard_map/ppermute | solution.py:77
  68.4 1.5 %pad_maximum_fusion = bf16[4096,256]{0,1:T(8,128)(2,1)} fusion(bf16[1024,256]{0,1:T(8,128)(2,1)S(1)} %fusion.22, bf16[1024,256]{0,1:T(8,128)(2,1)S(1)} %fusion.21, bf16[1024,256]{0,1:T(8,128)(2,1)S(1)} %fusion.20, bf16[1024,256]{0,1:T(8,128)(2,1)S(1)} %fusion.19), kind=kLoop, calls=%fused_computation.1 | loop fusion | flops 8388608 | bytes 4194304 | tf_op jit(solution)/shard_map/concatenate | solution.py:143
  69.9 3.0 %fusion.80 = f32[1024,512]{1,0:T(8,128)S(1)} fusion(bf16[1024,1024]{0,1:T(8,128)(2,1)} %all-gather.2.cloned.1.call-done, bf16[512,1024]{1,0:T(8,128)(2,1)S(1)} %copy-done), kind=kOutput, calls=%fused_computation.188 | convolution fusion | flops 1073741824 | bytes 5242880 | tf_op jit(solution)/shard_map/dot_general | solution.py:164
  74.2 1.6 %collective-permute-start.9 = (bf16[512,256]{0,1:T(8,128)(2,1)S(1)}, bf16[512,256]{0,1:T(8,128)(2,1)S(1)}, u32[]{:S(2)}, u32[]{:S(2)}) collective-permute-start(bf16[512,256]{0,1:T(8,128)(2,1)S(1)} %get-tuple-element.36), channel_id=1, source_target_pairs={{0,16},{8,24},{16,0},{24,8},{1,17},{9,25},{17,1},{25,9},{2,18},{10... | collective-permute-start | bytes 786440 | tf_op jit(solution)/shard_map/ppermute | solution.py:77
  77.3 3.2 %collective-permute-done.8 = bf16[512,256]{0,1:T(8,128)(2,1)S(1)} collective-permute-done((bf16[512,256]{0,1:T(8,128)(2,1)S(1)}, bf16[512,256]{0,1:T(8,128)(2,1)S(1)}, u32[]{:S(2)}, u32[]{:S(2)}) %collective-permute-start.8) | collective-permute-done | bytes 262176 | tf_op jit(solution)/shard_map/ppermute | solution.py:77
  80.4 5.1 %collective-permute-done.10 = bf16[512,256]{0,1:T(8,128)(2,1)S(1)} collective-permute-done((bf16[512,256]{0,1:T(8,128)(2,1)S(1)}, bf16[512,256]{0,1:T(8,128)(2,1)S(1)}, u32[]{:S(2)}, u32[]{:S(2)}) %collective-permute-start.10) | collective-permute-done | bytes 262176 | tf_op jit(solution)/shard_map/ppermute | solution.py:77
  85.6 1.3 collective-permute-done.9
  87.1 2.1 %collective-permute-start.11 = (bf16[512,133]{0,1:T(8,128)(2,1)S(1)}, bf16[512,133]{0,1:T(8,128)(2,1)S(1)}, u32[]{:S(2)}, u32[]{:S(2)}) collective-permute-start(bf16[512,133]{0,1:T(8,128)(2,1)S(1)} %slice.652), channel_id=1, source_target_pairs={{8,0},{16,8},{24,16},{9,1},{17,9},{25,17},{10,2},{18,10},{26,18},{... | collective-permute-start | bytes 408584 | tf_op jit(solution)/shard_map/ppermute | solution.py:37
  89.2 2.0 %add_convert_fusion = bf16[512,1024]{1,0:T(8,128)(2,1)} fusion(f32[512,1024]{1,0:T(8,128)S(1)} %fusion.52, f32[512,1024]{1,0:T(8,128)S(1)} %fusion.54, f32[512,1024]{1,0:T(8,128)S(1)} %fusion.56, bf16[512,256]{0,1:T(8,128)(2,1)S(1)} %copy-done.5, bf16[1024,1024]{0,1:T(8,128)(2,1)S(1)} %copy-done.3, s32[]{:T(128)S(6)} %select_n.112), kind=kOutput, calls=%fused_computation.2 | convolution fusion | flops 274726912 | bytes 8126468 | tf_op jit(solution)/shard_map/dot_general | solution.py:181
  91.2 2.6 %collective-permute-done.11 = bf16[512,133]{0,1:T(8,128)(2,1)S(1)} collective-permute-done((bf16[512,133]{0,1:T(8,128)(2,1)S(1)}, bf16[512,133]{0,1:T(8,128)(2,1)S(1)}, u32[]{:S(2)}, u32[]{:S(2)}) %collective-permute-start.11) | collective-permute-done | bytes 136224 | tf_op jit(solution)/shard_map/ppermute | solution.py:37
  94.9 5.5 %fusion.30 = f32[1,512,262]{1,0,2:T(1,128)S(1)} fusion(f32[512,1,128]{0,1,2:T(1,128)S(1)} %copy-done.12, f32[1,512,389]{1,2,0:T(8,128)S(1)} %bitcast.148), kind=kOutput, calls=%fused_computation.73 | convolution fusion | flops 206045184 | bytes 1595392 | tf_op jit(solution)/shard_map/conv_general_dilated | solution.py:41
  100.8 1.3 fusion.7
  102.1 3.4 %reduce-scatter.2.cloned.1.call-done = bf16[512,256]{0,1:T(8,128)(2,1)} async-done(((bf16[4096,256]{0,1:T(8,128)(2,1)}), bf16[512,256]{0,1:T(8,128)(2,1)}) %reduce-scatter.2.cloned.1.call-update) | async-done | bytes 262160 | tf_op jit(solution)/shard_map/reduce_scatter | solution.py:144
  105.6 2.0 %collective-permute-start.13 = (bf16[512,256]{0,1:T(8,128)(2,1)}, bf16[512,256]{0,1:T(8,128)(2,1)S(1)}, u32[]{:S(2)}, u32[]{:S(2)}) collective-permute-start(bf16[512,256]{0,1:T(8,128)(2,1)} %reduce-scatter.2.cloned.1.call-done), channel_id=1, source_target_pairs={{0,0},{1,1},{2,8},{3,9},{4,16},{5,17},{6,24},{7,25},{8,10},{9,11},... | collective-permute-start | bytes 786440 | tf_op jit(solution)/shard_map/ppermute | solution.py:202
  108.8 19.3 %collective-permute-done.13 = bf16[512,256]{0,1:T(8,128)(2,1)S(1)} collective-permute-done((bf16[512,256]{0,1:T(8,128)(2,1)}, bf16[512,256]{0,1:T(8,128)(2,1)S(1)}, u32[]{:S(2)}, u32[]{:S(2)}) %collective-permute-start.13) | collective-permute-done | bytes 262176 | tf_op jit(solution)/shard_map/ppermute | solution.py:202
  (134 shorter events, 28.5 us)
Async XLA Ops:
  7.2 50.8 %copy-start = (bf16[512,1024]{1,0:T(8,128)(2,1)S(1)}, bf16[512,1024]{1,0:T(8,128)(2,1)}, u32[]{:S(2)}) copy-start(bf16[512,1024]{1,0:T(8,128)(2,1)} %param.10) | copy-start | bytes 3145732
  7.2 62.7 %all-gather.2.cloned.1.call-start = ((), (), s32[]{:S(2)}) async-start(), calls=%async_computation.2 | async-start | bytes 2359296 | tf_op jit(solution)/shard_map/all_gather | solution.py:104
  8.3 11.3 %collective-permute-start.2 = (bf16[128,256]{1,0:T(8,128)(2,1)S(1)}, bf16[128,256]{1,0:T(8,128)(2,1)S(1)}, u32[]{:S(2)}, u32[]{:S(2)}) collective-permute-start(bf16[128,256]{1,0:T(8,128)(2,1)S(1)} %get-tuple-element.53), channel_id=1, source_target_pairs={{0,24},{8,16},{16,8},{24,0},{1,25},{9,17},{17,9},{25,1},{2,26},{10... | collective-permute-start | bytes 196616 | tf_op jit(solution)/shard_map/ppermute | solution.py:77
  9.6 10.1 %collective-permute-start.1 = (bf16[128,256]{1,0:T(8,128)(2,1)S(1)}, bf16[128,256]{1,0:T(8,128)(2,1)S(1)}, u32[]{:S(2)}, u32[]{:S(2)}) collective-permute-start(bf16[128,256]{1,0:T(8,128)(2,1)S(1)} %get-tuple-element.54), channel_id=1, source_target_pairs={{0,16},{8,24},{16,0},{24,8},{1,17},{9,25},{17,1},{25,9},{2,18},{10... | collective-permute-start | bytes 196616 | tf_op jit(solution)/shard_map/ppermute | solution.py:77
  9.8 9.9 %collective-permute-start = (bf16[128,256]{1,0:T(8,128)(2,1)S(1)}, bf16[128,256]{1,0:T(8,128)(2,1)S(1)}, u32[]{:S(2)}, u32[]{:S(2)}) collective-permute-start(bf16[128,256]{1,0:T(8,128)(2,1)S(1)} %get-tuple-element.55), channel_id=1, source_target_pairs={{0,8},{8,0},{16,24},{24,16},{1,9},{9,1},{17,25},{25,17},{2,10},{10... | collective-permute-start | bytes 196616 | tf_op jit(solution)/shard_map/ppermute | solution.py:77
  21.6 17.7 %collective-permute-start.7 = (bf16[128,1024]{0,1:T(8,128)(2,1)}, bf16[128,1024]{0,1:T(8,128)(2,1)S(1)}, u32[]{:S(2)}, u32[]{:S(2)}) collective-permute-start(bf16[128,1024]{0,1:T(8,128)(2,1)} %bitcast.11), channel_id=1, source_target_pairs={{0,0},{1,4},{2,8},{3,12},{4,16},{5,20},{6,24},{7,28},{8,1},{9,5},{... | collective-permute-start | bytes 786440 | tf_op jit(solution)/shard_map/ppermute | solution.py:103
  24.7 13.9 %collective-permute-start.12 = (bf16[512,145]{0,1:T(8,128)(2,1)S(1)}, bf16[512,145]{0,1:T(8,128)(2,1)S(1)}, u32[]{:S(2)}, u32[]{:S(2)}) collective-permute-start(bf16[512,145]{0,1:T(8,128)(2,1)S(1)} %pad_maximum_fusion.5), channel_id=1, source_target_pairs={{8,0},{16,8},{24,16},{9,1},{17,9},{25,17},{10,2},{18,10},{26,18},{... | collective-permute-start | bytes 445448 | tf_op jit(solution)/shard_map/ppermute | solution.py:20
  29.2 10.8 %collective-permute-start.3 = (bf16[512,272]{0,1:T(8,128)(2,1)S(1)}, bf16[512,272]{0,1:T(8,128)(2,1)S(1)}, u32[]{:S(2)}, u32[]{:S(2)}) collective-permute-start(bf16[512,272]{0,1:T(8,128)(2,1)S(1)} %pad_maximum_fusion.3), channel_id=1, source_target_pairs={{0,8},{8,16},{16,24},{1,9},{9,17},{17,25},{2,10},{10,18},{18,26},{... | collective-permute-start | bytes 835592 | tf_op jit(solution)/shard_map/ppermute | solution.py:19
  40.0 65.6 %reduce-scatter.2.cloned.1.call-start = ((), (), s32[]{:S(2)}) async-start(), calls=%async_computation.1 | async-start | bytes 2359296 | tf_op jit(solution)/shard_map/reduce_scatter | solution.py:144
  42.7 5.4 %copy-start.23 = (f32[512]{0:T(512)S(1)}, f32[512]{0:T(512)}, u32[]{:S(2)}) copy-start(f32[512]{0:T(512)} %param.9) | copy-start | bytes 6148
  48.2 5.8 %slice-start = ((bf16[512,145]{0,1:T(8,128)(2,1)}), bf16[512,133]{0,1:T(8,128)(2,1)S(1)}, s32[]{:S(2)}) async-start(bf16[512,145]{0,1:T(8,128)(2,1)} %copy-done.11), calls=%async_computation.3 | async-start | bytes 278528 | tf_op jit(solution)/shard_map/slice | solution.py:28
  48.7 18.5 %collective-permute-start.6 = (bf16[512,256]{0,1:T(8,128)(2,1)S(1)}, bf16[512,256]{0,1:T(8,128)(2,1)S(1)}, u32[]{:S(2)}, u32[]{:S(2)}) collective-permute-start(bf16[512,256]{0,1:T(8,128)(2,1)S(1)} %get-tuple-element.16), channel_id=1, source_target_pairs={{0,24},{8,16},{16,8},{24,0},{1,25},{9,17},{17,9},{25,1},{2,26},{10... | collective-permute-start | bytes 786440 | tf_op jit(solution)/shard_map/ppermute | solution.py:77
  52.1 14.6 %collective-permute-start.5 = (bf16[512,256]{0,1:T(8,128)(2,1)S(1)}, bf16[512,256]{0,1:T(8,128)(2,1)S(1)}, u32[]{:S(2)}, u32[]{:S(2)}) collective-permute-start(bf16[512,256]{0,1:T(8,128)(2,1)S(1)} %get-tuple-element.16), channel_id=1, source_target_pairs={{0,16},{8,24},{16,0},{24,8},{1,17},{9,25},{17,1},{25,9},{2,18},{10... | collective-permute-start | bytes 786440 | tf_op jit(solution)/shard_map/ppermute | solution.py:77
  52.9 13.3 %collective-permute-start.4 = (bf16[512,256]{0,1:T(8,128)(2,1)S(1)}, bf16[512,256]{0,1:T(8,128)(2,1)S(1)}, u32[]{:S(2)}, u32[]{:S(2)}) collective-permute-start(bf16[512,256]{0,1:T(8,128)(2,1)S(1)} %get-tuple-element.16), channel_id=1, source_target_pairs={{0,8},{8,0},{16,24},{24,16},{1,9},{9,1},{17,25},{25,17},{2,10},{10... | collective-permute-start | bytes 786440 | tf_op jit(solution)/shard_map/ppermute | solution.py:77
  69.9 5.9 %copy-start.3 = (bf16[1024,1024]{0,1:T(8,128)(2,1)S(1)}, bf16[1024,1024]{0,1:T(8,128)(2,1)}, u32[]{:S(2)}) copy-start(bf16[1024,1024]{0,1:T(8,128)(2,1)} %all-gather.2.cloned.1.call-done) | copy-start | bytes 6291460
  73.1 7.3 %collective-permute-start.8 = (bf16[512,256]{0,1:T(8,128)(2,1)S(1)}, bf16[512,256]{0,1:T(8,128)(2,1)S(1)}, u32[]{:S(2)}, u32[]{:S(2)}) collective-permute-start(bf16[512,256]{0,1:T(8,128)(2,1)S(1)} %get-tuple-element.34), channel_id=1, source_target_pairs={{0,8},{8,0},{16,24},{24,16},{1,9},{9,1},{17,25},{25,17},{2,10},{10... | collective-permute-start | bytes 786440 | tf_op jit(solution)/shard_map/ppermute | solution.py:77
  73.2 12.4 %collective-permute-start.10 = (bf16[512,256]{0,1:T(8,128)(2,1)S(1)}, bf16[512,256]{0,1:T(8,128)(2,1)S(1)}, u32[]{:S(2)}, u32[]{:S(2)}) collective-permute-start(bf16[512,256]{0,1:T(8,128)(2,1)S(1)} %get-tuple-element.35), channel_id=1, source_target_pairs={{0,24},{8,16},{16,8},{24,0},{1,25},{9,17},{17,9},{25,1},{2,26},{10... | collective-permute-start | bytes 786440 | tf_op jit(solution)/shard_map/ppermute | solution.py:77
  74.2 12.7 %collective-permute-start.9 = (bf16[512,256]{0,1:T(8,128)(2,1)S(1)}, bf16[512,256]{0,1:T(8,128)(2,1)S(1)}, u32[]{:S(2)}, u32[]{:S(2)}) collective-permute-start(bf16[512,256]{0,1:T(8,128)(2,1)S(1)} %get-tuple-element.36), channel_id=1, source_target_pairs={{0,16},{8,24},{16,0},{24,8},{1,17},{9,25},{17,1},{25,9},{2,18},{10... | collective-permute-start | bytes 786440 | tf_op jit(solution)/shard_map/ppermute | solution.py:77
  77.2 11.9 %copy-start.5 = (bf16[512,256]{0,1:T(8,128)(2,1)S(1)}, bf16[512,256]{0,1:T(8,128)(2,1)}, u32[]{:S(2)}) copy-start(bf16[512,256]{0,1:T(8,128)(2,1)} %copy-done.4) | copy-start | bytes 786436
  87.1 6.7 %collective-permute-start.11 = (bf16[512,133]{0,1:T(8,128)(2,1)S(1)}, bf16[512,133]{0,1:T(8,128)(2,1)S(1)}, u32[]{:S(2)}, u32[]{:S(2)}) collective-permute-start(bf16[512,133]{0,1:T(8,128)(2,1)S(1)} %slice.652), channel_id=1, source_target_pairs={{8,0},{16,8},{24,16},{9,1},{17,9},{25,17},{10,2},{18,10},{26,18},{... | collective-permute-start | bytes 408584 | tf_op jit(solution)/shard_map/ppermute | solution.py:37
  94.9 5.5 %copy-start.1 = (f32[512,389]{0,1:T(8,128)S(1)}, f32[512,389]{0,1:T(8,128)}, u32[]{:S(2)}) copy-start(f32[512,389]{0,1:T(8,128)} %get-tuple-element.37) | copy-start | bytes 2390020
  94.9 5.5 %copy-start.2 = (f32[512,389]{0,1:T(8,128)S(1)}, f32[512,389]{0,1:T(8,128)}, u32[]{:S(2)}) copy-start(f32[512,389]{0,1:T(8,128)} %get-tuple-element.38) | copy-start | bytes 2390020
  94.9 5.5 %copy-start.24 = (f32[512]{0:T(512)S(1)}, f32[512]{0:T(512)}, u32[]{:S(2)}) copy-start(f32[512]{0:T(512)} %param.9) | copy-start | bytes 6148
  105.6 22.5 %collective-permute-start.13 = (bf16[512,256]{0,1:T(8,128)(2,1)}, bf16[512,256]{0,1:T(8,128)(2,1)S(1)}, u32[]{:S(2)}, u32[]{:S(2)}) collective-permute-start(bf16[512,256]{0,1:T(8,128)(2,1)} %reduce-scatter.2.cloned.1.call-done), channel_id=1, source_target_pairs={{0,0},{1,1},{2,8},{3,9},{4,16},{5,17},{6,24},{7,25},{8,10},{9,11},... | collective-permute-start | bytes 786440 | tf_op jit(solution)/shard_map/ppermute | solution.py:202
  (18 other events, 49.6 us)
Sparse Core Ops, SparseCore 0:
  40.1 28.1 all-gather.1
  70.6 34.8 reduce-scatter.1

commit v12 on v9

--- a/solution.py
+++ b/solution.py
@@ -110,11 +110,19 @@
     reach = taps_long + taps_short - 2
     keep = length + taps_short - 1
 
-    slab_piece = rows_of_slab(out_grad, n_seq, n_tp)
-    streams, slab_piece = lax.optimization_barrier((streams, slab_piece))
     query_in, key_value_in = halo(streams, "seq", reach, taps_short - 1)
-    slab_grad = rows_gathered(slab_piece, n_seq, n_tp)
-    slab_width = slab_grad.shape[0]
+    grad_rows = lax.all_gather(out_grad, "tp", axis=0, tiled=True)
+    slab_width = out_weight.shape[1]
+    slab_grad = jnp.concatenate(
+        [lax.dynamic_slice_in_dim(grad_rows, me * slab_width, slab_width, axis=0)]
+        + exchange(
+            lambda step: lax.dynamic_slice_in_dim(
+                grad_rows, partner(me, step, n_seq) * slab_width, slab_width, axis=0
+            ),
+            "seq",
+        ),
+        axis=1,
+    )
 
     key_value = short_correlate(key_value_in.astype(jnp.float32), feat_weight[1:, :, ::-1])
     key_feat, value_feat = key_value[0], key_value[1]
@@ -144,21 +152,24 @@
     slab_grad, gated_blocks = lax.optimization_barrier((slab_grad, gated_blocks))
     partial_grad = jnp.dot(out_weight, slab_grad, preferred_element_type=jnp.float32)
 
+    def relative(step):
+        if n_seq & (n_seq - 1) == 0:
+            return step
+        return (n_seq - step) % n_seq
+
     def grad_block(step):
-        start = partner(me, step, n_seq) * length
-        block = lax.dynamic_slice_in_dim(partial_grad, start, length, axis=1)
+        block = partial_grad[:, relative(step) * length : (relative(step) + 1) * length]
         return block.astype(jnp.bfloat16)
 
     arrived = exchange(grad_block, "seq")
-    gated_grad = lax.dynamic_slice_in_dim(partial_grad, me * length, length, axis=1)
+    gated_grad = partial_grad[:, :length]
     for block in arrived:
         gated_grad = gated_grad + block.astype(jnp.float32)
 
     scale = 1.0 / math.sqrt(length * n_seq)
     weight_sum = None
     for step, block in enumerate(gated_blocks):
-        origin = source(me, step, n_seq) if step else me
-        grad_part = lax.dynamic_slice_in_dim(slab_grad, origin * length, length, axis=1)
+        grad_part = slab_grad[:, step * length : (step + 1) * length]
         term = lax.dot_general(
             block, grad_part, (((1,), (1,)), ((), ())), preferred_element_type=jnp.float32
         )

time: 135 us -> 145 us (1.074)
  waiting for transfers between devices: 51.3 us -> 61.9 us
  starting transfers between devices: 26.5 us -> 18.5 us
  local copies, waits for them, and re-layouts: 15 us -> 17.7 us
  matrix products: 19.1 us -> 21.6 us
  other arithmetic: 7.22 us -> 9.58 us
    ppermute x9, waiting for transfers between devices: 20 us -> 39.9 us  [exchange(): got.append(lax.ppermute(block_of(step), axis, route))]
    ppermute x1, waiting for transfers between devices: 7.26 us -> 0.01 us  [halo(): high = lax.ppermute(high, axis, backward)]
    unnamed x46 -> x69, local copies, waits for them, and re-layouts: 3.36 us -> 7.5 us
    ppermute x9, starting transfers between devices: 11.8 us -> 8.14 us  [exchange(): got.append(lax.ppermute(block_of(step), axis, route))]
    reduce_scatter x1, waiting for transfers between devices: 3.69 us -> 0.02 us  [shards(): lax.psum_scatter(partial_out, 'tp', scatter_dimension=0, tiled=True)]
    dot_general x4, matrix products: 1.76 us -> 5.12 us  [shards(): jnp.dot(weight_t, block, preferred_element_type=jnp.float32)]
    ppermute x1 -> x0, starting transfers between devices: 3.04 us -> none  [rows_gathered(): moved = lax.ppermute(mine, ('seq', 'tp'), route)]
    slice x0 -> x4, local copies, waits for them, and re-layouts: none -> 2.69 us  [the longest x1 1.37 us: halo(): block[1, :, length - width:]]
  transfers between devices with their start and end apart: 16 -> 15, of which waited for: 8 -> 8; matrix products, arithmetic and copies ran while one was open for 27% -> 29% of each run, Pallas kernels for 0% -> 0%
where the time goes in v12:
time: 145 us; the launch traced here: 144 us
  waiting for transfers between devices  61.9 us (43%)
  matrix products  21.6 us (15%)
  starting transfers between devices  18.5 us (13%)
  local copies, waits for them, and re-layouts  17.7 us (12%)
  between operations  14.6 us (10%)
  other arithmetic  9.58 us (7%)
    ppermute x9, waiting for transfers between devices, exchange(): got.append(lax.ppermute(block_of(step), axis, route))  39.9 us
    ppermute x1, waiting for transfers between devices, shards(): mixed = lax.ppermute(output_sum, ('seq', 'tp'), mixed_route)  18.4 us
    conv_general_dilated x2, matrix products, correlate(): lax.conv_general_dilated(signal[None], taps[:, None, :], (1,), 'VALID', d...  10.8 us
    ppermute x9, starting transfers between devices, exchange(): got.append(lax.ppermute(block_of(step), axis, route))  8.14 us
    unnamed x69, local copies, waits for them, and re-layouts  7.5 us
    dot_general x4, matrix products, shards(): jnp.dot(weight_t, block, preferred_element_type=jnp.float32)  5.12 us
    dot_general x4, matrix products, shards(): lax.dot_general(block, grad_part, (((1,), (1,)), ((), ())), preferred_ele...  4.34 us
    ppermute x1, starting transfers between devices, halo(): low = lax.ppermute(low, axis, forward)  4.02 us
  transfers between devices with their start and end apart: 15, of which 8 were waited for; matrix products, arithmetic and copies ran while one was open for 29% of the time, Pallas kernels for 0%

profile of v12, /device:TPU:27, one launch (start us, length us, event | category | flops | bytes accessed | tf_op | source)
XLA Modules:
  0.0 143.7 jit_solution(7915775645468980671)
XLA Ops:
  8.4 1.4 fusion.44
  10.9 2.2 %collective-permute-start.1 = (bf16[512,145]{0,1:T(8,128)(2,1)}, bf16[512,145]{0,1:T(8,128)(2,1)}, u32[]{:S(2)}, u32[]{:S(2)}) collective-permute-start(bf16[512,145]{0,1:T(8,128)(2,1)} %pad_maximum_fusion.5), channel_id=1, source_target_pairs={{8,0},{16,8},{24,16},{9,1},{17,9},{25,17},{10,2},{18,10},{26,18},{... | collective-permute-start | bytes 445448 | tf_op jit(solution)/shard_map/ppermute | solution.py:20
  13.4 4.0 %collective-permute-start = (bf16[512,272]{0,1:T(8,128)(2,1)S(1)}, bf16[512,272]{0,1:T(8,128)(2,1)S(1)}, u32[]{:S(2)}, u32[]{:S(2)}) collective-permute-start(bf16[512,272]{0,1:T(8,128)(2,1)S(1)} %pad_maximum_fusion.4), channel_id=1, source_target_pairs={{0,8},{8,16},{16,24},{1,9},{9,17},{17,25},{2,10},{10,18},{18,26},{... | collective-permute-start | bytes 835592 | tf_op jit(solution)/shard_map/ppermute | solution.py:19
  27.7 5.4 %fusion.26 = f32[1,512,262]{1,0,2:T(1,128)S(1)} fusion(f32[512,1,128]{0,1,2:T(1,128)S(1)} %copy-done.13, f32[1,512,389]{1,2,0:T(8,128)S(1)} %get-tuple-element.31), kind=kOutput, calls=%fused_computation.60 | convolution fusion | flops 206045184 | bytes 1595392 | tf_op jit(solution)/shard_map/conv_general_dilated | solution.py:36
  35.7 1.5 %collective-permute-start.2 = (bf16[512,256]{0,1:T(8,128)(2,1)S(1)}, bf16[512,256]{0,1:T(8,128)(2,1)}, u32[]{:S(2)}, u32[]{:S(2)}) collective-permute-start(bf16[512,256]{0,1:T(8,128)(2,1)S(1)} %fusion.34), channel_id=1, source_target_pairs={{0,8},{8,0},{16,24},{24,16},{1,9},{9,1},{17,25},{25,17},{2,10},{10... | collective-permute-start | bytes 786440 | tf_op jit(solution)/shard_map/ppermute | solution.py:72
  38.5 3.8 %collective-permute-done.4 = bf16[512,256]{0,1:T(8,128)(2,1)S(1)} collective-permute-done((bf16[512,256]{0,1:T(8,128)(2,1)S(1)}, bf16[512,256]{0,1:T(8,128)(2,1)S(1)}, u32[]{:S(2)}, u32[]{:S(2)}) %collective-permute-start.4) | collective-permute-done | bytes 262176 | tf_op jit(solution)/shard_map/ppermute | solution.py:72
  43.5 5.8 %collective-permute-done.3 = bf16[512,256]{0,1:T(8,128)(2,1)S(1)} collective-permute-done((bf16[512,256]{0,1:T(8,128)(2,1)S(1)}, bf16[512,256]{0,1:T(8,128)(2,1)S(1)}, u32[]{:S(2)}, u32[]{:S(2)}) %collective-permute-start.3) | collective-permute-done | bytes 262176 | tf_op jit(solution)/shard_map/ppermute | solution.py:72
  51.3 2.9 %constant_dynamic-slice_fusion.3 = (bf16[1024,256]{1,0:T(8,128)(2,1)}, bf16[1024,256]{1,0:T(8,128)(2,1)}, bf16[1024,256]{1,0:T(8,128)(2,1)}, bf16[1024,256]{1,0:T(8,128)(2,1)}) fusion(bf16[4096,256]{1,0:T(8,128)(2,1)} %all-gather.2.cloned.1.call-done, s32[]{:T(128)S(6)} %select_n.12, s32[]{:T(128)S(6)} %select_n.15, s32[]{:T(128)S(6)} %select_n.14, ...), kind=kLoop, calls=%fused_computation.108 | loop fusion | bytes 4194320 | tf_op jit(solution)/shard_map/dynamic_slice | solution.py:117
  55.3 1.5 %collective-permute-start.5 = (bf16[1024,256]{1,0:T(8,128)(2,1)}, bf16[1024,256]{1,0:T(8,128)(2,1)}, u32[]{:S(2)}, u32[]{:S(2)}) collective-permute-start(bf16[1024,256]{1,0:T(8,128)(2,1)} %get-tuple-element.28), channel_id=1, source_target_pairs={{0,8},{8,0},{16,24},{24,16},{1,9},{9,1},{17,25},{25,17},{2,10},{10... | collective-permute-start | bytes 1572872 | tf_op jit(solution)/shard_map/ppermute | solution.py:72
  56.9 1.4 fusion.14
  58.3 1.5 %pad_maximum_fusion = bf16[4096,256]{0,1:T(8,128)(2,1)} fusion(bf16[1024,256]{0,1:T(8,128)(2,1)S(1)} %copy-done.5, bf16[1024,256]{0,1:T(8,128)(2,1)S(1)} %copy-done.6, bf16[1024,256]{0,1:T(8,128)(2,1)S(1)} %fusion.14, bf16[1024,256]{0,1:T(8,128)(2,1)S(1)} %copy-done.4), kind=kLoop, calls=%fused_computation | loop fusion | flops 8388608 | bytes 4194304 | tf_op jit(solution)/shard_map/concatenate | solution.py:142
  59.9 8.6 %collective-permute-done.7 = bf16[1024,256]{1,0:T(8,128)(2,1)} collective-permute-done((bf16[1024,256]{1,0:T(8,128)(2,1)}, bf16[1024,256]{1,0:T(8,128)(2,1)}, u32[]{:S(2)}, u32[]{:S(2)}) %collective-permute-start.7) | collective-permute-done | bytes 524320 | tf_op jit(solution)/shard_map/ppermute | solution.py:72
  68.5 12.0 %collective-permute-done.6 = bf16[1024,256]{1,0:T(8,128)(2,1)} collective-permute-done((bf16[1024,256]{1,0:T(8,128)(2,1)}, bf16[1024,256]{1,0:T(8,128)(2,1)}, u32[]{:S(2)}, u32[]{:S(2)}) %collective-permute-start.6) | collective-permute-done | bytes 524320 | tf_op jit(solution)/shard_map/ppermute | solution.py:72
  80.5 1.8 %pad_maximum_fusion.1 = bf16[1024,1024]{1,0:T(8,128)(2,1)S(1)} fusion(bf16[1024,256]{1,0:T(8,128)(2,1)} %collective-permute-done.7, bf16[1024,256]{1,0:T(8,128)(2,1)} %collective-permute-done.6, bf16[1024,256]{1,0:T(8,128)(2,1)} %collective-permute-done.5, bf16[1024,256]{1,0:T(8,128)(2,1)} %get-tuple-element.25), kind=kLoop, calls=%fused_computation.1 | loop fusion | flops 8388608 | bytes 4194304 | tf_op jit(solution)/shard_map/concatenate | solution.py:116
  84.9 1.5 %collective-permute-start.8 = (bf16[512,256]{0,1:T(8,128)(2,1)S(1)}, bf16[512,256]{0,1:T(8,128)(2,1)S(1)}, u32[]{:S(2)}, u32[]{:S(2)}) collective-permute-start(bf16[512,256]{0,1:T(8,128)(2,1)S(1)} %get-tuple-element.34), channel_id=1, source_target_pairs={{0,8},{8,0},{16,24},{24,16},{1,9},{9,1},{17,25},{25,17},{2,10},{10... | collective-permute-start | bytes 786440 | tf_op jit(solution)/shard_map/ppermute | solution.py:72
  86.9 1.4 fusion.38
  88.9 3.2 %collective-permute-done.10 = bf16[512,256]{0,1:T(8,128)(2,1)S(1)} collective-permute-done((bf16[512,256]{0,1:T(8,128)(2,1)S(1)}, bf16[512,256]{0,1:T(8,128)(2,1)S(1)}, u32[]{:S(2)}, u32[]{:S(2)}) %collective-permute-start.10) | collective-permute-done | bytes 262176 | tf_op jit(solution)/shard_map/ppermute | solution.py:72
  92.1 6.5 %collective-permute-done.9 = bf16[512,256]{0,1:T(8,128)(2,1)S(1)} collective-permute-done((bf16[512,256]{0,1:T(8,128)(2,1)S(1)}, bf16[512,256]{0,1:T(8,128)(2,1)S(1)}, u32[]{:S(2)}, u32[]{:S(2)}) %collective-permute-start.9) | collective-permute-done | bytes 262176 | tf_op jit(solution)/shard_map/ppermute | solution.py:72
  98.7 2.1 %collective-permute-start.11 = (bf16[512,133]{0,1:T(8,128)(2,1)S(1)}, bf16[512,133]{0,1:T(8,128)(2,1)S(1)}, u32[]{:S(2)}, u32[]{:S(2)}) collective-permute-start(bf16[512,133]{0,1:T(8,128)(2,1)S(1)} %slice.511), channel_id=1, source_target_pairs={{8,0},{16,8},{24,16},{9,1},{17,9},{25,17},{10,2},{18,10},{26,18},{... | collective-permute-start | bytes 408584 | tf_op jit(solution)/shard_map/ppermute | solution.py:32
  100.8 1.9 %add_convert_fusion = bf16[512,1024]{1,0:T(8,128)(2,1)} fusion(f32[512,1024]{1,0:T(8,128)S(1)} %fusion.36, f32[512,1024]{1,0:T(8,128)S(1)} %fusion.38, f32[512,1024]{1,0:T(8,128)S(1)} %fusion.40, bf16[512,256]{0,1:T(8,128)(2,1)S(1)} %copy-done.8, bf16[1024,1024]{1,0:T(8,128)(2,1)S(1)} %pad_maximum_fusion.1), kind=kOutput, calls=%fused_computation.2 | convolution fusion | flops 274726912 | bytes 8126464 | tf_op jit(solution)/shard_map/dot_general | solution.py:173
  102.8 3.5 %collective-permute-done.11 = bf16[512,133]{0,1:T(8,128)(2,1)S(1)} collective-permute-done((bf16[512,133]{0,1:T(8,128)(2,1)S(1)}, bf16[512,133]{0,1:T(8,128)(2,1)S(1)}, u32[]{:S(2)}, u32[]{:S(2)}) %collective-permute-start.11) | collective-permute-done | bytes 136224 | tf_op jit(solution)/shard_map/ppermute | solution.py:32
  107.3 5.4 %fusion.24 = f32[1,512,262]{1,0,2:T(1,128)S(1)} fusion(f32[512,1,128]{0,1,2:T(1,128)S(1)} %copy-done.12, f32[1,512,389]{1,2,0:T(8,128)S(1)} %bitcast.98), kind=kOutput, calls=%fused_computation.58 | convolution fusion | flops 206045184 | bytes 1595392 | tf_op jit(solution)/shard_map/conv_general_dilated | solution.py:36
  114.5 2.0 %collective-permute-start.12 = (bf16[512,256]{0,1:T(8,128)(2,1)}, bf16[512,256]{0,1:T(8,128)(2,1)S(1)}, u32[]{:S(2)}, u32[]{:S(2)}) collective-permute-start(bf16[512,256]{0,1:T(8,128)(2,1)} %reduce-scatter.2.cloned.1.call-done), channel_id=1, source_target_pairs={{0,0},{1,1},{2,8},{3,9},{4,16},{5,17},{6,24},{7,25},{8,10},{9,11},... | collective-permute-start | bytes 786440 | tf_op jit(solution)/shard_map/ppermute | solution.py:194
  117.7 18.4 %collective-permute-done.12 = bf16[512,256]{0,1:T(8,128)(2,1)S(1)} collective-permute-done((bf16[512,256]{0,1:T(8,128)(2,1)}, bf16[512,256]{0,1:T(8,128)(2,1)S(1)}, u32[]{:S(2)}, u32[]{:S(2)}) %collective-permute-start.12) | collective-permute-done | bytes 262176 | tf_op jit(solution)/shard_map/ppermute | solution.py:194
  (126 shorter events, 29.4 us)
Async XLA Ops:
  7.2 30.1 %copy-start = (bf16[512,1024]{1,0:T(8,128)(2,1)S(1)}, bf16[512,1024]{1,0:T(8,128)(2,1)}, u32[]{:S(2)}) copy-start(bf16[512,1024]{1,0:T(8,128)(2,1)} %param.10) | copy-start | bytes 3145732
  7.2 44.1 %all-gather.2.cloned.1.call-start = ((), (), s32[]{:S(2)}) async-start(), calls=%async_computation.2 | async-start | bytes 2359296 | tf_op jit(solution)/shard_map/all_gather | solution.py:114
  9.8 7.7 %copy-start.1 = (bf16[3,512,256]{2,1,0:T(8,128)(2,1)S(1)}, bf16[3,512,256]{2,1,0:T(8,128)(2,1)}, u32[]{:S(2)}) copy-start(bf16[3,512,256]{2,1,0:T(8,128)(2,1)} %param.6) | copy-start | bytes 2359300
  10.9 11.9 %collective-permute-start.1 = (bf16[512,145]{0,1:T(8,128)(2,1)}, bf16[512,145]{0,1:T(8,128)(2,1)}, u32[]{:S(2)}, u32[]{:S(2)}) collective-permute-start(bf16[512,145]{0,1:T(8,128)(2,1)} %pad_maximum_fusion.5), channel_id=1, source_target_pairs={{8,0},{16,8},{24,16},{9,1},{17,9},{25,17},{10,2},{18,10},{26,18},{... | collective-permute-start | bytes 445448 | tf_op jit(solution)/shard_map/ppermute | solution.py:20
  13.2 7.0 %copy-start.9 = (f32[512,128]{1,0:T(8,128)S(1)}, f32[512,128]{1,0:T(8,128)}, u32[]{:S(2)}) copy-start(f32[512,128]{1,0:T(8,128)} %param.8) | copy-start | bytes 786436
  13.4 11.0 %collective-permute-start = (bf16[512,272]{0,1:T(8,128)(2,1)S(1)}, bf16[512,272]{0,1:T(8,128)(2,1)S(1)}, u32[]{:S(2)}, u32[]{:S(2)}) collective-permute-start(bf16[512,272]{0,1:T(8,128)(2,1)S(1)} %pad_maximum_fusion.4), channel_id=1, source_target_pairs={{0,8},{8,16},{16,24},{1,9},{9,17},{17,25},{2,10},{10,18},{18,26},{... | collective-permute-start | bytes 835592 | tf_op jit(solution)/shard_map/ppermute | solution.py:19
  17.5 97.0 %reduce-scatter.2.cloned.1.call-start = ((), (), s32[]{:S(2)}) async-start(), calls=%async_computation.1 | async-start | bytes 2359296 | tf_op jit(solution)/shard_map/reduce_scatter | solution.py:143
  26.9 6.2 %copy-start.2 = (f32[512,389]{0,1:T(8,128)}, f32[512,389]{0,1:T(8,128)S(1)}, u32[]{:S(2)}) copy-start(f32[512,389]{0,1:T(8,128)S(1)} %get-tuple-element.30) | copy-start | bytes 2390020
  27.7 5.4 %copy-start.23 = (f32[512]{0:T(512)S(1)}, f32[512]{0:T(512)}, u32[]{:S(2)}) copy-start(f32[512]{0:T(512)} %param.9) | copy-start | bytes 6148
  34.5 7.7 %collective-permute-start.4 = (bf16[512,256]{0,1:T(8,128)(2,1)S(1)}, bf16[512,256]{0,1:T(8,128)(2,1)S(1)}, u32[]{:S(2)}, u32[]{:S(2)}) collective-permute-start(bf16[512,256]{0,1:T(8,128)(2,1)S(1)} %fusion.34), channel_id=1, source_target_pairs={{0,24},{8,16},{16,8},{24,0},{1,25},{9,17},{17,9},{25,1},{2,26},{10... | collective-permute-start | bytes 786440 | tf_op jit(solution)/shard_map/ppermute | solution.py:72
  35.7 13.6 %collective-permute-start.3 = (bf16[512,256]{0,1:T(8,128)(2,1)S(1)}, bf16[512,256]{0,1:T(8,128)(2,1)S(1)}, u32[]{:S(2)}, u32[]{:S(2)}) collective-permute-start(bf16[512,256]{0,1:T(8,128)(2,1)S(1)} %fusion.34), channel_id=1, source_target_pairs={{0,16},{8,24},{16,0},{24,8},{1,17},{9,25},{17,1},{25,9},{2,18},{10... | collective-permute-start | bytes 786440 | tf_op jit(solution)/shard_map/ppermute | solution.py:72
  35.7 21.2 %collective-permute-start.2 = (bf16[512,256]{0,1:T(8,128)(2,1)S(1)}, bf16[512,256]{0,1:T(8,128)(2,1)}, u32[]{:S(2)}, u32[]{:S(2)}) collective-permute-start(bf16[512,256]{0,1:T(8,128)(2,1)S(1)} %fusion.34), channel_id=1, source_target_pairs={{0,8},{8,0},{16,24},{24,16},{1,9},{9,1},{17,25},{25,17},{2,10},{10... | collective-permute-start | bytes 786440 | tf_op jit(solution)/shard_map/ppermute | solution.py:72
  42.2 7.1 %copy-start.7 = (bf16[512,256]{0,1:T(8,128)(2,1)}, bf16[512,256]{0,1:T(8,128)(2,1)S(1)}, u32[]{:S(2)}) copy-start(bf16[512,256]{0,1:T(8,128)(2,1)S(1)} %collective-permute-done.4) | copy-start | bytes 786436
  54.2 14.3 %collective-permute-start.7 = (bf16[1024,256]{1,0:T(8,128)(2,1)}, bf16[1024,256]{1,0:T(8,128)(2,1)}, u32[]{:S(2)}, u32[]{:S(2)}) collective-permute-start(bf16[1024,256]{1,0:T(8,128)(2,1)} %get-tuple-element.26), channel_id=1, source_target_pairs={{0,24},{8,16},{16,8},{24,0},{1,25},{9,17},{17,9},{25,1},{2,26},{10... | collective-permute-start | bytes 1572872 | tf_op jit(solution)/shard_map/ppermute | solution.py:72
  55.3 25.2 %collective-permute-start.6 = (bf16[1024,256]{1,0:T(8,128)(2,1)}, bf16[1024,256]{1,0:T(8,128)(2,1)}, u32[]{:S(2)}, u32[]{:S(2)}) collective-permute-start(bf16[1024,256]{1,0:T(8,128)(2,1)} %get-tuple-element.27), channel_id=1, source_target_pairs={{0,16},{8,24},{16,0},{24,8},{1,17},{9,25},{17,1},{25,9},{2,18},{10... | collective-permute-start | bytes 1572872 | tf_op jit(solution)/shard_map/ppermute | solution.py:72
  55.3 25.2 %collective-permute-start.5 = (bf16[1024,256]{1,0:T(8,128)(2,1)}, bf16[1024,256]{1,0:T(8,128)(2,1)}, u32[]{:S(2)}, u32[]{:S(2)}) collective-permute-start(bf16[1024,256]{1,0:T(8,128)(2,1)} %get-tuple-element.28), channel_id=1, source_target_pairs={{0,8},{8,0},{16,24},{24,16},{1,9},{9,1},{17,25},{25,17},{2,10},{10... | collective-permute-start | bytes 1572872 | tf_op jit(solution)/shard_map/ppermute | solution.py:72
  83.7 8.4 %collective-permute-start.10 = (bf16[512,256]{0,1:T(8,128)(2,1)S(1)}, bf16[512,256]{0,1:T(8,128)(2,1)S(1)}, u32[]{:S(2)}, u32[]{:S(2)}) collective-permute-start(bf16[512,256]{0,1:T(8,128)(2,1)S(1)} %get-tuple-element.35), channel_id=1, source_target_pairs={{0,24},{8,16},{16,8},{24,0},{1,25},{9,17},{17,9},{25,1},{2,26},{10... | collective-permute-start | bytes 786440 | tf_op jit(solution)/shard_map/ppermute | solution.py:72
  84.9 13.6 %collective-permute-start.9 = (bf16[512,256]{0,1:T(8,128)(2,1)S(1)}, bf16[512,256]{0,1:T(8,128)(2,1)S(1)}, u32[]{:S(2)}, u32[]{:S(2)}) collective-permute-start(bf16[512,256]{0,1:T(8,128)(2,1)S(1)} %get-tuple-element.36), channel_id=1, source_target_pairs={{0,16},{8,24},{16,0},{24,8},{1,17},{9,25},{17,1},{25,9},{2,18},{10... | collective-permute-start | bytes 786440 | tf_op jit(solution)/shard_map/ppermute | solution.py:72
  84.9 13.6 %collective-permute-start.8 = (bf16[512,256]{0,1:T(8,128)(2,1)S(1)}, bf16[512,256]{0,1:T(8,128)(2,1)S(1)}, u32[]{:S(2)}, u32[]{:S(2)}) collective-permute-start(bf16[512,256]{0,1:T(8,128)(2,1)S(1)} %get-tuple-element.34), channel_id=1, source_target_pairs={{0,8},{8,0},{16,24},{24,16},{1,9},{9,1},{17,25},{25,17},{2,10},{10... | collective-permute-start | bytes 786440 | tf_op jit(solution)/shard_map/ppermute | solution.py:72
  88.8 12.0 %copy-start.8 = (bf16[512,256]{0,1:T(8,128)(2,1)S(1)}, bf16[512,256]{0,1:T(8,128)(2,1)}, u32[]{:S(2)}) copy-start(bf16[512,256]{0,1:T(8,128)(2,1)} %copy-done.7) | copy-start | bytes 786436
  98.7 7.5 %collective-permute-start.11 = (bf16[512,133]{0,1:T(8,128)(2,1)S(1)}, bf16[512,133]{0,1:T(8,128)(2,1)S(1)}, u32[]{:S(2)}, u32[]{:S(2)}) collective-permute-start(bf16[512,133]{0,1:T(8,128)(2,1)S(1)} %slice.511), channel_id=1, source_target_pairs={{8,0},{16,8},{24,16},{9,1},{17,9},{25,17},{10,2},{18,10},{26,18},{... | collective-permute-start | bytes 408584 | tf_op jit(solution)/shard_map/ppermute | solution.py:32
  107.3 5.4 %copy-start.3 = (f32[512,389]{0,1:T(8,128)S(1)}, f32[512,389]{0,1:T(8,128)}, u32[]{:S(2)}) copy-start(f32[512,389]{0,1:T(8,128)} %copy-done.2) | copy-start | bytes 2390020
  107.3 5.4 %copy-start.24 = (f32[512]{0:T(512)S(1)}, f32[512]{0:T(512)}, u32[]{:S(2)}) copy-start(f32[512]{0:T(512)} %param.9) | copy-start | bytes 6148
  114.5 21.5 %collective-permute-start.12 = (bf16[512,256]{0,1:T(8,128)(2,1)}, bf16[512,256]{0,1:T(8,128)(2,1)S(1)}, u32[]{:S(2)}, u32[]{:S(2)}) collective-permute-start(bf16[512,256]{0,1:T(8,128)(2,1)} %reduce-scatter.2.cloned.1.call-done), channel_id=1, source_target_pairs={{0,0},{1,1},{2,8},{3,9},{4,16},{5,17},{6,24},{7,25},{8,10},{9,11},... | collective-permute-start | bytes 786440 | tf_op jit(solution)/shard_map/ppermute | solution.py:194
  (17 other events, 35.2 us)
Sparse Core Ops, SparseCore 0:
  17.6 28.5 all-gather.1
  60.0 35.0 reduce-scatter.1

commit v13 on v9

--- a/solution.py
+++ b/solution.py
@@ -127,11 +127,10 @@
     gated_blocks = [gated] + exchange(lambda step: gated, "seq")
     group = n_tp // n_seq
     weight_t = out_weight.T
-    pieces = [
-        jnp.dot(weight_t, block, preferred_element_type=jnp.float32).astype(jnp.bfloat16)
-        for block in gated_blocks
-    ]
-    partial_out = jnp.concatenate(pieces, axis=0)
+    partial_out = jnp.zeros((n_seq * slab_width, length), jnp.bfloat16)
+    for m, block in enumerate(gated_blocks):
+        piece = jnp.dot(weight_t, block, preferred_element_type=jnp.float32).astype(jnp.bfloat16)
+        partial_out = lax.dynamic_update_slice_in_dim(partial_out, piece, m * slab_width, axis=0)
     output_sum = lax.psum_scatter(partial_out, "tp", scatter_dimension=0, tiled=True)
     route = []
     for s in range(n_seq):

time: 135 us -> 136 us (level)
  matrix products: 19.1 us -> 21.7 us
  other arithmetic: 7.22 us -> 5.7 us
    dot_general x4, matrix products: 1.76 us -> 4.34 us  [shards(): jnp.dot(weight_t, block, preferred_element_type=jnp.float32)]
    dynamic_update_slice x0 -> x1, local copies, waits for them, and re-layouts: none -> 1.6 us  [shards(): lax.dynamic_update_slice_in_dim(partial_out, piece, m * slab_width, axis=0)]
    concatenate x1 -> x0, other arithmetic: 1.53 us -> none  [shards(): partial_out = jnp.concatenate(pieces, axis=0)]
    reduce_scatter x1, waiting for transfers between devices: 3.69 us -> 2.29 us  [shards(): lax.psum_scatter(partial_out, 'tp', scatter_dimension=0, tiled=True)]
    unnamed x46 -> x44, local copies, waits for them, and re-layouts: 3.36 us -> 3.78 us
  transfers between devices with their start and end apart: 16 -> 16, of which waited for: 8 -> 9; matrix products, arithmetic and copies ran while one was open for 27% -> 28% of each run, Pallas kernels for 0% -> 0%
where the time goes in v13:
time: 136 us; the launch traced here: 134 us
  waiting for transfers between devices  50.5 us (37%)
  starting transfers between devices  25.5 us (19%)
  matrix products  21.7 us (16%)
  local copies, waits for them, and re-layouts  16.3 us (12%)
  between operations  14.6 us (11%)
  other arithmetic  5.7 us (4%)
    ppermute x9, waiting for transfers between devices, exchange(): got.append(lax.ppermute(block_of(step), axis, route))  19.7 us
    ppermute x1, waiting for transfers between devices, shards(): mixed = lax.ppermute(output_sum, ('seq', 'tp'), mixed_route)  18.4 us
    ppermute x9, starting transfers between devices, exchange(): got.append(lax.ppermute(block_of(step), axis, route))  11.9 us
    conv_general_dilated x2, matrix products, correlate(): lax.conv_general_dilated(signal[None], taps[:, None, :], (1,), 'VALID', d...  11 us
    ppermute x1, waiting for transfers between devices, halo(): high = lax.ppermute(high, axis, backward)  7.26 us
    ppermute x1, starting transfers between devices, halo(): high = lax.ppermute(high, axis, backward)  4.49 us
    dot_general x4, matrix products, shards(): jnp.dot(weight_t, block, preferred_element_type=jnp.float32)  4.34 us
    unnamed x44, local copies, waits for them, and re-layouts  3.78 us
  transfers between devices with their start and end apart: 16, of which 9 were waited for; matrix products, arithmetic and copies ran while one was open for 28% of the time, Pallas kernels for 0%

profile of v13, /device:TPU:27, one launch (start us, length us, event | category | flops | bytes accessed | tf_op | source)
XLA Modules:
  0.0 134.2 jit_solution(3622029299796875788)
XLA Ops:
  14.3 1.9 %rev.8 = f32[512,128]{1,0:T(8,128)S(1)} reverse(f32[512,128]{1,0:T(8,128)} %param.8), dimensions={1} | reverse | bytes 524288 | tf_op jit(solution)/shard_map/rev | solution.py:123
  16.2 1.9 %copy.52 = f32[512,1,128]{0,1,2:T(1,128)} copy(f32[512,1,128]{2,0,1:T(8,128)} %bitcast.139) | data formatting | bytes 524288 | tf_op jit(solution)/shard_map/broadcast_in_dim | solution.py:38
  21.0 3.0 %collective-permute-start.8 = (bf16[128,1024]{0,1:T(8,128)(2,1)}, bf16[128,1024]{0,1:T(8,128)(2,1)}, u32[]{:S(2)}, u32[]{:S(2)}) collective-permute-start(bf16[128,1024]{0,1:T(8,128)(2,1)} %bitcast.11), channel_id=1, source_target_pairs={{0,0},{1,4},{2,8},{3,12},{4,16},{5,20},{6,24},{7,28},{8,1},{9,5},{... | collective-permute-start | bytes 786440 | tf_op jit(solution)/shard_map/ppermute | solution.py:98
  24.1 4.5 %collective-permute-start.4 = (bf16[512,145]{0,1:T(8,128)(2,1)S(1)}, bf16[512,145]{0,1:T(8,128)(2,1)S(1)}, u32[]{:S(2)}, u32[]{:S(2)}) collective-permute-start(bf16[512,145]{0,1:T(8,128)(2,1)S(1)} %pad_maximum_fusion.4), channel_id=1, source_target_pairs={{8,0},{16,8},{24,16},{9,1},{17,9},{25,17},{10,2},{18,10},{26,18},{... | collective-permute-start | bytes 445448 | tf_op jit(solution)/shard_map/ppermute | solution.py:20
  28.6 2.0 %collective-permute-start.3 = (bf16[512,272]{0,1:T(8,128)(2,1)S(1)}, bf16[512,272]{0,1:T(8,128)(2,1)S(1)}, u32[]{:S(2)}, u32[]{:S(2)}) collective-permute-start(bf16[512,272]{0,1:T(8,128)(2,1)S(1)} %pad_maximum_fusion.2), channel_id=1, source_target_pairs={{0,8},{8,16},{16,24},{1,9},{9,17},{17,25},{2,10},{10,18},{18,26},{... | collective-permute-start | bytes 835592 | tf_op jit(solution)/shard_map/ppermute | solution.py:19
  30.7 7.3 %collective-permute-done.4 = bf16[512,145]{0,1:T(8,128)(2,1)S(1)} collective-permute-done((bf16[512,145]{0,1:T(8,128)(2,1)S(1)}, bf16[512,145]{0,1:T(8,128)(2,1)S(1)}, u32[]{:S(2)}, u32[]{:S(2)}) %collective-permute-start.4) | collective-permute-done | bytes 148512 | tf_op jit(solution)/shard_map/ppermute | solution.py:20
  41.0 5.5 %fusion.29 = f32[1,512,262]{1,0,2:T(1,128)S(1)} fusion(f32[512,1,128]{0,1,2:T(1,128)S(1)} %copy-done.12, f32[1,512,389]{1,2,0:T(8,128)S(1)} %get-tuple-element.37), kind=kOutput, calls=%fused_computation.61 | convolution fusion | flops 206045184 | bytes 1595392 | tf_op jit(solution)/shard_map/conv_general_dilated | solution.py:36
  47.5 4.5 %collective-permute-start.7 = (bf16[512,256]{0,1:T(8,128)(2,1)S(1)}, bf16[512,256]{0,1:T(8,128)(2,1)S(1)}, u32[]{:S(2)}, u32[]{:S(2)}) collective-permute-start(bf16[512,256]{0,1:T(8,128)(2,1)S(1)} %fusion.35), channel_id=1, source_target_pairs={{0,24},{8,16},{16,8},{24,0},{1,25},{9,17},{17,9},{25,1},{2,26},{10... | collective-permute-start | bytes 786440 | tf_op jit(solution)/shard_map/ppermute | solution.py:72
  54.4 1.6 %dynamic_update_slice.12 = bf16[4096,256]{0,1:T(8,128)(2,1)} pad(bf16[1024,256]{0,1:T(8,128)(2,1)S(1)} %fusion.13, bf16[]{:T(256)} %constant.38.clone.1), padding=0_3072x0_0 | pad | bytes 2621442 | tf_op jit(solution)/shard_map/dynamic_update_slice | solution.py:133
  56.0 10.1 %collective-permute-done.5 = bf16[512,256]{0,1:T(8,128)(2,1)S(1)} collective-permute-done((bf16[512,256]{0,1:T(8,128)(2,1)S(1)}, bf16[512,256]{0,1:T(8,128)(2,1)S(1)}, u32[]{:S(2)}, u32[]{:S(2)}) %collective-permute-start.5) | collective-permute-done | bytes 262176 | tf_op jit(solution)/shard_map/ppermute | solution.py:72
  67.4 1.3 fusion.17
  70.8 3.0 %fusion.62 = f32[1024,512]{1,0:T(8,128)S(1)} fusion(bf16[1024,1024]{0,1:T(8,128)(2,1)} %all-gather.2.cloned.1.call-done, bf16[512,1024]{1,0:T(8,128)(2,1)S(1)} %copy-done), kind=kOutput, calls=%fused_computation.151 | convolution fusion | flops 1073741824 | bytes 5242880 | tf_op jit(solution)/shard_map/dot_general | solution.py:144
  74.4 2.3 %collective-permute-start.10 = (bf16[512,256]{0,1:T(8,128)(2,1)S(1)}, bf16[512,256]{0,1:T(8,128)(2,1)S(1)}, u32[]{:S(2)}, u32[]{:S(2)}) collective-permute-start(bf16[512,256]{0,1:T(8,128)(2,1)S(1)} %get-tuple-element.34), channel_id=1, source_target_pairs={{0,16},{8,24},{16,0},{24,8},{1,17},{9,25},{17,1},{25,9},{2,18},{10... | collective-permute-start | bytes 786440 | tf_op jit(solution)/shard_map/ppermute | solution.py:72
  78.1 3.1 %collective-permute-done.9 = bf16[512,256]{0,1:T(8,128)(2,1)S(1)} collective-permute-done((bf16[512,256]{0,1:T(8,128)(2,1)S(1)}, bf16[512,256]{0,1:T(8,128)(2,1)S(1)}, u32[]{:S(2)}, u32[]{:S(2)}) %collective-permute-start.9) | collective-permute-done | bytes 262176 | tf_op jit(solution)/shard_map/ppermute | solution.py:72
  81.2 4.5 %collective-permute-done.11 = bf16[512,256]{0,1:T(8,128)(2,1)S(1)} collective-permute-done((bf16[512,256]{0,1:T(8,128)(2,1)S(1)}, bf16[512,256]{0,1:T(8,128)(2,1)S(1)}, u32[]{:S(2)}, u32[]{:S(2)}) %collective-permute-start.11) | collective-permute-done | bytes 262176 | tf_op jit(solution)/shard_map/ppermute | solution.py:72
  85.7 2.0 %collective-permute-done.10 = bf16[512,256]{0,1:T(8,128)(2,1)S(1)} collective-permute-done((bf16[512,256]{0,1:T(8,128)(2,1)S(1)}, bf16[512,256]{0,1:T(8,128)(2,1)S(1)}, u32[]{:S(2)}, u32[]{:S(2)}) %collective-permute-start.10) | collective-permute-done | bytes 262176 | tf_op jit(solution)/shard_map/ppermute | solution.py:72
  87.8 2.1 %collective-permute-start.12 = (bf16[512,133]{0,1:T(8,128)(2,1)S(1)}, bf16[512,133]{0,1:T(8,128)(2,1)S(1)}, u32[]{:S(2)}, u32[]{:S(2)}) collective-permute-start(bf16[512,133]{0,1:T(8,128)(2,1)S(1)} %slice.479), channel_id=1, source_target_pairs={{8,0},{16,8},{24,16},{9,1},{17,9},{25,17},{10,2},{18,10},{26,18},{... | collective-permute-start | bytes 408584 | tf_op jit(solution)/shard_map/ppermute | solution.py:32
  89.9 1.9 %add_convert_fusion = bf16[512,1024]{1,0:T(8,128)(2,1)} fusion(f32[512,1024]{1,0:T(8,128)S(1)} %fusion.39, f32[512,1024]{1,0:T(8,128)S(1)} %fusion.41, f32[512,1024]{1,0:T(8,128)S(1)} %fusion.43, bf16[512,256]{0,1:T(8,128)(2,1)S(1)} %copy-done.5, bf16[1024,1024]{0,1:T(8,128)(2,1)S(1)} %copy-done.3, s32[]{:T(128)S(6)} %select_n.112), kind=kOutput, calls=%fused_computation.1 | convolution fusion | flops 274726912 | bytes 8126468 | tf_op jit(solution)/shard_map/dot_general | solution.py:161
  91.9 2.7 %collective-permute-done.12 = bf16[512,133]{0,1:T(8,128)(2,1)S(1)} collective-permute-done((bf16[512,133]{0,1:T(8,128)(2,1)S(1)}, bf16[512,133]{0,1:T(8,128)(2,1)S(1)}, u32[]{:S(2)}, u32[]{:S(2)}) %collective-permute-start.12) | collective-permute-done | bytes 136224 | tf_op jit(solution)/shard_map/ppermute | solution.py:32
  95.6 5.5 %fusion.27 = f32[1,512,262]{1,0,2:T(1,128)S(1)} fusion(f32[512,1,128]{0,1,2:T(1,128)S(1)} %copy-done.11, f32[1,512,389]{1,2,0:T(8,128)S(1)} %bitcast.138), kind=kOutput, calls=%fused_computation.59 | convolution fusion | flops 206045184 | bytes 1595392 | tf_op jit(solution)/shard_map/conv_general_dilated | solution.py:36
  101.5 1.3 fusion.7
  102.8 2.3 %reduce-scatter.2.cloned.1.call-done = bf16[512,256]{0,1:T(8,128)(2,1)} async-done(((bf16[4096,256]{0,1:T(8,128)(2,1)}), bf16[512,256]{0,1:T(8,128)(2,1)}) %reduce-scatter.2.cloned.1.call-update) | async-done | bytes 262160 | tf_op jit(solution)/shard_map/reduce_scatter | solution.py:134
  105.1 1.9 %collective-permute-start.13 = (bf16[512,256]{0,1:T(8,128)(2,1)}, bf16[512,256]{0,1:T(8,128)(2,1)S(1)}, u32[]{:S(2)}, u32[]{:S(2)}) collective-permute-start(bf16[512,256]{0,1:T(8,128)(2,1)} %reduce-scatter.2.cloned.1.call-done), channel_id=1, source_target_pairs={{0,0},{1,1},{2,8},{3,9},{4,16},{5,17},{6,24},{7,25},{8,10},{9,11},... | collective-permute-start | bytes 786440 | tf_op jit(solution)/shard_map/ppermute | solution.py:182
  108.2 18.4 %collective-permute-done.13 = bf16[512,256]{0,1:T(8,128)(2,1)S(1)} collective-permute-done((bf16[512,256]{0,1:T(8,128)(2,1)}, bf16[512,256]{0,1:T(8,128)(2,1)S(1)}, u32[]{:S(2)}, u32[]{:S(2)}) %collective-permute-start.13) | collective-permute-done | bytes 262176 | tf_op jit(solution)/shard_map/ppermute | solution.py:182
  (109 shorter events, 25.0 us)
Async XLA Ops:
  7.2 46.8 %copy-start = (bf16[512,1024]{1,0:T(8,128)(2,1)S(1)}, bf16[512,1024]{1,0:T(8,128)(2,1)}, u32[]{:S(2)}) copy-start(bf16[512,1024]{1,0:T(8,128)(2,1)} %param.10) | copy-start | bytes 3145732
  7.2 63.6 %all-gather.2.cloned.1.call-start = ((), (), s32[]{:S(2)}) async-start(), calls=%async_computation.2 | async-start | bytes 2359296 | tf_op jit(solution)/shard_map/all_gather | solution.py:99
  8.3 10.7 %collective-permute-start.2 = (bf16[128,256]{1,0:T(8,128)(2,1)S(1)}, bf16[128,256]{1,0:T(8,128)(2,1)S(1)}, u32[]{:S(2)}, u32[]{:S(2)}) collective-permute-start(bf16[128,256]{1,0:T(8,128)(2,1)S(1)} %get-tuple-element.52), channel_id=1, source_target_pairs={{0,24},{8,16},{16,8},{24,0},{1,25},{9,17},{17,9},{25,1},{2,26},{10... | collective-permute-start | bytes 196616 | tf_op jit(solution)/shard_map/ppermute | solution.py:72
  9.6 9.5 %collective-permute-start.1 = (bf16[128,256]{1,0:T(8,128)(2,1)S(1)}, bf16[128,256]{1,0:T(8,128)(2,1)S(1)}, u32[]{:S(2)}, u32[]{:S(2)}) collective-permute-start(bf16[128,256]{1,0:T(8,128)(2,1)S(1)} %get-tuple-element.53), channel_id=1, source_target_pairs={{0,16},{8,24},{16,0},{24,8},{1,17},{9,25},{17,1},{25,9},{2,18},{10... | collective-permute-start | bytes 196616 | tf_op jit(solution)/shard_map/ppermute | solution.py:72
  9.8 9.3 %collective-permute-start = (bf16[128,256]{1,0:T(8,128)(2,1)S(1)}, bf16[128,256]{1,0:T(8,128)(2,1)S(1)}, u32[]{:S(2)}, u32[]{:S(2)}) collective-permute-start(bf16[128,256]{1,0:T(8,128)(2,1)S(1)} %get-tuple-element.54), channel_id=1, source_target_pairs={{0,8},{8,0},{16,24},{24,16},{1,9},{9,1},{17,25},{25,17},{2,10},{10... | collective-permute-start | bytes 196616 | tf_op jit(solution)/shard_map/ppermute | solution.py:72
  14.3 32.4 %copy-start.13 = (f32[512,1]{0,1:T(1,128)}, f32[512,1]{0,1:T(1,128)S(1)}, u32[]{:S(2)}) copy-start(f32[512,1]{0,1:T(1,128)S(1)} %get-tuple-element.77) | copy-start | bytes 6148
  21.0 17.0 %collective-permute-start.8 = (bf16[128,1024]{0,1:T(8,128)(2,1)}, bf16[128,1024]{0,1:T(8,128)(2,1)}, u32[]{:S(2)}, u32[]{:S(2)}) collective-permute-start(bf16[128,1024]{0,1:T(8,128)(2,1)} %bitcast.11), channel_id=1, source_target_pairs={{0,0},{1,4},{2,8},{3,12},{4,16},{5,20},{6,24},{7,28},{8,1},{9,5},{... | collective-permute-start | bytes 786440 | tf_op jit(solution)/shard_map/ppermute | solution.py:98
  24.1 13.9 %collective-permute-start.4 = (bf16[512,145]{0,1:T(8,128)(2,1)S(1)}, bf16[512,145]{0,1:T(8,128)(2,1)S(1)}, u32[]{:S(2)}, u32[]{:S(2)}) collective-permute-start(bf16[512,145]{0,1:T(8,128)(2,1)S(1)} %pad_maximum_fusion.4), channel_id=1, source_target_pairs={{8,0},{16,8},{24,16},{9,1},{17,9},{25,17},{10,2},{18,10},{26,18},{... | collective-permute-start | bytes 445448 | tf_op jit(solution)/shard_map/ppermute | solution.py:20
  28.6 9.7 %collective-permute-start.3 = (bf16[512,272]{0,1:T(8,128)(2,1)S(1)}, bf16[512,272]{0,1:T(8,128)(2,1)S(1)}, u32[]{:S(2)}, u32[]{:S(2)}) collective-permute-start(bf16[512,272]{0,1:T(8,128)(2,1)S(1)} %pad_maximum_fusion.2), channel_id=1, source_target_pairs={{0,8},{8,16},{16,24},{1,9},{9,17},{17,25},{2,10},{10,18},{18,26},{... | collective-permute-start | bytes 835592 | tf_op jit(solution)/shard_map/ppermute | solution.py:19
  38.0 67.1 %reduce-scatter.2.cloned.1.call-start = ((), (), s32[]{:S(2)}) async-start(), calls=%async_computation.1 | async-start | bytes 2359296 | tf_op jit(solution)/shard_map/reduce_scatter | solution.py:134
  40.2 6.2 %copy-start.1 = (f32[512,389]{0,1:T(8,128)}, f32[512,389]{0,1:T(8,128)S(1)}, u32[]{:S(2)}) copy-start(f32[512,389]{0,1:T(8,128)S(1)} %get-tuple-element.36) | copy-start | bytes 2390020
  41.0 5.5 %copy-start.15 = (f32[512]{0:T(512)S(1)}, f32[512]{0:T(512)}, u32[]{:S(2)}) copy-start(f32[512]{0:T(512)} %param.9) | copy-start | bytes 6148
  47.5 21.2 %collective-permute-start.7 = (bf16[512,256]{0,1:T(8,128)(2,1)S(1)}, bf16[512,256]{0,1:T(8,128)(2,1)S(1)}, u32[]{:S(2)}, u32[]{:S(2)}) collective-permute-start(bf16[512,256]{0,1:T(8,128)(2,1)S(1)} %fusion.35), channel_id=1, source_target_pairs={{0,24},{8,16},{16,8},{24,0},{1,25},{9,17},{17,9},{25,1},{2,26},{10... | collective-permute-start | bytes 786440 | tf_op jit(solution)/shard_map/ppermute | solution.py:72
  52.0 15.4 %collective-permute-start.6 = (bf16[512,256]{0,1:T(8,128)(2,1)S(1)}, bf16[512,256]{0,1:T(8,128)(2,1)S(1)}, u32[]{:S(2)}, u32[]{:S(2)}) collective-permute-start(bf16[512,256]{0,1:T(8,128)(2,1)S(1)} %fusion.35), channel_id=1, source_target_pairs={{0,16},{8,24},{16,0},{24,8},{1,17},{9,25},{17,1},{25,9},{2,18},{10... | collective-permute-start | bytes 786440 | tf_op jit(solution)/shard_map/ppermute | solution.py:72
  52.8 13.2 %collective-permute-start.5 = (bf16[512,256]{0,1:T(8,128)(2,1)S(1)}, bf16[512,256]{0,1:T(8,128)(2,1)S(1)}, u32[]{:S(2)}, u32[]{:S(2)}) collective-permute-start(bf16[512,256]{0,1:T(8,128)(2,1)S(1)} %fusion.35), channel_id=1, source_target_pairs={{0,8},{8,0},{16,24},{24,16},{1,9},{9,1},{17,25},{25,17},{2,10},{10... | collective-permute-start | bytes 786440 | tf_op jit(solution)/shard_map/ppermute | solution.py:72
  70.8 5.9 %copy-start.3 = (bf16[1024,1024]{0,1:T(8,128)(2,1)S(1)}, bf16[1024,1024]{0,1:T(8,128)(2,1)}, u32[]{:S(2)}) copy-start(bf16[1024,1024]{0,1:T(8,128)(2,1)} %all-gather.2.cloned.1.call-done) | copy-start | bytes 6291460
  74.0 7.2 %collective-permute-start.9 = (bf16[512,256]{0,1:T(8,128)(2,1)S(1)}, bf16[512,256]{0,1:T(8,128)(2,1)S(1)}, u32[]{:S(2)}, u32[]{:S(2)}) collective-permute-start(bf16[512,256]{0,1:T(8,128)(2,1)S(1)} %get-tuple-element.32), channel_id=1, source_target_pairs={{0,8},{8,0},{16,24},{24,16},{1,9},{9,1},{17,25},{25,17},{2,10},{10... | collective-permute-start | bytes 786440 | tf_op jit(solution)/shard_map/ppermute | solution.py:72
  74.0 11.6 %collective-permute-start.11 = (bf16[512,256]{0,1:T(8,128)(2,1)S(1)}, bf16[512,256]{0,1:T(8,128)(2,1)S(1)}, u32[]{:S(2)}, u32[]{:S(2)}) collective-permute-start(bf16[512,256]{0,1:T(8,128)(2,1)S(1)} %get-tuple-element.33), channel_id=1, source_target_pairs={{0,24},{8,16},{16,8},{24,0},{1,25},{9,17},{17,9},{25,1},{2,26},{10... | collective-permute-start | bytes 786440 | tf_op jit(solution)/shard_map/ppermute | solution.py:72
  74.4 13.3 %collective-permute-start.10 = (bf16[512,256]{0,1:T(8,128)(2,1)S(1)}, bf16[512,256]{0,1:T(8,128)(2,1)S(1)}, u32[]{:S(2)}, u32[]{:S(2)}) collective-permute-start(bf16[512,256]{0,1:T(8,128)(2,1)S(1)} %get-tuple-element.34), channel_id=1, source_target_pairs={{0,16},{8,24},{16,0},{24,8},{1,17},{9,25},{17,1},{25,9},{2,18},{10... | collective-permute-start | bytes 786440 | tf_op jit(solution)/shard_map/ppermute | solution.py:72
  78.1 11.9 %copy-start.5 = (bf16[512,256]{0,1:T(8,128)(2,1)S(1)}, bf16[512,256]{0,1:T(8,128)(2,1)}, u32[]{:S(2)}) copy-start(bf16[512,256]{0,1:T(8,128)(2,1)} %copy-done.4) | copy-start | bytes 786436
  87.8 6.7 %collective-permute-start.12 = (bf16[512,133]{0,1:T(8,128)(2,1)S(1)}, bf16[512,133]{0,1:T(8,128)(2,1)S(1)}, u32[]{:S(2)}, u32[]{:S(2)}) collective-permute-start(bf16[512,133]{0,1:T(8,128)(2,1)S(1)} %slice.479), channel_id=1, source_target_pairs={{8,0},{16,8},{24,16},{9,1},{17,9},{25,17},{10,2},{18,10},{26,18},{... | collective-permute-start | bytes 408584 | tf_op jit(solution)/shard_map/ppermute | solution.py:32
  95.6 5.5 %copy-start.2 = (f32[512,389]{0,1:T(8,128)S(1)}, f32[512,389]{0,1:T(8,128)}, u32[]{:S(2)}) copy-start(f32[512,389]{0,1:T(8,128)} %copy-done.1) | copy-start | bytes 2390020
  95.6 5.5 %copy-start.16 = (f32[512]{0:T(512)S(1)}, f32[512]{0:T(512)}, u32[]{:S(2)}) copy-start(f32[512]{0:T(512)} %param.9) | copy-start | bytes 6148
  105.1 21.4 %collective-permute-start.13 = (bf16[512,256]{0,1:T(8,128)(2,1)}, bf16[512,256]{0,1:T(8,128)(2,1)S(1)}, u32[]{:S(2)}, u32[]{:S(2)}) collective-permute-start(bf16[512,256]{0,1:T(8,128)(2,1)} %reduce-scatter.2.cloned.1.call-done), channel_id=1, source_target_pairs={{0,0},{1,1},{2,8},{3,9},{4,16},{5,17},{6,24},{7,25},{8,10},{9,11},... | collective-permute-start | bytes 786440 | tf_op jit(solution)/shard_map/ppermute | solution.py:182
  (9 other events, 19.8 us)
Sparse Core Ops, SparseCore 0:
  38.2 28.1 all-gather.1
  70.9 34.2 reduce-scatter.1

commit v14 on v9

--- a/solution.py
+++ b/solution.py
@@ -3,6 +3,7 @@
 import jax
 import jax.numpy as jnp
 from jax import lax
+from jax.experimental.layout import Layout, with_layout_constraint
 from jax.sharding import PartitionSpec as P
 
 
@@ -132,6 +133,7 @@
         for block in gated_blocks
     ]
     partial_out = jnp.concatenate(pieces, axis=0)
+    partial_out = with_layout_constraint(partial_out, Layout(major_to_minor=(0, 1)))
     output_sum = lax.psum_scatter(partial_out, "tp", scatter_dimension=0, tiled=True)
     route = []
     for s in range(n_seq):

time: 135 us -> 135 us (level)
  transfers between devices with their start and end apart: 16 -> 16, of which waited for: 8 -> 9; matrix products, arithmetic and copies ran while one was open for 27% -> 27% of each run, Pallas kernels for 0% -> 0%
where the time goes in v14:
time: 135 us; the launch traced here: 134 us
  waiting for transfers between devices  52.3 us (39%)
  starting transfers between devices  25.5 us (19%)
  matrix products  19.6 us (15%)
  local copies, waits for them, and re-layouts  14.7 us (11%)
  between operations  14.7 us (11%)
  other arithmetic  7.19 us (5%)
    ppermute x9, waiting for transfers between devices, exchange(): got.append(lax.ppermute(block_of(step), axis, route))  21.1 us
    ppermute x1, waiting for transfers between devices, shards(): mixed = lax.ppermute(output_sum, ('seq', 'tp'), mixed_route)  18.5 us
    ppermute x9, starting transfers between devices, exchange(): got.append(lax.ppermute(block_of(step), axis, route))  11.8 us
    conv_general_dilated x2, matrix products, correlate(): lax.conv_general_dilated(signal[None], taps[:, None, :], (1,), 'VALID', d...  11 us
    ppermute x1, waiting for transfers between devices, halo(): high = lax.ppermute(high, axis, backward)  7.26 us
    ppermute x1, starting transfers between devices, halo(): high = lax.ppermute(high, axis, backward)  4.49 us
    dot_general x4, matrix products, shards(): lax.dot_general(block, grad_part, (((1,), (1,)), ((), ())), preferred_ele...  3.3 us
    unnamed x46, local copies, waits for them, and re-layouts  3.11 us
  transfers between devices with their start and end apart: 16, of which 9 were waited for; matrix products, arithmetic and copies ran while one was open for 27% of the time, Pallas kernels for 0%

profile of v14, /device:TPU:27, one launch (start us, length us, event | category | flops | bytes accessed | tf_op | source)
XLA Modules:
  0.0 133.9 jit_solution(5119461057147355541)
XLA Ops:
  14.3 1.9 %rev.8 = f32[512,128]{1,0:T(8,128)S(1)} reverse(f32[512,128]{1,0:T(8,128)} %param.8), dimensions={1} | reverse | bytes 524288 | tf_op jit(solution)/shard_map/rev | solution.py:124
  16.2 1.9 %copy.62 = f32[512,1,128]{0,1,2:T(1,128)} copy(f32[512,1,128]{2,0,1:T(8,128)} %bitcast.133) | data formatting | bytes 524288 | tf_op jit(solution)/shard_map/broadcast_in_dim | solution.py:39
  21.0 3.0 %collective-permute-start.8 = (bf16[128,1024]{0,1:T(8,128)(2,1)}, bf16[128,1024]{0,1:T(8,128)(2,1)}, u32[]{:S(2)}, u32[]{:S(2)}) collective-permute-start(bf16[128,1024]{0,1:T(8,128)(2,1)} %bitcast.11), channel_id=1, source_target_pairs={{0,0},{1,4},{2,8},{3,12},{4,16},{5,20},{6,24},{7,28},{8,1},{9,5},{... | collective-permute-start | bytes 786440 | tf_op jit(solution)/shard_map/ppermute | solution.py:99
  24.1 4.5 %collective-permute-start.4 = (bf16[512,145]{0,1:T(8,128)(2,1)S(1)}, bf16[512,145]{0,1:T(8,128)(2,1)S(1)}, u32[]{:S(2)}, u32[]{:S(2)}) collective-permute-start(bf16[512,145]{0,1:T(8,128)(2,1)S(1)} %pad_maximum_fusion.5), channel_id=1, source_target_pairs={{8,0},{16,8},{24,16},{9,1},{17,9},{25,17},{10,2},{18,10},{26,18},{... | collective-permute-start | bytes 445448 | tf_op jit(solution)/shard_map/ppermute | solution.py:21
  28.6 2.0 %collective-permute-start.3 = (bf16[512,272]{0,1:T(8,128)(2,1)S(1)}, bf16[512,272]{0,1:T(8,128)(2,1)S(1)}, u32[]{:S(2)}, u32[]{:S(2)}) collective-permute-start(bf16[512,272]{0,1:T(8,128)(2,1)S(1)} %pad_maximum_fusion.3), channel_id=1, source_target_pairs={{0,8},{8,16},{16,24},{1,9},{9,17},{17,25},{2,10},{10,18},{18,26},{... | collective-permute-start | bytes 835592 | tf_op jit(solution)/shard_map/ppermute | solution.py:20
  30.7 7.3 %collective-permute-done.4 = bf16[512,145]{0,1:T(8,128)(2,1)S(1)} collective-permute-done((bf16[512,145]{0,1:T(8,128)(2,1)S(1)}, bf16[512,145]{0,1:T(8,128)(2,1)S(1)}, u32[]{:S(2)}, u32[]{:S(2)}) %collective-permute-start.4) | collective-permute-done | bytes 148512 | tf_op jit(solution)/shard_map/ppermute | solution.py:21
  38.6 1.3 fusion
  41.1 5.5 %fusion.26 = f32[1,512,262]{1,0,2:T(1,128)S(1)} fusion(f32[512,1,128]{0,1,2:T(1,128)S(1)} %copy-done.13, f32[1,512,389]{1,2,0:T(8,128)S(1)} %get-tuple-element.37), kind=kOutput, calls=%fused_computation.59 | convolution fusion | flops 206045184 | bytes 1595392 | tf_op jit(solution)/shard_map/conv_general_dilated | solution.py:37
  47.6 4.5 %collective-permute-start.7 = (bf16[512,256]{0,1:T(8,128)(2,1)S(1)}, bf16[512,256]{0,1:T(8,128)(2,1)S(1)}, u32[]{:S(2)}, u32[]{:S(2)}) collective-permute-start(bf16[512,256]{0,1:T(8,128)(2,1)S(1)} %fusion.32), channel_id=1, source_target_pairs={{0,24},{8,16},{16,8},{24,0},{1,25},{9,17},{17,9},{25,1},{2,26},{10... | collective-permute-start | bytes 786440 | tf_op jit(solution)/shard_map/ppermute | solution.py:73
  54.6 11.6 %collective-permute-done.5 = bf16[512,256]{0,1:T(8,128)(2,1)S(1)} collective-permute-done((bf16[512,256]{0,1:T(8,128)(2,1)S(1)}, bf16[512,256]{0,1:T(8,128)(2,1)S(1)}, u32[]{:S(2)}, u32[]{:S(2)}) %collective-permute-start.5) | collective-permute-done | bytes 262176 | tf_op jit(solution)/shard_map/ppermute | solution.py:73
  68.7 1.5 %pad_maximum_fusion = bf16[4096,256]{1,0:T(8,128)(2,1)} fusion(bf16[1024,256]{1,0:T(8,128)(2,1)S(1)} %fusion.16, bf16[1024,256]{1,0:T(8,128)(2,1)S(1)} %fusion.15, bf16[1024,256]{1,0:T(8,128)(2,1)S(1)} %fusion.14, bf16[1024,256]{1,0:T(8,128)(2,1)S(1)} %fusion.13), kind=kLoop, calls=%fused_computation.1 | loop fusion | flops 8388608 | bytes 4194304 | tf_op jit(solution)/shard_map/concatenate | solution.py:135
  70.3 3.0 %fusion.59 = f32[1024,512]{1,0:T(8,128)S(1)} fusion(bf16[1024,1024]{0,1:T(8,128)(2,1)} %all-gather.2.cloned.1.call-done, bf16[512,1024]{1,0:T(8,128)(2,1)S(1)} %copy-done), kind=kOutput, calls=%fused_computation.149 | convolution fusion | flops 1073741824 | bytes 5242880 | tf_op jit(solution)/shard_map/dot_general | solution.py:147
  74.4 1.7 %collective-permute-start.10 = (bf16[512,256]{0,1:T(8,128)(2,1)S(1)}, bf16[512,256]{0,1:T(8,128)(2,1)S(1)}, u32[]{:S(2)}, u32[]{:S(2)}) collective-permute-start(bf16[512,256]{0,1:T(8,128)(2,1)S(1)} %get-tuple-element.34), channel_id=1, source_target_pairs={{0,16},{8,24},{16,0},{24,8},{1,17},{9,25},{17,1},{25,9},{2,18},{10... | collective-permute-start | bytes 786440 | tf_op jit(solution)/shard_map/ppermute | solution.py:73
  77.6 3.1 %collective-permute-done.9 = bf16[512,256]{0,1:T(8,128)(2,1)S(1)} collective-permute-done((bf16[512,256]{0,1:T(8,128)(2,1)S(1)}, bf16[512,256]{0,1:T(8,128)(2,1)S(1)}, u32[]{:S(2)}, u32[]{:S(2)}) %collective-permute-start.9) | collective-permute-done | bytes 262176 | tf_op jit(solution)/shard_map/ppermute | solution.py:73
  80.7 5.1 %collective-permute-done.11 = bf16[512,256]{0,1:T(8,128)(2,1)S(1)} collective-permute-done((bf16[512,256]{0,1:T(8,128)(2,1)S(1)}, bf16[512,256]{0,1:T(8,128)(2,1)S(1)}, u32[]{:S(2)}, u32[]{:S(2)}) %collective-permute-start.11) | collective-permute-done | bytes 262176 | tf_op jit(solution)/shard_map/ppermute | solution.py:73
  85.7 1.4 %collective-permute-done.10 = bf16[512,256]{0,1:T(8,128)(2,1)S(1)} collective-permute-done((bf16[512,256]{0,1:T(8,128)(2,1)S(1)}, bf16[512,256]{0,1:T(8,128)(2,1)S(1)}, u32[]{:S(2)}, u32[]{:S(2)}) %collective-permute-start.10) | collective-permute-done | bytes 262176 | tf_op jit(solution)/shard_map/ppermute | solution.py:73
  87.3 2.1 %collective-permute-start.12 = (bf16[512,133]{0,1:T(8,128)(2,1)S(1)}, bf16[512,133]{0,1:T(8,128)(2,1)S(1)}, u32[]{:S(2)}, u32[]{:S(2)}) collective-permute-start(bf16[512,133]{0,1:T(8,128)(2,1)S(1)} %slice.479), channel_id=1, source_target_pairs={{8,0},{16,8},{24,16},{9,1},{17,9},{25,17},{10,2},{18,10},{26,18},{... | collective-permute-start | bytes 408584 | tf_op jit(solution)/shard_map/ppermute | solution.py:33
  89.4 1.9 %add_convert_fusion = bf16[512,1024]{1,0:T(8,128)(2,1)} fusion(f32[512,1024]{1,0:T(8,128)S(1)} %fusion.36, f32[512,1024]{1,0:T(8,128)S(1)} %fusion.38, f32[512,1024]{1,0:T(8,128)S(1)} %fusion.40, bf16[512,256]{0,1:T(8,128)(2,1)S(1)} %copy-done.5, bf16[1024,1024]{0,1:T(8,128)(2,1)S(1)} %copy-done.3, s32[]{:T(128)S(6)} %select_n.112), kind=kOutput, calls=%fused_computation.2 | convolution fusion | flops 274726912 | bytes 8126468 | tf_op jit(solution)/shard_map/dot_general | solution.py:164
  91.3 2.7 %collective-permute-done.12 = bf16[512,133]{0,1:T(8,128)(2,1)S(1)} collective-permute-done((bf16[512,133]{0,1:T(8,128)(2,1)S(1)}, bf16[512,133]{0,1:T(8,128)(2,1)S(1)}, u32[]{:S(2)}, u32[]{:S(2)}) %collective-permute-start.12) | collective-permute-done | bytes 136224 | tf_op jit(solution)/shard_map/ppermute | solution.py:33
  95.0 5.5 %fusion.24 = f32[1,512,262]{1,0,2:T(1,128)S(1)} fusion(f32[512,1,128]{0,1,2:T(1,128)S(1)} %copy-done.12, f32[1,512,389]{1,2,0:T(8,128)S(1)} %bitcast.132), kind=kOutput, calls=%fused_computation.57 | convolution fusion | flops 206045184 | bytes 1595392 | tf_op jit(solution)/shard_map/conv_general_dilated | solution.py:37
  101.0 1.3 fusion.7
  102.3 2.5 %reduce-scatter.2.cloned.1.call-done = bf16[512,256]{1,0:T(8,128)(2,1)} async-done(((bf16[4096,256]{1,0:T(8,128)(2,1)}), bf16[512,256]{1,0:T(8,128)(2,1)}) %reduce-scatter.2.cloned.1.call-update) | async-done | bytes 262160 | tf_op jit(solution)/shard_map/reduce_scatter | solution.py:137
  104.8 1.9 %collective-permute-start.13 = (bf16[512,256]{1,0:T(8,128)(2,1)}, bf16[512,256]{1,0:T(8,128)(2,1)S(1)}, u32[]{:S(2)}, u32[]{:S(2)}) collective-permute-start(bf16[512,256]{1,0:T(8,128)(2,1)} %reduce-scatter.2.cloned.1.call-done), channel_id=1, source_target_pairs={{0,0},{1,1},{2,8},{3,9},{4,16},{5,17},{6,24},{7,25},{8,10},{9,11},... | collective-permute-start | bytes 786440 | tf_op jit(solution)/shard_map/ppermute | solution.py:185
  107.9 18.5 %collective-permute-done.13 = bf16[512,256]{1,0:T(8,128)(2,1)S(1)} collective-permute-done((bf16[512,256]{1,0:T(8,128)(2,1)}, bf16[512,256]{1,0:T(8,128)(2,1)S(1)}, u32[]{:S(2)}, u32[]{:S(2)}) %collective-permute-start.13) | collective-permute-done | bytes 262176 | tf_op jit(solution)/shard_map/ppermute | solution.py:185
  (112 shorter events, 23.6 us)
Async XLA Ops:
  7.2 46.9 %copy-start = (bf16[512,1024]{1,0:T(8,128)(2,1)S(1)}, bf16[512,1024]{1,0:T(8,128)(2,1)}, u32[]{:S(2)}) copy-start(bf16[512,1024]{1,0:T(8,128)(2,1)} %param.10) | copy-start | bytes 3145732
  7.2 63.1 %all-gather.2.cloned.1.call-start = ((), (), s32[]{:S(2)}) async-start(), calls=%async_computation.2 | async-start | bytes 2359296 | tf_op jit(solution)/shard_map/all_gather | solution.py:100
  8.3 10.7 %collective-permute-start.2 = (bf16[128,256]{1,0:T(8,128)(2,1)S(1)}, bf16[128,256]{1,0:T(8,128)(2,1)S(1)}, u32[]{:S(2)}, u32[]{:S(2)}) collective-permute-start(bf16[128,256]{1,0:T(8,128)(2,1)S(1)} %get-tuple-element.52), channel_id=1, source_target_pairs={{0,24},{8,16},{16,8},{24,0},{1,25},{9,17},{17,9},{25,1},{2,26},{10... | collective-permute-start | bytes 196616 | tf_op jit(solution)/shard_map/ppermute | solution.py:73
  9.6 9.5 %collective-permute-start.1 = (bf16[128,256]{1,0:T(8,128)(2,1)S(1)}, bf16[128,256]{1,0:T(8,128)(2,1)S(1)}, u32[]{:S(2)}, u32[]{:S(2)}) collective-permute-start(bf16[128,256]{1,0:T(8,128)(2,1)S(1)} %get-tuple-element.53), channel_id=1, source_target_pairs={{0,16},{8,24},{16,0},{24,8},{1,17},{9,25},{17,1},{25,9},{2,18},{10... | collective-permute-start | bytes 196616 | tf_op jit(solution)/shard_map/ppermute | solution.py:73
  9.8 9.3 %collective-permute-start = (bf16[128,256]{1,0:T(8,128)(2,1)S(1)}, bf16[128,256]{1,0:T(8,128)(2,1)S(1)}, u32[]{:S(2)}, u32[]{:S(2)}) collective-permute-start(bf16[128,256]{1,0:T(8,128)(2,1)S(1)} %get-tuple-element.54), channel_id=1, source_target_pairs={{0,8},{8,0},{16,24},{24,16},{1,9},{9,1},{17,25},{25,17},{2,10},{10... | collective-permute-start | bytes 196616 | tf_op jit(solution)/shard_map/ppermute | solution.py:73
  14.3 32.6 %copy-start.14 = (f32[512,1]{0,1:T(1,128)}, f32[512,1]{0,1:T(1,128)S(1)}, u32[]{:S(2)}) copy-start(f32[512,1]{0,1:T(1,128)S(1)} %get-tuple-element.77) | copy-start | bytes 6148
  21.0 17.0 %collective-permute-start.8 = (bf16[128,1024]{0,1:T(8,128)(2,1)}, bf16[128,1024]{0,1:T(8,128)(2,1)}, u32[]{:S(2)}, u32[]{:S(2)}) collective-permute-start(bf16[128,1024]{0,1:T(8,128)(2,1)} %bitcast.11), channel_id=1, source_target_pairs={{0,0},{1,4},{2,8},{3,12},{4,16},{5,20},{6,24},{7,28},{8,1},{9,5},{... | collective-permute-start | bytes 786440 | tf_op jit(solution)/shard_map/ppermute | solution.py:99
  24.1 13.9 %collective-permute-start.4 = (bf16[512,145]{0,1:T(8,128)(2,1)S(1)}, bf16[512,145]{0,1:T(8,128)(2,1)S(1)}, u32[]{:S(2)}, u32[]{:S(2)}) collective-permute-start(bf16[512,145]{0,1:T(8,128)(2,1)S(1)} %pad_maximum_fusion.5), channel_id=1, source_target_pairs={{8,0},{16,8},{24,16},{9,1},{17,9},{25,17},{10,2},{18,10},{26,18},{... | collective-permute-start | bytes 445448 | tf_op jit(solution)/shard_map/ppermute | solution.py:21
  28.6 9.7 %collective-permute-start.3 = (bf16[512,272]{0,1:T(8,128)(2,1)S(1)}, bf16[512,272]{0,1:T(8,128)(2,1)S(1)}, u32[]{:S(2)}, u32[]{:S(2)}) collective-permute-start(bf16[512,272]{0,1:T(8,128)(2,1)S(1)} %pad_maximum_fusion.3), channel_id=1, source_target_pairs={{0,8},{8,16},{16,24},{1,9},{9,17},{17,25},{2,10},{10,18},{18,26},{... | collective-permute-start | bytes 835592 | tf_op jit(solution)/shard_map/ppermute | solution.py:20
  38.0 66.8 %reduce-scatter.2.cloned.1.call-start = ((), (), s32[]{:S(2)}) async-start(), calls=%async_computation.1 | async-start | bytes 2359296 | tf_op jit(solution)/shard_map/reduce_scatter | solution.py:137
  40.2 6.4 %copy-start.1 = (f32[512,389]{0,1:T(8,128)}, f32[512,389]{0,1:T(8,128)S(1)}, u32[]{:S(2)}) copy-start(f32[512,389]{0,1:T(8,128)S(1)} %get-tuple-element.36) | copy-start | bytes 2390020
  41.1 5.5 %copy-start.16 = (f32[512]{0:T(512)S(1)}, f32[512]{0:T(512)}, u32[]{:S(2)}) copy-start(f32[512]{0:T(512)} %param.9) | copy-start | bytes 6148
  47.6 19.7 %collective-permute-start.7 = (bf16[512,256]{0,1:T(8,128)(2,1)S(1)}, bf16[512,256]{0,1:T(8,128)(2,1)S(1)}, u32[]{:S(2)}, u32[]{:S(2)}) collective-permute-start(bf16[512,256]{0,1:T(8,128)(2,1)S(1)} %fusion.32), channel_id=1, source_target_pairs={{0,24},{8,16},{16,8},{24,0},{1,25},{9,17},{17,9},{25,1},{2,26},{10... | collective-permute-start | bytes 786440 | tf_op jit(solution)/shard_map/ppermute | solution.py:73
  52.1 14.6 %collective-permute-start.6 = (bf16[512,256]{0,1:T(8,128)(2,1)S(1)}, bf16[512,256]{0,1:T(8,128)(2,1)S(1)}, u32[]{:S(2)}, u32[]{:S(2)}) collective-permute-start(bf16[512,256]{0,1:T(8,128)(2,1)S(1)} %fusion.32), channel_id=1, source_target_pairs={{0,16},{8,24},{16,0},{24,8},{1,17},{9,25},{17,1},{25,9},{2,18},{10... | collective-permute-start | bytes 786440 | tf_op jit(solution)/shard_map/ppermute | solution.py:73
  52.9 13.3 %collective-permute-start.5 = (bf16[512,256]{0,1:T(8,128)(2,1)S(1)}, bf16[512,256]{0,1:T(8,128)(2,1)S(1)}, u32[]{:S(2)}, u32[]{:S(2)}) collective-permute-start(bf16[512,256]{0,1:T(8,128)(2,1)S(1)} %fusion.32), channel_id=1, source_target_pairs={{0,8},{8,0},{16,24},{24,16},{1,9},{9,1},{17,25},{25,17},{2,10},{10... | collective-permute-start | bytes 786440 | tf_op jit(solution)/shard_map/ppermute | solution.py:73
  70.3 5.9 %copy-start.3 = (bf16[1024,1024]{0,1:T(8,128)(2,1)S(1)}, bf16[1024,1024]{0,1:T(8,128)(2,1)}, u32[]{:S(2)}) copy-start(bf16[1024,1024]{0,1:T(8,128)(2,1)} %all-gather.2.cloned.1.call-done) | copy-start | bytes 6291460
  73.4 7.2 %collective-permute-start.9 = (bf16[512,256]{0,1:T(8,128)(2,1)S(1)}, bf16[512,256]{0,1:T(8,128)(2,1)S(1)}, u32[]{:S(2)}, u32[]{:S(2)}) collective-permute-start(bf16[512,256]{0,1:T(8,128)(2,1)S(1)} %get-tuple-element.32), channel_id=1, source_target_pairs={{0,8},{8,0},{16,24},{24,16},{1,9},{9,1},{17,25},{25,17},{2,10},{10... | collective-permute-start | bytes 786440 | tf_op jit(solution)/shard_map/ppermute | solution.py:73
  73.5 12.2 %collective-permute-start.11 = (bf16[512,256]{0,1:T(8,128)(2,1)S(1)}, bf16[512,256]{0,1:T(8,128)(2,1)S(1)}, u32[]{:S(2)}, u32[]{:S(2)}) collective-permute-start(bf16[512,256]{0,1:T(8,128)(2,1)S(1)} %get-tuple-element.33), channel_id=1, source_target_pairs={{0,24},{8,16},{16,8},{24,0},{1,25},{9,17},{17,9},{25,1},{2,26},{10... | collective-permute-start | bytes 786440 | tf_op jit(solution)/shard_map/ppermute | solution.py:73
  74.4 12.7 %collective-permute-start.10 = (bf16[512,256]{0,1:T(8,128)(2,1)S(1)}, bf16[512,256]{0,1:T(8,128)(2,1)S(1)}, u32[]{:S(2)}, u32[]{:S(2)}) collective-permute-start(bf16[512,256]{0,1:T(8,128)(2,1)S(1)} %get-tuple-element.34), channel_id=1, source_target_pairs={{0,16},{8,24},{16,0},{24,8},{1,17},{9,25},{17,1},{25,9},{2,18},{10... | collective-permute-start | bytes 786440 | tf_op jit(solution)/shard_map/ppermute | solution.py:73
  77.5 11.8 %copy-start.5 = (bf16[512,256]{0,1:T(8,128)(2,1)S(1)}, bf16[512,256]{0,1:T(8,128)(2,1)}, u32[]{:S(2)}) copy-start(bf16[512,256]{0,1:T(8,128)(2,1)} %copy-done.4) | copy-start | bytes 786436
  87.3 6.7 %collective-permute-start.12 = (bf16[512,133]{0,1:T(8,128)(2,1)S(1)}, bf16[512,133]{0,1:T(8,128)(2,1)S(1)}, u32[]{:S(2)}, u32[]{:S(2)}) collective-permute-start(bf16[512,133]{0,1:T(8,128)(2,1)S(1)} %slice.479), channel_id=1, source_target_pairs={{8,0},{16,8},{24,16},{9,1},{17,9},{25,17},{10,2},{18,10},{26,18},{... | collective-permute-start | bytes 408584 | tf_op jit(solution)/shard_map/ppermute | solution.py:33
  95.0 5.5 %copy-start.2 = (f32[512,389]{0,1:T(8,128)S(1)}, f32[512,389]{0,1:T(8,128)}, u32[]{:S(2)}) copy-start(f32[512,389]{0,1:T(8,128)} %copy-done.1) | copy-start | bytes 2390020
  95.0 5.5 %copy-start.17 = (f32[512]{0:T(512)S(1)}, f32[512]{0:T(512)}, u32[]{:S(2)}) copy-start(f32[512]{0:T(512)} %param.9) | copy-start | bytes 6148
  104.8 21.6 %collective-permute-start.13 = (bf16[512,256]{1,0:T(8,128)(2,1)}, bf16[512,256]{1,0:T(8,128)(2,1)S(1)}, u32[]{:S(2)}, u32[]{:S(2)}) collective-permute-start(bf16[512,256]{1,0:T(8,128)(2,1)} %reduce-scatter.2.cloned.1.call-done), channel_id=1, source_target_pairs={{0,0},{1,1},{2,8},{3,9},{4,16},{5,17},{6,24},{7,25},{8,10},{9,11},... | collective-permute-start | bytes 786440 | tf_op jit(solution)/shard_map/ppermute | solution.py:185
  (11 other events, 19.5 us)
Sparse Core Ops, SparseCore 0:
  38.1 28.1 all-gather.1
  70.3 34.4 reduce-scatter.1

commit v15 on v11

--- a/solution.py
+++ b/solution.py
@@ -136,11 +136,10 @@
     gated_blocks = [gated] + exchange(lambda step: gated, "seq")
     group = n_tp // n_seq
     weight_t = out_weight.T
-    pieces = [
-        jnp.dot(weight_t, block, preferred_element_type=jnp.float32).astype(jnp.bfloat16)
-        for block in gated_blocks
-    ]
-    partial_out = jnp.concatenate(pieces, axis=0)
+    partial_out = jnp.zeros((n_seq * slab_width, length), jnp.bfloat16)
+    for m, block in enumerate(gated_blocks):
+        piece = jnp.dot(weight_t, block, preferred_element_type=jnp.float32).astype(jnp.bfloat16)
+        partial_out = lax.dynamic_update_slice_in_dim(partial_out, piece, m * slab_width, axis=0)
     output_sum = lax.psum_scatter(partial_out, "tp", scatter_dimension=0, tiled=True)
     route = []
     for s in range(n_seq):

time: 136 us -> 136 us (level)
  waiting for transfers between devices: 50.1 us -> 46.9 us
  matrix products: 19.7 us -> 22.3 us
  local copies, waits for them, and re-layouts: 18 us -> 19.7 us
  other arithmetic: 8.65 us -> 7.13 us
    dot_general x4, matrix products: 1.81 us -> 4.33 us  [shards(): jnp.dot(weight_t, block, preferred_element_type=jnp.float32)]
    dynamic_update_slice x0 -> x1, local copies, waits for them, and re-layouts: none -> 1.6 us  [shards(): lax.dynamic_update_slice_in_dim(partial_out, piece, m * slab_width, axis=0)]
    concatenate x1 -> x0, other arithmetic: 1.52 us -> none  [shards(): partial_out = jnp.concatenate(pieces, axis=0)]
    ppermute x9, waiting for transfers between devices: 17.5 us -> 16 us  [exchange(): got.append(lax.ppermute(block_of(step), axis, route))]
  transfers between devices with their start and end apart: 16 -> 16, of which waited for: 8 -> 8; matrix products, arithmetic and copies ran while one was open for 29% -> 31% of each run, Pallas kernels for 0% -> 0%
where the time goes in v15:
time: 136 us; the launch traced here: 135 us
  waiting for transfers between devices  46.9 us (34%)
  starting transfers between devices  24.3 us (18%)
  matrix products  22.3 us (16%)
  local copies, waits for them, and re-layouts  19.7 us (14%)
  between operations  14.7 us (11%)
  other arithmetic  7.13 us (5%)
    ppermute x1, waiting for transfers between devices, shards(): mixed = lax.ppermute(output_sum, ('seq', 'tp'), mixed_route)  18.6 us
    ppermute x9, waiting for transfers between devices, exchange(): got.append(lax.ppermute(block_of(step), axis, route))  16 us
    conv_general_dilated x3, matrix products, correlate(): lax.conv_general_dilated(signal[None], taps[:, None, :], (1,), 'VALID', d...  11.6 us
    ppermute x9, starting transfers between devices, exchange(): got.append(lax.ppermute(block_of(step), axis, route))  10.7 us
    ppermute x1, waiting for transfers between devices, halo(): high = lax.ppermute(high, axis, backward)  7.26 us
    unnamed x60, local copies, waits for them, and re-layouts  5.22 us
    ppermute x1, starting transfers between devices, halo(): high = lax.ppermute(high, axis, backward)  4.49 us
    dot_general x4, matrix products, shards(): jnp.dot(weight_t, block, preferred_element_type=jnp.float32)  4.33 us
  transfers between devices with their start and end apart: 16, of which 8 were waited for; matrix products, arithmetic and copies ran while one was open for 31% of the time, Pallas kernels for 0%

profile of v15, /device:TPU:27, one launch (start us, length us, event | category | flops | bytes accessed | tf_op | source)
XLA Modules:
  0.0 135.1 jit_solution(5490773935360445354)
XLA Ops:
  14.9 1.9 %rev.5 = f32[512,128]{1,0:T(8,128)S(1)} reverse(f32[512,128]{1,0:T(8,128)} %param.8), dimensions={1} | reverse | bytes 524288 | tf_op jit(solution)/shard_map/rev | solution.py:131
  16.8 1.9 %copy.58 = f32[512,1,128]{0,1,2:T(1,128)} copy(f32[512,1,128]{2,0,1:T(8,128)} %bitcast.155) | data formatting | bytes 524288 | tf_op jit(solution)/shard_map/broadcast_in_dim | solution.py:43
  21.6 3.0 %collective-permute-start.7 = (bf16[128,1024]{0,1:T(8,128)(2,1)}, bf16[128,1024]{0,1:T(8,128)(2,1)S(1)}, u32[]{:S(2)}, u32[]{:S(2)}) collective-permute-start(bf16[128,1024]{0,1:T(8,128)(2,1)} %bitcast.11), channel_id=1, source_target_pairs={{0,0},{1,4},{2,8},{3,12},{4,16},{5,20},{6,24},{7,28},{8,1},{9,5},{... | collective-permute-start | bytes 786440 | tf_op jit(solution)/shard_map/ppermute | solution.py:103
  24.7 4.5 %collective-permute-start.12 = (bf16[512,145]{0,1:T(8,128)(2,1)S(1)}, bf16[512,145]{0,1:T(8,128)(2,1)S(1)}, u32[]{:S(2)}, u32[]{:S(2)}) collective-permute-start(bf16[512,145]{0,1:T(8,128)(2,1)S(1)} %pad_maximum_fusion.4), channel_id=1, source_target_pairs={{8,0},{16,8},{24,16},{9,1},{17,9},{25,17},{10,2},{18,10},{26,18},{... | collective-permute-start | bytes 445448 | tf_op jit(solution)/shard_map/ppermute | solution.py:20
  29.2 2.0 %collective-permute-start.3 = (bf16[512,272]{0,1:T(8,128)(2,1)S(1)}, bf16[512,272]{0,1:T(8,128)(2,1)S(1)}, u32[]{:S(2)}, u32[]{:S(2)}) collective-permute-start(bf16[512,272]{0,1:T(8,128)(2,1)S(1)} %pad_maximum_fusion.2), channel_id=1, source_target_pairs={{0,8},{8,16},{16,24},{1,9},{9,17},{17,25},{2,10},{10,18},{18,26},{... | collective-permute-start | bytes 835592 | tf_op jit(solution)/shard_map/ppermute | solution.py:19
  31.3 7.3 %collective-permute-done.12 = bf16[512,145]{0,1:T(8,128)(2,1)S(1)} collective-permute-done((bf16[512,145]{0,1:T(8,128)(2,1)S(1)}, bf16[512,145]{0,1:T(8,128)(2,1)S(1)}, u32[]{:S(2)}, u32[]{:S(2)}) %collective-permute-start.12) | collective-permute-done | bytes 148512 | tf_op jit(solution)/shard_map/ppermute | solution.py:20
  42.8 5.3 %fusion.35 = f32[1,512,256]{1,0,2:T(1,128)S(1)} fusion(f32[512,1,128]{0,1,2:T(1,128)S(1)} %copy-done.13, f32[1,512,383]{1,2,0:T(8,128)S(1)} %slice_multiply_fusion.28), kind=kOutput, calls=%fused_computation.78 | convolution fusion | flops 201326592 | bytes 1570816 | tf_op jit(solution)/shard_map/conv_general_dilated | solution.py:41
  48.8 3.4 %collective-permute-start.6 = (bf16[512,256]{0,1:T(8,128)(2,1)S(1)}, bf16[512,256]{0,1:T(8,128)(2,1)S(1)}, u32[]{:S(2)}, u32[]{:S(2)}) collective-permute-start(bf16[512,256]{0,1:T(8,128)(2,1)S(1)} %get-tuple-element.16), channel_id=1, source_target_pairs={{0,24},{8,16},{16,8},{24,0},{1,25},{9,17},{17,9},{25,1},{2,26},{10... | collective-permute-start | bytes 786440 | tf_op jit(solution)/shard_map/ppermute | solution.py:77
  54.5 1.6 %dynamic_update_slice.12 = bf16[4096,256]{0,1:T(8,128)(2,1)} pad(bf16[1024,256]{0,1:T(8,128)(2,1)S(1)} %fusion.19, bf16[]{:T(256)} %constant.40.clone.1), padding=0_3072x0_0 | pad | bytes 2621442 | tf_op jit(solution)/shard_map/dynamic_update_slice | solution.py:142
  58.7 1.3 slice_bitcast_fusion
  60.1 6.2 %collective-permute-done.4 = bf16[512,256]{0,1:T(8,128)(2,1)S(1)} collective-permute-done((bf16[512,256]{0,1:T(8,128)(2,1)S(1)}, bf16[512,256]{0,1:T(8,128)(2,1)S(1)}, u32[]{:S(2)}, u32[]{:S(2)}) %collective-permute-start.4) | collective-permute-done | bytes 262176 | tf_op jit(solution)/shard_map/ppermute | solution.py:77
  67.6 1.3 fusion.23
  71.0 3.0 %fusion.83 = f32[1024,512]{1,0:T(8,128)S(1)} fusion(bf16[1024,1024]{0,1:T(8,128)(2,1)} %all-gather.2.cloned.1.call-done, bf16[512,1024]{1,0:T(8,128)(2,1)S(1)} %copy-done), kind=kOutput, calls=%fused_computation.190 | convolution fusion | flops 1073741824 | bytes 5242880 | tf_op jit(solution)/shard_map/dot_general | solution.py:163
  74.6 2.3 %collective-permute-start.9 = (bf16[512,256]{0,1:T(8,128)(2,1)S(1)}, bf16[512,256]{0,1:T(8,128)(2,1)S(1)}, u32[]{:S(2)}, u32[]{:S(2)}) collective-permute-start(bf16[512,256]{0,1:T(8,128)(2,1)S(1)} %get-tuple-element.36), channel_id=1, source_target_pairs={{0,16},{8,24},{16,0},{24,8},{1,17},{9,25},{17,1},{25,9},{2,18},{10... | collective-permute-start | bytes 786440 | tf_op jit(solution)/shard_map/ppermute | solution.py:77
  78.3 3.2 %collective-permute-done.8 = bf16[512,256]{0,1:T(8,128)(2,1)S(1)} collective-permute-done((bf16[512,256]{0,1:T(8,128)(2,1)S(1)}, bf16[512,256]{0,1:T(8,128)(2,1)S(1)}, u32[]{:S(2)}, u32[]{:S(2)}) %collective-permute-start.8) | collective-permute-done | bytes 262176 | tf_op jit(solution)/shard_map/ppermute | solution.py:77
  81.5 4.4 %collective-permute-done.10 = bf16[512,256]{0,1:T(8,128)(2,1)S(1)} collective-permute-done((bf16[512,256]{0,1:T(8,128)(2,1)S(1)}, bf16[512,256]{0,1:T(8,128)(2,1)S(1)}, u32[]{:S(2)}, u32[]{:S(2)}) %collective-permute-start.10) | collective-permute-done | bytes 262176 | tf_op jit(solution)/shard_map/ppermute | solution.py:77
  85.9 2.1 %collective-permute-done.9 = bf16[512,256]{0,1:T(8,128)(2,1)S(1)} collective-permute-done((bf16[512,256]{0,1:T(8,128)(2,1)S(1)}, bf16[512,256]{0,1:T(8,128)(2,1)S(1)}, u32[]{:S(2)}, u32[]{:S(2)}) %collective-permute-start.9) | collective-permute-done | bytes 262176 | tf_op jit(solution)/shard_map/ppermute | solution.py:77
  88.2 2.1 %collective-permute-start.11 = (bf16[512,133]{0,1:T(8,128)(2,1)S(1)}, bf16[512,133]{0,1:T(8,128)(2,1)S(1)}, u32[]{:S(2)}, u32[]{:S(2)}) collective-permute-start(bf16[512,133]{0,1:T(8,128)(2,1)S(1)} %slice.652), channel_id=1, source_target_pairs={{8,0},{16,8},{24,16},{9,1},{17,9},{25,17},{10,2},{18,10},{26,18},{... | collective-permute-start | bytes 408584 | tf_op jit(solution)/shard_map/ppermute | solution.py:37
  90.3 2.0 %add_convert_fusion = bf16[512,1024]{1,0:T(8,128)(2,1)} fusion(f32[512,1024]{1,0:T(8,128)S(1)} %fusion.55, f32[512,1024]{1,0:T(8,128)S(1)} %fusion.57, f32[512,1024]{1,0:T(8,128)S(1)} %fusion.59, bf16[512,256]{0,1:T(8,128)(2,1)S(1)} %copy-done.5, bf16[1024,1024]{0,1:T(8,128)(2,1)S(1)} %copy-done.3, s32[]{:T(128)S(6)} %select_n.112), kind=kOutput, calls=%fused_computation.1 | convolution fusion | flops 274726912 | bytes 8126468 | tf_op jit(solution)/shard_map/dot_general | solution.py:180
  92.3 2.6 %collective-permute-done.11 = bf16[512,133]{0,1:T(8,128)(2,1)S(1)} collective-permute-done((bf16[512,133]{0,1:T(8,128)(2,1)S(1)}, bf16[512,133]{0,1:T(8,128)(2,1)S(1)}, u32[]{:S(2)}, u32[]{:S(2)}) %collective-permute-start.11) | collective-permute-done | bytes 136224 | tf_op jit(solution)/shard_map/ppermute | solution.py:37
  96.0 5.5 %fusion.33 = f32[1,512,262]{1,0,2:T(1,128)S(1)} fusion(f32[512,1,128]{0,1,2:T(1,128)S(1)} %copy-done.12, f32[1,512,389]{1,2,0:T(8,128)S(1)} %bitcast.154), kind=kOutput, calls=%fused_computation.75 | convolution fusion | flops 206045184 | bytes 1595392 | tf_op jit(solution)/shard_map/conv_general_dilated | solution.py:41
  103.3 2.5 %reduce-scatter.2.cloned.1.call-done = bf16[512,256]{0,1:T(8,128)(2,1)} async-done(((bf16[4096,256]{0,1:T(8,128)(2,1)}), bf16[512,256]{0,1:T(8,128)(2,1)}) %reduce-scatter.2.cloned.1.call-update) | async-done | bytes 262160 | tf_op jit(solution)/shard_map/reduce_scatter | solution.py:143
  105.7 1.9 %collective-permute-start.13 = (bf16[512,256]{0,1:T(8,128)(2,1)}, bf16[512,256]{0,1:T(8,128)(2,1)S(1)}, u32[]{:S(2)}, u32[]{:S(2)}) collective-permute-start(bf16[512,256]{0,1:T(8,128)(2,1)} %reduce-scatter.2.cloned.1.call-done), channel_id=1, source_target_pairs={{0,0},{1,1},{2,8},{3,9},{4,16},{5,17},{6,24},{7,25},{8,10},{9,11},... | collective-permute-start | bytes 786440 | tf_op jit(solution)/shard_map/ppermute | solution.py:201
  108.8 18.6 %collective-permute-done.13 = bf16[512,256]{0,1:T(8,128)(2,1)S(1)} collective-permute-done((bf16[512,256]{0,1:T(8,128)(2,1)}, bf16[512,256]{0,1:T(8,128)(2,1)S(1)}, u32[]{:S(2)}, u32[]{:S(2)}) %collective-permute-start.13) | collective-permute-done | bytes 262176 | tf_op jit(solution)/shard_map/ppermute | solution.py:201
  (134 shorter events, 30.4 us)
Async XLA Ops:
  7.2 46.9 %copy-start = (bf16[512,1024]{1,0:T(8,128)(2,1)S(1)}, bf16[512,1024]{1,0:T(8,128)(2,1)}, u32[]{:S(2)}) copy-start(bf16[512,1024]{1,0:T(8,128)(2,1)} %param.10) | copy-start | bytes 3145732
  7.2 63.8 %all-gather.2.cloned.1.call-start = ((), (), s32[]{:S(2)}) async-start(), calls=%async_computation.2 | async-start | bytes 2359296 | tf_op jit(solution)/shard_map/all_gather | solution.py:104
  8.3 11.3 %collective-permute-start.2 = (bf16[128,256]{1,0:T(8,128)(2,1)S(1)}, bf16[128,256]{1,0:T(8,128)(2,1)S(1)}, u32[]{:S(2)}, u32[]{:S(2)}) collective-permute-start(bf16[128,256]{1,0:T(8,128)(2,1)S(1)} %get-tuple-element.53), channel_id=1, source_target_pairs={{0,24},{8,16},{16,8},{24,0},{1,25},{9,17},{17,9},{25,1},{2,26},{10... | collective-permute-start | bytes 196616 | tf_op jit(solution)/shard_map/ppermute | solution.py:77
  9.6 10.1 %collective-permute-start.1 = (bf16[128,256]{1,0:T(8,128)(2,1)S(1)}, bf16[128,256]{1,0:T(8,128)(2,1)S(1)}, u32[]{:S(2)}, u32[]{:S(2)}) collective-permute-start(bf16[128,256]{1,0:T(8,128)(2,1)S(1)} %get-tuple-element.54), channel_id=1, source_target_pairs={{0,16},{8,24},{16,0},{24,8},{1,17},{9,25},{17,1},{25,9},{2,18},{10... | collective-permute-start | bytes 196616 | tf_op jit(solution)/shard_map/ppermute | solution.py:77
  9.8 9.9 %collective-permute-start = (bf16[128,256]{1,0:T(8,128)(2,1)S(1)}, bf16[128,256]{1,0:T(8,128)(2,1)S(1)}, u32[]{:S(2)}, u32[]{:S(2)}) collective-permute-start(bf16[128,256]{1,0:T(8,128)(2,1)S(1)} %get-tuple-element.55), channel_id=1, source_target_pairs={{0,8},{8,0},{16,24},{24,16},{1,9},{9,1},{17,25},{25,17},{2,10},{10... | collective-permute-start | bytes 196616 | tf_op jit(solution)/shard_map/ppermute | solution.py:77
  21.6 17.7 %collective-permute-start.7 = (bf16[128,1024]{0,1:T(8,128)(2,1)}, bf16[128,1024]{0,1:T(8,128)(2,1)S(1)}, u32[]{:S(2)}, u32[]{:S(2)}) collective-permute-start(bf16[128,1024]{0,1:T(8,128)(2,1)} %bitcast.11), channel_id=1, source_target_pairs={{0,0},{1,4},{2,8},{3,12},{4,16},{5,20},{6,24},{7,28},{8,1},{9,5},{... | collective-permute-start | bytes 786440 | tf_op jit(solution)/shard_map/ppermute | solution.py:103
  24.7 13.9 %collective-permute-start.12 = (bf16[512,145]{0,1:T(8,128)(2,1)S(1)}, bf16[512,145]{0,1:T(8,128)(2,1)S(1)}, u32[]{:S(2)}, u32[]{:S(2)}) collective-permute-start(bf16[512,145]{0,1:T(8,128)(2,1)S(1)} %pad_maximum_fusion.4), channel_id=1, source_target_pairs={{8,0},{16,8},{24,16},{9,1},{17,9},{25,17},{10,2},{18,10},{26,18},{... | collective-permute-start | bytes 445448 | tf_op jit(solution)/shard_map/ppermute | solution.py:20
  29.2 10.8 %collective-permute-start.3 = (bf16[512,272]{0,1:T(8,128)(2,1)S(1)}, bf16[512,272]{0,1:T(8,128)(2,1)S(1)}, u32[]{:S(2)}, u32[]{:S(2)}) collective-permute-start(bf16[512,272]{0,1:T(8,128)(2,1)S(1)} %pad_maximum_fusion.2), channel_id=1, source_target_pairs={{0,8},{8,16},{16,24},{1,9},{9,17},{17,25},{2,10},{10,18},{18,26},{... | collective-permute-start | bytes 835592 | tf_op jit(solution)/shard_map/ppermute | solution.py:19
  40.0 65.8 %reduce-scatter.2.cloned.1.call-start = ((), (), s32[]{:S(2)}) async-start(), calls=%async_computation.1 | async-start | bytes 2359296 | tf_op jit(solution)/shard_map/reduce_scatter | solution.py:143
  42.7 5.5 %copy-start.21 = (f32[512,1]{0,1:T(1,128)S(1)}, f32[512,1]{0,1:T(1,128)}, u32[]{:S(2)}) copy-start(f32[512,1]{0,1:T(1,128)} %get-tuple-element.78) | copy-start | bytes 6148
  42.7 5.5 %copy-start.23 = (f32[512]{0:T(512)S(1)}, f32[512]{0:T(512)}, u32[]{:S(2)}) copy-start(f32[512]{0:T(512)} %param.9) | copy-start | bytes 6148
  48.8 20.1 %collective-permute-start.6 = (bf16[512,256]{0,1:T(8,128)(2,1)S(1)}, bf16[512,256]{0,1:T(8,128)(2,1)S(1)}, u32[]{:S(2)}, u32[]{:S(2)}) collective-permute-start(bf16[512,256]{0,1:T(8,128)(2,1)S(1)} %get-tuple-element.16), channel_id=1, source_target_pairs={{0,24},{8,16},{16,8},{24,0},{1,25},{9,17},{17,9},{25,1},{2,26},{10... | collective-permute-start | bytes 786440 | tf_op jit(solution)/shard_map/ppermute | solution.py:77
  52.1 15.4 %collective-permute-start.5 = (bf16[512,256]{0,1:T(8,128)(2,1)S(1)}, bf16[512,256]{0,1:T(8,128)(2,1)S(1)}, u32[]{:S(2)}, u32[]{:S(2)}) collective-permute-start(bf16[512,256]{0,1:T(8,128)(2,1)S(1)} %get-tuple-element.16), channel_id=1, source_target_pairs={{0,16},{8,24},{16,0},{24,8},{1,17},{9,25},{17,1},{25,9},{2,18},{10... | collective-permute-start | bytes 786440 | tf_op jit(solution)/shard_map/ppermute | solution.py:77
  52.9 13.3 %collective-permute-start.4 = (bf16[512,256]{0,1:T(8,128)(2,1)S(1)}, bf16[512,256]{0,1:T(8,128)(2,1)S(1)}, u32[]{:S(2)}, u32[]{:S(2)}) collective-permute-start(bf16[512,256]{0,1:T(8,128)(2,1)S(1)} %get-tuple-element.16), channel_id=1, source_target_pairs={{0,8},{8,0},{16,24},{24,16},{1,9},{9,1},{17,25},{25,17},{2,10},{10... | collective-permute-start | bytes 786440 | tf_op jit(solution)/shard_map/ppermute | solution.py:77
  71.0 5.9 %copy-start.3 = (bf16[1024,1024]{0,1:T(8,128)(2,1)S(1)}, bf16[1024,1024]{0,1:T(8,128)(2,1)}, u32[]{:S(2)}) copy-start(bf16[1024,1024]{0,1:T(8,128)(2,1)} %all-gather.2.cloned.1.call-done) | copy-start | bytes 6291460
  74.1 7.4 %collective-permute-start.8 = (bf16[512,256]{0,1:T(8,128)(2,1)S(1)}, bf16[512,256]{0,1:T(8,128)(2,1)S(1)}, u32[]{:S(2)}, u32[]{:S(2)}) collective-permute-start(bf16[512,256]{0,1:T(8,128)(2,1)S(1)} %get-tuple-element.34), channel_id=1, source_target_pairs={{0,8},{8,0},{16,24},{24,16},{1,9},{9,1},{17,25},{25,17},{2,10},{10... | collective-permute-start | bytes 786440 | tf_op jit(solution)/shard_map/ppermute | solution.py:77
  74.2 11.7 %collective-permute-start.10 = (bf16[512,256]{0,1:T(8,128)(2,1)S(1)}, bf16[512,256]{0,1:T(8,128)(2,1)S(1)}, u32[]{:S(2)}, u32[]{:S(2)}) collective-permute-start(bf16[512,256]{0,1:T(8,128)(2,1)S(1)} %get-tuple-element.35), channel_id=1, source_target_pairs={{0,24},{8,16},{16,8},{24,0},{1,25},{9,17},{17,9},{25,1},{2,26},{10... | collective-permute-start | bytes 786440 | tf_op jit(solution)/shard_map/ppermute | solution.py:77
  74.6 13.5 %collective-permute-start.9 = (bf16[512,256]{0,1:T(8,128)(2,1)S(1)}, bf16[512,256]{0,1:T(8,128)(2,1)S(1)}, u32[]{:S(2)}, u32[]{:S(2)}) collective-permute-start(bf16[512,256]{0,1:T(8,128)(2,1)S(1)} %get-tuple-element.36), channel_id=1, source_target_pairs={{0,16},{8,24},{16,0},{24,8},{1,17},{9,25},{17,1},{25,9},{2,18},{10... | collective-permute-start | bytes 786440 | tf_op jit(solution)/shard_map/ppermute | solution.py:77
  78.3 12.0 %copy-start.5 = (bf16[512,256]{0,1:T(8,128)(2,1)S(1)}, bf16[512,256]{0,1:T(8,128)(2,1)}, u32[]{:S(2)}) copy-start(bf16[512,256]{0,1:T(8,128)(2,1)} %copy-done.4) | copy-start | bytes 786436
  88.2 6.7 %collective-permute-start.11 = (bf16[512,133]{0,1:T(8,128)(2,1)S(1)}, bf16[512,133]{0,1:T(8,128)(2,1)S(1)}, u32[]{:S(2)}, u32[]{:S(2)}) collective-permute-start(bf16[512,133]{0,1:T(8,128)(2,1)S(1)} %slice.652), channel_id=1, source_target_pairs={{8,0},{16,8},{24,16},{9,1},{17,9},{25,17},{10,2},{18,10},{26,18},{... | collective-permute-start | bytes 408584 | tf_op jit(solution)/shard_map/ppermute | solution.py:37
  96.0 5.5 %copy-start.1 = (f32[512,389]{0,1:T(8,128)S(1)}, f32[512,389]{0,1:T(8,128)}, u32[]{:S(2)}) copy-start(f32[512,389]{0,1:T(8,128)} %get-tuple-element.37) | copy-start | bytes 2390020
  96.0 5.5 %copy-start.2 = (f32[512,389]{0,1:T(8,128)S(1)}, f32[512,389]{0,1:T(8,128)}, u32[]{:S(2)}) copy-start(f32[512,389]{0,1:T(8,128)} %get-tuple-element.38) | copy-start | bytes 2390020
  96.0 5.5 %copy-start.24 = (f32[512]{0:T(512)S(1)}, f32[512]{0:T(512)}, u32[]{:S(2)}) copy-start(f32[512]{0:T(512)} %param.9) | copy-start | bytes 6148
  105.7 21.7 %collective-permute-start.13 = (bf16[512,256]{0,1:T(8,128)(2,1)}, bf16[512,256]{0,1:T(8,128)(2,1)S(1)}, u32[]{:S(2)}, u32[]{:S(2)}) collective-permute-start(bf16[512,256]{0,1:T(8,128)(2,1)} %reduce-scatter.2.cloned.1.call-done), channel_id=1, source_target_pairs={{0,0},{1,1},{2,8},{3,9},{4,16},{5,17},{6,24},{7,25},{8,10},{9,11},... | collective-permute-start | bytes 786440 | tf_op jit(solution)/shard_map/ppermute | solution.py:201
  (18 other events, 47.4 us)
Sparse Core Ops, SparseCore 0:
  40.1 28.1 all-gather.1
  71.0 34.6 reduce-scatter.1

commit v16 on v14

--- a/solution.py
+++ b/solution.py
@@ -97,7 +97,9 @@
             flat = n_seq * b + a
             route.append((a * n_tp + b, (flat // n_tp) * n_tp + flat % n_tp))
     moved = lax.ppermute(mine, ("seq", "tp"), route)
-    return lax.all_gather(moved, "tp", axis=0, tiled=True)
+    moved = with_layout_constraint(moved, Layout(major_to_minor=(0, 1)))
+    gathered = lax.all_gather(moved, "tp", axis=0, tiled=True)
+    return with_layout_constraint(gathered, Layout(major_to_minor=(0, 1)))
 
 
 def shards(streams, feat_weight, long_filter, skip_gain, out_weight, out_grad):
@@ -133,7 +135,6 @@
         for block in gated_blocks
     ]
     partial_out = jnp.concatenate(pieces, axis=0)
-    partial_out = with_layout_constraint(partial_out, Layout(major_to_minor=(0, 1)))
     output_sum = lax.psum_scatter(partial_out, "tp", scatter_dimension=0, tiled=True)
     route = []
     for s in range(n_seq):

time: 135 us -> 135 us (level)
  transfers between devices with their start and end apart: 16 -> 16, of which waited for: 9 -> 8; matrix products, arithmetic and copies ran while one was open for 27% -> 27% of each run, Pallas kernels for 0% -> 0%
where the time goes in v16:
time: 135 us; the launch traced here: 134 us
  waiting for transfers between devices  51.2 us (38%)
  starting transfers between devices  26.5 us (20%)
  matrix products  19.2 us (14%)
  local copies, waits for them, and re-layouts  14.9 us (11%)
  between operations  14.7 us (11%)
  other arithmetic  7.26 us (5%)
    ppermute x9, waiting for transfers between devices, exchange(): got.append(lax.ppermute(block_of(step), axis, route))  19.9 us
    ppermute x1, waiting for transfers between devices, shards(): mixed = lax.ppermute(output_sum, ('seq', 'tp'), mixed_route)  18.5 us
    ppermute x9, starting transfers between devices, exchange(): got.append(lax.ppermute(block_of(step), axis, route))  11.8 us
    conv_general_dilated x2, matrix products, correlate(): lax.conv_general_dilated(signal[None], taps[:, None, :], (1,), 'VALID', d...  11 us
    ppermute x1, waiting for transfers between devices, halo(): high = lax.ppermute(high, axis, backward)  7.26 us
    ppermute x1, starting transfers between devices, halo(): high = lax.ppermute(high, axis, backward)  4.49 us
    reduce_scatter x1, waiting for transfers between devices, shards(): lax.psum_scatter(partial_out, 'tp', scatter_dimension=0, tiled=True)  3.65 us
    dot_general x4, matrix products, shards(): lax.dot_general(block, grad_part, (((1,), (1,)), ((), ())), preferred_ele...  3.41 us
  transfers between devices with their start and end apart: 16, of which 8 were waited for; matrix products, arithmetic and copies ran while one was open for 27% of the time, Pallas kernels for 0%

profile of v16, /device:TPU:27, one launch (start us, length us, event | category | flops | bytes accessed | tf_op | source)
XLA Modules:
  0.0 133.7 jit_solution(2436296935766754301)
XLA Ops:
  8.3 1.3 collective-permute-start.2
  14.3 1.9 %rev.8 = f32[512,128]{1,0:T(8,128)S(1)} reverse(f32[512,128]{1,0:T(8,128)} %param.8), dimensions={1} | reverse | bytes 524288 | tf_op jit(solution)/shard_map/rev | solution.py:126
  16.2 1.9 %copy.37 = f32[512,1,128]{0,1,2:T(1,128)} copy(f32[512,1,128]{2,0,1:T(8,128)} %bitcast.134) | data formatting | bytes 524288 | tf_op jit(solution)/shard_map/broadcast_in_dim | solution.py:39
  20.9 3.0 %collective-permute-start.8 = (bf16[128,1024]{1,0:T(8,128)(2,1)}, bf16[128,1024]{1,0:T(8,128)(2,1)}, u32[]{:S(2)}, u32[]{:S(2)}) collective-permute-start(bf16[128,1024]{1,0:T(8,128)(2,1)} %bitcast.61), channel_id=1, source_target_pairs={{0,0},{1,4},{2,8},{3,12},{4,16},{5,20},{6,24},{7,28},{8,1},{9,5},{... | collective-permute-start | bytes 786440 | tf_op jit(solution)/shard_map/ppermute | solution.py:99
  24.0 4.5 %collective-permute-start.4 = (bf16[512,145]{0,1:T(8,128)(2,1)S(1)}, bf16[512,145]{0,1:T(8,128)(2,1)S(1)}, u32[]{:S(2)}, u32[]{:S(2)}) collective-permute-start(bf16[512,145]{0,1:T(8,128)(2,1)S(1)} %pad_maximum_fusion.5), channel_id=1, source_target_pairs={{8,0},{16,8},{24,16},{9,1},{17,9},{25,17},{10,2},{18,10},{26,18},{... | collective-permute-start | bytes 445448 | tf_op jit(solution)/shard_map/ppermute | solution.py:21
  28.5 2.0 %collective-permute-start.3 = (bf16[512,272]{0,1:T(8,128)(2,1)S(1)}, bf16[512,272]{0,1:T(8,128)(2,1)S(1)}, u32[]{:S(2)}, u32[]{:S(2)}) collective-permute-start(bf16[512,272]{0,1:T(8,128)(2,1)S(1)} %pad_maximum_fusion.3), channel_id=1, source_target_pairs={{0,8},{8,16},{16,24},{1,9},{9,17},{17,25},{2,10},{10,18},{18,26},{... | collective-permute-start | bytes 835592 | tf_op jit(solution)/shard_map/ppermute | solution.py:20
  30.6 7.3 %collective-permute-done.4 = bf16[512,145]{0,1:T(8,128)(2,1)S(1)} collective-permute-done((bf16[512,145]{0,1:T(8,128)(2,1)S(1)}, bf16[512,145]{0,1:T(8,128)(2,1)S(1)}, u32[]{:S(2)}, u32[]{:S(2)}) %collective-permute-start.4) | collective-permute-done | bytes 148512 | tf_op jit(solution)/shard_map/ppermute | solution.py:21
  38.5 1.3 fusion
  41.0 5.5 %fusion.26 = f32[1,512,262]{1,0,2:T(1,128)S(1)} fusion(f32[512,1,128]{0,1,2:T(1,128)S(1)} %copy-done.13, f32[1,512,389]{1,2,0:T(8,128)S(1)} %get-tuple-element.34), kind=kOutput, calls=%fused_computation.59 | convolution fusion | flops 206045184 | bytes 1595392 | tf_op jit(solution)/shard_map/conv_general_dilated | solution.py:37
  47.5 4.5 %collective-permute-start.7 = (bf16[512,256]{0,1:T(8,128)(2,1)S(1)}, bf16[512,256]{0,1:T(8,128)(2,1)S(1)}, u32[]{:S(2)}, u32[]{:S(2)}) collective-permute-start(bf16[512,256]{0,1:T(8,128)(2,1)S(1)} %fusion.32), channel_id=1, source_target_pairs={{0,24},{8,16},{16,8},{24,0},{1,25},{9,17},{17,9},{25,1},{2,26},{10... | collective-permute-start | bytes 786440 | tf_op jit(solution)/shard_map/ppermute | solution.py:73
  54.4 11.7 %collective-permute-done.5 = bf16[512,256]{0,1:T(8,128)(2,1)S(1)} collective-permute-done((bf16[512,256]{0,1:T(8,128)(2,1)S(1)}, bf16[512,256]{0,1:T(8,128)(2,1)S(1)}, u32[]{:S(2)}, u32[]{:S(2)}) %collective-permute-start.5) | collective-permute-done | bytes 262176 | tf_op jit(solution)/shard_map/ppermute | solution.py:73
  68.4 1.5 %pad_maximum_fusion = bf16[4096,256]{0,1:T(8,128)(2,1)} fusion(bf16[1024,256]{0,1:T(8,128)(2,1)S(1)} %fusion.16, bf16[1024,256]{0,1:T(8,128)(2,1)S(1)} %fusion.15, bf16[1024,256]{0,1:T(8,128)(2,1)S(1)} %fusion.14, bf16[1024,256]{0,1:T(8,128)(2,1)S(1)} %fusion.13), kind=kLoop, calls=%fused_computation.1 | loop fusion | flops 8388608 | bytes 4194304 | tf_op jit(solution)/shard_map/concatenate | solution.py:137
  70.0 3.0 %fusion.59 = f32[1024,512]{1,0:T(8,128)S(1)} fusion(bf16[1024,1024]{1,0:T(8,128)(2,1)} %all-gather.2.cloned.1.call-done, bf16[512,1024]{1,0:T(8,128)(2,1)S(1)} %copy-done), kind=kOutput, calls=%fused_computation.149 | convolution fusion | flops 1073741824 | bytes 5242880 | tf_op jit(solution)/shard_map/dot_general | solution.py:148
  74.2 1.6 %collective-permute-start.10 = (bf16[512,256]{0,1:T(8,128)(2,1)S(1)}, bf16[512,256]{0,1:T(8,128)(2,1)S(1)}, u32[]{:S(2)}, u32[]{:S(2)}) collective-permute-start(bf16[512,256]{0,1:T(8,128)(2,1)S(1)} %get-tuple-element.31), channel_id=1, source_target_pairs={{0,16},{8,24},{16,0},{24,8},{1,17},{9,25},{17,1},{25,9},{2,18},{10... | collective-permute-start | bytes 786440 | tf_op jit(solution)/shard_map/ppermute | solution.py:73
  77.4 3.0 %collective-permute-done.9 = bf16[512,256]{0,1:T(8,128)(2,1)S(1)} collective-permute-done((bf16[512,256]{0,1:T(8,128)(2,1)S(1)}, bf16[512,256]{0,1:T(8,128)(2,1)S(1)}, u32[]{:S(2)}, u32[]{:S(2)}) %collective-permute-start.9) | collective-permute-done | bytes 262176 | tf_op jit(solution)/shard_map/ppermute | solution.py:73
  80.4 5.2 %collective-permute-done.11 = bf16[512,256]{0,1:T(8,128)(2,1)S(1)} collective-permute-done((bf16[512,256]{0,1:T(8,128)(2,1)S(1)}, bf16[512,256]{0,1:T(8,128)(2,1)S(1)}, u32[]{:S(2)}, u32[]{:S(2)}) %collective-permute-start.11) | collective-permute-done | bytes 262176 | tf_op jit(solution)/shard_map/ppermute | solution.py:73
  85.7 3.1 %collective-permute-start.12 = (bf16[512,133]{0,1:T(8,128)(2,1)S(1)}, bf16[512,133]{0,1:T(8,128)(2,1)S(1)}, u32[]{:S(2)}, u32[]{:S(2)}) collective-permute-start(bf16[512,133]{0,1:T(8,128)(2,1)S(1)} %slice.479), channel_id=1, source_target_pairs={{8,0},{16,8},{24,16},{9,1},{17,9},{25,17},{10,2},{18,10},{26,18},{... | collective-permute-start | bytes 408584 | tf_op jit(solution)/shard_map/ppermute | solution.py:33
  88.8 1.9 %add_convert_fusion = bf16[512,1024]{1,0:T(8,128)(2,1)} fusion(f32[512,1024]{1,0:T(8,128)S(1)} %fusion.36, f32[512,1024]{1,0:T(8,128)S(1)} %fusion.38, f32[512,1024]{1,0:T(8,128)S(1)} %fusion.40, bf16[512,256]{0,1:T(8,128)(2,1)S(1)} %copy-done.5, bf16[1024,1024]{1,0:T(8,128)(2,1)S(1)} %copy-done.3, s32[]{:T(128)S(6)} %select_n.112), kind=kOutput, calls=%fused_computation.2 | convolution fusion | flops 274726912 | bytes 8126468 | tf_op jit(solution)/shard_map/dot_general | solution.py:165
  90.8 1.6 %collective-permute-done.12 = bf16[512,133]{0,1:T(8,128)(2,1)S(1)} collective-permute-done((bf16[512,133]{0,1:T(8,128)(2,1)S(1)}, bf16[512,133]{0,1:T(8,128)(2,1)S(1)}, u32[]{:S(2)}, u32[]{:S(2)}) %collective-permute-start.12) | collective-permute-done | bytes 136224 | tf_op jit(solution)/shard_map/ppermute | solution.py:33
  93.5 5.5 %fusion.24 = f32[1,512,262]{1,0,2:T(1,128)S(1)} fusion(f32[512,1,128]{0,1,2:T(1,128)S(1)} %copy-done.12, f32[1,512,389]{1,2,0:T(8,128)S(1)} %bitcast.133), kind=kOutput, calls=%fused_computation.57 | convolution fusion | flops 206045184 | bytes 1595392 | tf_op jit(solution)/shard_map/conv_general_dilated | solution.py:37
  99.5 1.3 fusion.7
  100.8 3.7 %reduce-scatter.2.cloned.1.call-done = bf16[512,256]{0,1:T(8,128)(2,1)} async-done(((bf16[4096,256]{0,1:T(8,128)(2,1)}), bf16[512,256]{0,1:T(8,128)(2,1)}) %reduce-scatter.2.cloned.1.call-update) | async-done | bytes 262160 | tf_op jit(solution)/shard_map/reduce_scatter | solution.py:138
  104.4 1.9 %collective-permute-start.13 = (bf16[512,256]{0,1:T(8,128)(2,1)}, bf16[512,256]{0,1:T(8,128)(2,1)S(1)}, u32[]{:S(2)}, u32[]{:S(2)}) collective-permute-start(bf16[512,256]{0,1:T(8,128)(2,1)} %reduce-scatter.2.cloned.1.call-done), channel_id=1, source_target_pairs={{0,0},{1,1},{2,8},{3,9},{4,16},{5,17},{6,24},{7,25},{8,10},{9,11},... | collective-permute-start | bytes 786440 | tf_op jit(solution)/shard_map/ppermute | solution.py:186
  107.5 18.5 %collective-permute-done.13 = bf16[512,256]{0,1:T(8,128)(2,1)S(1)} collective-permute-done((bf16[512,256]{0,1:T(8,128)(2,1)}, bf16[512,256]{0,1:T(8,128)(2,1)S(1)}, u32[]{:S(2)}, u32[]{:S(2)}) %collective-permute-start.13) | collective-permute-done | bytes 262176 | tf_op jit(solution)/shard_map/ppermute | solution.py:186
  (112 shorter events, 22.2 us)
Async XLA Ops:
  7.2 46.8 %copy-start = (bf16[512,1024]{1,0:T(8,128)(2,1)S(1)}, bf16[512,1024]{1,0:T(8,128)(2,1)}, u32[]{:S(2)}) copy-start(bf16[512,1024]{1,0:T(8,128)(2,1)} %param.10) | copy-start | bytes 3145732
  7.2 62.8 %all-gather.2.cloned.1.call-start = ((), (), s32[]{:S(2)}) async-start(), calls=%async_computation.2 | async-start | bytes 2359296 | tf_op jit(solution)/shard_map/all_gather | solution.py:101
  8.3 10.7 %collective-permute-start.2 = (bf16[128,256]{1,0:T(8,128)(2,1)S(1)}, bf16[128,256]{1,0:T(8,128)(2,1)S(1)}, u32[]{:S(2)}, u32[]{:S(2)}) collective-permute-start(bf16[128,256]{1,0:T(8,128)(2,1)S(1)} %get-tuple-element.49), channel_id=1, source_target_pairs={{0,24},{8,16},{16,8},{24,0},{1,25},{9,17},{17,9},{25,1},{2,26},{10... | collective-permute-start | bytes 196616 | tf_op jit(solution)/shard_map/ppermute | solution.py:73
  9.6 9.5 %collective-permute-start.1 = (bf16[128,256]{1,0:T(8,128)(2,1)S(1)}, bf16[128,256]{1,0:T(8,128)(2,1)S(1)}, u32[]{:S(2)}, u32[]{:S(2)}) collective-permute-start(bf16[128,256]{1,0:T(8,128)(2,1)S(1)} %get-tuple-element.50), channel_id=1, source_target_pairs={{0,16},{8,24},{16,0},{24,8},{1,17},{9,25},{17,1},{25,9},{2,18},{10... | collective-permute-start | bytes 196616 | tf_op jit(solution)/shard_map/ppermute | solution.py:73
  9.8 9.3 %collective-permute-start = (bf16[128,256]{1,0:T(8,128)(2,1)S(1)}, bf16[128,256]{1,0:T(8,128)(2,1)S(1)}, u32[]{:S(2)}, u32[]{:S(2)}) collective-permute-start(bf16[128,256]{1,0:T(8,128)(2,1)S(1)} %get-tuple-element.51), channel_id=1, source_target_pairs={{0,8},{8,0},{16,24},{24,16},{1,9},{9,1},{17,25},{25,17},{2,10},{10... | collective-permute-start | bytes 196616 | tf_op jit(solution)/shard_map/ppermute | solution.py:73
  14.3 32.4 %copy-start.14 = (f32[512,1]{0,1:T(1,128)}, f32[512,1]{0,1:T(1,128)S(1)}, u32[]{:S(2)}) copy-start(f32[512,1]{0,1:T(1,128)S(1)} %get-tuple-element.74) | copy-start | bytes 6148
  20.9 17.0 %collective-permute-start.8 = (bf16[128,1024]{1,0:T(8,128)(2,1)}, bf16[128,1024]{1,0:T(8,128)(2,1)}, u32[]{:S(2)}, u32[]{:S(2)}) collective-permute-start(bf16[128,1024]{1,0:T(8,128)(2,1)} %bitcast.61), channel_id=1, source_target_pairs={{0,0},{1,4},{2,8},{3,12},{4,16},{5,20},{6,24},{7,28},{8,1},{9,5},{... | collective-permute-start | bytes 786440 | tf_op jit(solution)/shard_map/ppermute | solution.py:99
  24.0 13.9 %collective-permute-start.4 = (bf16[512,145]{0,1:T(8,128)(2,1)S(1)}, bf16[512,145]{0,1:T(8,128)(2,1)S(1)}, u32[]{:S(2)}, u32[]{:S(2)}) collective-permute-start(bf16[512,145]{0,1:T(8,128)(2,1)S(1)} %pad_maximum_fusion.5), channel_id=1, source_target_pairs={{8,0},{16,8},{24,16},{9,1},{17,9},{25,17},{10,2},{18,10},{26,18},{... | collective-permute-start | bytes 445448 | tf_op jit(solution)/shard_map/ppermute | solution.py:21
  28.5 9.7 %collective-permute-start.3 = (bf16[512,272]{0,1:T(8,128)(2,1)S(1)}, bf16[512,272]{0,1:T(8,128)(2,1)S(1)}, u32[]{:S(2)}, u32[]{:S(2)}) collective-permute-start(bf16[512,272]{0,1:T(8,128)(2,1)S(1)} %pad_maximum_fusion.3), channel_id=1, source_target_pairs={{0,8},{8,16},{16,24},{1,9},{9,17},{17,25},{2,10},{10,18},{18,26},{... | collective-permute-start | bytes 835592 | tf_op jit(solution)/shard_map/ppermute | solution.py:20
  37.9 66.5 %reduce-scatter.2.cloned.1.call-start = ((), (), s32[]{:S(2)}) async-start(), calls=%async_computation.1 | async-start | bytes 2359296 | tf_op jit(solution)/shard_map/reduce_scatter | solution.py:138
  40.1 6.4 %copy-start.1 = (f32[512,389]{0,1:T(8,128)}, f32[512,389]{0,1:T(8,128)S(1)}, u32[]{:S(2)}) copy-start(f32[512,389]{0,1:T(8,128)S(1)} %get-tuple-element.33) | copy-start | bytes 2390020
  41.0 5.5 %copy-start.16 = (f32[512]{0:T(512)S(1)}, f32[512]{0:T(512)}, u32[]{:S(2)}) copy-start(f32[512]{0:T(512)} %param.9) | copy-start | bytes 6148
  47.5 19.5 %collective-permute-start.7 = (bf16[512,256]{0,1:T(8,128)(2,1)S(1)}, bf16[512,256]{0,1:T(8,128)(2,1)S(1)}, u32[]{:S(2)}, u32[]{:S(2)}) collective-permute-start(bf16[512,256]{0,1:T(8,128)(2,1)S(1)} %fusion.32), channel_id=1, source_target_pairs={{0,24},{8,16},{16,8},{24,0},{1,25},{9,17},{17,9},{25,1},{2,26},{10... | collective-permute-start | bytes 786440 | tf_op jit(solution)/shard_map/ppermute | solution.py:73
  52.0 14.5 %collective-permute-start.6 = (bf16[512,256]{0,1:T(8,128)(2,1)S(1)}, bf16[512,256]{0,1:T(8,128)(2,1)S(1)}, u32[]{:S(2)}, u32[]{:S(2)}) collective-permute-start(bf16[512,256]{0,1:T(8,128)(2,1)S(1)} %fusion.32), channel_id=1, source_target_pairs={{0,16},{8,24},{16,0},{24,8},{1,17},{9,25},{17,1},{25,9},{2,18},{10... | collective-permute-start | bytes 786440 | tf_op jit(solution)/shard_map/ppermute | solution.py:73
  52.8 13.2 %collective-permute-start.5 = (bf16[512,256]{0,1:T(8,128)(2,1)S(1)}, bf16[512,256]{0,1:T(8,128)(2,1)S(1)}, u32[]{:S(2)}, u32[]{:S(2)}) collective-permute-start(bf16[512,256]{0,1:T(8,128)(2,1)S(1)} %fusion.32), channel_id=1, source_target_pairs={{0,8},{8,0},{16,24},{24,16},{1,9},{9,1},{17,25},{25,17},{2,10},{10... | collective-permute-start | bytes 786440 | tf_op jit(solution)/shard_map/ppermute | solution.py:73
  70.0 5.9 %copy-start.3 = (bf16[1024,1024]{1,0:T(8,128)(2,1)S(1)}, bf16[1024,1024]{1,0:T(8,128)(2,1)}, u32[]{:S(2)}) copy-start(bf16[1024,1024]{1,0:T(8,128)(2,1)} %all-gather.2.cloned.1.call-done) | copy-start | bytes 6291460
  73.1 7.2 %collective-permute-start.9 = (bf16[512,256]{0,1:T(8,128)(2,1)S(1)}, bf16[512,256]{0,1:T(8,128)(2,1)S(1)}, u32[]{:S(2)}, u32[]{:S(2)}) collective-permute-start(bf16[512,256]{0,1:T(8,128)(2,1)S(1)} %get-tuple-element.29), channel_id=1, source_target_pairs={{0,8},{8,0},{16,24},{24,16},{1,9},{9,1},{17,25},{25,17},{2,10},{10... | collective-permute-start | bytes 786440 | tf_op jit(solution)/shard_map/ppermute | solution.py:73
  73.2 12.3 %collective-permute-start.11 = (bf16[512,256]{0,1:T(8,128)(2,1)S(1)}, bf16[512,256]{0,1:T(8,128)(2,1)S(1)}, u32[]{:S(2)}, u32[]{:S(2)}) collective-permute-start(bf16[512,256]{0,1:T(8,128)(2,1)S(1)} %get-tuple-element.30), channel_id=1, source_target_pairs={{0,24},{8,16},{16,8},{24,0},{1,25},{9,17},{17,9},{25,1},{2,26},{10... | collective-permute-start | bytes 786440 | tf_op jit(solution)/shard_map/ppermute | solution.py:73
  74.2 11.3 %collective-permute-start.10 = (bf16[512,256]{0,1:T(8,128)(2,1)S(1)}, bf16[512,256]{0,1:T(8,128)(2,1)S(1)}, u32[]{:S(2)}, u32[]{:S(2)}) collective-permute-start(bf16[512,256]{0,1:T(8,128)(2,1)S(1)} %get-tuple-element.31), channel_id=1, source_target_pairs={{0,16},{8,24},{16,0},{24,8},{1,17},{9,25},{17,1},{25,9},{2,18},{10... | collective-permute-start | bytes 786440 | tf_op jit(solution)/shard_map/ppermute | solution.py:73
  77.4 11.5 %copy-start.5 = (bf16[512,256]{0,1:T(8,128)(2,1)S(1)}, bf16[512,256]{0,1:T(8,128)(2,1)}, u32[]{:S(2)}) copy-start(bf16[512,256]{0,1:T(8,128)(2,1)} %copy-done.4) | copy-start | bytes 786436
  85.7 6.7 %collective-permute-start.12 = (bf16[512,133]{0,1:T(8,128)(2,1)S(1)}, bf16[512,133]{0,1:T(8,128)(2,1)S(1)}, u32[]{:S(2)}, u32[]{:S(2)}) collective-permute-start(bf16[512,133]{0,1:T(8,128)(2,1)S(1)} %slice.479), channel_id=1, source_target_pairs={{8,0},{16,8},{24,16},{9,1},{17,9},{25,17},{10,2},{18,10},{26,18},{... | collective-permute-start | bytes 408584 | tf_op jit(solution)/shard_map/ppermute | solution.py:33
  93.5 5.5 %copy-start.2 = (f32[512,389]{0,1:T(8,128)S(1)}, f32[512,389]{0,1:T(8,128)}, u32[]{:S(2)}) copy-start(f32[512,389]{0,1:T(8,128)} %copy-done.1) | copy-start | bytes 2390020
  93.5 5.5 %copy-start.17 = (f32[512]{0:T(512)S(1)}, f32[512]{0:T(512)}, u32[]{:S(2)}) copy-start(f32[512]{0:T(512)} %param.9) | copy-start | bytes 6148
  104.4 21.5 %collective-permute-start.13 = (bf16[512,256]{0,1:T(8,128)(2,1)}, bf16[512,256]{0,1:T(8,128)(2,1)S(1)}, u32[]{:S(2)}, u32[]{:S(2)}) collective-permute-start(bf16[512,256]{0,1:T(8,128)(2,1)} %reduce-scatter.2.cloned.1.call-done), channel_id=1, source_target_pairs={{0,0},{1,1},{2,8},{3,9},{4,16},{5,17},{6,24},{7,25},{8,10},{9,11},... | collective-permute-start | bytes 786440 | tf_op jit(solution)/shard_map/ppermute | solution.py:186
  (11 other events, 18.2 us)
Sparse Core Ops, SparseCore 0:
  38.0 27.4 all-gather.1
  70.0 34.3 reduce-scatter.1
